TPU v7x, 768 devices: a whole 4x8x12 slice. The times are simulated.
768 devices in a mesh: face: 12 (over z), row: 4 (over y_hi), col: 16 (over x, y_lo, core).
Axes of the slice: x: 4, y: 8 (y_hi: 4, y_lo: 2; y = y_hi * 2 + y_lo), z: 12, core: 2. Of those that a mesh axis runs over, the one named last changes fastest.
Arguments:
- state: bfloat16 [12, 128, 8192], P('face', 'row', 'col'), may hold values from -8 to 8
- kernel: bfloat16 [9, 64, 64], replicated, may hold values from -0.25 to 0.25
- gain: float32 [64], replicated, may hold values from 0.1 to 1.9
- shift: float32 [64], replicated, may hold values from -3 to 3
- upstream: bfloat16 [12, 128, 8192], P('face', 'row', 'col'), may hold values from -6 to 6
- face_links: int32 [12, 8, 4], replicated, may hold values from 0 to 11, as said below
Outputs:
- state_grad: bfloat16 [12, 128, 8192], P('face', 'row', 'col')
- kernel_grad: float32 [9, 64, 64], replicated
- gain_grad: float32 [64], replicated
- shift_grad: float32 [64], replicated
Inputs may be any that keep to these rules, and one draw needn't show every extreme that they name: `face_links`: rows 0 to 3 of face f: the face across that side, the side of that face that touches it, the rotation code (that side + 2 - this side) mod 4, and 0. Rows 4 to 7: the face diagonally across that corner, its touching corner, the code (that corner + 2 - this corner) mod 4, and a flag 1 at the 24 face corners where only three faces meet (the face and corner then name the face itself). The links are those of the HEALPix base faces under some numbering of the faces and some quarter turn of each face, so that each link is the reverse of the link it names.
All inputs are finite; a program needn't handle non-finite values.
Results may differ from a plain program's by a relative error of at most 0.0049.
Values may be sent and summed in bfloat16 or wider, within the bound.
No kernel may reach another device: no remote copies, remote signals or barrier semaphores. Data moves between devices by JAX's collectives and lax.ppermute only.
A program may use at most 32 MiB of HBM per device.

v0:
```python
import jax
import jax.numpy as jnp
from jax import lax
from jax.sharding import PartitionSpec as P

FACES = 12


HALF_ROOT = 0.7071067811865476
GAUSS_NORM = 0.3989422804014327


def padded_2(cells, sides, width):
    for axis, dim in sides:
        count = lax.axis_size(axis)
        ends = count - 1
        head = lax.slice_in_dim(cells, 0, width, axis=dim)
        tail = lax.slice_in_dim(cells, cells.shape[dim] - width, cells.shape[dim], axis=dim)
        cells = jnp.concatenate(
            [
                lax.ppermute(tail, axis, [(i, (i + 1) % count) for i in range(ends)]),
                cells,
                lax.ppermute(head, axis, [((i + 1) % count, i) for i in range(ends)]),
            ],
            axis=dim,
        )
    return cells


def gelu_slope(values):
    return (
        0.5 * (1.0 + lax.erf(values * HALF_ROOT))
        + values * jnp.exp(-0.5 * values * values) * GAUSS_NORM
    )


def kernel_tap(row_step, col_step):
    return (row_step + 1) * 3 + (col_step + 1)


def turned_tap(turns, row_step, col_step):
    for repeat in range(turns):
        row_step, col_step = (-col_step, row_step)
    return kernel_tap(-row_step, -col_step)


def channel_pair(first_sum, second_sum):
    return lax.psum((first_sum, second_sum), ("face", "row", "col"))


def lined(first_val, middle_val, last_val, length):
    middle_part = jnp.broadcast_to(middle_val[:, None], (middle_val.shape[0], length))
    return jnp.concatenate([first_val[:, None], middle_part, last_val[:, None]], axis=1)


def on_device(state, kernel, gain, shift, upstream, face_links):
    local_faces = state.shape[0]
    tile_rows = state.shape[1]
    width = kernel.shape[1]
    tile_cols = state.shape[2] // width
    row_count = lax.axis_size("row")
    col_count = lax.axis_size("col")
    side = tile_rows * row_count
    row_index = lax.axis_index("row")
    col_index = lax.axis_index("col")
    face_ids = lax.axis_index("face") * local_faces + jnp.arange(local_faces, dtype=jnp.int32)
    links = face_links[face_ids]
    face_range = jnp.arange(FACES, dtype=jnp.int32)
    side_range = jnp.arange(4, dtype=jnp.int32)
    pixel_rows = local_faces * tile_rows * tile_cols

    def extend(values):
        padded = padded_2(values, (("row", 1), ("col", 2)), 1)
        row_strip = jnp.where(row_index == 0, values[:, 0], values[:, tile_rows - 1])
        col_strip = jnp.where(col_index == 0, values[:, :, 0], values[:, :, tile_cols - 1])
        row_parts, col_parts = (
            lax.all_gather(row_strip[None], ("row", "col"), axis=0, tiled=True),
            lax.all_gather(col_strip[None], ("row", "col"), axis=0, tiled=True),
        )
        row_parts = row_parts.reshape(row_count, col_count, local_faces, tile_cols, width)
        col_parts = col_parts.reshape(row_count, col_count, local_faces, tile_rows, width)
        top_row = jnp.moveaxis(row_parts[0], 0, 1).reshape(local_faces, side, width)
        bottom_row = jnp.moveaxis(row_parts[row_count - 1], 0, 1).reshape(local_faces, side, width)
        left_col = jnp.moveaxis(col_parts[:, 0], 0, 1).reshape(local_faces, side, width)
        right_col = jnp.moveaxis(col_parts[:, col_count - 1], 0, 1).reshape(
            local_faces, side, width
        )
        cycle = jnp.stack([top_row[:, ::-1], left_col, bottom_row, right_col[:, ::-1]], axis=1)
        corner_pix = jnp.stack(
            [top_row[:, 0], bottom_row[:, 0], bottom_row[:, side - 1], top_row[:, side - 1]], axis=1
        )
        all_cycle, all_corner = (
            lax.all_gather(cycle, "face", axis=0, tiled=True),
            lax.all_gather(corner_pix, "face", axis=0, tiled=True),
        )
        side_pick = (
            (links[:, :4, 0][:, :, None, None] == face_range[:, None])
            & (links[:, :4, 1][:, :, None, None] == side_range)
        ).astype(jnp.bfloat16)
        halo_sides = jnp.einsum(
            "ksgt,gtpc->kspc", side_pick, all_cycle, preferred_element_type=jnp.float32
        ).astype(jnp.bfloat16)[:, :, ::-1]
        corner_pick = (
            (links[:, 4:, 0][:, :, None, None] == face_range[:, None])
            & (links[:, 4:, 1][:, :, None, None] == side_range)
            & (links[:, 4:, 3] == 0)[:, :, None, None]
        ).astype(jnp.bfloat16)
        corner_vals = jnp.einsum(
            "kqgt,gtc->kqc", corner_pick, all_corner, preferred_element_type=jnp.float32
        ).astype(jnp.bfloat16)
        full_top = jnp.concatenate(
            [corner_vals[:, 0:1], halo_sides[:, 0, ::-1], corner_vals[:, 3:4]], axis=1
        )
        full_bottom = jnp.concatenate(
            [corner_vals[:, 1:2], halo_sides[:, 2], corner_vals[:, 2:3]], axis=1
        )
        full_left = jnp.concatenate(
            [corner_vals[:, 0:1], halo_sides[:, 1], corner_vals[:, 1:2]], axis=1
        )
        full_right = jnp.concatenate(
            [corner_vals[:, 3:4], halo_sides[:, 3, ::-1], corner_vals[:, 2:3]], axis=1
        )
        top_piece = lax.dynamic_slice_in_dim(full_top, col_index * tile_cols, tile_cols + 2, 1)
        bottom_piece = lax.dynamic_slice_in_dim(
            full_bottom, col_index * tile_cols, tile_cols + 2, 1
        )
        left_piece = lax.dynamic_slice_in_dim(full_left, row_index * tile_rows, tile_rows + 2, 1)
        right_piece = lax.dynamic_slice_in_dim(full_right, row_index * tile_rows, tile_rows + 2, 1)
        padded = padded.at[:, 0].set(jnp.where(row_index == 0, top_piece, padded[:, 0]))
        padded = padded.at[:, tile_rows + 1].set(
            jnp.where(row_index == row_count - 1, bottom_piece, padded[:, tile_rows + 1])
        )
        padded = padded.at[:, :, 0].set(jnp.where(col_index == 0, left_piece, padded[:, :, 0]))
        padded = padded.at[:, :, tile_cols + 1].set(
            jnp.where(col_index == col_count - 1, right_piece, padded[:, :, tile_cols + 1])
        )
        return padded

    values = state.reshape(local_faces, tile_rows, tile_cols, width)
    padded_state = extend(values)

    def window(padded, row_step, col_step):
        return padded[
            :, 1 + row_step : 1 + row_step + tile_rows, 1 + col_step : 1 + col_step + tile_cols
        ].reshape(pixel_rows, width)

    def row_band(padded, row_step):
        return jnp.concatenate(
            [window(padded, row_step, col_step) for col_step in (-1, 0, 1)], axis=1
        )

    state_bands = [row_band(padded_state, row_step) for row_step in (-1, 0, 1)]
    response = jnp.zeros((pixel_rows, width), jnp.float32)
    for position, row_step in enumerate((-1, 0, 1)):
        band_weight = kernel[3 * position : 3 * position + 3].reshape(3 * width, width)
        response = response + jnp.dot(
            state_bands[position], band_weight, preferred_element_type=jnp.float32
        )
    total = float(FACES * side * side)
    sum_first, sum_square = channel_pair(
        jnp.sum(response, axis=0), jnp.sum(response * response, axis=0)
    )
    centre = sum_first / total
    inverse_spread = lax.rsqrt(sum_square / total - centre * centre + 1e-05)
    normed = (response - centre) * inverse_spread
    before = gain * normed + shift
    incoming = upstream.reshape(pixel_rows, width).astype(jnp.float32)
    before_grad = incoming * gelu_slope(before)
    shift_grad, gain_grad = channel_pair(
        jnp.sum(before_grad, axis=0), jnp.sum(before_grad * normed, axis=0)
    )
    response_grad = (
        gain * inverse_spread * (before_grad - shift_grad / total - normed * gain_grad / total)
    ).astype(jnp.bfloat16)
    kernel_terms = []
    for position in range(3):
        band_term = lax.dot_general(
            state_bands[position],
            response_grad,
            (((0,), (0,)), ((), ())),
            preferred_element_type=jnp.float32,
        )
        kernel_terms.append(band_term.reshape(3, width, width))
    kernel_grad = lax.psum(jnp.concatenate(kernel_terms, axis=0), ("face", "row", "col"))
    grad_tile = response_grad.reshape(local_faces, tile_rows, tile_cols, width)
    padded_grad = extend(grad_tile)
    zero_padded = jnp.pad(grad_tile, ((0, 0), (1, 1), (1, 1), (0, 0)))
    state_part = jnp.zeros((pixel_rows, width), jnp.float32)
    for row_step in (-1, 0, 1):
        flipped = jnp.concatenate(
            [kernel[kernel_tap(-row_step, -col_step)].T for col_step in (-1, 0, 1)], axis=0
        )
        state_part = state_part + jnp.dot(
            row_band(zero_padded, row_step), flipped, preferred_element_type=jnp.float32
        )
    state_part = state_part.reshape(local_faces, tile_rows, tile_cols, width)
    side_turns = links[:, :4, 2]
    corner_turns = links[:, 4:, 2]
    full_top_turn = lined(corner_turns[:, 0], side_turns[:, 0], corner_turns[:, 3], side)
    full_bottom_turn = lined(corner_turns[:, 1], side_turns[:, 2], corner_turns[:, 2], side)
    full_left_turn = lined(corner_turns[:, 0], side_turns[:, 1], corner_turns[:, 1], side)
    full_right_turn = lined(corner_turns[:, 3], side_turns[:, 3], corner_turns[:, 2], side)
    top_turn = jnp.where(
        row_index == 0,
        lax.dynamic_slice_in_dim(full_top_turn, col_index * tile_cols, tile_cols + 2, 1),
        0,
    )
    top_turn = top_turn.at[:, 0].set(
        jnp.where(col_index == 0, full_left_turn[:, row_index * tile_rows], top_turn[:, 0])
    )
    top_turn = top_turn.at[:, tile_cols + 1].set(
        jnp.where(
            col_index == col_count - 1,
            full_right_turn[:, row_index * tile_rows],
            top_turn[:, tile_cols + 1],
        )
    )
    bottom_turn = jnp.where(
        row_index == row_count - 1,
        lax.dynamic_slice_in_dim(full_bottom_turn, col_index * tile_cols, tile_cols + 2, 1),
        0,
    )
    bottom_turn = bottom_turn.at[:, 0].set(
        jnp.where(
            col_index == 0,
            full_left_turn[:, row_index * tile_rows + tile_rows + 1],
            bottom_turn[:, 0],
        )
    )
    bottom_turn = bottom_turn.at[:, tile_cols + 1].set(
        jnp.where(
            col_index == col_count - 1,
            full_right_turn[:, row_index * tile_rows + tile_rows + 1],
            bottom_turn[:, tile_cols + 1],
        )
    )
    left_turn = jnp.broadcast_to(
        jnp.where(col_index == 0, side_turns[:, 1], 0)[:, None], (local_faces, tile_rows + 2)
    )
    right_turn = jnp.broadcast_to(
        jnp.where(col_index == col_count - 1, side_turns[:, 3], 0)[:, None],
        (local_faces, tile_rows + 2),
    )

    def strip_terms(strip, turn_codes, steps, length):
        selector = (turn_codes[:, :, None] == side_range).astype(jnp.bfloat16)
        spread = strip[:, :, None, :] * selector[:, :, :, None]
        pieces = jnp.stack(
            [spread[:, 1 + offset : 1 + offset + length] for offset in (-1, 0, 1)], axis=2
        )
        pieces = pieces.reshape(local_faces * length, 12 * width)
        stacked = jnp.concatenate(
            [
                kernel[turned_tap(turn, step_pair[0], step_pair[1])].T
                for step_pair in steps
                for turn in range(4)
            ],
            axis=0,
        )
        summed = jnp.dot(pieces, stacked, preferred_element_type=jnp.float32)
        return summed.reshape(local_faces, length, width)

    left_strip = jnp.pad(padded_grad[:, 1 : tile_rows + 1, 0], ((0, 0), (1, 1), (0, 0)))
    right_strip = jnp.pad(
        padded_grad[:, 1 : tile_rows + 1, tile_cols + 1], ((0, 0), (1, 1), (0, 0))
    )
    top_terms = strip_terms(padded_grad[:, 0], top_turn, ((-1, -1), (-1, 0), (-1, 1)), tile_cols)
    bottom_terms = strip_terms(
        padded_grad[:, tile_rows + 1], bottom_turn, ((1, -1), (1, 0), (1, 1)), tile_cols
    )
    left_terms = strip_terms(left_strip, left_turn, ((-1, -1), (0, -1), (1, -1)), tile_rows)
    right_terms = strip_terms(right_strip, right_turn, ((-1, 1), (0, 1), (1, 1)), tile_rows)
    state_part = state_part.at[:, 0].add(top_terms)
    state_part = state_part.at[:, tile_rows - 1].add(bottom_terms)
    state_part = state_part.at[:, :, 0].add(left_terms)
    state_part = state_part.at[:, :, tile_cols - 1].add(right_terms)
    state_grad = state_part.astype(jnp.bfloat16).reshape(local_faces, tile_rows, tile_cols * width)
    return (state_grad, kernel_grad, gain_grad, shift_grad)


def solution(mesh):
    return jax.shard_map(
        on_device,
        mesh=mesh,
        in_specs=(P("face", "row", "col"), P(), P(), P(), P("face", "row", "col"), P()),
        out_specs=(P("face", "row", "col"), P(), P(), P()),
        check_vma=False,
    )
```

profile of v0, /device:TPU:56, one launch (start us, length us, event | category | flops | bytes accessed | tf_op | source)
XLA Modules:
  0.0 997.7 jit_solution(10749499912005978915)
XLA Ops:
  8.1 1.3 collective-permute-start
  9.4 5.4 collective-permute-start.1
  16.6 63.1 %all_gather.24 = bf16[64,1,8,64]{3,2,1,0:T(8,128)(2,1)S(1)} all-gather(bf16[1,1,8,64]{3,2,1,0:T(8,128)(2,1)S(1)} %get-tuple-element.280), channel_id=1, replica_groups=mesh['face'=12,'row'=4,'col'=16] {'row','col'}, dimensions={0}, use_global_device_ids=true | all-gather | bytes 66560 | tf_op jit(solution)/shard_map/all_gather | solution.py:77
  79.8 32.1 %all_gather.25 = bf16[12,4,64]{2,1,0:T(4,128)(2,1)S(1)} all-gather(bf16[1,4,64]{2,1,0:T(4,128)(2,1)S(1)} %pad_maximum_fusion.21), channel_id=1, replica_groups=mesh['face'=12,'row'=4,'col'=16] {'face'}, dimensions={0}, use_global_device_ids=true | all-gather | bytes 6656 | tf_op jit(solution)/shard_map/all_gather | solution.py:94
  114.0 71.8 %all-gather = bf16[64,32,1,64]{3,1,2,0:T(8,128)(2,1)S(1)} all-gather(bf16[1,32,1,64]{3,1,2,0:T(8,128)(2,1)S(1)} %copy.511), channel_id=2, replica_groups=mesh['face'=12,'row'=4,'col'=16] {'row','col'}, dimensions={0}, use_global_device_ids=true | all-gather | bytes 266240 | tf_op jit(solution)/shard_map/all_gather | solution.py:78
  186.0 24.3 %all_gather.27 = bf16[12,4,128,64]{2,3,1,0:T(8,128)(2,1)S(1)} all-gather(bf16[1,4,128,64]{2,3,1,0:T(8,128)(2,1)S(1)} %pad_maximum_fusion.8), channel_id=1, replica_groups=mesh['face'=12,'row'=4,'col'=16] {'face'}, dimensions={0}, use_global_device_ids=true | all-gather | bytes 851968 | tf_op jit(solution)/shard_map/all_gather | solution.py:93
  214.5 2.5 pad_add_fusion
  222.1 1.3 constant_dynamic-update-slice_fusion.6
  224.1 1.3 broadcast_select_fusion.5
  227.4 1.3 constant_dynamic-update-slice_fusion.7
  229.6 1.9 collective-permute-start.2
  231.5 3.6 collective-permute-start.3
  239.9 112.4 %all-reduce.4 = (f32[64]{0:T(128)S(1)}, f32[64]{0:T(128)S(1)}) all-reduce(f32[64]{0:T(128)S(1)} %get-tuple-element.212, f32[64]{0:T(128)S(1)} %get-tuple-element.211), channel_id=1, replica_groups=mesh['face'=12,'row'=4,'col'=16] {'face','row','col'}, use_global_device_ids=true, to_apply=%region_1.2 | all-reduce | flops 128 | bytes 1024 | tf_op jit(solution)/shard_map/psum | solution.py:48
  353.9 104.5 %all-reduce.3 = (f32[64]{0:T(128)S(1)}, f32[64]{0:T(128)S(1)}) all-reduce(f32[64]{0:T(128)S(1)} %get-tuple-element.210, f32[64]{0:T(128)S(1)} %get-tuple-element.209), channel_id=1, replica_groups=mesh['face'=12,'row'=4,'col'=16] {'face','row','col'}, use_global_device_ids=true, to_apply=%region_7.8 | all-reduce | flops 128 | bytes 1024 | tf_op jit(solution)/shard_map/psum | solution.py:48
  460.1 62.5 %all_gather.28 = bf16[64,1,8,64]{3,2,1,0:T(8,128)(2,1)S(1)} all-gather(bf16[1,1,8,64]{3,2,1,0:T(8,128)(2,1)S(1)} %get-tuple-element.265), channel_id=1, replica_groups=mesh['face'=12,'row'=4,'col'=16] {'row','col'}, dimensions={0}, use_global_device_ids=true | all-gather | bytes 66560 | tf_op jit(solution)/shard_map/all_gather | solution.py:77
  523.5 70.8 %all-gather.1 = bf16[64,32,1,64]{3,1,2,0:T(8,128)(2,1)S(1)} all-gather(bf16[1,32,1,64]{3,1,2,0:T(8,128)(2,1)S(1)} %copy.541), channel_id=3, replica_groups=mesh['face'=12,'row'=4,'col'=16] {'row','col'}, dimensions={0}, use_global_device_ids=true | all-gather | bytes 266240 | tf_op jit(solution)/shard_map/all_gather | solution.py:78
  594.7 26.5 %all_gather.31 = bf16[12,4,128,64]{2,3,1,0:T(8,128)(2,1)S(1)} all-gather(bf16[1,4,128,64]{2,3,1,0:T(8,128)(2,1)S(1)} %pad_maximum_fusion.9), channel_id=1, replica_groups=mesh['face'=12,'row'=4,'col'=16] {'face'}, dimensions={0}, use_global_device_ids=true | all-gather | bytes 851968 | tf_op jit(solution)/shard_map/all_gather | solution.py:93
  622.0 19.6 %all_gather.29 = bf16[12,4,64]{2,1,0:T(4,128)(2,1)S(1)} all-gather(bf16[1,4,64]{2,1,0:T(4,128)(2,1)S(1)} %pad_maximum_fusion.22), channel_id=1, replica_groups=mesh['face'=12,'row'=4,'col'=16] {'face'}, dimensions={0}, use_global_device_ids=true | all-gather | bytes 6656 | tf_op jit(solution)/shard_map/all_gather | solution.py:94
  642.9 13.6 %collective-permute-start.5 = (bf16[1,1,8,64]{3,2,1,0:T(8,128)(2,1)S(1)}, bf16[1,1,8,64]{3,2,1,0:T(8,128)(2,1)S(1)}, u32[]{:S(2)}, u32[]{:S(2)}) collective-permute-start(bf16[1,1,8,64]{3,2,1,0:T(8,128)(2,1)S(1)} %get-tuple-element.266), channel_id=1, source_target_pairs={{16,0},{32,16},{48,32},{17,1},{33,17},{49,33},{18,2},{34,18},{50,3... | collective-permute-start | bytes 3080 | tf_op jit(solution)/shard_map/ppermute | solution.py:23
  658.3 1.9 collective-permute-start.6
  660.2 3.8 collective-permute-start.7
  667.8 1.5 scatter.49
  673.2 316.0 %all-reduce.7.cloned.1.call-done = f32[9,64,64]{2,1,0:T(8,128)} async-done(((f32[9,64,64]{2,1,0:T(8,128)}), f32[9,64,64]{2,1,0:T(8,128)}) %all-reduce.7.cloned.1.call-update) | async-done | bytes 147472 | tf_op jit(solution)/shard_map/psum | solution.py:184
  989.1 1.7 copy.632
  (212 shorter events, 34.0 us)
Async XLA Ops:
  7.2 982.0 %all-reduce.7.cloned.1.call-start = ((), (), s32[]{:S(2)}) async-start(), calls=%async_computation | async-start | bytes 589824 | tf_op jit(solution)/shard_map/psum | solution.py:184
  8.1 221.4 %collective-permute-start = (bf16[1,1,8,64]{3,2,1,0:T(8,128)(2,1)S(1)}, bf16[1,1,8,64]{3,2,1,0:T(8,128)(2,1)S(1)}, u32[]{:S(2)}, u32[]{:S(2)}) collective-permute-start(bf16[1,1,8,64]{3,2,1,0:T(8,128)(2,1)S(1)} %get-tuple-element.282), channel_id=1, source_target_pairs={{0,16},{16,32},{32,48},{1,17},{17,33},{33,49},{2,18},{18,34},{34,5... | collective-permute-start | bytes 3080 | tf_op jit(solution)/shard_map/ppermute | solution.py:21
  9.4 220.1 %collective-permute-start.1 = (bf16[1,1,8,64]{3,2,1,0:T(8,128)(2,1)S(1)}, bf16[1,1,8,64]{3,2,1,0:T(8,128)(2,1)S(1)}, u32[]{:S(2)}, u32[]{:S(2)}) collective-permute-start(bf16[1,1,8,64]{3,2,1,0:T(8,128)(2,1)S(1)} %get-tuple-element.281), channel_id=1, source_target_pairs={{16,0},{32,16},{48,32},{17,1},{33,17},{49,33},{18,2},{34,18},{50,3... | collective-permute-start | bytes 3080 | tf_op jit(solution)/shard_map/ppermute | solution.py:23
  14.9 1.0 copy-start
  111.8 0.7 copy-start.2
  229.6 7.9 collective-permute-start.2
  231.5 6.0 collective-permute-start.3
  236.6 0.8 copy-start.1
  352.3 0.7 copy-start.3
  353.0 0.7 copy-start.4
  458.4 0.5 copy-start.6
  458.4 0.5 copy-start.5
  641.6 16.3 %collective-permute-start.4 = (bf16[1,1,8,64]{3,2,1,0:T(8,128)(2,1)S(1)}, bf16[1,1,8,64]{3,2,1,0:T(8,128)(2,1)S(1)}, u32[]{:S(2)}, u32[]{:S(2)}) collective-permute-start(bf16[1,1,8,64]{3,2,1,0:T(8,128)(2,1)S(1)} %get-tuple-element.267), channel_id=1, source_target_pairs={{0,16},{16,32},{32,48},{1,17},{17,33},{33,49},{2,18},{18,34},{34,5... | collective-permute-start | bytes 3080 | tf_op jit(solution)/shard_map/ppermute | solution.py:21
  642.9 15.1 %collective-permute-start.5 = (bf16[1,1,8,64]{3,2,1,0:T(8,128)(2,1)S(1)}, bf16[1,1,8,64]{3,2,1,0:T(8,128)(2,1)S(1)}, u32[]{:S(2)}, u32[]{:S(2)}) collective-permute-start(bf16[1,1,8,64]{3,2,1,0:T(8,128)(2,1)S(1)} %get-tuple-element.266), channel_id=1, source_target_pairs={{16,0},{32,16},{48,32},{17,1},{33,17},{49,33},{18,2},{34,18},{50,3... | collective-permute-start | bytes 3080 | tf_op jit(solution)/shard_map/ppermute | solution.py:23
  658.3 6.9 collective-permute-start.6
  660.2 5.1 collective-permute-start.7
Sparse Core Ops, SparseCore 0:
  523.6 465.4 all-reduce.6
where the time goes:
time: 1000 us; the launch traced here: 998 us
  blocking collectives  588 us (59%)
  waiting for transfers between devices  316 us (32%)
  starting transfers between devices  33 us (3%)
  local copies, waits for them, and re-layouts  25.3 us (3%)
  between operations  18.9 us (2%)
  other arithmetic  12 us (1%)
    psum x1, waiting for transfers between devices, on_device(): lax.psum(jnp.concatenate(kernel_terms, axis=0), ('face', 'row', 'col'))  316 us
    psum x2, blocking collectives, channel_pair(): return lax.psum((first_sum, second_sum), ('face', 'row', 'col'))  217 us
    all_gather x2, blocking collectives, extend(): lax.all_gather(col_strip[None], ('row', 'col'), axis=0, tiled=True)  143 us
    all_gather x2, blocking collectives, extend(): lax.all_gather(row_strip[None], ('row', 'col'), axis=0, tiled=True)  126 us
    all_gather x2, blocking collectives, extend(): lax.all_gather(corner_pix, 'face', axis=0, tiled=True)  51.7 us
    all_gather x2, blocking collectives, extend(): lax.all_gather(cycle, 'face', axis=0, tiled=True)  50.8 us
    ppermute x4, starting transfers between devices, padded_2(): lax.ppermute(head, axis, [((i + 1) % count, i) for i in range(ends)])  26.5 us
  transfers between devices with their start and end apart: 9, of which 2 were waited for; matrix products, arithmetic and copies ran while one was open for 3% of the time, Pallas kernels for 0%

commit v1 on v0

--- a/solution.py
+++ b/solution.py
@@ -44,8 +44,36 @@
     return kernel_tap(-row_step, -col_step)
 
 
+def nested_sum(values):
+    for axis in ("col", "row", "face"):
+        values = lax.psum(values, axis)
+    return values
+
+
 def channel_pair(first_sum, second_sum):
-    return lax.psum((first_sum, second_sum), ("face", "row", "col"))
+    return nested_sum((first_sum, second_sum))
+
+
+def butterfly(values, axis, count, span=None):
+    span = count if span is None else span
+    step = 1
+    while step < span:
+        values = values + lax.ppermute(values, axis, [(i, i ^ step) for i in range(count)])
+        step *= 2
+    return values
+
+
+def mesh_sum(values):
+    values = butterfly(butterfly(values, "col", lax.axis_size("col")), "row", lax.axis_size("row"))
+    faces = lax.axis_size("face")
+    values = butterfly(values, "face", faces, 4)
+    from_before = lax.ppermute(values, "face", [(i, (i + 4) % faces) for i in range(faces)])
+    from_after = lax.ppermute(values, "face", [(i, (i + 8) % faces) for i in range(faces)])
+    group = lax.axis_index("face") // 4
+    first = jnp.where(group == 0, values, jnp.where(group == 1, from_before, from_after))
+    second = jnp.where(group == 0, from_after, jnp.where(group == 1, values, from_before))
+    third = jnp.where(group == 0, from_before, jnp.where(group == 1, from_after, values))
+    return (first + second) + third
 
 
 def lined(first_val, middle_val, last_val, length):
@@ -73,26 +101,24 @@
         padded = padded_2(values, (("row", 1), ("col", 2)), 1)
         row_strip = jnp.where(row_index == 0, values[:, 0], values[:, tile_rows - 1])
         col_strip = jnp.where(col_index == 0, values[:, :, 0], values[:, :, tile_cols - 1])
-        row_parts, col_parts = (
-            lax.all_gather(row_strip[None], ("row", "col"), axis=0, tiled=True),
-            lax.all_gather(col_strip[None], ("row", "col"), axis=0, tiled=True),
-        )
-        row_parts = row_parts.reshape(row_count, col_count, local_faces, tile_cols, width)
-        col_parts = col_parts.reshape(row_count, col_count, local_faces, tile_rows, width)
-        top_row = jnp.moveaxis(row_parts[0], 0, 1).reshape(local_faces, side, width)
-        bottom_row = jnp.moveaxis(row_parts[row_count - 1], 0, 1).reshape(local_faces, side, width)
-        left_col = jnp.moveaxis(col_parts[:, 0], 0, 1).reshape(local_faces, side, width)
-        right_col = jnp.moveaxis(col_parts[:, col_count - 1], 0, 1).reshape(
+        by_row = lax.all_gather(
+            jnp.concatenate([row_strip, col_strip], axis=1), "row", axis=0, tiled=False
+        )
+        top_seg = by_row[0, :, :tile_cols]
+        bottom_seg = by_row[row_count - 1, :, :tile_cols]
+        side_line = jnp.moveaxis(by_row[:, :, tile_cols:], 0, 1).reshape(local_faces, side, width)
+        by_col = lax.all_gather(
+            jnp.concatenate([top_seg, bottom_seg, side_line], axis=1), "col", axis=0, tiled=False
+        )
+        top_row = jnp.moveaxis(by_col[:, :, :tile_cols], 0, 1).reshape(local_faces, side, width)
+        bottom_row = jnp.moveaxis(by_col[:, :, tile_cols : 2 * tile_cols], 0, 1).reshape(
             local_faces, side, width
         )
+        left_col = by_col[0, :, 2 * tile_cols :]
+        right_col = by_col[col_count - 1, :, 2 * tile_cols :]
         cycle = jnp.stack([top_row[:, ::-1], left_col, bottom_row, right_col[:, ::-1]], axis=1)
-        corner_pix = jnp.stack(
-            [top_row[:, 0], bottom_row[:, 0], bottom_row[:, side - 1], top_row[:, side - 1]], axis=1
-        )
-        all_cycle, all_corner = (
-            lax.all_gather(cycle, "face", axis=0, tiled=True),
-            lax.all_gather(corner_pix, "face", axis=0, tiled=True),
-        )
+        all_cycle = lax.all_gather(cycle, "face", axis=0, tiled=True)
+        all_corner = all_cycle[:, :, side - 1]
         side_pick = (
             (links[:, :4, 0][:, :, None, None] == face_range[:, None])
             & (links[:, :4, 1][:, :, None, None] == side_range)
@@ -181,7 +207,7 @@
             preferred_element_type=jnp.float32,
         )
         kernel_terms.append(band_term.reshape(3, width, width))
-    kernel_grad = lax.psum(jnp.concatenate(kernel_terms, axis=0), ("face", "row", "col"))
+    kernel_grad = mesh_sum(jnp.concatenate(kernel_terms, axis=0))
     grad_tile = response_grad.reshape(local_faces, tile_rows, tile_cols, width)
     padded_grad = extend(grad_tile)
     zero_padded = jnp.pad(grad_tile, ((0, 0), (1, 1), (1, 1), (0, 0)))

time: 1000 us -> 456 us (0.46)
  blocking collectives: 588 us -> 245 us
  waiting for transfers between devices: 316 us -> 95.4 us
  starting transfers between devices: 33 us -> 61.1 us
  between operations: 18.9 us -> 5.48 us
    psum x1 -> x0, waiting for transfers between devices: 316 us -> none  [on_device(): lax.psum(jnp.concatenate(kernel_terms, axis=0), ('face', 'row', 'col'))]
    all_gather x8 -> x6, blocking collectives: 371 us -> 130 us  [the longest x2 57.6 us: extend(): all_cycle = lax.all_gather(cycle, 'face', axis=0, tiled=True)]
    psum x2 -> x6, blocking collectives: 217 us -> 115 us  [nested_sum(): values = lax.psum(values, axis)]
    ppermute x0 -> x10, waiting for transfers between devices: none -> 95.2 us  [the longest x8 74.6 us: butterfly(): lax.ppermute(values, axis, [(i, i ^ step) for i in range(count)])]
    ppermute x0 -> x10, starting transfers between devices: none -> 36.3 us  [the longest x8 26.5 us: butterfly(): lax.ppermute(values, axis, [(i, i ^ step) for i in range(count)])]
  transfers between devices with their start and end apart: 9 -> 18, of which waited for: 2 -> 9; matrix products, arithmetic and copies ran while one was open for 3% -> 7% of each run, Pallas kernels for 0% -> 0%
where the time goes in v1:
time: 456 us; the launch traced here: 451 us
  blocking collectives  245 us (54%)
  waiting for transfers between devices  95.4 us (21%)
  starting transfers between devices  61.1 us (13%)
  local copies, waits for them, and re-layouts  26.3 us (6%)
  other arithmetic  12.3 us (3%)
  between operations  5.48 us (1%)
  matrix products  4.76 us (1%)
    psum x6, blocking collectives, nested_sum(): values = lax.psum(values, axis)  115 us
    ppermute x8, waiting for transfers between devices, butterfly(): lax.ppermute(values, axis, [(i, i ^ step) for i in range(count)])  74.6 us
    all_gather x2, blocking collectives, extend(): all_cycle = lax.all_gather(cycle, 'face', axis=0, tiled=True)  57.6 us
    all_gather x2, blocking collectives, extend(): lax.all_gather(jnp.concatenate([top_seg, bottom_seg, side_line], axis=1),...  45.3 us
    all_gather x2, blocking collectives, extend(): lax.all_gather(jnp.concatenate([row_strip, col_strip], axis=1), 'row', ax...  27.4 us
    ppermute x8, starting transfers between devices, butterfly(): lax.ppermute(values, axis, [(i, i ^ step) for i in range(count)])  26.5 us
    ppermute x1, waiting for transfers between devices, mesh_sum(): lax.ppermute(values, 'face', [(i, (i + 4) % faces) for i in range(faces)])  20.6 us
    ppermute x4, starting transfers between devices, padded_2(): lax.ppermute(head, axis, [((i + 1) % count, i) for i in range(ends)])  18.3 us
  transfers between devices with their start and end apart: 18, of which 9 were waited for; matrix products, arithmetic and copies ran while one was open for 7% of the time, Pallas kernels for 0%

profile of v1, /device:TPU:56, one launch (start us, length us, event | category | flops | bytes accessed | tf_op | source)
XLA Modules:
  0.0 450.6 jit_solution(7712103232530394631)
XLA Ops:
  8.3 13.7 %all-gather = bf16[4,40,64]{2,1,0:T(8,128)(2,1)S(1)} all-gather(bf16[1,40,64]{2,1,0:T(8,128)(2,1)S(1)} %pad_maximum_fusion.23), channel_id=2, replica_groups=mesh['face'=12,'row'=4,'col'=16] {'row'}, dimensions={0}, use_global_device_ids=true | all-gather | bytes 25600 | tf_op jit(solution)/shard_map/all_gather | solution.py:104
  22.5 23.2 %all-gather.1 = bf16[16,144,64]{1,2,0:T(8,128)(2,1)S(1)} all-gather(bf16[1,144,64]{1,2,0:T(8,128)(2,1)S(1)} %pad_maximum_fusion.10), channel_id=3, replica_groups=mesh['face'=12,'row'=4,'col'=16] {'col'}, dimensions={0}, use_global_device_ids=true | all-gather | bytes 313344 | tf_op jit(solution)/shard_map/all_gather | solution.py:110
  47.9 33.3 %all_gather.34 = bf16[12,4,128,64]{2,3,1,0:T(8,128)(2,1)S(1)} all-gather(bf16[1,4,128,64]{2,3,1,0:T(8,128)(2,1)S(1)} %pad_maximum_fusion.8), channel_id=1, replica_groups=mesh['face'=12,'row'=4,'col'=16] {'face'}, dimensions={0}, use_global_device_ids=true | all-gather | bytes 851968 | tf_op jit(solution)/shard_map/all_gather | solution.py:120
  113.5 24.0 %all-reduce.4 = (f32[64]{0:T(128)S(1)}, f32[64]{0:T(128)S(1)}) all-reduce(f32[64]{0:T(128)S(1)} %get-tuple-element.212, f32[64]{0:T(128)S(1)} %get-tuple-element.211), channel_id=1, replica_groups=mesh['face'=12,'row'=4,'col'=16] {'col'}, use_global_device_ids=true, to_apply=%region_1.2 | all-reduce | flops 128 | bytes 1024 | tf_op jit(solution)/shard_map/psum | solution.py:49
  137.5 12.0 %all-reduce.8 = (f32[64]{0:T(128)S(1)}, f32[64]{0:T(128)S(1)}) all-reduce(f32[64]{0:T(128)S(1)} %get-tuple-element.221, f32[64]{0:T(128)S(1)} %get-tuple-element.222), channel_id=1, replica_groups=mesh['face'=12,'row'=4,'col'=16] {'row'}, use_global_device_ids=true, to_apply=%region_2.3 | all-reduce | flops 128 | bytes 1024 | tf_op jit(solution)/shard_map/psum | solution.py:49
  149.5 20.6 %all-reduce.6 = (f32[64]{0:T(128)S(1)}, f32[64]{0:T(128)S(1)}) all-reduce(f32[64]{0:T(128)S(1)} %get-tuple-element.229, f32[64]{0:T(128)S(1)} %get-tuple-element.230), channel_id=1, replica_groups=mesh['face'=12,'row'=4,'col'=16] {'face'}, use_global_device_ids=true, to_apply=%region_3.4 | all-reduce | flops 128 | bytes 1024 | tf_op jit(solution)/shard_map/psum | solution.py:49
  171.6 27.2 %all-reduce.3 = (f32[64]{0:T(128)S(1)}, f32[64]{0:T(128)S(1)}) all-reduce(f32[64]{0:T(128)S(1)} %get-tuple-element.210, f32[64]{0:T(128)S(1)} %get-tuple-element.209), channel_id=1, replica_groups=mesh['face'=12,'row'=4,'col'=16] {'col'}, use_global_device_ids=true, to_apply=%region_13.14 | all-reduce | flops 128 | bytes 1024 | tf_op jit(solution)/shard_map/psum | solution.py:49
  198.8 8.7 %all-reduce.7 = (f32[64]{0:T(128)S(1)}, f32[64]{0:T(128)S(1)}) all-reduce(f32[64]{0:T(128)S(1)} %get-tuple-element.219, f32[64]{0:T(128)S(1)} %get-tuple-element.220), channel_id=1, replica_groups=mesh['face'=12,'row'=4,'col'=16] {'row'}, use_global_device_ids=true, to_apply=%region_14.15 | all-reduce | flops 128 | bytes 1024 | tf_op jit(solution)/shard_map/psum | solution.py:49
  207.5 22.6 %all-reduce.5 = (f32[64]{0:T(128)S(1)}, f32[64]{0:T(128)S(1)}) all-reduce(f32[64]{0:T(128)S(1)} %get-tuple-element.227, f32[64]{0:T(128)S(1)} %get-tuple-element.228), channel_id=1, replica_groups=mesh['face'=12,'row'=4,'col'=16] {'face'}, use_global_device_ids=true, to_apply=%region_15.16 | all-reduce | flops 128 | bytes 1024 | tf_op jit(solution)/shard_map/psum | solution.py:49
  231.7 13.7 %all-gather.2 = bf16[4,40,64]{2,1,0:T(8,128)(2,1)S(1)} all-gather(bf16[1,40,64]{2,1,0:T(8,128)(2,1)S(1)} %pad_maximum_fusion.24), channel_id=4, replica_groups=mesh['face'=12,'row'=4,'col'=16] {'row'}, dimensions={0}, use_global_device_ids=true | all-gather | bytes 25600 | tf_op jit(solution)/shard_map/all_gather | solution.py:104
  245.9 22.1 %all-gather.3 = bf16[16,144,64]{1,2,0:T(8,128)(2,1)S(1)} all-gather(bf16[1,144,64]{1,2,0:T(8,128)(2,1)S(1)} %pad_maximum_fusion.11), channel_id=5, replica_groups=mesh['face'=12,'row'=4,'col'=16] {'col'}, dimensions={0}, use_global_device_ids=true | all-gather | bytes 313344 | tf_op jit(solution)/shard_map/all_gather | solution.py:110
  268.8 24.3 %all_gather.39 = bf16[12,4,128,64]{2,3,1,0:T(8,128)(2,1)S(1)} all-gather(bf16[1,4,128,64]{2,3,1,0:T(8,128)(2,1)S(1)} %pad_maximum_fusion.9), channel_id=1, replica_groups=mesh['face'=12,'row'=4,'col'=16] {'face'}, dimensions={0}, use_global_device_ids=true | all-gather | bytes 851968 | tf_op jit(solution)/shard_map/all_gather | solution.py:120
  297.9 5.5 %collective-permute-start.5 = (bf16[1,1,8,64]{3,2,1,0:T(8,128)(2,1)S(1)}, bf16[1,1,8,64]{3,2,1,0:T(8,128)(2,1)S(1)}, u32[]{:S(2)}, u32[]{:S(2)}) collective-permute-start(bf16[1,1,8,64]{3,2,1,0:T(8,128)(2,1)S(1)} %get-tuple-element.272), channel_id=1, source_target_pairs={{16,0},{32,16},{48,32},{17,1},{33,17},{49,33},{18,2},{34,18},{50,3... | collective-permute-start | bytes 3080 | tf_op jit(solution)/shard_map/ppermute | solution.py:23
  319.9 9.6 %collective-permute-done.9 = f32[9,64,64]{2,1,0:T(8,128)S(1)} collective-permute-done((f32[9,64,64]{2,1,0:T(8,128)S(1)}, f32[9,64,64]{2,1,0:T(8,128)S(1)}, u32[]{:S(2)}, u32[]{:S(2)}) %collective-permute-start.9) | collective-permute-done | bytes 147488 | tf_op jit(solution)/shard_map/ppermute | solution.py:61
  332.0 8.5 %collective-permute-done.10 = f32[9,64,64]{2,1,0:T(8,128)S(1)} collective-permute-done((f32[9,64,64]{2,1,0:T(8,128)S(1)}, f32[9,64,64]{2,1,0:T(8,128)S(1)}, u32[]{:S(2)}, u32[]{:S(2)}) %collective-permute-start.10) | collective-permute-done | bytes 147488 | tf_op jit(solution)/shard_map/ppermute | solution.py:61
  342.6 9.5 %collective-permute-done.11 = f32[9,64,64]{2,1,0:T(8,128)S(1)} collective-permute-done((f32[9,64,64]{2,1,0:T(8,128)S(1)}, f32[9,64,64]{2,1,0:T(8,128)S(1)}, u32[]{:S(2)}, u32[]{:S(2)}) %collective-permute-start.11) | collective-permute-done | bytes 147488 | tf_op jit(solution)/shard_map/ppermute | solution.py:61
  352.2 5.4 %collective-permute-start.12 = (f32[9,64,64]{2,1,0:T(8,128)S(1)}, f32[9,64,64]{2,1,0:T(8,128)S(1)}, u32[]{:S(2)}, u32[]{:S(2)}) collective-permute-start(f32[9,64,64]{2,1,0:T(8,128)S(1)} %add.208), channel_id=1, source_target_pairs={{0,16},{16,0},{32,48},{48,32},{1,17},{17,1},{33,49},{49,33},{2,18}... | collective-permute-start | bytes 442376 | tf_op jit(solution)/shard_map/ppermute | solution.py:61
  357.8 11.5 %collective-permute-done.12 = f32[9,64,64]{2,1,0:T(8,128)S(1)} collective-permute-done((f32[9,64,64]{2,1,0:T(8,128)S(1)}, f32[9,64,64]{2,1,0:T(8,128)S(1)}, u32[]{:S(2)}, u32[]{:S(2)}) %collective-permute-start.12) | collective-permute-done | bytes 147488 | tf_op jit(solution)/shard_map/ppermute | solution.py:61
  369.3 7.0 %collective-permute-start.13 = (f32[9,64,64]{2,1,0:T(8,128)S(1)}, f32[9,64,64]{2,1,0:T(8,128)S(1)}, u32[]{:S(2)}, u32[]{:S(2)}) collective-permute-start(f32[9,64,64]{2,1,0:T(8,128)S(1)} %add.209), channel_id=1, source_target_pairs={{0,32},{16,48},{32,0},{48,16},{1,33},{17,49},{33,1},{49,17},{2,34}... | collective-permute-start | bytes 442376 | tf_op jit(solution)/shard_map/ppermute | solution.py:61
  376.5 13.3 %collective-permute-done.13 = f32[9,64,64]{2,1,0:T(8,128)S(1)} collective-permute-done((f32[9,64,64]{2,1,0:T(8,128)S(1)}, f32[9,64,64]{2,1,0:T(8,128)S(1)}, u32[]{:S(2)}, u32[]{:S(2)}) %collective-permute-start.13) | collective-permute-done | bytes 147488 | tf_op jit(solution)/shard_map/ppermute | solution.py:61
  394.2 7.0 %collective-permute-done.14 = f32[9,64,64]{2,1,0:T(8,128)S(1)} collective-permute-done((f32[9,64,64]{2,1,0:T(8,128)S(1)}, f32[9,64,64]{2,1,0:T(8,128)S(1)}, u32[]{:S(2)}, u32[]{:S(2)}) %collective-permute-start.14) | collective-permute-done | bytes 147488 | tf_op jit(solution)/shard_map/ppermute | solution.py:61
  403.5 15.2 %collective-permute-done.15 = f32[9,64,64]{2,1,0:T(8,128)S(1)} collective-permute-done((f32[9,64,64]{2,1,0:T(8,128)S(1)}, f32[9,64,64]{2,1,0:T(8,128)S(1)}, u32[]{:S(2)}, u32[]{:S(2)}) %collective-permute-start.15) | collective-permute-done | bytes 147488 | tf_op jit(solution)/shard_map/ppermute | solution.py:61
  422.9 5.5 %collective-permute-start.17 = (f32[9,64,64]{2,1,0:T(8,128)S(1)}, f32[9,64,64]{2,1,0:T(8,128)S(1)}, u32[]{:S(2)}, u32[]{:S(2)}) collective-permute-start(f32[9,64,64]{2,1,0:T(8,128)S(1)} %add.212), channel_id=1, source_target_pairs={{0,512},{64,576},{128,640},{192,704},{256,0},{320,64},{384,128},{4... | collective-permute-start | bytes 442376 | tf_op jit(solution)/shard_map/ppermute | solution.py:71
  429.3 20.6 %collective-permute-done.16 = f32[9,64,64]{2,1,0:T(8,128)S(1)} collective-permute-done((f32[9,64,64]{2,1,0:T(8,128)S(1)}, f32[9,64,64]{2,1,0:T(8,128)S(1)}, u32[]{:S(2)}, u32[]{:S(2)}) %collective-permute-start.16) | collective-permute-done | bytes 147488 | tf_op jit(solution)/shard_map/ppermute | solution.py:70
  (249 shorter events, 81.2 us)
Async XLA Ops:
  1.5 101.5 %collective-permute-start = (bf16[1,1,8,64]{3,2,1,0:T(8,128)(2,1)S(1)}, bf16[1,1,8,64]{3,2,1,0:T(8,128)(2,1)S(1)}, u32[]{:S(2)}, u32[]{:S(2)}) collective-permute-start(bf16[1,1,8,64]{3,2,1,0:T(8,128)(2,1)S(1)} %get-tuple-element.288), channel_id=1, source_target_pairs={{0,16},{16,32},{32,48},{1,17},{17,33},{33,49},{2,18},{18,34},{34,5... | collective-permute-start | bytes 3080 | tf_op jit(solution)/shard_map/ppermute | solution.py:21
  2.8 100.3 %collective-permute-start.1 = (bf16[1,1,8,64]{3,2,1,0:T(8,128)(2,1)S(1)}, bf16[1,1,8,64]{3,2,1,0:T(8,128)(2,1)S(1)}, u32[]{:S(2)}, u32[]{:S(2)}) collective-permute-start(bf16[1,1,8,64]{3,2,1,0:T(8,128)(2,1)S(1)} %get-tuple-element.287), channel_id=1, source_target_pairs={{16,0},{32,16},{48,32},{17,1},{33,17},{49,33},{18,2},{34,18},{50,3... | collective-permute-start | bytes 3080 | tf_op jit(solution)/shard_map/ppermute | solution.py:23
  45.7 0.9 copy-start
  82.0 0.7 copy-start.2
  103.1 7.9 %collective-permute-start.2 = (bf16[1,34,1,64]{3,2,1,0:T(2,128)(2,1)S(1)}, bf16[1,34,1,64]{3,2,1,0:T(2,128)(2,1)S(1)}, u32[]{:S(2)}, u32[]{:S(2)}) collective-permute-start(bf16[1,34,1,64]{3,2,1,0:T(2,128)(2,1)S(1)} %get-tuple-element.265), channel_id=1, source_target_pairs={{0,1},{1,2},{2,3},{3,4},{4,5},{5,6},{6,7},{7,8},{8,9},{9,10},{10,1... | collective-permute-start | bytes 13064 | tf_op jit(solution)/shard_map/ppermute | solution.py:21
  105.1 6.0 %collective-permute-start.3 = (bf16[1,34,1,64]{3,2,1,0:T(2,128)(2,1)S(1)}, bf16[1,34,1,64]{3,2,1,0:T(2,128)(2,1)S(1)}, u32[]{:S(2)}, u32[]{:S(2)}) collective-permute-start(bf16[1,34,1,64]{3,2,1,0:T(2,128)(2,1)S(1)} %get-tuple-element.266), channel_id=1, source_target_pairs={{1,0},{2,1},{3,2},{4,3},{5,4},{6,5},{7,6},{8,7},{9,8},{10,9},{11,1... | collective-permute-start | bytes 13064 | tf_op jit(solution)/shard_map/ppermute | solution.py:23
  110.1 0.8 copy-start.1
  170.1 0.7 copy-start.3
  170.8 0.7 copy-start.4
  230.0 0.5 copy-start.5
  294.1 23.6 %collective-permute-start.8 = (f32[9,64,64]{2,1,0:T(8,128)S(1)}, f32[9,64,64]{2,1,0:T(8,128)S(1)}, u32[]{:S(2)}, u32[]{:S(2)}) collective-permute-start(f32[9,64,64]{2,1,0:T(8,128)S(1)} %pad_maximum_fusion), channel_id=1, source_target_pairs={{0,1},{1,0},{2,3},{3,2},{4,5},{5,4},{6,7},{7,6},{8,9},{9,8},{10,11... | collective-permute-start | bytes 442376 | tf_op jit(solution)/shard_map/ppermute | solution.py:61
  296.6 8.1 %collective-permute-start.4 = (bf16[1,1,8,64]{3,2,1,0:T(8,128)(2,1)S(1)}, bf16[1,1,8,64]{3,2,1,0:T(8,128)(2,1)S(1)}, u32[]{:S(2)}, u32[]{:S(2)}) collective-permute-start(bf16[1,1,8,64]{3,2,1,0:T(8,128)(2,1)S(1)} %get-tuple-element.273), channel_id=1, source_target_pairs={{0,16},{16,32},{32,48},{1,17},{17,33},{33,49},{2,18},{18,34},{34,5... | collective-permute-start | bytes 3080 | tf_op jit(solution)/shard_map/ppermute | solution.py:21
  297.9 7.0 %collective-permute-start.5 = (bf16[1,1,8,64]{3,2,1,0:T(8,128)(2,1)S(1)}, bf16[1,1,8,64]{3,2,1,0:T(8,128)(2,1)S(1)}, u32[]{:S(2)}, u32[]{:S(2)}) collective-permute-start(bf16[1,1,8,64]{3,2,1,0:T(8,128)(2,1)S(1)} %get-tuple-element.272), channel_id=1, source_target_pairs={{16,0},{32,16},{48,32},{17,1},{33,17},{49,33},{18,2},{34,18},{50,3... | collective-permute-start | bytes 3080 | tf_op jit(solution)/shard_map/ppermute | solution.py:23
  305.2 6.9 %collective-permute-start.6 = (bf16[1,34,1,64]{1,3,2,0:T(8,128)(2,1)S(1)}, bf16[1,34,1,64]{1,3,2,0:T(8,128)(2,1)S(1)}, u32[]{:S(2)}, u32[]{:S(2)}) collective-permute-start(bf16[1,34,1,64]{1,3,2,0:T(8,128)(2,1)S(1)} %get-tuple-element.242), channel_id=1, source_target_pairs={{0,1},{1,2},{2,3},{3,4},{4,5},{5,6},{6,7},{7,8},{8,9},{9,10},{10,1... | collective-permute-start | bytes 13064 | tf_op jit(solution)/shard_map/ppermute | solution.py:21
  307.2 5.0 %collective-permute-start.7 = (bf16[1,34,1,64]{1,3,2,0:T(8,128)(2,1)S(1)}, bf16[1,34,1,64]{1,3,2,0:T(8,128)(2,1)S(1)}, u32[]{:S(2)}, u32[]{:S(2)}) collective-permute-start(bf16[1,34,1,64]{1,3,2,0:T(8,128)(2,1)S(1)} %get-tuple-element.243), channel_id=1, source_target_pairs={{1,0},{2,1},{3,2},{4,3},{5,4},{6,5},{7,6},{8,7},{9,8},{10,9},{11,1... | collective-permute-start | bytes 13064 | tf_op jit(solution)/shard_map/ppermute | solution.py:23
  317.8 11.8 %collective-permute-start.9 = (f32[9,64,64]{2,1,0:T(8,128)S(1)}, f32[9,64,64]{2,1,0:T(8,128)S(1)}, u32[]{:S(2)}, u32[]{:S(2)}) collective-permute-start(f32[9,64,64]{2,1,0:T(8,128)S(1)} %fusion.129), channel_id=1, source_target_pairs={{0,2},{1,3},{2,0},{3,1},{4,6},{5,7},{6,4},{7,5},{8,10},{9,11},{10,... | collective-permute-start | bytes 442376 | tf_op jit(solution)/shard_map/ppermute | solution.py:61
  329.6 10.9 %collective-permute-start.10 = (f32[9,64,64]{2,1,0:T(8,128)S(1)}, f32[9,64,64]{2,1,0:T(8,128)S(1)}, u32[]{:S(2)}, u32[]{:S(2)}) collective-permute-start(f32[9,64,64]{2,1,0:T(8,128)S(1)} %add.206), channel_id=1, source_target_pairs={{0,4},{1,5},{2,6},{3,7},{4,0},{5,1},{6,2},{7,3},{8,12},{9,13},{10,... | collective-permute-start | bytes 442376 | tf_op jit(solution)/shard_map/ppermute | solution.py:61
  340.5 11.6 %collective-permute-start.11 = (f32[9,64,64]{2,1,0:T(8,128)S(1)}, f32[9,64,64]{2,1,0:T(8,128)S(1)}, u32[]{:S(2)}, u32[]{:S(2)}) collective-permute-start(f32[9,64,64]{2,1,0:T(8,128)S(1)} %add.207), channel_id=1, source_target_pairs={{0,8},{1,9},{2,10},{3,11},{4,12},{5,13},{6,14},{7,15},{8,0},{9,1},... | collective-permute-start | bytes 442376 | tf_op jit(solution)/shard_map/ppermute | solution.py:61
  352.2 17.1 %collective-permute-start.12 = (f32[9,64,64]{2,1,0:T(8,128)S(1)}, f32[9,64,64]{2,1,0:T(8,128)S(1)}, u32[]{:S(2)}, u32[]{:S(2)}) collective-permute-start(f32[9,64,64]{2,1,0:T(8,128)S(1)} %add.208), channel_id=1, source_target_pairs={{0,16},{16,0},{32,48},{48,32},{1,17},{17,1},{33,49},{49,33},{2,18}... | collective-permute-start | bytes 442376 | tf_op jit(solution)/shard_map/ppermute | solution.py:61
  369.3 20.4 %collective-permute-start.13 = (f32[9,64,64]{2,1,0:T(8,128)S(1)}, f32[9,64,64]{2,1,0:T(8,128)S(1)}, u32[]{:S(2)}, u32[]{:S(2)}) collective-permute-start(f32[9,64,64]{2,1,0:T(8,128)S(1)} %add.209), channel_id=1, source_target_pairs={{0,32},{16,48},{32,0},{48,16},{1,33},{17,49},{33,1},{49,17},{2,34}... | collective-permute-start | bytes 442376 | tf_op jit(solution)/shard_map/ppermute | solution.py:61
  389.8 11.3 %collective-permute-start.14 = (f32[9,64,64]{2,1,0:T(8,128)S(1)}, f32[9,64,64]{2,1,0:T(8,128)S(1)}, u32[]{:S(2)}, u32[]{:S(2)}) collective-permute-start(f32[9,64,64]{2,1,0:T(8,128)S(1)} %add.210), channel_id=1, source_target_pairs={{0,64},{64,0},{128,192},{192,128},{256,320},{320,256},{384,448},{4... | collective-permute-start | bytes 442376 | tf_op jit(solution)/shard_map/ppermute | solution.py:61
  401.2 17.4 %collective-permute-start.15 = (f32[9,64,64]{2,1,0:T(8,128)S(1)}, f32[9,64,64]{2,1,0:T(8,128)S(1)}, u32[]{:S(2)}, u32[]{:S(2)}) collective-permute-start(f32[9,64,64]{2,1,0:T(8,128)S(1)} %add.211), channel_id=1, source_target_pairs={{0,128},{64,192},{128,0},{192,64},{256,384},{320,448},{384,256},{4... | collective-permute-start | bytes 442376 | tf_op jit(solution)/shard_map/ppermute | solution.py:61
  418.7 31.2 %collective-permute-start.16 = (f32[9,64,64]{2,1,0:T(8,128)S(1)}, f32[9,64,64]{2,1,0:T(8,128)S(1)}, u32[]{:S(2)}, u32[]{:S(2)}) collective-permute-start(f32[9,64,64]{2,1,0:T(8,128)S(1)} %add.212), channel_id=1, source_target_pairs={{0,256},{64,320},{128,384},{192,448},{256,512},{320,576},{384,640}... | collective-permute-start | bytes 442376 | tf_op jit(solution)/shard_map/ppermute | solution.py:70
  422.9 26.9 %collective-permute-start.17 = (f32[9,64,64]{2,1,0:T(8,128)S(1)}, f32[9,64,64]{2,1,0:T(8,128)S(1)}, u32[]{:S(2)}, u32[]{:S(2)}) collective-permute-start(f32[9,64,64]{2,1,0:T(8,128)S(1)} %add.212), channel_id=1, source_target_pairs={{0,512},{64,576},{128,640},{192,704},{256,0},{320,64},{384,128},{4... | collective-permute-start | bytes 442376 | tf_op jit(solution)/shard_map/ppermute | solution.py:71
  (1 other events, 0.5 us)

commit v2 on v1

--- a/solution.py
+++ b/solution.py
@@ -44,36 +44,78 @@
     return kernel_tap(-row_step, -col_step)
 
 
-def nested_sum(values):
+def nested_sum(values, carried=None):
     for axis in ("col", "row", "face"):
-        values = lax.psum(values, axis)
+        if carried is None:
+            values = lax.psum(values, axis)
+        else:
+            values = carried.beside(lambda part, axis=axis: lax.psum(part, axis), values)
     return values
 
 
-def channel_pair(first_sum, second_sum):
-    return nested_sum((first_sum, second_sum))
-
-
-def butterfly(values, axis, count, span=None):
-    span = count if span is None else span
-    step = 1
-    while step < span:
-        values = values + lax.ppermute(values, axis, [(i, i ^ step) for i in range(count)])
-        step *= 2
-    return values
-
-
-def mesh_sum(values):
-    values = butterfly(butterfly(values, "col", lax.axis_size("col")), "row", lax.axis_size("row"))
+def channel_pair(first_sum, second_sum, carried=None):
+    return nested_sum((first_sum, second_sum), carried)
+
+
+def sum_steps():
+    steps = []
+    for axis in ("col", "row"):
+        count = lax.axis_size(axis)
+        step = 1
+        while step < count:
+            steps.append((axis, [[(i, i ^ step) for i in range(count)]]))
+            step *= 2
     faces = lax.axis_size("face")
-    values = butterfly(values, "face", faces, 4)
-    from_before = lax.ppermute(values, "face", [(i, (i + 4) % faces) for i in range(faces)])
-    from_after = lax.ppermute(values, "face", [(i, (i + 8) % faces) for i in range(faces)])
+    steps.append(("face", [[(i, i ^ 1) for i in range(faces)]]))
+    steps.append(("face", [[(i, i ^ 2) for i in range(faces)]]))
+    steps.append(
+        (
+            "face",
+            [
+                [(i, (i + 4) % faces) for i in range(faces)],
+                [(i, (i + 8) % faces) for i in range(faces)],
+            ],
+        )
+    )
+    return steps
+
+
+def step_send(step, values):
+    axis, pair_sets = step
+    return [lax.ppermute(values, axis, pairs) for pairs in pair_sets]
+
+
+def step_land(step, values, moved):
+    if len(moved) == 1:
+        return values + moved[0]
+    from_before, from_after = moved
     group = lax.axis_index("face") // 4
     first = jnp.where(group == 0, values, jnp.where(group == 1, from_before, from_after))
     second = jnp.where(group == 0, from_after, jnp.where(group == 1, values, from_before))
     third = jnp.where(group == 0, from_before, jnp.where(group == 1, from_after, values))
     return (first + second) + third
+
+
+class Carried:
+    def __init__(self, values):
+        self.values = values
+        self.steps = sum_steps()
+
+    def beside(self, collective, operand):
+        if not self.steps:
+            return collective(operand)
+        step = self.steps.pop(0)
+        values, operand = lax.optimization_barrier((self.values, operand))
+        moved = step_send(step, values)
+        result = collective(operand)
+        self.values = step_land(step, values, moved)
+        return result
+
+    def finish(self):
+        while self.steps:
+            step = self.steps.pop(0)
+            self.values = step_land(step, self.values, step_send(step, self.values))
+        return self.values
 
 
 def lined(first_val, middle_val, last_val, length):
@@ -97,19 +139,21 @@
     side_range = jnp.arange(4, dtype=jnp.int32)
     pixel_rows = local_faces * tile_rows * tile_cols
 
-    def extend(values):
+    def extend(values, carried=None):
+        def gather(part, axis, tiled):
+            def run(operand):
+                return lax.all_gather(operand, axis, axis=0, tiled=tiled)
+
+            return run(part) if carried is None else carried.beside(run, part)
+
         padded = padded_2(values, (("row", 1), ("col", 2)), 1)
         row_strip = jnp.where(row_index == 0, values[:, 0], values[:, tile_rows - 1])
         col_strip = jnp.where(col_index == 0, values[:, :, 0], values[:, :, tile_cols - 1])
-        by_row = lax.all_gather(
-            jnp.concatenate([row_strip, col_strip], axis=1), "row", axis=0, tiled=False
-        )
+        by_row = gather(jnp.concatenate([row_strip, col_strip], axis=1), "row", False)
         top_seg = by_row[0, :, :tile_cols]
         bottom_seg = by_row[row_count - 1, :, :tile_cols]
         side_line = jnp.moveaxis(by_row[:, :, tile_cols:], 0, 1).reshape(local_faces, side, width)
-        by_col = lax.all_gather(
-            jnp.concatenate([top_seg, bottom_seg, side_line], axis=1), "col", axis=0, tiled=False
-        )
+        by_col = gather(jnp.concatenate([top_seg, bottom_seg, side_line], axis=1), "col", False)
         top_row = jnp.moveaxis(by_col[:, :, :tile_cols], 0, 1).reshape(local_faces, side, width)
         bottom_row = jnp.moveaxis(by_col[:, :, tile_cols : 2 * tile_cols], 0, 1).reshape(
             local_faces, side, width
@@ -117,7 +161,7 @@
         left_col = by_col[0, :, 2 * tile_cols :]
         right_col = by_col[col_count - 1, :, 2 * tile_cols :]
         cycle = jnp.stack([top_row[:, ::-1], left_col, bottom_row, right_col[:, ::-1]], axis=1)
-        all_cycle = lax.all_gather(cycle, "face", axis=0, tiled=True)
+        all_cycle = gather(cycle, "face", True)
         all_corner = all_cycle[:, :, side - 1]
         side_pick = (
             (links[:, :4, 0][:, :, None, None] == face_range[:, None])
@@ -192,24 +236,58 @@
     before = gain * normed + shift
     incoming = upstream.reshape(pixel_rows, width).astype(jnp.float32)
     before_grad = incoming * gelu_slope(before)
+    centred = response - centre
+    state_sums = []
+    centred_sums = []
+    slope_sums = []
+    for position in range(3):
+        state_sums.append(jnp.sum(state_bands[position].astype(jnp.float32), axis=0))
+        centred_sums.append(
+            lax.dot_general(
+                state_bands[position],
+                centred,
+                (((0,), (0,)), ((), ())),
+                precision=lax.Precision.HIGHEST,
+                preferred_element_type=jnp.float32,
+            )
+        )
+        slope_sums.append(
+            lax.dot_general(
+                state_bands[position],
+                before_grad,
+                (((0,), (0,)), ((), ())),
+                precision=lax.Precision.HIGHEST,
+                preferred_element_type=jnp.float32,
+            )
+        )
+    taps = 9
+    carried = Carried(
+        jnp.concatenate(
+            [
+                jnp.stack(slope_sums).reshape(-1),
+                jnp.stack(centred_sums).reshape(-1),
+                jnp.stack(state_sums).reshape(-1),
+            ]
+        )
+    )
     shift_grad, gain_grad = channel_pair(
-        jnp.sum(before_grad, axis=0), jnp.sum(before_grad * normed, axis=0)
+        jnp.sum(before_grad, axis=0), jnp.sum(before_grad * normed, axis=0), carried
     )
     response_grad = (
         gain * inverse_spread * (before_grad - shift_grad / total - normed * gain_grad / total)
     ).astype(jnp.bfloat16)
-    kernel_terms = []
-    for position in range(3):
-        band_term = lax.dot_general(
-            state_bands[position],
-            response_grad,
-            (((0,), (0,)), ((), ())),
-            preferred_element_type=jnp.float32,
-        )
-        kernel_terms.append(band_term.reshape(3, width, width))
-    kernel_grad = mesh_sum(jnp.concatenate(kernel_terms, axis=0))
     grad_tile = response_grad.reshape(local_faces, tile_rows, tile_cols, width)
-    padded_grad = extend(grad_tile)
+    padded_grad = extend(grad_tile, carried)
+    kernel_sums = carried.finish()
+    block = taps * width * width
+    slope_total = kernel_sums[:block].reshape(taps, width, width)
+    centred_total = kernel_sums[block : 2 * block].reshape(taps, width, width)
+    state_total = kernel_sums[2 * block :].reshape(taps, width, 1)
+    kernel_grad = (gain * inverse_spread) * (
+        slope_total
+        - state_total * (shift_grad / total)
+        - centred_total * (gain_grad * inverse_spread / total)
+    )
     zero_padded = jnp.pad(grad_tile, ((0, 0), (1, 1), (1, 1), (0, 0)))
     state_part = jnp.zeros((pixel_rows, width), jnp.float32)
     for row_step in (-1, 0, 1):

time: 456 us -> 438 us (0.961)
  the two profiles are of different devices: /device:TPU:56 before, /device:TPU:136 now
where the time goes in v2:
time: 438 us; the launch traced here: 437 us
  blocking collectives  241 us (55%)
  waiting for transfers between devices  81.1 us (19%)
  starting transfers between devices  61.6 us (14%)
  local copies, waits for them, and re-layouts  28.5 us (7%)
  other arithmetic  13.1 us (3%)
  matrix products  5.66 us (1%)
  between operations  5.66 us (1%)
    all_gather x6, blocking collectives, run(): return lax.all_gather(operand, axis, axis=0, tiled=tiled)  125 us
    ppermute x10, waiting for transfers between devices, step_send(): return [lax.ppermute(values, axis, pairs) for pairs in pair_sets]  75.4 us
    psum x3, blocking collectives, nested_sum(): lax.psum(part, axis)  62.4 us
    psum x3, blocking collectives, nested_sum(): values = lax.psum(values, axis)  54 us
    ppermute x10, starting transfers between devices, step_send(): return [lax.ppermute(values, axis, pairs) for pairs in pair_sets]  40.5 us
    ppermute x4, starting transfers between devices, padded_2(): lax.ppermute(tail, axis, [(i, (i + 1) % count) for i in range(ends)])  11.2 us
    ppermute x4, starting transfers between devices, padded_2(): lax.ppermute(head, axis, [((i + 1) % count, i) for i in range(ends)])  9.87 us
  transfers between devices with their start and end apart: 18, of which 9 were waited for; matrix products, arithmetic and copies ran while one was open for 6% of the time, Pallas kernels for 0%

profile of v2, /device:TPU:136, one launch (start us, length us, event | category | flops | bytes accessed | tf_op | source)
XLA Modules:
  0.0 436.8 jit_solution(8100966812954027829)
XLA Ops:
  1.5 4.5 %collective-permute-start = (bf16[1,1,8,64]{3,2,1,0:T(8,128)(2,1)S(1)}, bf16[1,1,8,64]{3,2,1,0:T(8,128)(2,1)S(1)}, u32[]{:S(2)}, u32[]{:S(2)}) collective-permute-start(bf16[1,1,8,64]{3,2,1,0:T(8,128)(2,1)S(1)} %get-tuple-element.320), channel_id=1, source_target_pairs={{0,16},{16,32},{32,48},{1,17},{17,33},{33,49},{2,18},{18,34},{34,5... | collective-permute-start | bytes 3080 | tf_op jit(solution)/shard_map/ppermute | solution.py:21
  7.4 17.3 %all-gather = bf16[4,40,64]{2,1,0:T(8,128)(2,1)S(1)} all-gather(bf16[1,40,64]{2,1,0:T(8,128)(2,1)S(1)} %pad_maximum_fusion.19), channel_id=2, replica_groups=mesh['face'=12,'row'=4,'col'=16] {'row'}, dimensions={0}, use_global_device_ids=true | all-gather | bytes 25600 | tf_op jit(solution)/shard_map/all_gather | solution.py:145
  25.1 19.3 %all-gather.1 = bf16[16,144,64]{1,2,0:T(8,128)(2,1)S(1)} all-gather(bf16[1,144,64]{1,2,0:T(8,128)(2,1)S(1)} %pad_maximum_fusion.12), channel_id=3, replica_groups=mesh['face'=12,'row'=4,'col'=16] {'col'}, dimensions={0}, use_global_device_ids=true | all-gather | bytes 313344 | tf_op jit(solution)/shard_map/all_gather | solution.py:145
  46.0 33.3 %all_gather.34 = bf16[12,4,128,64]{2,3,1,0:T(8,128)(2,1)S(1)} all-gather(bf16[1,4,128,64]{2,3,1,0:T(8,128)(2,1)S(1)} %pad_maximum_fusion.10), channel_id=1, replica_groups=mesh['face'=12,'row'=4,'col'=16] {'face'}, dimensions={0}, use_global_device_ids=true | all-gather | bytes 851968 | tf_op jit(solution)/shard_map/all_gather | solution.py:145
  112.2 24.1 %all-reduce.4 = (f32[64]{0:T(128)S(1)}, f32[64]{0:T(128)S(1)}) all-reduce(f32[64]{0:T(128)S(1)} %get-tuple-element.242, f32[64]{0:T(128)S(1)} %get-tuple-element.241), channel_id=1, replica_groups=mesh['face'=12,'row'=4,'col'=16] {'col'}, use_global_device_ids=true, to_apply=%region_1.2 | all-reduce | flops 128 | bytes 1024 | tf_op jit(solution)/shard_map/psum | solution.py:50
  136.3 9.4 %all-reduce.8 = (f32[64]{0:T(128)S(1)}, f32[64]{0:T(128)S(1)}) all-reduce(f32[64]{0:T(128)S(1)} %get-tuple-element.251, f32[64]{0:T(128)S(1)} %get-tuple-element.252), channel_id=1, replica_groups=mesh['face'=12,'row'=4,'col'=16] {'row'}, use_global_device_ids=true, to_apply=%region_2.3 | all-reduce | flops 128 | bytes 1024 | tf_op jit(solution)/shard_map/psum | solution.py:50
  145.7 20.6 %all-reduce.6 = (f32[64]{0:T(128)S(1)}, f32[64]{0:T(128)S(1)}) all-reduce(f32[64]{0:T(128)S(1)} %get-tuple-element.259, f32[64]{0:T(128)S(1)} %get-tuple-element.260), channel_id=1, replica_groups=mesh['face'=12,'row'=4,'col'=16] {'face'}, use_global_device_ids=true, to_apply=%region_3.4 | all-reduce | flops 128 | bytes 1024 | tf_op jit(solution)/shard_map/psum | solution.py:50
  172.7 27.6 %all-reduce.3 = (f32[64]{0:T(128)S(1)}, f32[64]{0:T(128)S(1)}) all-reduce(f32[64]{0:T(128)S(1)} %get-tuple-element.212, f32[64]{0:T(128)S(1)} %get-tuple-element.213), channel_id=1, replica_groups=mesh['face'=12,'row'=4,'col'=16] {'col'}, use_global_device_ids=true, to_apply=%region_13.14 | all-reduce | flops 128 | bytes 1024 | tf_op jit(solution)/shard_map/psum | solution.py:52
  200.3 6.3 %collective-permute-start.5 = (f32[74304]{0:T(1024)S(1)}, f32[74304]{0:T(1024)S(1)}, u32[]{:S(2)}, u32[]{:S(2)}) collective-permute-start(f32[74304]{0:T(1024)S(1)} %add.197), channel_id=1, source_target_pairs={{0,2},{1,3},{2,0},{3,1},{4,6},{5,7},{6,4},{7,5},{8,10},{9,11},{10,... | collective-permute-start | bytes 891656 | tf_op jit(solution)/shard_map/ppermute | solution.py:85
  206.7 12.2 %all-reduce.7 = (f32[64]{0:T(128)S(1)}, f32[64]{0:T(128)S(1)}) all-reduce(f32[64]{0:T(128)S(1)} %get-tuple-element.215, f32[64]{0:T(128)S(1)} %get-tuple-element.216), channel_id=1, replica_groups=mesh['face'=12,'row'=4,'col'=16] {'row'}, use_global_device_ids=true, to_apply=%region_15.16 | all-reduce | flops 128 | bytes 1024 | tf_op jit(solution)/shard_map/psum | solution.py:52
  218.9 22.6 %all-reduce.5 = (f32[64]{0:T(128)S(1)}, f32[64]{0:T(128)S(1)}) all-reduce(f32[64]{0:T(128)S(1)} %get-tuple-element.218, f32[64]{0:T(128)S(1)} %get-tuple-element.217), channel_id=1, replica_groups=mesh['face'=12,'row'=4,'col'=16] {'face'}, use_global_device_ids=true, to_apply=%region_18.19 | all-reduce | flops 128 | bytes 1024 | tf_op jit(solution)/shard_map/psum | solution.py:52
  261.9 13.8 %all-gather.2 = bf16[4,40,64]{2,1,0:T(8,128)(2,1)S(1)} all-gather(bf16[1,40,64]{2,1,0:T(8,128)(2,1)S(1)} %pad_maximum_fusion.20), channel_id=4, replica_groups=mesh['face'=12,'row'=4,'col'=16] {'row'}, dimensions={0}, use_global_device_ids=true | all-gather | bytes 25600 | tf_op jit(solution)/shard_map/all_gather | solution.py:145
  278.0 10.6 %collective-permute-done.11 = f32[74304]{0:T(1024)S(1)} collective-permute-done((f32[74304]{0:T(1024)S(1)}, f32[74304]{0:T(1024)S(1)}, u32[]{:S(2)}, u32[]{:S(2)}) %collective-permute-start.11) | collective-permute-done | bytes 297248 | tf_op jit(solution)/shard_map/ppermute | solution.py:85
  288.6 16.5 %all-gather.3 = bf16[16,144,64]{1,2,0:T(8,128)(2,1)S(1)} all-gather(bf16[1,144,64]{1,2,0:T(8,128)(2,1)S(1)} %pad_maximum_fusion.13), channel_id=5, replica_groups=mesh['face'=12,'row'=4,'col'=16] {'col'}, dimensions={0}, use_global_device_ids=true | all-gather | bytes 313344 | tf_op jit(solution)/shard_map/all_gather | solution.py:145
  305.8 5.1 %collective-permute-start.12 = (f32[74304]{0:T(1024)S(1)}, f32[74304]{0:T(1024)S(1)}, u32[]{:S(2)}, u32[]{:S(2)}) collective-permute-start(f32[74304]{0:T(1024)S(1)} %add.202), channel_id=1, source_target_pairs={{0,16},{16,0},{32,48},{48,32},{1,17},{17,1},{33,49},{49,33},{2,18}... | collective-permute-start | bytes 891656 | tf_op jit(solution)/shard_map/ppermute | solution.py:85
  311.1 13.1 %collective-permute-done.12 = f32[74304]{0:T(1024)S(1)} collective-permute-done((f32[74304]{0:T(1024)S(1)}, f32[74304]{0:T(1024)S(1)}, u32[]{:S(2)}, u32[]{:S(2)}) %collective-permute-start.12) | collective-permute-done | bytes 297248 | tf_op jit(solution)/shard_map/ppermute | solution.py:85
  324.2 24.5 %all_gather.39 = bf16[12,4,128,64]{2,3,1,0:T(8,128)(2,1)S(1)} all-gather(bf16[1,4,128,64]{2,3,1,0:T(8,128)(2,1)S(1)} %pad_maximum_fusion.11), channel_id=1, replica_groups=mesh['face'=12,'row'=4,'col'=16] {'face'}, dimensions={0}, use_global_device_ids=true | all-gather | bytes 851968 | tf_op jit(solution)/shard_map/all_gather | solution.py:145
  356.1 4.8 %collective-permute-start.13 = (f32[74304]{0:T(1024)S(1)}, f32[74304]{0:T(1024)S(1)}, u32[]{:S(2)}, u32[]{:S(2)}) collective-permute-start(f32[74304]{0:T(1024)S(1)} %add.203), channel_id=1, source_target_pairs={{0,32},{16,48},{32,0},{48,16},{1,33},{17,49},{33,1},{49,17},{2,34}... | collective-permute-start | bytes 891656 | tf_op jit(solution)/shard_map/ppermute | solution.py:85
  362.0 12.4 %collective-permute-done.13 = f32[74304]{0:T(1024)S(1)} collective-permute-done((f32[74304]{0:T(1024)S(1)}, f32[74304]{0:T(1024)S(1)}, u32[]{:S(2)}, u32[]{:S(2)}) %collective-permute-start.13) | collective-permute-done | bytes 297248 | tf_op jit(solution)/shard_map/ppermute | solution.py:85
  378.3 6.0 %collective-permute-done.14 = f32[74304]{0:T(1024)S(1)} collective-permute-done((f32[74304]{0:T(1024)S(1)}, f32[74304]{0:T(1024)S(1)}, u32[]{:S(2)}, u32[]{:S(2)}) %collective-permute-start.14) | collective-permute-done | bytes 297248 | tf_op jit(solution)/shard_map/ppermute | solution.py:85
  384.3 5.4 %collective-permute-start.15 = (f32[74304]{0:T(1024)S(1)}, f32[74304]{0:T(1024)S(1)}, u32[]{:S(2)}, u32[]{:S(2)}) collective-permute-start(f32[74304]{0:T(1024)S(1)} %add.211), channel_id=1, source_target_pairs={{0,128},{64,192},{128,0},{192,64},{256,384},{320,448},{384,256},{4... | collective-permute-start | bytes 891656 | tf_op jit(solution)/shard_map/ppermute | solution.py:85
  390.1 18.9 %collective-permute-done.15 = f32[74304]{0:T(1024)S(1)} collective-permute-done((f32[74304]{0:T(1024)S(1)}, f32[74304]{0:T(1024)S(1)}, u32[]{:S(2)}, u32[]{:S(2)}) %collective-permute-start.15) | collective-permute-done | bytes 297248 | tf_op jit(solution)/shard_map/ppermute | solution.py:85
  413.3 5.5 %collective-permute-start.17 = (f32[74304]{0:T(1024)S(1)}, f32[74304]{0:T(1024)S(1)}, u32[]{:S(2)}, u32[]{:S(2)}) collective-permute-start(f32[74304]{0:T(1024)S(1)} %add.212), channel_id=1, source_target_pairs={{0,512},{64,576},{128,640},{192,704},{256,0},{320,64},{384,128},{4... | collective-permute-start | bytes 891656 | tf_op jit(solution)/shard_map/ppermute | solution.py:85
  422.3 12.0 %collective-permute-done.17 = f32[74304]{0:T(1024)S(1)} collective-permute-done((f32[74304]{0:T(1024)S(1)}, f32[74304]{0:T(1024)S(1)}, u32[]{:S(2)}, u32[]{:S(2)}) %collective-permute-start.17) | collective-permute-done | bytes 297248 | tf_op jit(solution)/shard_map/ppermute | solution.py:85
  (273 shorter events, 85.6 us)
Async XLA Ops:
  1.5 90.5 %collective-permute-start = (bf16[1,1,8,64]{3,2,1,0:T(8,128)(2,1)S(1)}, bf16[1,1,8,64]{3,2,1,0:T(8,128)(2,1)S(1)}, u32[]{:S(2)}, u32[]{:S(2)}) collective-permute-start(bf16[1,1,8,64]{3,2,1,0:T(8,128)(2,1)S(1)} %get-tuple-element.320), channel_id=1, source_target_pairs={{0,16},{16,32},{32,48},{1,17},{17,33},{33,49},{2,18},{18,34},{34,5... | collective-permute-start | bytes 3080 | tf_op jit(solution)/shard_map/ppermute | solution.py:21
  6.0 86.0 %collective-permute-start.1 = (bf16[1,1,8,64]{3,2,1,0:T(8,128)(2,1)S(1)}, bf16[1,1,8,64]{3,2,1,0:T(8,128)(2,1)S(1)}, u32[]{:S(2)}, u32[]{:S(2)}) collective-permute-start(bf16[1,1,8,64]{3,2,1,0:T(8,128)(2,1)S(1)} %get-tuple-element.319), channel_id=1, source_target_pairs={{16,0},{32,16},{48,32},{17,1},{33,17},{49,33},{18,2},{34,18},{50,3... | collective-permute-start | bytes 3080 | tf_op jit(solution)/shard_map/ppermute | solution.py:23
  44.4 0.9 copy-start.1
  80.0 0.7 copy-start.3
  92.1 17.8 %collective-permute-start.2 = (bf16[1,34,1,64]{3,2,1,0:T(2,128)(2,1)S(1)}, bf16[1,34,1,64]{3,2,1,0:T(2,128)(2,1)S(1)}, u32[]{:S(2)}, u32[]{:S(2)}) collective-permute-start(bf16[1,34,1,64]{3,2,1,0:T(2,128)(2,1)S(1)} %get-tuple-element.297), channel_id=1, source_target_pairs={{0,1},{1,2},{2,3},{3,4},{4,5},{5,6},{6,7},{7,8},{8,9},{9,10},{10,1... | collective-permute-start | bytes 13064 | tf_op jit(solution)/shard_map/ppermute | solution.py:21
  94.0 15.9 %collective-permute-start.3 = (bf16[1,34,1,64]{3,2,1,0:T(2,128)(2,1)S(1)}, bf16[1,34,1,64]{3,2,1,0:T(2,128)(2,1)S(1)}, u32[]{:S(2)}, u32[]{:S(2)}) collective-permute-start(bf16[1,34,1,64]{3,2,1,0:T(2,128)(2,1)S(1)} %get-tuple-element.298), channel_id=1, source_target_pairs={{1,0},{2,1},{3,2},{4,3},{5,4},{6,5},{7,6},{8,7},{9,8},{10,9},{11,1... | collective-permute-start | bytes 13064 | tf_op jit(solution)/shard_map/ppermute | solution.py:23
  99.0 0.8 copy-start.2
  170.7 29.6 %collective-permute-start.4 = (f32[74304]{0:T(1024)S(1)}, f32[74304]{0:T(1024)S(1)}, u32[]{:S(2)}, u32[]{:S(2)}) collective-permute-start(f32[74304]{0:T(1024)S(1)} %pad_maximum_fusion), channel_id=1, source_target_pairs={{0,1},{1,0},{2,3},{3,2},{4,5},{5,4},{6,7},{7,6},{8,9},{9,8},{10,11... | collective-permute-start | bytes 891656 | tf_op jit(solution)/shard_map/ppermute | solution.py:85
  200.3 18.5 %collective-permute-start.5 = (f32[74304]{0:T(1024)S(1)}, f32[74304]{0:T(1024)S(1)}, u32[]{:S(2)}, u32[]{:S(2)}) collective-permute-start(f32[74304]{0:T(1024)S(1)} %add.197), channel_id=1, source_target_pairs={{0,2},{1,3},{2,0},{3,1},{4,6},{5,7},{6,4},{7,5},{8,10},{9,11},{10,... | collective-permute-start | bytes 891656 | tf_op jit(solution)/shard_map/ppermute | solution.py:85
  241.5 0.8 copy-start.6
  242.5 19.4 %collective-permute-start.10 = (f32[74304]{0:T(1024)S(1)}, f32[74304]{0:T(1024)S(1)}, u32[]{:S(2)}, u32[]{:S(2)}) collective-permute-start(f32[74304]{0:T(1024)S(1)} %add.198), channel_id=1, source_target_pairs={{0,4},{1,5},{2,6},{3,7},{4,0},{5,1},{6,2},{7,3},{8,12},{9,13},{10,... | collective-permute-start | bytes 891656 | tf_op jit(solution)/shard_map/ppermute | solution.py:85
  244.4 5.2 %collective-permute-start.6 = (bf16[1,1,8,64]{3,2,1,0:T(8,128)(2,1)S(1)}, bf16[1,1,8,64]{3,2,1,0:T(8,128)(2,1)S(1)}, u32[]{:S(2)}, u32[]{:S(2)}) collective-permute-start(bf16[1,1,8,64]{3,2,1,0:T(8,128)(2,1)S(1)} %get-tuple-element.305), channel_id=1, source_target_pairs={{0,16},{16,32},{32,48},{1,17},{17,33},{33,49},{2,18},{18,34},{34,5... | collective-permute-start | bytes 3080 | tf_op jit(solution)/shard_map/ppermute | solution.py:21
  247.2 6.4 %collective-permute-start.7 = (bf16[1,1,8,64]{3,2,1,0:T(8,128)(2,1)S(1)}, bf16[1,1,8,64]{3,2,1,0:T(8,128)(2,1)S(1)}, u32[]{:S(2)}, u32[]{:S(2)}) collective-permute-start(bf16[1,1,8,64]{3,2,1,0:T(8,128)(2,1)S(1)} %get-tuple-element.304), channel_id=1, source_target_pairs={{16,0},{32,16},{48,32},{17,1},{33,17},{49,33},{18,2},{34,18},{50,3... | collective-permute-start | bytes 3080 | tf_op jit(solution)/shard_map/ppermute | solution.py:23
  253.9 5.7 %collective-permute-start.8 = (bf16[1,34,1,64]{1,3,2,0:T(8,128)(2,1)S(1)}, bf16[1,34,1,64]{1,3,2,0:T(8,128)(2,1)S(1)}, u32[]{:S(2)}, u32[]{:S(2)}) collective-permute-start(bf16[1,34,1,64]{1,3,2,0:T(8,128)(2,1)S(1)} %get-tuple-element.272), channel_id=1, source_target_pairs={{0,1},{1,2},{2,3},{3,4},{4,5},{5,6},{6,7},{7,8},{8,9},{9,10},{10,1... | collective-permute-start | bytes 13064 | tf_op jit(solution)/shard_map/ppermute | solution.py:21
  255.8 5.7 %collective-permute-start.9 = (bf16[1,34,1,64]{1,3,2,0:T(8,128)(2,1)S(1)}, bf16[1,34,1,64]{1,3,2,0:T(8,128)(2,1)S(1)}, u32[]{:S(2)}, u32[]{:S(2)}) collective-permute-start(bf16[1,34,1,64]{1,3,2,0:T(8,128)(2,1)S(1)} %get-tuple-element.273), channel_id=1, source_target_pairs={{1,0},{2,1},{3,2},{4,3},{5,4},{6,5},{7,6},{8,7},{9,8},{10,9},{11,1... | collective-permute-start | bytes 13064 | tf_op jit(solution)/shard_map/ppermute | solution.py:23
  275.7 12.8 %collective-permute-start.11 = (f32[74304]{0:T(1024)S(1)}, f32[74304]{0:T(1024)S(1)}, u32[]{:S(2)}, u32[]{:S(2)}) collective-permute-start(f32[74304]{0:T(1024)S(1)} %add.201), channel_id=1, source_target_pairs={{0,8},{1,9},{2,10},{3,11},{4,12},{5,13},{6,14},{7,15},{8,0},{9,1},... | collective-permute-start | bytes 891656 | tf_op jit(solution)/shard_map/ppermute | solution.py:85
  305.8 18.3 %collective-permute-start.12 = (f32[74304]{0:T(1024)S(1)}, f32[74304]{0:T(1024)S(1)}, u32[]{:S(2)}, u32[]{:S(2)}) collective-permute-start(f32[74304]{0:T(1024)S(1)} %add.202), channel_id=1, source_target_pairs={{0,16},{16,0},{32,48},{48,32},{1,17},{17,1},{33,49},{49,33},{2,18}... | collective-permute-start | bytes 891656 | tf_op jit(solution)/shard_map/ppermute | solution.py:85
  356.1 18.3 %collective-permute-start.13 = (f32[74304]{0:T(1024)S(1)}, f32[74304]{0:T(1024)S(1)}, u32[]{:S(2)}, u32[]{:S(2)}) collective-permute-start(f32[74304]{0:T(1024)S(1)} %add.203), channel_id=1, source_target_pairs={{0,32},{16,48},{32,0},{48,16},{1,33},{17,49},{33,1},{49,17},{2,34}... | collective-permute-start | bytes 891656 | tf_op jit(solution)/shard_map/ppermute | solution.py:85
  374.4 9.9 %collective-permute-start.14 = (f32[74304]{0:T(1024)S(1)}, f32[74304]{0:T(1024)S(1)}, u32[]{:S(2)}, u32[]{:S(2)}) collective-permute-start(f32[74304]{0:T(1024)S(1)} %add.210), channel_id=1, source_target_pairs={{0,64},{64,0},{128,192},{192,128},{256,320},{320,256},{384,448},{4... | collective-permute-start | bytes 891656 | tf_op jit(solution)/shard_map/ppermute | solution.py:85
  384.3 24.7 %collective-permute-start.15 = (f32[74304]{0:T(1024)S(1)}, f32[74304]{0:T(1024)S(1)}, u32[]{:S(2)}, u32[]{:S(2)}) collective-permute-start(f32[74304]{0:T(1024)S(1)} %add.211), channel_id=1, source_target_pairs={{0,128},{64,192},{128,0},{192,64},{256,384},{320,448},{384,256},{4... | collective-permute-start | bytes 891656 | tf_op jit(solution)/shard_map/ppermute | solution.py:85
  409.1 13.2 %collective-permute-start.16 = (f32[74304]{0:T(1024)S(1)}, f32[74304]{0:T(1024)S(1)}, u32[]{:S(2)}, u32[]{:S(2)}) collective-permute-start(f32[74304]{0:T(1024)S(1)} %add.212), channel_id=1, source_target_pairs={{0,256},{64,320},{128,384},{192,448},{256,512},{320,576},{384,640}... | collective-permute-start | bytes 891656 | tf_op jit(solution)/shard_map/ppermute | solution.py:85
  413.3 20.9 %collective-permute-start.17 = (f32[74304]{0:T(1024)S(1)}, f32[74304]{0:T(1024)S(1)}, u32[]{:S(2)}, u32[]{:S(2)}) collective-permute-start(f32[74304]{0:T(1024)S(1)} %add.212), channel_id=1, source_target_pairs={{0,512},{64,576},{128,640},{192,704},{256,0},{320,64},{384,128},{4... | collective-permute-start | bytes 891656 | tf_op jit(solution)/shard_map/ppermute | solution.py:85
  434.3 0.7 copy-start
  435.1 0.7 slice-start
  (3 other events, 1.8 us)

commit v3 on v2

--- a/solution.py
+++ b/solution.py
@@ -57,26 +57,31 @@
     return nested_sum((first_sum, second_sum), carried)
 
 
+def gathered_sum(values):
+    for axis in ("col", "row", "face"):
+        values = jnp.sum(lax.all_gather(values, axis, axis=0, tiled=False), axis=0)
+    return values
+
+
 def sum_steps():
-    steps = []
-    for axis in ("col", "row"):
-        count = lax.axis_size(axis)
-        step = 1
-        while step < count:
-            steps.append((axis, [[(i, i ^ step) for i in range(count)]]))
-            step *= 2
     faces = lax.axis_size("face")
-    steps.append(("face", [[(i, i ^ 1) for i in range(faces)]]))
-    steps.append(("face", [[(i, i ^ 2) for i in range(faces)]]))
-    steps.append(
+    steps = [
+        ("face", [[(i, i ^ 1) for i in range(faces)]]),
+        ("face", [[(i, i ^ 2) for i in range(faces)]]),
         (
             "face",
             [
                 [(i, (i + 4) % faces) for i in range(faces)],
                 [(i, (i + 8) % faces) for i in range(faces)],
             ],
-        )
-    )
+        ),
+    ]
+    for axis in ("row", "col"):
+        count = lax.axis_size(axis)
+        step = count // 2
+        while step >= 1:
+            steps.append((axis, [[(i, i ^ step) for i in range(count)]]))
+            step //= 2
     return steps
 
 
@@ -227,8 +232,8 @@
             state_bands[position], band_weight, preferred_element_type=jnp.float32
         )
     total = float(FACES * side * side)
-    sum_first, sum_square = channel_pair(
-        jnp.sum(response, axis=0), jnp.sum(response * response, axis=0)
+    sum_first, sum_square = gathered_sum(
+        jnp.stack([jnp.sum(response, axis=0), jnp.sum(response * response, axis=0)])
     )
     centre = sum_first / total
     inverse_spread = lax.rsqrt(sum_square / total - centre * centre + 1e-05)

time: 438 us -> 410 us (0.936)
  the two profiles are of different devices: /device:TPU:136 before, /device:TPU:56 now
where the time goes in v3:
time: 410 us; the launch traced here: 406 us
  blocking collectives  234 us (57%)
  waiting for transfers between devices  59.2 us (14%)
  starting transfers between devices  58.9 us (14%)
  local copies, waits for them, and re-layouts  28.5 us (7%)
  other arithmetic  13.2 us (3%)
  between operations  5.67 us (1%)
  matrix products  5.65 us (1%)
    all_gather x6, blocking collectives, run(): return lax.all_gather(operand, axis, axis=0, tiled=tiled)  133 us
    ppermute x10, waiting for transfers between devices, step_send(): return [lax.ppermute(values, axis, pairs) for pairs in pair_sets]  57.9 us
    psum x3, blocking collectives, nested_sum(): lax.psum(part, axis)  53.9 us
    all_gather x3, blocking collectives, gathered_sum(): values = jnp.sum(lax.all_gather(values, axis, axis=0, tiled=False), axis=0)  48 us
    ppermute x10, starting transfers between devices, step_send(): return [lax.ppermute(values, axis, pairs) for pairs in pair_sets]  34.3 us
    ppermute x4, starting transfers between devices, padded_2(): lax.ppermute(head, axis, [((i + 1) % count, i) for i in range(ends)])  18.2 us
  transfers between devices with their start and end apart: 18, of which 9 were waited for; matrix products, arithmetic and copies ran while one was open for 6% of the time, Pallas kernels for 0%

profile of v3, /device:TPU:56, one launch (start us, length us, event | category | flops | bytes accessed | tf_op | source)
XLA Modules:
  0.0 405.5 jit_solution(16778382398122703773)
XLA Ops:
  2.8 5.4 %collective-permute-start.1 = (bf16[1,1,8,64]{3,2,1,0:T(8,128)(2,1)S(1)}, bf16[1,1,8,64]{3,2,1,0:T(8,128)(2,1)S(1)}, u32[]{:S(2)}, u32[]{:S(2)}) collective-permute-start(bf16[1,1,8,64]{3,2,1,0:T(8,128)(2,1)S(1)} %get-tuple-element.313), channel_id=1, source_target_pairs={{16,0},{32,16},{48,32},{17,1},{33,17},{49,33},{18,2},{34,18},{50,3... | collective-permute-start | bytes 3080 | tf_op jit(solution)/shard_map/ppermute | solution.py:23
  8.3 13.7 %all-gather = bf16[4,40,64]{2,1,0:T(8,128)(2,1)S(1)} all-gather(bf16[1,40,64]{2,1,0:T(8,128)(2,1)S(1)} %pad_maximum_fusion.19), channel_id=2, replica_groups=mesh['face'=12,'row'=4,'col'=16] {'row'}, dimensions={0}, use_global_device_ids=true | all-gather | bytes 25600 | tf_op jit(solution)/shard_map/all_gather | solution.py:150
  22.5 23.2 %all-gather.1 = bf16[16,144,64]{1,2,0:T(8,128)(2,1)S(1)} all-gather(bf16[1,144,64]{1,2,0:T(8,128)(2,1)S(1)} %pad_maximum_fusion.12), channel_id=3, replica_groups=mesh['face'=12,'row'=4,'col'=16] {'col'}, dimensions={0}, use_global_device_ids=true | all-gather | bytes 313344 | tf_op jit(solution)/shard_map/all_gather | solution.py:150
  47.2 33.3 %all_gather.52 = bf16[12,4,128,64]{2,3,1,0:T(8,128)(2,1)S(1)} all-gather(bf16[1,4,128,64]{2,3,1,0:T(8,128)(2,1)S(1)} %pad_maximum_fusion.10), channel_id=1, replica_groups=mesh['face'=12,'row'=4,'col'=16] {'face'}, dimensions={0}, use_global_device_ids=true | all-gather | bytes 851968 | tf_op jit(solution)/shard_map/all_gather | solution.py:150
  113.6 17.2 %all-gather.7 = f32[16,2,64]{2,1,0:T(2,128)S(1)} all-gather(f32[1,2,64]{2,1,0:T(2,128)S(1)} %maximum_bitcast_fusion), channel_id=4, replica_groups=mesh['face'=12,'row'=4,'col'=16] {'col'}, dimensions={0}, use_global_device_ids=true | all-gather | bytes 8704 | tf_op jit(solution)/shard_map/all_gather | solution.py:62
  130.8 11.2 %all-gather.8 = f32[4,2,64]{2,1,0:T(2,128)S(1)} all-gather(f32[1,2,64]{2,1,0:T(2,128)S(1)} %bitcast.411), channel_id=5, replica_groups=mesh['face'=12,'row'=4,'col'=16] {'row'}, dimensions={0}, use_global_device_ids=true | all-gather | bytes 2560 | tf_op jit(solution)/shard_map/all_gather | solution.py:62
  142.1 19.6 %all-gather.9 = f32[12,2,64]{2,1,0:T(2,128)S(1)} all-gather(f32[1,2,64]{2,1,0:T(2,128)S(1)} %bitcast.414), channel_id=6, replica_groups=mesh['face'=12,'row'=4,'col'=16] {'face'}, dimensions={0}, use_global_device_ids=true | all-gather | bytes 6656 | tf_op jit(solution)/shard_map/all_gather | solution.py:62
  170.1 24.1 %all-reduce.3 = (f32[64]{0:T(128)S(1)}, f32[64]{0:T(128)S(1)}) all-reduce(f32[64]{0:T(128)S(1)} %get-tuple-element.212, f32[64]{0:T(128)S(1)} %get-tuple-element.213), channel_id=1, replica_groups=mesh['face'=12,'row'=4,'col'=16] {'col'}, use_global_device_ids=true, to_apply=%region_10.11 | all-reduce | flops 128 | bytes 1024 | tf_op jit(solution)/shard_map/psum | solution.py:52
  196.5 8.6 %all-reduce.5 = (f32[64]{0:T(128)S(1)}, f32[64]{0:T(128)S(1)}) all-reduce(f32[64]{0:T(128)S(1)} %get-tuple-element.215, f32[64]{0:T(128)S(1)} %get-tuple-element.216), channel_id=1, replica_groups=mesh['face'=12,'row'=4,'col'=16] {'row'}, use_global_device_ids=true, to_apply=%region_12.13 | all-reduce | flops 128 | bytes 1024 | tf_op jit(solution)/shard_map/psum | solution.py:52
  205.1 6.6 %collective-permute-done.5 = f32[74304]{0:T(1024)S(1)} collective-permute-done((f32[74304]{0:T(1024)S(1)}, f32[74304]{0:T(1024)S(1)}, u32[]{:S(2)}, u32[]{:S(2)}) %collective-permute-start.5) | collective-permute-done | bytes 297248 | tf_op jit(solution)/shard_map/ppermute | solution.py:90
  211.8 21.2 %all-reduce.4 = (f32[64]{0:T(128)S(1)}, f32[64]{0:T(128)S(1)}) all-reduce(f32[64]{0:T(128)S(1)} %get-tuple-element.218, f32[64]{0:T(128)S(1)} %get-tuple-element.217), channel_id=1, replica_groups=mesh['face'=12,'row'=4,'col'=16] {'face'}, use_global_device_ids=true, to_apply=%region_15.16 | all-reduce | flops 128 | bytes 1024 | tf_op jit(solution)/shard_map/psum | solution.py:52
  233.7 4.3 %collective-permute-start.10 = (f32[74304]{0:T(1024)S(1)}, f32[74304]{0:T(1024)S(1)}, u32[]{:S(2)}, u32[]{:S(2)}) collective-permute-start(f32[74304]{0:T(1024)S(1)} %add.191), channel_id=1, source_target_pairs={{0,256},{64,320},{128,384},{192,448},{256,512},{320,576},{384,640}... | collective-permute-start | bytes 891656 | tf_op jit(solution)/shard_map/ppermute | solution.py:90
  238.1 5.4 %collective-permute-start.11 = (f32[74304]{0:T(1024)S(1)}, f32[74304]{0:T(1024)S(1)}, u32[]{:S(2)}, u32[]{:S(2)}) collective-permute-start(f32[74304]{0:T(1024)S(1)} %add.191), channel_id=1, source_target_pairs={{0,512},{64,576},{128,640},{192,704},{256,0},{320,64},{384,128},{4... | collective-permute-start | bytes 891656 | tf_op jit(solution)/shard_map/ppermute | solution.py:90
  244.9 5.4 %collective-permute-start.7 = (bf16[1,1,8,64]{3,2,1,0:T(8,128)(2,1)S(1)}, bf16[1,1,8,64]{3,2,1,0:T(8,128)(2,1)S(1)}, u32[]{:S(2)}, u32[]{:S(2)}) collective-permute-start(bf16[1,1,8,64]{3,2,1,0:T(8,128)(2,1)S(1)} %get-tuple-element.298), channel_id=1, source_target_pairs={{16,0},{32,16},{48,32},{17,1},{33,17},{49,33},{18,2},{34,18},{50,3... | collective-permute-start | bytes 3080 | tf_op jit(solution)/shard_map/ppermute | solution.py:23
  259.2 6.1 %collective-permute-done.11 = f32[74304]{0:T(1024)S(1)} collective-permute-done((f32[74304]{0:T(1024)S(1)}, f32[74304]{0:T(1024)S(1)}, u32[]{:S(2)}, u32[]{:S(2)}) %collective-permute-start.11) | collective-permute-done | bytes 297248 | tf_op jit(solution)/shard_map/ppermute | solution.py:90
  265.4 13.7 %all-gather.5 = bf16[4,40,64]{2,1,0:T(8,128)(2,1)S(1)} all-gather(bf16[1,40,64]{2,1,0:T(8,128)(2,1)S(1)} %pad_maximum_fusion.20), channel_id=7, replica_groups=mesh['face'=12,'row'=4,'col'=16] {'row'}, dimensions={0}, use_global_device_ids=true | all-gather | bytes 25600 | tf_op jit(solution)/shard_map/all_gather | solution.py:150
  283.9 9.2 %collective-permute-done.12 = f32[74304]{0:T(1024)S(1)} collective-permute-done((f32[74304]{0:T(1024)S(1)}, f32[74304]{0:T(1024)S(1)}, u32[]{:S(2)}, u32[]{:S(2)}) %collective-permute-start.12) | collective-permute-done | bytes 297248 | tf_op jit(solution)/shard_map/ppermute | solution.py:90
  293.1 22.5 %all-gather.6 = bf16[16,144,64]{1,2,0:T(8,128)(2,1)S(1)} all-gather(bf16[1,144,64]{1,2,0:T(8,128)(2,1)S(1)} %pad_maximum_fusion.13), channel_id=8, replica_groups=mesh['face'=12,'row'=4,'col'=16] {'col'}, dimensions={0}, use_global_device_ids=true | all-gather | bytes 313344 | tf_op jit(solution)/shard_map/all_gather | solution.py:150
  316.3 6.5 %collective-permute-start.13 = (f32[74304]{0:T(1024)S(1)}, f32[74304]{0:T(1024)S(1)}, u32[]{:S(2)}, u32[]{:S(2)}) collective-permute-start(f32[74304]{0:T(1024)S(1)} %add.196), channel_id=1, source_target_pairs={{0,16},{16,0},{32,48},{48,32},{1,17},{17,1},{33,49},{49,33},{2,18}... | collective-permute-start | bytes 891656 | tf_op jit(solution)/shard_map/ppermute | solution.py:90
  323.0 13.8 %collective-permute-done.13 = f32[74304]{0:T(1024)S(1)} collective-permute-done((f32[74304]{0:T(1024)S(1)}, f32[74304]{0:T(1024)S(1)}, u32[]{:S(2)}, u32[]{:S(2)}) %collective-permute-start.13) | collective-permute-done | bytes 297248 | tf_op jit(solution)/shard_map/ppermute | solution.py:90
  336.8 26.0 %all_gather.63 = bf16[12,4,128,64]{2,3,1,0:T(8,128)(2,1)S(1)} all-gather(bf16[1,4,128,64]{2,3,1,0:T(8,128)(2,1)S(1)} %pad_maximum_fusion.11), channel_id=1, replica_groups=mesh['face'=12,'row'=4,'col'=16] {'face'}, dimensions={0}, use_global_device_ids=true | all-gather | bytes 851968 | tf_op jit(solution)/shard_map/all_gather | solution.py:150
  373.3 8.8 %collective-permute-done.14 = f32[74304]{0:T(1024)S(1)} collective-permute-done((f32[74304]{0:T(1024)S(1)}, f32[74304]{0:T(1024)S(1)}, u32[]{:S(2)}, u32[]{:S(2)}) %collective-permute-start.14) | collective-permute-done | bytes 297248 | tf_op jit(solution)/shard_map/ppermute | solution.py:90
  384.4 6.4 %collective-permute-done.15 = f32[74304]{0:T(1024)S(1)} collective-permute-done((f32[74304]{0:T(1024)S(1)}, f32[74304]{0:T(1024)S(1)}, u32[]{:S(2)}, u32[]{:S(2)}) %collective-permute-start.15) | collective-permute-done | bytes 297248 | tf_op jit(solution)/shard_map/ppermute | solution.py:90
  393.1 6.4 %collective-permute-done.16 = f32[74304]{0:T(1024)S(1)} collective-permute-done((f32[74304]{0:T(1024)S(1)}, f32[74304]{0:T(1024)S(1)}, u32[]{:S(2)}, u32[]{:S(2)}) %collective-permute-start.16) | collective-permute-done | bytes 297248 | tf_op jit(solution)/shard_map/ppermute | solution.py:90
  (278 shorter events, 81.0 us)
Async XLA Ops:
  1.5 91.8 %collective-permute-start = (bf16[1,1,8,64]{3,2,1,0:T(8,128)(2,1)S(1)}, bf16[1,1,8,64]{3,2,1,0:T(8,128)(2,1)S(1)}, u32[]{:S(2)}, u32[]{:S(2)}) collective-permute-start(bf16[1,1,8,64]{3,2,1,0:T(8,128)(2,1)S(1)} %get-tuple-element.314), channel_id=1, source_target_pairs={{0,16},{16,32},{32,48},{1,17},{17,33},{33,49},{2,18},{18,34},{34,5... | collective-permute-start | bytes 3080 | tf_op jit(solution)/shard_map/ppermute | solution.py:21
  2.8 90.5 %collective-permute-start.1 = (bf16[1,1,8,64]{3,2,1,0:T(8,128)(2,1)S(1)}, bf16[1,1,8,64]{3,2,1,0:T(8,128)(2,1)S(1)}, u32[]{:S(2)}, u32[]{:S(2)}) collective-permute-start(bf16[1,1,8,64]{3,2,1,0:T(8,128)(2,1)S(1)} %get-tuple-element.313), channel_id=1, source_target_pairs={{16,0},{32,16},{48,32},{17,1},{33,17},{49,33},{18,2},{34,18},{50,3... | collective-permute-start | bytes 3080 | tf_op jit(solution)/shard_map/ppermute | solution.py:23
  45.7 0.9 copy-start.1
  81.3 0.7 copy-start.3
  93.4 17.8 %collective-permute-start.2 = (bf16[1,34,1,64]{3,2,1,0:T(2,128)(2,1)S(1)}, bf16[1,34,1,64]{3,2,1,0:T(2,128)(2,1)S(1)}, u32[]{:S(2)}, u32[]{:S(2)}) collective-permute-start(bf16[1,34,1,64]{3,2,1,0:T(2,128)(2,1)S(1)} %get-tuple-element.291), channel_id=1, source_target_pairs={{0,1},{1,2},{2,3},{3,4},{4,5},{5,6},{6,7},{7,8},{8,9},{9,10},{10,1... | collective-permute-start | bytes 13064 | tf_op jit(solution)/shard_map/ppermute | solution.py:21
  95.3 15.9 %collective-permute-start.3 = (bf16[1,34,1,64]{3,2,1,0:T(2,128)(2,1)S(1)}, bf16[1,34,1,64]{3,2,1,0:T(2,128)(2,1)S(1)}, u32[]{:S(2)}, u32[]{:S(2)}) collective-permute-start(bf16[1,34,1,64]{3,2,1,0:T(2,128)(2,1)S(1)} %get-tuple-element.292), channel_id=1, source_target_pairs={{1,0},{2,1},{3,2},{4,3},{5,4},{6,5},{7,6},{8,7},{9,8},{10,9},{11,1... | collective-permute-start | bytes 13064 | tf_op jit(solution)/shard_map/ppermute | solution.py:23
  100.4 0.8 copy-start.2
  166.1 28.1 %collective-permute-start.4 = (f32[74304]{0:T(1024)S(1)}, f32[74304]{0:T(1024)S(1)}, u32[]{:S(2)}, u32[]{:S(2)}) collective-permute-start(f32[74304]{0:T(1024)S(1)} %pad_maximum_fusion), channel_id=1, source_target_pairs={{0,64},{64,0},{128,192},{192,128},{256,320},{320,256},{384,448},{4... | collective-permute-start | bytes 891656 | tf_op jit(solution)/shard_map/ppermute | solution.py:90
  194.2 17.5 %collective-permute-start.5 = (f32[74304]{0:T(1024)S(1)}, f32[74304]{0:T(1024)S(1)}, u32[]{:S(2)}, u32[]{:S(2)}) collective-permute-start(f32[74304]{0:T(1024)S(1)} %add.190), channel_id=1, source_target_pairs={{0,128},{64,192},{128,0},{192,64},{256,384},{320,448},{384,256},{4... | collective-permute-start | bytes 891656 | tf_op jit(solution)/shard_map/ppermute | solution.py:90
  232.9 18.3 %copy-start.6 = (f32[64]{0:T(128)}, f32[64]{0:T(128)S(1)}, u32[]{:S(2)}) copy-start(f32[64]{0:T(128)S(1)} %get-tuple-element.251) | copy-start | bytes 772
  233.7 25.5 %collective-permute-start.10 = (f32[74304]{0:T(1024)S(1)}, f32[74304]{0:T(1024)S(1)}, u32[]{:S(2)}, u32[]{:S(2)}) collective-permute-start(f32[74304]{0:T(1024)S(1)} %add.191), channel_id=1, source_target_pairs={{0,256},{64,320},{128,384},{192,448},{256,512},{320,576},{384,640}... | collective-permute-start | bytes 891656 | tf_op jit(solution)/shard_map/ppermute | solution.py:90
  238.1 27.3 %collective-permute-start.11 = (f32[74304]{0:T(1024)S(1)}, f32[74304]{0:T(1024)S(1)}, u32[]{:S(2)}, u32[]{:S(2)}) collective-permute-start(f32[74304]{0:T(1024)S(1)} %add.191), channel_id=1, source_target_pairs={{0,512},{64,576},{128,640},{192,704},{256,0},{320,64},{384,128},{4... | collective-permute-start | bytes 891656 | tf_op jit(solution)/shard_map/ppermute | solution.py:90
  243.6 7.9 %collective-permute-start.6 = (bf16[1,1,8,64]{3,2,1,0:T(8,128)(2,1)S(1)}, bf16[1,1,8,64]{3,2,1,0:T(8,128)(2,1)S(1)}, u32[]{:S(2)}, u32[]{:S(2)}) collective-permute-start(bf16[1,1,8,64]{3,2,1,0:T(8,128)(2,1)S(1)} %get-tuple-element.299), channel_id=1, source_target_pairs={{0,16},{16,32},{32,48},{1,17},{17,33},{33,49},{2,18},{18,34},{34,5... | collective-permute-start | bytes 3080 | tf_op jit(solution)/shard_map/ppermute | solution.py:21
  244.9 6.7 %collective-permute-start.7 = (bf16[1,1,8,64]{3,2,1,0:T(8,128)(2,1)S(1)}, bf16[1,1,8,64]{3,2,1,0:T(8,128)(2,1)S(1)}, u32[]{:S(2)}, u32[]{:S(2)}) collective-permute-start(bf16[1,1,8,64]{3,2,1,0:T(8,128)(2,1)S(1)} %get-tuple-element.298), channel_id=1, source_target_pairs={{16,0},{32,16},{48,32},{17,1},{33,17},{49,33},{18,2},{34,18},{50,3... | collective-permute-start | bytes 3080 | tf_op jit(solution)/shard_map/ppermute | solution.py:23
  251.9 5.7 %collective-permute-start.8 = (bf16[1,34,1,64]{1,3,2,0:T(8,128)(2,1)S(1)}, bf16[1,34,1,64]{1,3,2,0:T(8,128)(2,1)S(1)}, u32[]{:S(2)}, u32[]{:S(2)}) collective-permute-start(bf16[1,34,1,64]{1,3,2,0:T(8,128)(2,1)S(1)} %get-tuple-element.266), channel_id=1, source_target_pairs={{0,1},{1,2},{2,3},{3,4},{4,5},{5,6},{6,7},{7,8},{8,9},{9,10},{10,1... | collective-permute-start | bytes 13064 | tf_op jit(solution)/shard_map/ppermute | solution.py:21
  253.8 5.1 %collective-permute-start.9 = (bf16[1,34,1,64]{1,3,2,0:T(8,128)(2,1)S(1)}, bf16[1,34,1,64]{1,3,2,0:T(8,128)(2,1)S(1)}, u32[]{:S(2)}, u32[]{:S(2)}) collective-permute-start(bf16[1,34,1,64]{1,3,2,0:T(8,128)(2,1)S(1)} %get-tuple-element.267), channel_id=1, source_target_pairs={{1,0},{2,1},{3,2},{4,3},{5,4},{6,5},{7,6},{8,7},{9,8},{10,9},{11,1... | collective-permute-start | bytes 13064 | tf_op jit(solution)/shard_map/ppermute | solution.py:23
  279.3 13.8 %collective-permute-start.12 = (f32[74304]{0:T(1024)S(1)}, f32[74304]{0:T(1024)S(1)}, u32[]{:S(2)}, u32[]{:S(2)}) collective-permute-start(f32[74304]{0:T(1024)S(1)} %select_add_fusion), channel_id=1, source_target_pairs={{0,32},{16,48},{32,0},{48,16},{1,33},{17,49},{33,1},{49,17},{2,34}... | collective-permute-start | bytes 891656 | tf_op jit(solution)/shard_map/ppermute | solution.py:90
  316.3 20.5 %collective-permute-start.13 = (f32[74304]{0:T(1024)S(1)}, f32[74304]{0:T(1024)S(1)}, u32[]{:S(2)}, u32[]{:S(2)}) collective-permute-start(f32[74304]{0:T(1024)S(1)} %add.196), channel_id=1, source_target_pairs={{0,16},{16,0},{32,48},{48,32},{1,17},{17,1},{33,49},{49,33},{2,18}... | collective-permute-start | bytes 891656 | tf_op jit(solution)/shard_map/ppermute | solution.py:90
  370.2 11.8 %collective-permute-start.14 = (f32[74304]{0:T(1024)S(1)}, f32[74304]{0:T(1024)S(1)}, u32[]{:S(2)}, u32[]{:S(2)}) collective-permute-start(f32[74304]{0:T(1024)S(1)} %add.197), channel_id=1, source_target_pairs={{0,8},{1,9},{2,10},{3,11},{4,12},{5,13},{6,14},{7,15},{8,0},{9,1},... | collective-permute-start | bytes 891656 | tf_op jit(solution)/shard_map/ppermute | solution.py:90
  382.1 8.7 %collective-permute-start.15 = (f32[74304]{0:T(1024)S(1)}, f32[74304]{0:T(1024)S(1)}, u32[]{:S(2)}, u32[]{:S(2)}) collective-permute-start(f32[74304]{0:T(1024)S(1)} %add.204), channel_id=1, source_target_pairs={{0,4},{1,5},{2,6},{3,7},{4,0},{5,1},{6,2},{7,3},{8,12},{9,13},{10,... | collective-permute-start | bytes 891656 | tf_op jit(solution)/shard_map/ppermute | solution.py:90
  390.8 8.7 %collective-permute-start.16 = (f32[74304]{0:T(1024)S(1)}, f32[74304]{0:T(1024)S(1)}, u32[]{:S(2)}, u32[]{:S(2)}) collective-permute-start(f32[74304]{0:T(1024)S(1)} %add.205), channel_id=1, source_target_pairs={{0,2},{1,3},{2,0},{3,1},{4,6},{5,7},{6,4},{7,5},{8,10},{9,11},{10,... | collective-permute-start | bytes 891656 | tf_op jit(solution)/shard_map/ppermute | solution.py:90
  399.5 3.5 collective-permute-start.17
  403.1 0.7 copy-start
  403.9 0.7 slice-start
  (3 other events, 1.8 us)

commit v4 on v3

--- a/solution.py
+++ b/solution.py
@@ -66,8 +66,6 @@
 def sum_steps():
     faces = lax.axis_size("face")
     steps = [
-        ("face", [[(i, i ^ 1) for i in range(faces)]]),
-        ("face", [[(i, i ^ 2) for i in range(faces)]]),
         (
             "face",
             [
@@ -75,6 +73,8 @@
                 [(i, (i + 8) % faces) for i in range(faces)],
             ],
         ),
+        ("face", [[(i, i ^ 1) for i in range(faces)]]),
+        ("face", [[(i, i ^ 2) for i in range(faces)]]),
     ]
     for axis in ("row", "col"):
         count = lax.axis_size(axis)

time: 410 us -> 403 us (0.983)
  waiting for transfers between devices: 59.2 us -> 53.9 us
    ppermute x10, waiting for transfers between devices: 57.9 us -> 48.6 us  [step_send(): return [lax.ppermute(values, axis, pairs) for pairs in pair_sets]]
    ppermute x4, waiting for transfers between devices: 0.01 us -> 5.27 us  [padded_2(): lax.ppermute(tail, axis, [(i, (i + 1) % count) for i in range(ends)])]
  transfers between devices with their start and end apart: 18 -> 18, of which waited for: 9 -> 7; matrix products, arithmetic and copies ran while one was open for 6% -> 7% of each run, Pallas kernels for 0% -> 0%
where the time goes in v4:
time: 403 us; the launch traced here: 399 us
  blocking collectives  235 us (58%)
  starting transfers between devices  57.2 us (14%)
  waiting for transfers between devices  53.9 us (13%)
  local copies, waits for them, and re-layouts  28.5 us (7%)
  other arithmetic  13.2 us (3%)
  between operations  5.68 us (1%)
  matrix products  5.66 us (1%)
    all_gather x6, blocking collectives, run(): return lax.all_gather(operand, axis, axis=0, tiled=tiled)  133 us
    psum x3, blocking collectives, nested_sum(): lax.psum(part, axis)  54.2 us
    ppermute x10, waiting for transfers between devices, step_send(): return [lax.ppermute(values, axis, pairs) for pairs in pair_sets]  48.6 us
    all_gather x3, blocking collectives, gathered_sum(): values = jnp.sum(lax.all_gather(values, axis, axis=0, tiled=False), axis=0)  48 us
    ppermute x10, starting transfers between devices, step_send(): return [lax.ppermute(values, axis, pairs) for pairs in pair_sets]  33.8 us
    ppermute x4, starting transfers between devices, padded_2(): lax.ppermute(head, axis, [((i + 1) % count, i) for i in range(ends)])  16.5 us
  transfers between devices with their start and end apart: 18, of which 7 were waited for; matrix products, arithmetic and copies ran while one was open for 7% of the time, Pallas kernels for 0%

profile of v4, /device:TPU:56, one launch (start us, length us, event | category | flops | bytes accessed | tf_op | source)
XLA Modules:
  0.0 399.0 jit_solution(13875293886976676065)
XLA Ops:
  2.8 5.4 %collective-permute-start.1 = (bf16[1,1,8,64]{3,2,1,0:T(8,128)(2,1)S(1)}, bf16[1,1,8,64]{3,2,1,0:T(8,128)(2,1)S(1)}, u32[]{:S(2)}, u32[]{:S(2)}) collective-permute-start(bf16[1,1,8,64]{3,2,1,0:T(8,128)(2,1)S(1)} %get-tuple-element.313), channel_id=1, source_target_pairs={{16,0},{32,16},{48,32},{17,1},{33,17},{49,33},{18,2},{34,18},{50,3... | collective-permute-start | bytes 3080 | tf_op jit(solution)/shard_map/ppermute | solution.py:23
  8.3 13.7 %all-gather = bf16[4,40,64]{2,1,0:T(8,128)(2,1)S(1)} all-gather(bf16[1,40,64]{2,1,0:T(8,128)(2,1)S(1)} %pad_maximum_fusion.19), channel_id=2, replica_groups=mesh['face'=12,'row'=4,'col'=16] {'row'}, dimensions={0}, use_global_device_ids=true | all-gather | bytes 25600 | tf_op jit(solution)/shard_map/all_gather | solution.py:150
  22.5 23.2 %all-gather.1 = bf16[16,144,64]{1,2,0:T(8,128)(2,1)S(1)} all-gather(bf16[1,144,64]{1,2,0:T(8,128)(2,1)S(1)} %pad_maximum_fusion.12), channel_id=3, replica_groups=mesh['face'=12,'row'=4,'col'=16] {'col'}, dimensions={0}, use_global_device_ids=true | all-gather | bytes 313344 | tf_op jit(solution)/shard_map/all_gather | solution.py:150
  47.2 33.3 %all_gather.52 = bf16[12,4,128,64]{2,3,1,0:T(8,128)(2,1)S(1)} all-gather(bf16[1,4,128,64]{2,3,1,0:T(8,128)(2,1)S(1)} %pad_maximum_fusion.10), channel_id=1, replica_groups=mesh['face'=12,'row'=4,'col'=16] {'face'}, dimensions={0}, use_global_device_ids=true | all-gather | bytes 851968 | tf_op jit(solution)/shard_map/all_gather | solution.py:150
  113.6 17.2 %all-gather.7 = f32[16,2,64]{2,1,0:T(2,128)S(1)} all-gather(f32[1,2,64]{2,1,0:T(2,128)S(1)} %maximum_bitcast_fusion), channel_id=4, replica_groups=mesh['face'=12,'row'=4,'col'=16] {'col'}, dimensions={0}, use_global_device_ids=true | all-gather | bytes 8704 | tf_op jit(solution)/shard_map/all_gather | solution.py:62
  130.8 11.2 %all-gather.8 = f32[4,2,64]{2,1,0:T(2,128)S(1)} all-gather(f32[1,2,64]{2,1,0:T(2,128)S(1)} %bitcast.411), channel_id=5, replica_groups=mesh['face'=12,'row'=4,'col'=16] {'row'}, dimensions={0}, use_global_device_ids=true | all-gather | bytes 2560 | tf_op jit(solution)/shard_map/all_gather | solution.py:62
  142.1 19.6 %all-gather.9 = f32[12,2,64]{2,1,0:T(2,128)S(1)} all-gather(f32[1,2,64]{2,1,0:T(2,128)S(1)} %bitcast.414), channel_id=6, replica_groups=mesh['face'=12,'row'=4,'col'=16] {'face'}, dimensions={0}, use_global_device_ids=true | all-gather | bytes 6656 | tf_op jit(solution)/shard_map/all_gather | solution.py:62
  169.5 6.4 %collective-permute-start.5 = (f32[74304]{0:T(1024)S(1)}, f32[74304]{0:T(1024)S(1)}, u32[]{:S(2)}, u32[]{:S(2)}) collective-permute-start(f32[74304]{0:T(1024)S(1)} %pad_maximum_fusion), channel_id=1, source_target_pairs={{0,512},{64,576},{128,640},{192,704},{256,0},{320,64},{384,128},{4... | collective-permute-start | bytes 891656 | tf_op jit(solution)/shard_map/ppermute | solution.py:90
  175.9 24.7 %all-reduce.3 = (f32[64]{0:T(128)S(1)}, f32[64]{0:T(128)S(1)}) all-reduce(f32[64]{0:T(128)S(1)} %get-tuple-element.212, f32[64]{0:T(128)S(1)} %get-tuple-element.213), channel_id=1, replica_groups=mesh['face'=12,'row'=4,'col'=16] {'col'}, use_global_device_ids=true, to_apply=%region_10.11 | all-reduce | flops 128 | bytes 1024 | tf_op jit(solution)/shard_map/psum | solution.py:52
  200.7 3.9 collective-permute-start.6
  204.7 8.6 %all-reduce.5 = (f32[64]{0:T(128)S(1)}, f32[64]{0:T(128)S(1)}) all-reduce(f32[64]{0:T(128)S(1)} %get-tuple-element.215, f32[64]{0:T(128)S(1)} %get-tuple-element.216), channel_id=1, replica_groups=mesh['face'=12,'row'=4,'col'=16] {'row'}, use_global_device_ids=true, to_apply=%region_12.13 | all-reduce | flops 128 | bytes 1024 | tf_op jit(solution)/shard_map/psum | solution.py:52
  213.4 20.9 %all-reduce.4 = (f32[64]{0:T(128)S(1)}, f32[64]{0:T(128)S(1)}) all-reduce(f32[64]{0:T(128)S(1)} %get-tuple-element.218, f32[64]{0:T(128)S(1)} %get-tuple-element.217), channel_id=1, replica_groups=mesh['face'=12,'row'=4,'col'=16] {'face'}, use_global_device_ids=true, to_apply=%region_15.16 | all-reduce | flops 128 | bytes 1024 | tf_op jit(solution)/shard_map/psum | solution.py:52
  235.3 5.0 %collective-permute-start.11 = (f32[74304]{0:T(1024)S(1)}, f32[74304]{0:T(1024)S(1)}, u32[]{:S(2)}, u32[]{:S(2)}) collective-permute-start(f32[74304]{0:T(1024)S(1)} %add.192), channel_id=1, source_target_pairs={{0,128},{64,192},{128,0},{192,64},{256,384},{320,448},{384,256},{4... | collective-permute-start | bytes 891656 | tf_op jit(solution)/shard_map/ppermute | solution.py:90
  241.6 5.4 %collective-permute-start.8 = (bf16[1,1,8,64]{3,2,1,0:T(8,128)(2,1)S(1)}, bf16[1,1,8,64]{3,2,1,0:T(8,128)(2,1)S(1)}, u32[]{:S(2)}, u32[]{:S(2)}) collective-permute-start(bf16[1,1,8,64]{3,2,1,0:T(8,128)(2,1)S(1)} %get-tuple-element.298), channel_id=1, source_target_pairs={{16,0},{32,16},{48,32},{17,1},{33,17},{49,33},{18,2},{34,18},{50,3... | collective-permute-start | bytes 3080 | tf_op jit(solution)/shard_map/ppermute | solution.py:23
  253.1 5.3 %collective-permute-done.9 = bf16[1,34,1,64]{1,3,2,0:T(8,128)(2,1)S(1)} collective-permute-done((bf16[1,34,1,64]{1,3,2,0:T(8,128)(2,1)S(1)}, bf16[1,34,1,64]{1,3,2,0:T(8,128)(2,1)S(1)}, u32[]{:S(2)}, u32[]{:S(2)}) %collective-permute-start.9) | collective-permute-done | bytes 4384 | tf_op jit(solution)/shard_map/ppermute | solution.py:21
  258.7 17.1 %all-gather.5 = bf16[4,40,64]{2,1,0:T(8,128)(2,1)S(1)} all-gather(bf16[1,40,64]{2,1,0:T(8,128)(2,1)S(1)} %pad_maximum_fusion.20), channel_id=7, replica_groups=mesh['face'=12,'row'=4,'col'=16] {'row'}, dimensions={0}, use_global_device_ids=true | all-gather | bytes 25600 | tf_op jit(solution)/shard_map/all_gather | solution.py:150
  275.9 5.5 %collective-permute-start.12 = (f32[74304]{0:T(1024)S(1)}, f32[74304]{0:T(1024)S(1)}, u32[]{:S(2)}, u32[]{:S(2)}) collective-permute-start(f32[74304]{0:T(1024)S(1)} %add.195), channel_id=1, source_target_pairs={{0,32},{16,48},{32,0},{48,16},{1,33},{17,49},{33,1},{49,17},{2,34}... | collective-permute-start | bytes 891656 | tf_op jit(solution)/shard_map/ppermute | solution.py:90
  281.8 9.9 %collective-permute-done.12 = f32[74304]{0:T(1024)S(1)} collective-permute-done((f32[74304]{0:T(1024)S(1)}, f32[74304]{0:T(1024)S(1)}, u32[]{:S(2)}, u32[]{:S(2)}) %collective-permute-start.12) | collective-permute-done | bytes 297248 | tf_op jit(solution)/shard_map/ppermute | solution.py:90
  291.6 20.3 %all-gather.6 = bf16[16,144,64]{1,2,0:T(8,128)(2,1)S(1)} all-gather(bf16[1,144,64]{1,2,0:T(8,128)(2,1)S(1)} %pad_maximum_fusion.13), channel_id=8, replica_groups=mesh['face'=12,'row'=4,'col'=16] {'col'}, dimensions={0}, use_global_device_ids=true | all-gather | bytes 313344 | tf_op jit(solution)/shard_map/all_gather | solution.py:150
  314.7 16.4 %collective-permute-done.13 = f32[74304]{0:T(1024)S(1)} collective-permute-done((f32[74304]{0:T(1024)S(1)}, f32[74304]{0:T(1024)S(1)}, u32[]{:S(2)}, u32[]{:S(2)}) %collective-permute-start.13) | collective-permute-done | bytes 297248 | tf_op jit(solution)/shard_map/ppermute | solution.py:90
  331.2 25.0 %all_gather.63 = bf16[12,4,128,64]{2,3,1,0:T(8,128)(2,1)S(1)} all-gather(bf16[1,4,128,64]{2,3,1,0:T(8,128)(2,1)S(1)} %pad_maximum_fusion.11), channel_id=1, replica_groups=mesh['face'=12,'row'=4,'col'=16] {'face'}, dimensions={0}, use_global_device_ids=true | all-gather | bytes 851968 | tf_op jit(solution)/shard_map/all_gather | solution.py:150
  366.7 9.0 %collective-permute-done.14 = f32[74304]{0:T(1024)S(1)} collective-permute-done((f32[74304]{0:T(1024)S(1)}, f32[74304]{0:T(1024)S(1)}, u32[]{:S(2)}, u32[]{:S(2)}) %collective-permute-start.14) | collective-permute-done | bytes 297248 | tf_op jit(solution)/shard_map/ppermute | solution.py:90
  377.9 6.4 %collective-permute-done.15 = f32[74304]{0:T(1024)S(1)} collective-permute-done((f32[74304]{0:T(1024)S(1)}, f32[74304]{0:T(1024)S(1)}, u32[]{:S(2)}, u32[]{:S(2)}) %collective-permute-start.15) | collective-permute-done | bytes 297248 | tf_op jit(solution)/shard_map/ppermute | solution.py:90
  386.6 6.4 %collective-permute-done.16 = f32[74304]{0:T(1024)S(1)} collective-permute-done((f32[74304]{0:T(1024)S(1)}, f32[74304]{0:T(1024)S(1)}, u32[]{:S(2)}, u32[]{:S(2)}) %collective-permute-start.16) | collective-permute-done | bytes 297248 | tf_op jit(solution)/shard_map/ppermute | solution.py:90
  (278 shorter events, 73.4 us)
Async XLA Ops:
  1.5 91.8 %collective-permute-start = (bf16[1,1,8,64]{3,2,1,0:T(8,128)(2,1)S(1)}, bf16[1,1,8,64]{3,2,1,0:T(8,128)(2,1)S(1)}, u32[]{:S(2)}, u32[]{:S(2)}) collective-permute-start(bf16[1,1,8,64]{3,2,1,0:T(8,128)(2,1)S(1)} %get-tuple-element.314), channel_id=1, source_target_pairs={{0,16},{16,32},{32,48},{1,17},{17,33},{33,49},{2,18},{18,34},{34,5... | collective-permute-start | bytes 3080 | tf_op jit(solution)/shard_map/ppermute | solution.py:21
  2.8 90.5 %collective-permute-start.1 = (bf16[1,1,8,64]{3,2,1,0:T(8,128)(2,1)S(1)}, bf16[1,1,8,64]{3,2,1,0:T(8,128)(2,1)S(1)}, u32[]{:S(2)}, u32[]{:S(2)}) collective-permute-start(bf16[1,1,8,64]{3,2,1,0:T(8,128)(2,1)S(1)} %get-tuple-element.313), channel_id=1, source_target_pairs={{16,0},{32,16},{48,32},{17,1},{33,17},{49,33},{18,2},{34,18},{50,3... | collective-permute-start | bytes 3080 | tf_op jit(solution)/shard_map/ppermute | solution.py:23
  45.7 0.9 copy-start.1
  81.3 0.7 copy-start.3
  93.4 17.8 %collective-permute-start.2 = (bf16[1,34,1,64]{3,2,1,0:T(2,128)(2,1)S(1)}, bf16[1,34,1,64]{3,2,1,0:T(2,128)(2,1)S(1)}, u32[]{:S(2)}, u32[]{:S(2)}) collective-permute-start(bf16[1,34,1,64]{3,2,1,0:T(2,128)(2,1)S(1)} %get-tuple-element.291), channel_id=1, source_target_pairs={{0,1},{1,2},{2,3},{3,4},{4,5},{5,6},{6,7},{7,8},{8,9},{9,10},{10,1... | collective-permute-start | bytes 13064 | tf_op jit(solution)/shard_map/ppermute | solution.py:21
  95.3 15.9 %collective-permute-start.3 = (bf16[1,34,1,64]{3,2,1,0:T(2,128)(2,1)S(1)}, bf16[1,34,1,64]{3,2,1,0:T(2,128)(2,1)S(1)}, u32[]{:S(2)}, u32[]{:S(2)}) collective-permute-start(bf16[1,34,1,64]{3,2,1,0:T(2,128)(2,1)S(1)} %get-tuple-element.292), channel_id=1, source_target_pairs={{1,0},{2,1},{3,2},{4,3},{5,4},{6,5},{7,6},{8,7},{9,8},{10,9},{11,1... | collective-permute-start | bytes 13064 | tf_op jit(solution)/shard_map/ppermute | solution.py:23
  100.4 0.8 copy-start.2
  166.1 34.5 %collective-permute-start.4 = (f32[74304]{0:T(1024)S(1)}, f32[74304]{0:T(1024)S(1)}, u32[]{:S(2)}, u32[]{:S(2)}) collective-permute-start(f32[74304]{0:T(1024)S(1)} %pad_maximum_fusion), channel_id=1, source_target_pairs={{0,256},{64,320},{128,384},{192,448},{256,512},{320,576},{384,640}... | collective-permute-start | bytes 891656 | tf_op jit(solution)/shard_map/ppermute | solution.py:90
  169.5 31.2 %collective-permute-start.5 = (f32[74304]{0:T(1024)S(1)}, f32[74304]{0:T(1024)S(1)}, u32[]{:S(2)}, u32[]{:S(2)}) collective-permute-start(f32[74304]{0:T(1024)S(1)} %pad_maximum_fusion), channel_id=1, source_target_pairs={{0,512},{64,576},{128,640},{192,704},{256,0},{320,64},{384,128},{4... | collective-permute-start | bytes 891656 | tf_op jit(solution)/shard_map/ppermute | solution.py:90
  200.7 12.7 %collective-permute-start.6 = (f32[74304]{0:T(1024)S(1)}, f32[74304]{0:T(1024)S(1)}, u32[]{:S(2)}, u32[]{:S(2)}) collective-permute-start(f32[74304]{0:T(1024)S(1)} %select_add_fusion), channel_id=1, source_target_pairs={{0,64},{64,0},{128,192},{192,128},{256,320},{320,256},{384,448},{4... | collective-permute-start | bytes 891656 | tf_op jit(solution)/shard_map/ppermute | solution.py:90
  234.3 0.8 copy-start.6
  235.3 23.4 %collective-permute-start.11 = (f32[74304]{0:T(1024)S(1)}, f32[74304]{0:T(1024)S(1)}, u32[]{:S(2)}, u32[]{:S(2)}) collective-permute-start(f32[74304]{0:T(1024)S(1)} %add.192), channel_id=1, source_target_pairs={{0,128},{64,192},{128,0},{192,64},{256,384},{320,448},{384,256},{4... | collective-permute-start | bytes 891656 | tf_op jit(solution)/shard_map/ppermute | solution.py:90
  240.3 7.8 %collective-permute-start.7 = (bf16[1,1,8,64]{3,2,1,0:T(8,128)(2,1)S(1)}, bf16[1,1,8,64]{3,2,1,0:T(8,128)(2,1)S(1)}, u32[]{:S(2)}, u32[]{:S(2)}) collective-permute-start(bf16[1,1,8,64]{3,2,1,0:T(8,128)(2,1)S(1)} %get-tuple-element.299), channel_id=1, source_target_pairs={{0,16},{16,32},{32,48},{1,17},{17,33},{33,49},{2,18},{18,34},{34,5... | collective-permute-start | bytes 3080 | tf_op jit(solution)/shard_map/ppermute | solution.py:21
  241.6 6.7 %collective-permute-start.8 = (bf16[1,1,8,64]{3,2,1,0:T(8,128)(2,1)S(1)}, bf16[1,1,8,64]{3,2,1,0:T(8,128)(2,1)S(1)}, u32[]{:S(2)}, u32[]{:S(2)}) collective-permute-start(bf16[1,1,8,64]{3,2,1,0:T(8,128)(2,1)S(1)} %get-tuple-element.298), channel_id=1, source_target_pairs={{16,0},{32,16},{48,32},{17,1},{33,17},{49,33},{18,2},{34,18},{50,3... | collective-permute-start | bytes 3080 | tf_op jit(solution)/shard_map/ppermute | solution.py:23
  248.6 4.5 %collective-permute-start.10 = (bf16[1,34,1,64]{1,3,2,0:T(8,128)(2,1)S(1)}, bf16[1,34,1,64]{1,3,2,0:T(8,128)(2,1)S(1)}, u32[]{:S(2)}, u32[]{:S(2)}) collective-permute-start(bf16[1,34,1,64]{1,3,2,0:T(8,128)(2,1)S(1)} %get-tuple-element.267), channel_id=1, source_target_pairs={{1,0},{2,1},{3,2},{4,3},{5,4},{6,5},{7,6},{8,7},{9,8},{10,9},{11,1... | collective-permute-start | bytes 13064 | tf_op jit(solution)/shard_map/ppermute | solution.py:23
  250.5 7.8 %collective-permute-start.9 = (bf16[1,34,1,64]{1,3,2,0:T(8,128)(2,1)S(1)}, bf16[1,34,1,64]{1,3,2,0:T(8,128)(2,1)S(1)}, u32[]{:S(2)}, u32[]{:S(2)}) collective-permute-start(bf16[1,34,1,64]{1,3,2,0:T(8,128)(2,1)S(1)} %get-tuple-element.266), channel_id=1, source_target_pairs={{0,1},{1,2},{2,3},{3,4},{4,5},{5,6},{6,7},{7,8},{8,9},{9,10},{10,1... | collective-permute-start | bytes 13064 | tf_op jit(solution)/shard_map/ppermute | solution.py:21
  275.9 15.7 %collective-permute-start.12 = (f32[74304]{0:T(1024)S(1)}, f32[74304]{0:T(1024)S(1)}, u32[]{:S(2)}, u32[]{:S(2)}) collective-permute-start(f32[74304]{0:T(1024)S(1)} %add.195), channel_id=1, source_target_pairs={{0,32},{16,48},{32,0},{48,16},{1,33},{17,49},{33,1},{49,17},{2,34}... | collective-permute-start | bytes 891656 | tf_op jit(solution)/shard_map/ppermute | solution.py:90
  312.6 18.5 %collective-permute-start.13 = (f32[74304]{0:T(1024)S(1)}, f32[74304]{0:T(1024)S(1)}, u32[]{:S(2)}, u32[]{:S(2)}) collective-permute-start(f32[74304]{0:T(1024)S(1)} %add.196), channel_id=1, source_target_pairs={{0,16},{16,0},{32,48},{48,32},{1,17},{17,1},{33,49},{49,33},{2,18}... | collective-permute-start | bytes 891656 | tf_op jit(solution)/shard_map/ppermute | solution.py:90
  363.6 12.0 %collective-permute-start.14 = (f32[74304]{0:T(1024)S(1)}, f32[74304]{0:T(1024)S(1)}, u32[]{:S(2)}, u32[]{:S(2)}) collective-permute-start(f32[74304]{0:T(1024)S(1)} %add.197), channel_id=1, source_target_pairs={{0,8},{1,9},{2,10},{3,11},{4,12},{5,13},{6,14},{7,15},{8,0},{9,1},... | collective-permute-start | bytes 891656 | tf_op jit(solution)/shard_map/ppermute | solution.py:90
  375.7 8.7 %collective-permute-start.15 = (f32[74304]{0:T(1024)S(1)}, f32[74304]{0:T(1024)S(1)}, u32[]{:S(2)}, u32[]{:S(2)}) collective-permute-start(f32[74304]{0:T(1024)S(1)} %add.204), channel_id=1, source_target_pairs={{0,4},{1,5},{2,6},{3,7},{4,0},{5,1},{6,2},{7,3},{8,12},{9,13},{10,... | collective-permute-start | bytes 891656 | tf_op jit(solution)/shard_map/ppermute | solution.py:90
  384.4 8.7 %collective-permute-start.16 = (f32[74304]{0:T(1024)S(1)}, f32[74304]{0:T(1024)S(1)}, u32[]{:S(2)}, u32[]{:S(2)}) collective-permute-start(f32[74304]{0:T(1024)S(1)} %add.205), channel_id=1, source_target_pairs={{0,2},{1,3},{2,0},{3,1},{4,6},{5,7},{6,4},{7,5},{8,10},{9,11},{10,... | collective-permute-start | bytes 891656 | tf_op jit(solution)/shard_map/ppermute | solution.py:90
  393.1 3.5 collective-permute-start.17
  396.6 0.7 copy-start
  397.4 0.7 slice-start
  (3 other events, 1.8 us)

commit v5 on v4

--- a/solution.py
+++ b/solution.py
@@ -116,6 +116,27 @@
         self.values = step_land(step, values, moved)
         return result
 
+    def doubling(self, part, axis):
+        count = lax.axis_size(axis)
+        index = lax.axis_index(axis)
+        gathered = part[None]
+        step_size = 1
+        while step_size < count:
+            step = self.steps.pop(0) if self.steps else None
+            values, gathered = lax.optimization_barrier((self.values, gathered))
+            moved = step_send(step, values) if step else None
+            arrived = lax.ppermute(
+                gathered, axis, [(i, i ^ step_size) for i in range(count)]
+            )
+            gathered = jnp.where(
+                (index // step_size) % 2 == 1,
+                jnp.concatenate([arrived, gathered], axis=0),
+                jnp.concatenate([gathered, arrived], axis=0),
+            )
+            self.values = step_land(step, values, moved) if step else values
+            step_size *= 2
+        return gathered
+
     def finish(self):
         while self.steps:
             step = self.steps.pop(0)
@@ -146,10 +167,9 @@
 
     def extend(values, carried=None):
         def gather(part, axis, tiled):
-            def run(operand):
-                return lax.all_gather(operand, axis, axis=0, tiled=tiled)
-
-            return run(part) if carried is None else carried.beside(run, part)
+            if carried is None or axis == "face":
+                return lax.all_gather(part, axis, axis=0, tiled=tiled)
+            return carried.doubling(part, axis)
 
         padded = padded_2(values, (("row", 1), ("col", 2)), 1)
         row_strip = jnp.where(row_index == 0, values[:, 0], values[:, tile_rows - 1])

time: 403 us -> 375 us (0.931)
  blocking collectives: 235 us -> 198 us
  starting transfers between devices: 57.2 us -> 90.2 us
  waiting for transfers between devices: 53.9 us -> 29.3 us
    all_gather x6 -> x4, blocking collectives: 133 us -> 95.5 us  [gather(): return lax.all_gather(part, axis, axis=0, tiled=tiled)]
    ppermute x10, waiting for transfers between devices: 48.6 us -> 23.5 us  [step_send(): return [lax.ppermute(values, axis, pairs) for pairs in pair_sets]]
    ppermute x0 -> x6, starting transfers between devices: none -> 24.4 us  [doubling(): lax.ppermute(gathered, axis, [(i, i ^ step_size) for i in range(count)])]
    ppermute x0 -> x6, waiting for transfers between devices: none -> 5.78 us  [doubling(): lax.ppermute(gathered, axis, [(i, i ^ step_size) for i in range(count)])]
    ppermute x10, starting transfers between devices: 33.8 us -> 39.5 us  [step_send(): return [lax.ppermute(values, axis, pairs) for pairs in pair_sets]]
    ppermute x4, waiting for transfers between devices: 5.27 us -> 0.01 us  [padded_2(): lax.ppermute(tail, axis, [(i, (i + 1) % count) for i in range(ends)])]
  transfers between devices with their start and end apart: 18 -> 24, of which waited for: 7 -> 10; matrix products, arithmetic and copies ran while one was open for 7% -> 9% of each run, Pallas kernels for 0% -> 0%
where the time goes in v5:
time: 375 us; the launch traced here: 371 us
  blocking collectives  198 us (53%)
  starting transfers between devices  90.2 us (24%)
  waiting for transfers between devices  29.3 us (8%)
  local copies, waits for them, and re-layouts  28.5 us (8%)
  other arithmetic  13.5 us (4%)
  between operations  5.96 us (2%)
  matrix products  5.74 us (2%)
    all_gather x4, blocking collectives, gather(): return lax.all_gather(part, axis, axis=0, tiled=tiled)  95.5 us
    psum x3, blocking collectives, nested_sum(): lax.psum(part, axis)  54.3 us
    all_gather x3, blocking collectives, gathered_sum(): values = jnp.sum(lax.all_gather(values, axis, axis=0, tiled=False), axis=0)  48 us
    ppermute x10, starting transfers between devices, step_send(): return [lax.ppermute(values, axis, pairs) for pairs in pair_sets]  39.5 us
    ppermute x6, starting transfers between devices, doubling(): lax.ppermute(gathered, axis, [(i, i ^ step_size) for i in range(count)])  24.4 us
    ppermute x10, waiting for transfers between devices, step_send(): return [lax.ppermute(values, axis, pairs) for pairs in pair_sets]  23.5 us
    ppermute x4, starting transfers between devices, padded_2(): lax.ppermute(head, axis, [((i + 1) % count, i) for i in range(ends)])  19.3 us
  transfers between devices with their start and end apart: 24, of which 10 were waited for; matrix products, arithmetic and copies ran while one was open for 9% of the time, Pallas kernels for 0%

profile of v5, /device:TPU:56, one launch (start us, length us, event | category | flops | bytes accessed | tf_op | source)
XLA Modules:
  0.0 371.0 jit_solution(2329728543673382438)
XLA Ops:
  2.8 5.4 %collective-permute-start.1 = (bf16[1,1,8,64]{3,2,1,0:T(8,128)(2,1)S(1)}, bf16[1,1,8,64]{3,2,1,0:T(8,128)(2,1)S(1)}, u32[]{:S(2)}, u32[]{:S(2)}) collective-permute-start(bf16[1,1,8,64]{3,2,1,0:T(8,128)(2,1)S(1)} %get-tuple-element.325), channel_id=1, source_target_pairs={{16,0},{32,16},{48,32},{17,1},{33,17},{49,33},{18,2},{34,18},{50,3... | collective-permute-start | bytes 3080 | tf_op jit(solution)/shard_map/ppermute | solution.py:23
  8.3 13.7 %all-gather = bf16[4,40,64]{2,1,0:T(8,128)(2,1)S(1)} all-gather(bf16[1,40,64]{2,1,0:T(8,128)(2,1)S(1)} %pad_maximum_fusion.18), channel_id=2, replica_groups=mesh['face'=12,'row'=4,'col'=16] {'row'}, dimensions={0}, use_global_device_ids=true | all-gather | bytes 25600 | tf_op jit(solution)/shard_map/all_gather | solution.py:171
  22.5 23.2 %all-gather.1 = bf16[16,144,64]{1,2,0:T(8,128)(2,1)S(1)} all-gather(bf16[1,144,64]{1,2,0:T(8,128)(2,1)S(1)} %pad_maximum_fusion.12), channel_id=3, replica_groups=mesh['face'=12,'row'=4,'col'=16] {'col'}, dimensions={0}, use_global_device_ids=true | all-gather | bytes 313344 | tf_op jit(solution)/shard_map/all_gather | solution.py:171
  46.5 33.3 %all_gather.40 = bf16[12,4,128,64]{2,3,1,0:T(8,128)(2,1)S(1)} all-gather(bf16[1,4,128,64]{2,3,1,0:T(8,128)(2,1)S(1)} %pad_maximum_fusion.10), channel_id=1, replica_groups=mesh['face'=12,'row'=4,'col'=16] {'face'}, dimensions={0}, use_global_device_ids=true | all-gather | bytes 851968 | tf_op jit(solution)/shard_map/all_gather | solution.py:171
  113.0 17.2 %all-gather.5 = f32[16,2,64]{2,1,0:T(2,128)S(1)} all-gather(f32[1,2,64]{2,1,0:T(2,128)S(1)} %maximum_bitcast_fusion.2), channel_id=4, replica_groups=mesh['face'=12,'row'=4,'col'=16] {'col'}, dimensions={0}, use_global_device_ids=true | all-gather | bytes 8704 | tf_op jit(solution)/shard_map/all_gather | solution.py:62
  130.2 11.2 %all-gather.6 = f32[4,2,64]{2,1,0:T(2,128)S(1)} all-gather(f32[1,2,64]{2,1,0:T(2,128)S(1)} %bitcast.409), channel_id=5, replica_groups=mesh['face'=12,'row'=4,'col'=16] {'row'}, dimensions={0}, use_global_device_ids=true | all-gather | bytes 2560 | tf_op jit(solution)/shard_map/all_gather | solution.py:62
  141.5 19.6 %all-gather.7 = f32[12,2,64]{2,1,0:T(2,128)S(1)} all-gather(f32[1,2,64]{2,1,0:T(2,128)S(1)} %bitcast.412), channel_id=6, replica_groups=mesh['face'=12,'row'=4,'col'=16] {'face'}, dimensions={0}, use_global_device_ids=true | all-gather | bytes 6656 | tf_op jit(solution)/shard_map/all_gather | solution.py:62
  168.8 6.4 %collective-permute-start.5 = (f32[74304]{0:T(1024)S(1)}, f32[74304]{0:T(1024)S(1)}, u32[]{:S(2)}, u32[]{:S(2)}) collective-permute-start(f32[74304]{0:T(1024)S(1)} %pad_maximum_fusion), channel_id=1, source_target_pairs={{0,512},{64,576},{128,640},{192,704},{256,0},{320,64},{384,128},{4... | collective-permute-start | bytes 891656 | tf_op jit(solution)/shard_map/ppermute | solution.py:90
  175.3 24.7 %all-reduce.3 = (f32[64]{0:T(128)S(1)}, f32[64]{0:T(128)S(1)}) all-reduce(f32[64]{0:T(128)S(1)} %get-tuple-element.218, f32[64]{0:T(128)S(1)} %get-tuple-element.219), channel_id=1, replica_groups=mesh['face'=12,'row'=4,'col'=16] {'col'}, use_global_device_ids=true, to_apply=%region_10.11 | all-reduce | flops 128 | bytes 1024 | tf_op jit(solution)/shard_map/psum | solution.py:52
  200.1 3.9 %collective-permute-start.6 = (f32[74304]{0:T(1024)S(1)}, f32[74304]{0:T(1024)S(1)}, u32[]{:S(2)}, u32[]{:S(2)}) collective-permute-start(f32[74304]{0:T(1024)S(1)} %select_add_fusion), channel_id=1, source_target_pairs={{0,64},{64,0},{128,192},{192,128},{256,320},{320,256},{384,448},{4... | collective-permute-start | bytes 891656 | tf_op jit(solution)/shard_map/ppermute | solution.py:90
  204.1 8.7 %all-reduce.5 = (f32[64]{0:T(128)S(1)}, f32[64]{0:T(128)S(1)}) all-reduce(f32[64]{0:T(128)S(1)} %get-tuple-element.221, f32[64]{0:T(128)S(1)} %get-tuple-element.222), channel_id=1, replica_groups=mesh['face'=12,'row'=4,'col'=16] {'row'}, use_global_device_ids=true, to_apply=%region_12.13 | all-reduce | flops 128 | bytes 1024 | tf_op jit(solution)/shard_map/psum | solution.py:52
  212.8 20.9 %all-reduce.4 = (f32[64]{0:T(128)S(1)}, f32[64]{0:T(128)S(1)}) all-reduce(f32[64]{0:T(128)S(1)} %get-tuple-element.224, f32[64]{0:T(128)S(1)} %get-tuple-element.223), channel_id=1, replica_groups=mesh['face'=12,'row'=4,'col'=16] {'face'}, use_global_device_ids=true, to_apply=%region_15.16 | all-reduce | flops 128 | bytes 1024 | tf_op jit(solution)/shard_map/psum | solution.py:52
  234.5 4.9 %collective-permute-start.11 = (f32[74304]{0:T(1024)S(1)}, f32[74304]{0:T(1024)S(1)}, u32[]{:S(2)}, u32[]{:S(2)}) collective-permute-start(f32[74304]{0:T(1024)S(1)} %add.217), channel_id=1, source_target_pairs={{0,128},{64,192},{128,0},{192,64},{256,384},{320,448},{384,256},{4... | collective-permute-start | bytes 891656 | tf_op jit(solution)/shard_map/ppermute | solution.py:90
  239.5 7.9 %collective-permute-done.11 = f32[74304]{0:T(1024)S(1)} collective-permute-done((f32[74304]{0:T(1024)S(1)}, f32[74304]{0:T(1024)S(1)}, u32[]{:S(2)}, u32[]{:S(2)}) %collective-permute-start.11) | collective-permute-done | bytes 297248 | tf_op jit(solution)/shard_map/ppermute | solution.py:90
  247.4 4.9 %collective-permute-start.12 = (f32[74304]{0:T(1024)S(1)}, f32[74304]{0:T(1024)S(1)}, u32[]{:S(2)}, u32[]{:S(2)}) collective-permute-start(f32[74304]{0:T(1024)S(1)} %add.221), channel_id=1, source_target_pairs={{0,32},{16,48},{32,0},{48,16},{1,33},{17,49},{33,1},{49,17},{2,34}... | collective-permute-start | bytes 891656 | tf_op jit(solution)/shard_map/ppermute | solution.py:90
  252.4 5.2 %collective-permute-start.13 = (bf16[1,1,40,64]{3,2,1,0:T(8,128)(2,1)S(1)}, bf16[1,1,40,64]{3,2,1,0:T(8,128)(2,1)S(1)}, u32[]{:S(2)}, u32[]{:S(2)}) collective-permute-start(bf16[1,1,40,64]{3,2,1,0:T(8,128)(2,1)S(1)} %maximum_bitcast_fusion.1), channel_id=1, source_target_pairs={{0,16},{16,0},{32,48},{48,32},{1,17},{17,1},{33,49},{49,33},{2,18}... | collective-permute-start | bytes 15368 | tf_op jit(solution)/shard_map/ppermute | solution.py:128
  260.3 4.9 %collective-permute-start.15 = (bf16[2,1,40,64]{3,2,1,0:T(8,128)(2,1)S(1)}, bf16[2,1,40,64]{3,2,1,0:T(8,128)(2,1)S(1)}, u32[]{:S(2)}, u32[]{:S(2)}) collective-permute-start(bf16[2,1,40,64]{3,2,1,0:T(8,128)(2,1)S(1)} %maximum_select_fusion.5), channel_id=1, source_target_pairs={{0,32},{16,48},{32,0},{48,16},{1,33},{17,49},{33,1},{49,17},{2,34}... | collective-permute-start | bytes 30728 | tf_op jit(solution)/shard_map/ppermute | solution.py:128
  266.6 8.3 %collective-permute-start.8 = (bf16[1,1,8,64]{3,2,1,0:T(8,128)(2,1)S(1)}, bf16[1,1,8,64]{3,2,1,0:T(8,128)(2,1)S(1)}, u32[]{:S(2)}, u32[]{:S(2)}) collective-permute-start(bf16[1,1,8,64]{3,2,1,0:T(8,128)(2,1)S(1)} %get-tuple-element.310), channel_id=1, source_target_pairs={{16,0},{32,16},{48,32},{17,1},{33,17},{49,33},{18,2},{34,18},{50,3... | collective-permute-start | bytes 3080 | tf_op jit(solution)/shard_map/ppermute | solution.py:23
  275.0 6.0 %collective-permute-start.14 = (f32[74304]{0:T(1024)S(1)}, f32[74304]{0:T(1024)S(1)}, u32[]{:S(2)}, u32[]{:S(2)}) collective-permute-start(f32[74304]{0:T(1024)S(1)} %add.222), channel_id=1, source_target_pairs={{0,16},{16,0},{32,48},{48,32},{1,17},{17,1},{33,49},{49,33},{2,18}... | collective-permute-start | bytes 891656 | tf_op jit(solution)/shard_map/ppermute | solution.py:90
  281.5 4.3 %collective-permute-done.14 = f32[74304]{0:T(1024)S(1)} collective-permute-done((f32[74304]{0:T(1024)S(1)}, f32[74304]{0:T(1024)S(1)}, u32[]{:S(2)}, u32[]{:S(2)}) %collective-permute-start.14) | collective-permute-done | bytes 297248 | tf_op jit(solution)/shard_map/ppermute | solution.py:90
  291.9 4.1 %collective-permute-done.16 = f32[74304]{0:T(1024)S(1)} collective-permute-done((f32[74304]{0:T(1024)S(1)}, f32[74304]{0:T(1024)S(1)}, u32[]{:S(2)}, u32[]{:S(2)}) %collective-permute-start.16) | collective-permute-done | bytes 297248 | tf_op jit(solution)/shard_map/ppermute | solution.py:90
  296.0 6.8 %collective-permute-start.19 = (bf16[2,1,144,64]{2,3,1,0:T(8,128)(2,1)S(1)}, bf16[2,1,144,64]{2,3,1,0:T(8,128)(2,1)S(1)}, u32[]{:S(2)}, u32[]{:S(2)}) collective-permute-start(bf16[2,1,144,64]{2,3,1,0:T(8,128)(2,1)S(1)} %maximum_select_fusion.3), channel_id=1, source_target_pairs={{0,2},{1,3},{2,0},{3,1},{4,6},{5,7},{6,4},{7,5},{8,10},{9,11},{10,... | collective-permute-start | bytes 110600 | tf_op jit(solution)/shard_map/ppermute | solution.py:128
  305.0 6.4 %collective-permute-done.18 = f32[74304]{0:T(1024)S(1)} collective-permute-done((f32[74304]{0:T(1024)S(1)}, f32[74304]{0:T(1024)S(1)}, u32[]{:S(2)}, u32[]{:S(2)}) %collective-permute-start.18) | collective-permute-done | bytes 297248 | tf_op jit(solution)/shard_map/ppermute | solution.py:90
  333.0 25.3 %all_gather.47 = bf16[12,4,128,64]{2,3,1,0:T(8,128)(2,1)S(1)} all-gather(bf16[1,4,128,64]{2,3,1,0:T(8,128)(2,1)S(1)} %pad_maximum_fusion.11), channel_id=1, replica_groups=mesh['face'=12,'row'=4,'col'=16] {'face'}, dimensions={0}, use_global_device_ids=true | all-gather | bytes 851968 | tf_op jit(solution)/shard_map/all_gather | solution.py:171
  (294 shorter events, 87.8 us)
Async XLA Ops:
  1.5 91.9 %collective-permute-start = (bf16[1,1,8,64]{3,2,1,0:T(8,128)(2,1)S(1)}, bf16[1,1,8,64]{3,2,1,0:T(8,128)(2,1)S(1)}, u32[]{:S(2)}, u32[]{:S(2)}) collective-permute-start(bf16[1,1,8,64]{3,2,1,0:T(8,128)(2,1)S(1)} %get-tuple-element.326), channel_id=1, source_target_pairs={{0,16},{16,32},{32,48},{1,17},{17,33},{33,49},{2,18},{18,34},{34,5... | collective-permute-start | bytes 3080 | tf_op jit(solution)/shard_map/ppermute | solution.py:21
  2.8 90.6 %collective-permute-start.1 = (bf16[1,1,8,64]{3,2,1,0:T(8,128)(2,1)S(1)}, bf16[1,1,8,64]{3,2,1,0:T(8,128)(2,1)S(1)}, u32[]{:S(2)}, u32[]{:S(2)}) collective-permute-start(bf16[1,1,8,64]{3,2,1,0:T(8,128)(2,1)S(1)} %get-tuple-element.325), channel_id=1, source_target_pairs={{16,0},{32,16},{48,32},{17,1},{33,17},{49,33},{18,2},{34,18},{50,3... | collective-permute-start | bytes 3080 | tf_op jit(solution)/shard_map/ppermute | solution.py:23
  93.5 17.1 %collective-permute-start.2 = (bf16[1,34,1,64]{3,2,1,0:T(2,128)(2,1)S(1)}, bf16[1,34,1,64]{3,2,1,0:T(2,128)(2,1)S(1)}, u32[]{:S(2)}, u32[]{:S(2)}) collective-permute-start(bf16[1,34,1,64]{3,2,1,0:T(2,128)(2,1)S(1)} %get-tuple-element.303), channel_id=1, source_target_pairs={{0,1},{1,2},{2,3},{3,4},{4,5},{5,6},{6,7},{7,8},{8,9},{9,10},{10,1... | collective-permute-start | bytes 13064 | tf_op jit(solution)/shard_map/ppermute | solution.py:21
  95.4 15.2 %collective-permute-start.3 = (bf16[1,34,1,64]{3,2,1,0:T(2,128)(2,1)S(1)}, bf16[1,34,1,64]{3,2,1,0:T(2,128)(2,1)S(1)}, u32[]{:S(2)}, u32[]{:S(2)}) collective-permute-start(bf16[1,34,1,64]{3,2,1,0:T(2,128)(2,1)S(1)} %get-tuple-element.304), channel_id=1, source_target_pairs={{1,0},{2,1},{3,2},{4,3},{5,4},{6,5},{7,6},{8,7},{9,8},{10,9},{11,1... | collective-permute-start | bytes 13064 | tf_op jit(solution)/shard_map/ppermute | solution.py:23
  165.5 34.5 %collective-permute-start.4 = (f32[74304]{0:T(1024)S(1)}, f32[74304]{0:T(1024)S(1)}, u32[]{:S(2)}, u32[]{:S(2)}) collective-permute-start(f32[74304]{0:T(1024)S(1)} %pad_maximum_fusion), channel_id=1, source_target_pairs={{0,256},{64,320},{128,384},{192,448},{256,512},{320,576},{384,640}... | collective-permute-start | bytes 891656 | tf_op jit(solution)/shard_map/ppermute | solution.py:90
  168.8 31.2 %collective-permute-start.5 = (f32[74304]{0:T(1024)S(1)}, f32[74304]{0:T(1024)S(1)}, u32[]{:S(2)}, u32[]{:S(2)}) collective-permute-start(f32[74304]{0:T(1024)S(1)} %pad_maximum_fusion), channel_id=1, source_target_pairs={{0,512},{64,576},{128,640},{192,704},{256,0},{320,64},{384,128},{4... | collective-permute-start | bytes 891656 | tf_op jit(solution)/shard_map/ppermute | solution.py:90
  200.1 12.6 %collective-permute-start.6 = (f32[74304]{0:T(1024)S(1)}, f32[74304]{0:T(1024)S(1)}, u32[]{:S(2)}, u32[]{:S(2)}) collective-permute-start(f32[74304]{0:T(1024)S(1)} %select_add_fusion), channel_id=1, source_target_pairs={{0,64},{64,0},{128,192},{192,128},{256,320},{320,256},{384,448},{4... | collective-permute-start | bytes 891656 | tf_op jit(solution)/shard_map/ppermute | solution.py:90
  234.5 12.8 %collective-permute-start.11 = (f32[74304]{0:T(1024)S(1)}, f32[74304]{0:T(1024)S(1)}, u32[]{:S(2)}, u32[]{:S(2)}) collective-permute-start(f32[74304]{0:T(1024)S(1)} %add.217), channel_id=1, source_target_pairs={{0,128},{64,192},{128,0},{192,64},{256,384},{320,448},{384,256},{4... | collective-permute-start | bytes 891656 | tf_op jit(solution)/shard_map/ppermute | solution.py:90
  247.4 12.9 %collective-permute-start.12 = (f32[74304]{0:T(1024)S(1)}, f32[74304]{0:T(1024)S(1)}, u32[]{:S(2)}, u32[]{:S(2)}) collective-permute-start(f32[74304]{0:T(1024)S(1)} %add.221), channel_id=1, source_target_pairs={{0,32},{16,48},{32,0},{48,16},{1,33},{17,49},{33,1},{49,17},{2,34}... | collective-permute-start | bytes 891656 | tf_op jit(solution)/shard_map/ppermute | solution.py:90
  252.4 7.0 %collective-permute-start.13 = (bf16[1,1,40,64]{3,2,1,0:T(8,128)(2,1)S(1)}, bf16[1,1,40,64]{3,2,1,0:T(8,128)(2,1)S(1)}, u32[]{:S(2)}, u32[]{:S(2)}) collective-permute-start(bf16[1,1,40,64]{3,2,1,0:T(8,128)(2,1)S(1)} %maximum_bitcast_fusion.1), channel_id=1, source_target_pairs={{0,16},{16,0},{32,48},{48,32},{1,17},{17,1},{33,49},{49,33},{2,18}... | collective-permute-start | bytes 15368 | tf_op jit(solution)/shard_map/ppermute | solution.py:128
  260.3 20.7 %collective-permute-start.15 = (bf16[2,1,40,64]{3,2,1,0:T(8,128)(2,1)S(1)}, bf16[2,1,40,64]{3,2,1,0:T(8,128)(2,1)S(1)}, u32[]{:S(2)}, u32[]{:S(2)}) collective-permute-start(bf16[2,1,40,64]{3,2,1,0:T(8,128)(2,1)S(1)} %maximum_select_fusion.5), channel_id=1, source_target_pairs={{0,32},{16,48},{32,0},{48,16},{1,33},{17,49},{33,1},{49,17},{2,34}... | collective-permute-start | bytes 30728 | tf_op jit(solution)/shard_map/ppermute | solution.py:128
  265.3 48.3 %collective-permute-start.7 = (bf16[1,1,8,64]{3,2,1,0:T(8,128)(2,1)S(1)}, bf16[1,1,8,64]{3,2,1,0:T(8,128)(2,1)S(1)}, u32[]{:S(2)}, u32[]{:S(2)}) collective-permute-start(bf16[1,1,8,64]{3,2,1,0:T(8,128)(2,1)S(1)} %get-tuple-element.311), channel_id=1, source_target_pairs={{0,16},{16,32},{32,48},{1,17},{17,33},{33,49},{2,18},{18,34},{34,5... | collective-permute-start | bytes 3080 | tf_op jit(solution)/shard_map/ppermute | solution.py:21
  266.6 47.2 %collective-permute-start.8 = (bf16[1,1,8,64]{3,2,1,0:T(8,128)(2,1)S(1)}, bf16[1,1,8,64]{3,2,1,0:T(8,128)(2,1)S(1)}, u32[]{:S(2)}, u32[]{:S(2)}) collective-permute-start(bf16[1,1,8,64]{3,2,1,0:T(8,128)(2,1)S(1)} %get-tuple-element.310), channel_id=1, source_target_pairs={{16,0},{32,16},{48,32},{17,1},{33,17},{49,33},{18,2},{34,18},{50,3... | collective-permute-start | bytes 3080 | tf_op jit(solution)/shard_map/ppermute | solution.py:23
  275.0 10.8 %collective-permute-start.14 = (f32[74304]{0:T(1024)S(1)}, f32[74304]{0:T(1024)S(1)}, u32[]{:S(2)}, u32[]{:S(2)}) collective-permute-start(f32[74304]{0:T(1024)S(1)} %add.222), channel_id=1, source_target_pairs={{0,16},{16,0},{32,48},{48,32},{1,17},{17,1},{33,49},{49,33},{2,18}... | collective-permute-start | bytes 891656 | tf_op jit(solution)/shard_map/ppermute | solution.py:90
  285.8 10.2 %collective-permute-start.16 = (f32[74304]{0:T(1024)S(1)}, f32[74304]{0:T(1024)S(1)}, u32[]{:S(2)}, u32[]{:S(2)}) collective-permute-start(f32[74304]{0:T(1024)S(1)} %add.224), channel_id=1, source_target_pairs={{0,8},{1,9},{2,10},{3,11},{4,12},{5,13},{6,14},{7,15},{8,0},{9,1},... | collective-permute-start | bytes 891656 | tf_op jit(solution)/shard_map/ppermute | solution.py:90
  288.7 3.1 collective-permute-start.17
  296.0 9.0 %collective-permute-start.19 = (bf16[2,1,144,64]{2,3,1,0:T(8,128)(2,1)S(1)}, bf16[2,1,144,64]{2,3,1,0:T(8,128)(2,1)S(1)}, u32[]{:S(2)}, u32[]{:S(2)}) collective-permute-start(bf16[2,1,144,64]{2,3,1,0:T(8,128)(2,1)S(1)} %maximum_select_fusion.3), channel_id=1, source_target_pairs={{0,2},{1,3},{2,0},{3,1},{4,6},{5,7},{6,4},{7,5},{8,10},{9,11},{10,... | collective-permute-start | bytes 110600 | tf_op jit(solution)/shard_map/ppermute | solution.py:128
  302.8 8.7 %collective-permute-start.18 = (f32[74304]{0:T(1024)S(1)}, f32[74304]{0:T(1024)S(1)}, u32[]{:S(2)}, u32[]{:S(2)}) collective-permute-start(f32[74304]{0:T(1024)S(1)} %add.226), channel_id=1, source_target_pairs={{0,4},{1,5},{2,6},{3,7},{4,0},{5,1},{6,2},{7,3},{8,12},{9,13},{10,... | collective-permute-start | bytes 891656 | tf_op jit(solution)/shard_map/ppermute | solution.py:90
  311.5 9.5 %collective-permute-start.20 = (f32[74304]{0:T(1024)S(1)}, f32[74304]{0:T(1024)S(1)}, u32[]{:S(2)}, u32[]{:S(2)}) collective-permute-start(f32[74304]{0:T(1024)S(1)} %add.228), channel_id=1, source_target_pairs={{0,2},{1,3},{2,0},{3,1},{4,6},{5,7},{6,4},{7,5},{8,10},{9,11},{10,... | collective-permute-start | bytes 891656 | tf_op jit(solution)/shard_map/ppermute | solution.py:90
  314.0 6.9 %collective-permute-start.21 = (bf16[4,1,144,64]{2,3,1,0:T(8,128)(2,1)S(1)}, bf16[4,1,144,64]{2,3,1,0:T(8,128)(2,1)S(1)}, u32[]{:S(2)}, u32[]{:S(2)}) collective-permute-start(bf16[4,1,144,64]{2,3,1,0:T(8,128)(2,1)S(1)} %maximum_select_fusion.2), channel_id=1, source_target_pairs={{0,4},{1,5},{2,6},{3,7},{4,0},{5,1},{6,2},{7,3},{8,12},{9,13},{10,... | collective-permute-start | bytes 221192 | tf_op jit(solution)/shard_map/ppermute | solution.py:128
  316.1 8.7 %collective-permute-start.10 = (bf16[1,34,1,64]{1,3,2,0:T(8,128)(2,1)S(1)}, bf16[1,34,1,64]{1,3,2,0:T(8,128)(2,1)S(1)}, u32[]{:S(2)}, u32[]{:S(2)}) collective-permute-start(bf16[1,34,1,64]{1,3,2,0:T(8,128)(2,1)S(1)} %get-tuple-element.279), channel_id=1, source_target_pairs={{1,0},{2,1},{3,2},{4,3},{5,4},{6,5},{7,6},{8,7},{9,8},{10,9},{11,1... | collective-permute-start | bytes 13064 | tf_op jit(solution)/shard_map/ppermute | solution.py:23
  318.0 6.7 %collective-permute-start.9 = (bf16[1,34,1,64]{1,3,2,0:T(8,128)(2,1)S(1)}, bf16[1,34,1,64]{1,3,2,0:T(8,128)(2,1)S(1)}, u32[]{:S(2)}, u32[]{:S(2)}) collective-permute-start(bf16[1,34,1,64]{1,3,2,0:T(8,128)(2,1)S(1)} %get-tuple-element.278), channel_id=1, source_target_pairs={{0,1},{1,2},{2,3},{3,4},{4,5},{5,6},{6,7},{7,8},{8,9},{9,10},{10,1... | collective-permute-start | bytes 13064 | tf_op jit(solution)/shard_map/ppermute | solution.py:21
  321.0 10.9 %collective-permute-start.22 = (bf16[8,1,144,64]{2,3,1,0:T(8,128)(2,1)S(1)}, bf16[8,1,144,64]{2,3,1,0:T(8,128)(2,1)S(1)}, u32[]{:S(2)}, u32[]{:S(2)}) collective-permute-start(bf16[8,1,144,64]{2,3,1,0:T(8,128)(2,1)S(1)} %maximum_select_fusion.1), channel_id=1, source_target_pairs={{0,8},{1,9},{2,10},{3,11},{4,12},{5,13},{6,14},{7,15},{8,0},{9,1},... | collective-permute-start | bytes 442376 | tf_op jit(solution)/shard_map/ppermute | solution.py:128
  325.1 43.5 %collective-permute-start.23 = (f32[74304]{0:T(1024)S(1)}, f32[74304]{0:T(1024)S(1)}, u32[]{:S(2)}, u32[]{:S(2)}) collective-permute-start(f32[74304]{0:T(1024)S(1)} %add.230), channel_id=1, source_target_pairs={{0,1},{1,0},{2,3},{3,2},{4,5},{5,4},{6,7},{7,6},{8,9},{9,8},{10,11... | collective-permute-start | bytes 891656 | tf_op jit(solution)/shard_map/ppermute | solution.py:90
  (9 other events, 85.3 us)

commit v6 on v4

--- a/solution.py
+++ b/solution.py
@@ -44,83 +44,123 @@
     return kernel_tap(-row_step, -col_step)
 
 
-def nested_sum(values, carried=None):
-    for axis in ("col", "row", "face"):
-        if carried is None:
-            values = lax.psum(values, axis)
-        else:
-            values = carried.beside(lambda part, axis=axis: lax.psum(part, axis), values)
-    return values
-
-
-def channel_pair(first_sum, second_sum, carried=None):
-    return nested_sum((first_sum, second_sum), carried)
-
-
 def gathered_sum(values):
     for axis in ("col", "row", "face"):
         values = jnp.sum(lax.all_gather(values, axis, axis=0, tiled=False), axis=0)
     return values
 
 
-def sum_steps():
-    faces = lax.axis_size("face")
-    steps = [
-        (
-            "face",
-            [
-                [(i, (i + 4) % faces) for i in range(faces)],
-                [(i, (i + 8) % faces) for i in range(faces)],
-            ],
-        ),
-        ("face", [[(i, i ^ 1) for i in range(faces)]]),
-        ("face", [[(i, i ^ 2) for i in range(faces)]]),
-    ]
-    for axis in ("row", "col"):
-        count = lax.axis_size(axis)
-        step = count // 2
-        while step >= 1:
-            steps.append((axis, [[(i, i ^ step) for i in range(count)]]))
-            step //= 2
-    return steps
-
-
-def step_send(step, values):
-    axis, pair_sets = step
-    return [lax.ppermute(values, axis, pairs) for pairs in pair_sets]
-
-
-def step_land(step, values, moved):
-    if len(moved) == 1:
+def axis_pairs(axis, step_size):
+    return [(i, i ^ step_size) for i in range(lax.axis_size(axis))]
+
+
+def upper(axis, step_size):
+    return (lax.axis_index(axis) // step_size) % 2 == 1
+
+
+def adding_step(axis, step_size):
+    def send(values):
+        return [lax.ppermute(values, axis, axis_pairs(axis, step_size))]
+
+    def land(values, moved):
         return values + moved[0]
-    from_before, from_after = moved
-    group = lax.axis_index("face") // 4
-    first = jnp.where(group == 0, values, jnp.where(group == 1, from_before, from_after))
-    second = jnp.where(group == 0, from_after, jnp.where(group == 1, values, from_before))
-    third = jnp.where(group == 0, from_before, jnp.where(group == 1, from_after, values))
-    return (first + second) + third
-
-
-class Carried:
-    def __init__(self, values):
+
+    return send, land
+
+
+def grouping_step():
+    def send(values):
+        faces = lax.axis_size("face")
+        return [
+            lax.ppermute(values, "face", [(i, (i + 4) % faces) for i in range(faces)]),
+            lax.ppermute(values, "face", [(i, (i + 8) % faces) for i in range(faces)]),
+        ]
+
+    def land(values, moved):
+        from_before, from_after = moved
+        group = lax.axis_index("face") // 4
+        first = jnp.where(group == 0, values, jnp.where(group == 1, from_before, from_after))
+        second = jnp.where(group == 0, from_after, jnp.where(group == 1, values, from_before))
+        third = jnp.where(group == 0, from_before, jnp.where(group == 1, from_after, values))
+        return (first + second) + third
+
+    return send, land
+
+
+def halving_step(axis, step_size):
+    def send(values):
+        half = values.shape[0] // 2
+        given = jnp.where(upper(axis, step_size), values[:half], values[half:])
+        return [lax.ppermute(given, axis, axis_pairs(axis, step_size))]
+
+    def land(values, moved):
+        half = values.shape[0] // 2
+        return jnp.where(upper(axis, step_size), values[half:], values[:half]) + moved[0]
+
+    return send, land
+
+
+def doubling_step(axis, step_size):
+    def send(values):
+        return [lax.ppermute(values, axis, axis_pairs(axis, step_size))]
+
+    def land(values, moved):
+        return jnp.where(
+            upper(axis, step_size),
+            jnp.concatenate([moved[0], values], axis=0),
+            jnp.concatenate([values, moved[0]], axis=0),
+        )
+
+    return send, land
+
+
+def bits(axis):
+    count = lax.axis_size(axis)
+    sizes = []
+    step_size = 1
+    while step_size < count:
+        sizes.append(step_size)
+        step_size *= 2
+    return sizes
+
+
+def face_steps():
+    return [grouping_step(), adding_step("face", 1), adding_step("face", 2)]
+
+
+def butterfly_steps():
+    steps = [adding_step("col", b) for b in bits("col")]
+    steps += [adding_step("row", b) for b in bits("row")]
+    return steps + face_steps()
+
+
+def scatter_gather_steps():
+    steps = [halving_step("col", b) for b in bits("col")]
+    steps += [halving_step("row", b) for b in bits("row")]
+    steps += face_steps()
+    steps += [doubling_step("row", b) for b in reversed(bits("row"))]
+    return steps + [doubling_step("col", b) for b in reversed(bits("col"))]
+
+
+class Chain:
+    def __init__(self, values, steps):
         self.values = values
-        self.steps = sum_steps()
-
-    def beside(self, collective, operand):
-        if not self.steps:
-            return collective(operand)
-        step = self.steps.pop(0)
-        values, operand = lax.optimization_barrier((self.values, operand))
-        moved = step_send(step, values)
-        result = collective(operand)
-        self.values = step_land(step, values, moved)
-        return result
-
-    def finish(self):
-        while self.steps:
-            step = self.steps.pop(0)
-            self.values = step_land(step, self.values, step_send(step, self.values))
-        return self.values
+        self.steps = steps
+
+
+def lockstep(chains):
+    active = [chain for chain in chains if chain.steps]
+    steps = [chain.steps.pop(0) for chain in active]
+    values = lax.optimization_barrier(tuple(chain.values for chain in active))
+    moved = [step[0](value) for step, value in zip(steps, values)]
+    for chain, step, value, arrived in zip(active, steps, values, moved):
+        chain.values = step[1](value, arrived)
+
+
+def run_chains(chains):
+    while any(chain.steps for chain in chains):
+        lockstep(chains)
+    return [chain.values for chain in chains]
 
 
 def lined(first_val, middle_val, last_val, length):
@@ -146,10 +186,12 @@
 
     def extend(values, carried=None):
         def gather(part, axis, tiled):
-            def run(operand):
-                return lax.all_gather(operand, axis, axis=0, tiled=tiled)
-
-            return run(part) if carried is None else carried.beside(run, part)
+            if carried is None or axis == "face":
+                return lax.all_gather(part, axis, axis=0, tiled=tiled)
+            own = Chain(part[None], [doubling_step(axis, b) for b in bits(axis)])
+            while own.steps:
+                lockstep([own, carried])
+            return own.values
 
         padded = padded_2(values, (("row", 1), ("col", 2)), 1)
         row_strip = jnp.where(row_index == 0, values[:, 0], values[:, tile_rows - 1])
@@ -266,24 +308,29 @@
             )
         )
     taps = 9
-    carried = Carried(
-        jnp.concatenate(
-            [
-                jnp.stack(slope_sums).reshape(-1),
-                jnp.stack(centred_sums).reshape(-1),
-                jnp.stack(state_sums).reshape(-1),
-            ]
-        )
-    )
-    shift_grad, gain_grad = channel_pair(
-        jnp.sum(before_grad, axis=0), jnp.sum(before_grad * normed, axis=0), carried
-    )
+    payload = jnp.concatenate(
+        [
+            jnp.stack(slope_sums).reshape(-1),
+            jnp.stack(centred_sums).reshape(-1),
+            jnp.stack(state_sums).reshape(-1),
+        ]
+    )
+    pieces = row_count * col_count
+    padding = (-payload.shape[0]) % pieces
+    carried = Chain(jnp.pad(payload, (0, padding)), scatter_gather_steps())
+    stats = Chain(
+        jnp.stack([jnp.sum(before_grad, axis=0), jnp.sum(before_grad * normed, axis=0)]),
+        butterfly_steps(),
+    )
+    while stats.steps:
+        lockstep([stats, carried])
+    shift_grad, gain_grad = stats.values[0], stats.values[1]
     response_grad = (
         gain * inverse_spread * (before_grad - shift_grad / total - normed * gain_grad / total)
     ).astype(jnp.bfloat16)
     grad_tile = response_grad.reshape(local_faces, tile_rows, tile_cols, width)
     padded_grad = extend(grad_tile, carried)
-    kernel_sums = carried.finish()
+    kernel_sums = run_chains([carried])[0]
     block = taps * width * width
     slope_total = kernel_sums[:block].reshape(taps, width, width)
     centred_total = kernel_sums[block : 2 * block].reshape(taps, width, width)

time: 403 us -> 379 us (0.940)
  blocking collectives: 235 us -> 145 us
  starting transfers between devices: 57.2 us -> 134 us
  waiting for transfers between devices: 53.9 us -> 42 us
    ppermute x10 -> x32, starting transfers between devices: 33.8 us -> 109 us  [the longest x22 73.8 us: send(): return [lax.ppermute(values, axis, axis_pairs(axis, step_size))]]
    psum x3 -> x0, blocking collectives: 54.2 us -> none  [nested_sum(): lax.psum(part, axis)]
    all_gather x6 -> x4, blocking collectives: 133 us -> 97.2 us  [gather(): return lax.all_gather(part, axis, axis=0, tiled=tiled)]
    ppermute x10 -> x32, waiting for transfers between devices: 48.6 us -> 42 us  [the longest x22 39 us: send(): return [lax.ppermute(values, axis, axis_pairs(axis, step_size))]]
    ppermute x4, waiting for transfers between devices: 5.27 us -> 0.01 us  [padded_2(): lax.ppermute(tail, axis, [(i, (i + 1) % count) for i in range(ends)])]
  transfers between devices with their start and end apart: 18 -> 40, of which waited for: 7 -> 13; matrix products, arithmetic and copies ran while one was open for 7% -> 10% of each run, Pallas kernels for 0% -> 0%
where the time goes in v6:
time: 379 us; the launch traced here: 377 us
  blocking collectives  145 us (38%)
  starting transfers between devices  134 us (35%)
  waiting for transfers between devices  42 us (11%)
  local copies, waits for them, and re-layouts  28.6 us (8%)
  other arithmetic  15.5 us (4%)
  between operations  6.13 us (2%)
  matrix products  5.68 us (1%)
    all_gather x4, blocking collectives, gather(): return lax.all_gather(part, axis, axis=0, tiled=tiled)  97.2 us
    ppermute x22, starting transfers between devices, send(): return [lax.ppermute(values, axis, axis_pairs(axis, step_size))]  73.8 us
    all_gather x3, blocking collectives, gathered_sum(): values = jnp.sum(lax.all_gather(values, axis, axis=0, tiled=False), axis=0)  48 us
    ppermute x22, waiting for transfers between devices, send(): return [lax.ppermute(values, axis, axis_pairs(axis, step_size))]  39 us
    ppermute x4, starting transfers between devices, padded_2(): lax.ppermute(head, axis, [((i + 1) % count, i) for i in range(ends)])  18.2 us
    ppermute x6, starting transfers between devices, send(): return [lax.ppermute(given, axis, axis_pairs(axis, step_size))]  15.9 us
    ppermute x2, starting transfers between devices, send(): lax.ppermute(values, 'face', [(i, (i + 8) % faces) for i in range(faces)])  12.8 us
  transfers between devices with their start and end apart: 40, of which 13 were waited for; matrix products, arithmetic and copies ran while one was open for 10% of the time, Pallas kernels for 0%

profile of v6, /device:TPU:56, one launch (start us, length us, event | category | flops | bytes accessed | tf_op | source)
XLA Modules:
  0.0 377.0 jit_solution(11583709487205818633)
XLA Ops:
  2.8 5.4 %collective-permute-start.1 = (bf16[1,1,8,64]{3,2,1,0:T(8,128)(2,1)S(1)}, bf16[1,1,8,64]{3,2,1,0:T(8,128)(2,1)S(1)}, u32[]{:S(2)}, u32[]{:S(2)}) collective-permute-start(bf16[1,1,8,64]{3,2,1,0:T(8,128)(2,1)S(1)} %get-tuple-element.341), channel_id=1, source_target_pairs={{16,0},{32,16},{48,32},{17,1},{33,17},{49,33},{18,2},{34,18},{50,3... | collective-permute-start | bytes 3080 | tf_op jit(solution)/shard_map/ppermute | solution.py:23
  8.3 13.7 %all-gather = bf16[4,40,64]{2,1,0:T(8,128)(2,1)S(1)} all-gather(bf16[1,40,64]{2,1,0:T(8,128)(2,1)S(1)} %pad_maximum_fusion.18), channel_id=2, replica_groups=mesh['face'=12,'row'=4,'col'=16] {'row'}, dimensions={0}, use_global_device_ids=true | all-gather | bytes 25600 | tf_op jit(solution)/shard_map/all_gather | solution.py:190
  22.5 23.2 %all-gather.1 = bf16[16,144,64]{1,2,0:T(8,128)(2,1)S(1)} all-gather(bf16[1,144,64]{1,2,0:T(8,128)(2,1)S(1)} %pad_maximum_fusion.12), channel_id=3, replica_groups=mesh['face'=12,'row'=4,'col'=16] {'col'}, dimensions={0}, use_global_device_ids=true | all-gather | bytes 313344 | tf_op jit(solution)/shard_map/all_gather | solution.py:190
  47.2 33.3 %all_gather.40 = bf16[12,4,128,64]{2,3,1,0:T(8,128)(2,1)S(1)} all-gather(bf16[1,4,128,64]{2,3,1,0:T(8,128)(2,1)S(1)} %pad_maximum_fusion.10), channel_id=1, replica_groups=mesh['face'=12,'row'=4,'col'=16] {'face'}, dimensions={0}, use_global_device_ids=true | all-gather | bytes 851968 | tf_op jit(solution)/shard_map/all_gather | solution.py:190
  93.9 17.2 %all-gather.5 = f32[16,2,64]{2,1,0:T(2,128)S(1)} all-gather(f32[1,2,64]{2,1,0:T(2,128)S(1)} %maximum_bitcast_fusion.2), channel_id=4, replica_groups=mesh['face'=12,'row'=4,'col'=16] {'col'}, dimensions={0}, use_global_device_ids=true | all-gather | bytes 8704 | tf_op jit(solution)/shard_map/all_gather | solution.py:49
  111.2 11.2 %all-gather.6 = f32[4,2,64]{2,1,0:T(2,128)S(1)} all-gather(f32[1,2,64]{2,1,0:T(2,128)S(1)} %bitcast.419), channel_id=5, replica_groups=mesh['face'=12,'row'=4,'col'=16] {'row'}, dimensions={0}, use_global_device_ids=true | all-gather | bytes 2560 | tf_op jit(solution)/shard_map/all_gather | solution.py:49
  122.4 19.6 %all-gather.7 = f32[12,2,64]{2,1,0:T(2,128)S(1)} all-gather(f32[1,2,64]{2,1,0:T(2,128)S(1)} %bitcast.422), channel_id=6, replica_groups=mesh['face'=12,'row'=4,'col'=16] {'face'}, dimensions={0}, use_global_device_ids=true | all-gather | bytes 6656 | tf_op jit(solution)/shard_map/all_gather | solution.py:49
  171.9 3.9 %collective-permute-start.8 = (f32[2,64]{1,0:T(2,128)S(1)}, f32[2,64]{1,0:T(2,128)S(1)}, u32[]{:S(2)}, u32[]{:S(2)}) collective-permute-start(f32[2,64]{1,0:T(2,128)S(1)} %add.258), channel_id=1, source_target_pairs={{0,4},{1,5},{2,6},{3,7},{4,0},{5,1},{6,2},{7,3},{8,12},{9,13},{10,... | collective-permute-start | bytes 1544 | tf_op jit(solution)/shard_map/ppermute | solution.py:63
  181.4 5.4 %collective-permute-start.10 = (f32[2,64]{1,0:T(2,128)S(1)}, f32[2,64]{1,0:T(2,128)S(1)}, u32[]{:S(2)}, u32[]{:S(2)}) collective-permute-start(f32[2,64]{1,0:T(2,128)S(1)} %add.261), channel_id=1, source_target_pairs={{0,8},{1,9},{2,10},{3,11},{4,12},{5,13},{6,14},{7,15},{8,0},{9,1},... | collective-permute-start | bytes 1544 | tf_op jit(solution)/shard_map/ppermute | solution.py:63
  192.3 4.8 %collective-permute-start.12 = (f32[2,64]{1,0:T(2,128)S(1)}, f32[2,64]{1,0:T(2,128)S(1)}, u32[]{:S(2)}, u32[]{:S(2)}) collective-permute-start(f32[2,64]{1,0:T(2,128)S(1)} %add.264), channel_id=1, source_target_pairs={{0,16},{16,0},{32,48},{48,32},{1,17},{17,1},{33,49},{49,33},{2,18}... | collective-permute-start | bytes 1544 | tf_op jit(solution)/shard_map/ppermute | solution.py:63
  198.8 5.0 %collective-permute-start.15 = (f32[1161]{0:T(1024)S(1)}, f32[1161]{0:T(1024)S(1)}, u32[]{:S(2)}, u32[]{:S(2)}) collective-permute-start(f32[1161]{0:T(1024)S(1)} %slice_select_fusion.5), channel_id=1, source_target_pairs={{0,32},{16,48},{32,0},{48,16},{1,33},{17,49},{33,1},{49,17},{2,34}... | collective-permute-start | bytes 13940 | tf_op jit(solution)/shard_map/ppermute | solution.py:94
  203.8 4.7 %collective-permute-start.14 = (f32[2,64]{1,0:T(2,128)S(1)}, f32[2,64]{1,0:T(2,128)S(1)}, u32[]{:S(2)}, u32[]{:S(2)}) collective-permute-start(f32[2,64]{1,0:T(2,128)S(1)} %add.267), channel_id=1, source_target_pairs={{0,32},{16,48},{32,0},{48,16},{1,33},{17,49},{33,1},{49,17},{2,34}... | collective-permute-start | bytes 1544 | tf_op jit(solution)/shard_map/ppermute | solution.py:63
  208.6 4.6 %collective-permute-done.14 = f32[2,64]{1,0:T(2,128)S(1)} collective-permute-done((f32[2,64]{1,0:T(2,128)S(1)}, f32[2,64]{1,0:T(2,128)S(1)}, u32[]{:S(2)}, u32[]{:S(2)}) %collective-permute-start.14) | collective-permute-done | bytes 544 | tf_op jit(solution)/shard_map/ppermute | solution.py:63
  216.6 6.4 %collective-permute-start.17 = (f32[2,64]{1,0:T(2,128)S(1)}, f32[2,64]{1,0:T(2,128)S(1)}, u32[]{:S(2)}, u32[]{:S(2)}) collective-permute-start(f32[2,64]{1,0:T(2,128)S(1)} %add.270), channel_id=1, source_target_pairs={{0,512},{64,576},{128,640},{192,704},{256,0},{320,64},{384,128},{4... | collective-permute-start | bytes 1544 | tf_op jit(solution)/shard_map/ppermute | solution.py:76
  227.0 6.4 %collective-permute-start.19 = (f32[1161]{0:T(1024)S(1)}, f32[1161]{0:T(1024)S(1)}, u32[]{:S(2)}, u32[]{:S(2)}) collective-permute-start(f32[1161]{0:T(1024)S(1)} %select_add_fusion.6), channel_id=1, source_target_pairs={{0,512},{64,576},{128,640},{192,704},{256,0},{320,64},{384,128},{4... | collective-permute-start | bytes 13940 | tf_op jit(solution)/shard_map/ppermute | solution.py:76
  255.9 4.7 %collective-permute-start.29 = (f32[1161]{0:T(1024)S(1)}, f32[1161]{0:T(1024)S(1)}, u32[]{:S(2)}, u32[]{:S(2)}) collective-permute-start(f32[1161]{0:T(1024)S(1)} %add.282), channel_id=1, source_target_pairs={{0,32},{16,48},{32,0},{48,16},{1,33},{17,49},{33,1},{49,17},{2,34}... | collective-permute-start | bytes 13940 | tf_op jit(solution)/shard_map/ppermute | solution.py:105
  262.0 5.4 %collective-permute-start.24 = (bf16[1,1,8,64]{3,2,1,0:T(8,128)(2,1)S(1)}, bf16[1,1,8,64]{3,2,1,0:T(8,128)(2,1)S(1)}, u32[]{:S(2)}, u32[]{:S(2)}) collective-permute-start(bf16[1,1,8,64]{3,2,1,0:T(8,128)(2,1)S(1)} %get-tuple-element.326), channel_id=1, source_target_pairs={{16,0},{32,16},{48,32},{17,1},{33,17},{49,33},{18,2},{34,18},{50,3... | collective-permute-start | bytes 3080 | tf_op jit(solution)/shard_map/ppermute | solution.py:23
  267.5 6.0 %collective-permute-start.28 = (bf16[1,1,40,64]{3,2,1,0:T(8,128)(2,1)S(1)}, bf16[1,1,40,64]{3,2,1,0:T(8,128)(2,1)S(1)}, u32[]{:S(2)}, u32[]{:S(2)}) collective-permute-start(bf16[1,1,40,64]{3,2,1,0:T(8,128)(2,1)S(1)} %maximum_bitcast_fusion.1), channel_id=1, source_target_pairs={{0,16},{16,0},{32,48},{48,32},{1,17},{17,1},{33,49},{49,33},{2,18}... | collective-permute-start | bytes 15368 | tf_op jit(solution)/shard_map/ppermute | solution.py:105
  275.2 4.8 %collective-permute-start.31 = (f32[2322]{0:T(1024)S(1)}, f32[2322]{0:T(1024)S(1)}, u32[]{:S(2)}, u32[]{:S(2)}) collective-permute-start(f32[2322]{0:T(1024)S(1)} %maximum_select_fusion.11), channel_id=1, source_target_pairs={{0,16},{16,0},{32,48},{48,32},{1,17},{17,1},{33,49},{49,33},{2,18}... | collective-permute-start | bytes 27872 | tf_op jit(solution)/shard_map/ppermute | solution.py:105
  282.3 7.6 %collective-permute-done.30 = bf16[2,1,40,64]{3,2,1,0:T(8,128)(2,1)S(1)} collective-permute-done((bf16[2,1,40,64]{3,2,1,0:T(8,128)(2,1)S(1)}, bf16[2,1,40,64]{3,2,1,0:T(8,128)(2,1)S(1)}, u32[]{:S(2)}, u32[]{:S(2)}) %collective-permute-start.30) | collective-permute-done | bytes 10272 | tf_op jit(solution)/shard_map/ppermute | solution.py:105
  292.7 3.7 collective-permute-start.33
  319.2 5.1 %collective-permute-done.37 = f32[18576]{0:T(1024)S(1)} collective-permute-done((f32[18576]{0:T(1024)S(1)}, f32[18576]{0:T(1024)S(1)}, u32[]{:S(2)}, u32[]{:S(2)}) %collective-permute-start.37) | collective-permute-done | bytes 74336 | tf_op jit(solution)/shard_map/ppermute | solution.py:105
  330.3 5.7 %collective-permute-done.38 = bf16[8,1,144,64]{2,3,1,0:T(8,128)(2,1)S(1)} collective-permute-done((bf16[8,1,144,64]{2,3,1,0:T(8,128)(2,1)S(1)}, bf16[8,1,144,64]{2,3,1,0:T(8,128)(2,1)S(1)}, u32[]{:S(2)}, u32[]{:S(2)}) %collective-permute-start.38) | collective-permute-done | bytes 147488 | tf_op jit(solution)/shard_map/ppermute | solution.py:105
  337.1 27.0 %all_gather.47 = bf16[12,4,128,64]{2,3,1,0:T(8,128)(2,1)S(1)} all-gather(bf16[1,4,128,64]{2,3,1,0:T(8,128)(2,1)S(1)} %pad_maximum_fusion.11), channel_id=1, replica_groups=mesh['face'=12,'row'=4,'col'=16] {'face'}, dimensions={0}, use_global_device_ids=true | all-gather | bytes 851968 | tf_op jit(solution)/shard_map/all_gather | solution.py:190
  (343 shorter events, 135.8 us)
Async XLA Ops:
  1.5 82.5 %collective-permute-start = (bf16[1,1,8,64]{3,2,1,0:T(8,128)(2,1)S(1)}, bf16[1,1,8,64]{3,2,1,0:T(8,128)(2,1)S(1)}, u32[]{:S(2)}, u32[]{:S(2)}) collective-permute-start(bf16[1,1,8,64]{3,2,1,0:T(8,128)(2,1)S(1)} %get-tuple-element.342), channel_id=1, source_target_pairs={{0,16},{16,32},{32,48},{1,17},{17,33},{33,49},{2,18},{18,34},{34,5... | collective-permute-start | bytes 3080 | tf_op jit(solution)/shard_map/ppermute | solution.py:21
  2.8 81.2 %collective-permute-start.1 = (bf16[1,1,8,64]{3,2,1,0:T(8,128)(2,1)S(1)}, bf16[1,1,8,64]{3,2,1,0:T(8,128)(2,1)S(1)}, u32[]{:S(2)}, u32[]{:S(2)}) collective-permute-start(bf16[1,1,8,64]{3,2,1,0:T(8,128)(2,1)S(1)} %get-tuple-element.341), channel_id=1, source_target_pairs={{16,0},{32,16},{48,32},{17,1},{33,17},{49,33},{18,2},{34,18},{50,3... | collective-permute-start | bytes 3080 | tf_op jit(solution)/shard_map/ppermute | solution.py:23
  153.8 11.3 %collective-permute-start.7 = (f32[18576]{0:T(1024)S(1)}, f32[18576]{0:T(1024)S(1)}, u32[]{:S(2)}, u32[]{:S(2)}) collective-permute-start(f32[18576]{0:T(1024)S(1)} %slice_select_fusion.1), channel_id=1, source_target_pairs={{0,2},{1,3},{2,0},{3,1},{4,6},{5,7},{6,4},{7,5},{8,10},{9,11},{10,... | collective-permute-start | bytes 222920 | tf_op jit(solution)/shard_map/ppermute | solution.py:94
  165.3 13.9 %collective-permute-start.9 = (f32[9288]{0:T(1024)S(1)}, f32[9288]{0:T(1024)S(1)}, u32[]{:S(2)}, u32[]{:S(2)}) collective-permute-start(f32[9288]{0:T(1024)S(1)} %slice_select_fusion.2), channel_id=1, source_target_pairs={{0,4},{1,5},{2,6},{3,7},{4,0},{5,1},{6,2},{7,3},{8,12},{9,13},{10,... | collective-permute-start | bytes 111464 | tf_op jit(solution)/shard_map/ppermute | solution.py:94
  179.4 10.7 %collective-permute-start.11 = (f32[4644]{0:T(1024)S(1)}, f32[4644]{0:T(1024)S(1)}, u32[]{:S(2)}, u32[]{:S(2)}) collective-permute-start(f32[4644]{0:T(1024)S(1)} %slice_select_fusion.3), channel_id=1, source_target_pairs={{0,8},{1,9},{2,10},{3,11},{4,12},{5,13},{6,14},{7,15},{8,0},{9,1},... | collective-permute-start | bytes 55736 | tf_op jit(solution)/shard_map/ppermute | solution.py:94
  181.4 8.7 %collective-permute-start.10 = (f32[2,64]{1,0:T(2,128)S(1)}, f32[2,64]{1,0:T(2,128)S(1)}, u32[]{:S(2)}, u32[]{:S(2)}) collective-permute-start(f32[2,64]{1,0:T(2,128)S(1)} %add.261), channel_id=1, source_target_pairs={{0,8},{1,9},{2,10},{3,11},{4,12},{5,13},{6,14},{7,15},{8,0},{9,1},... | collective-permute-start | bytes 1544 | tf_op jit(solution)/shard_map/ppermute | solution.py:63
  190.3 8.4 %collective-permute-start.13 = (f32[2322]{0:T(1024)S(1)}, f32[2322]{0:T(1024)S(1)}, u32[]{:S(2)}, u32[]{:S(2)}) collective-permute-start(f32[2322]{0:T(1024)S(1)} %slice_select_fusion.4), channel_id=1, source_target_pairs={{0,16},{16,0},{32,48},{48,32},{1,17},{17,1},{33,49},{49,33},{2,18}... | collective-permute-start | bytes 27872 | tf_op jit(solution)/shard_map/ppermute | solution.py:94
  198.8 14.4 %collective-permute-start.15 = (f32[1161]{0:T(1024)S(1)}, f32[1161]{0:T(1024)S(1)}, u32[]{:S(2)}, u32[]{:S(2)}) collective-permute-start(f32[1161]{0:T(1024)S(1)} %slice_select_fusion.5), channel_id=1, source_target_pairs={{0,32},{16,48},{32,0},{48,16},{1,33},{17,49},{33,1},{49,17},{2,34}... | collective-permute-start | bytes 13940 | tf_op jit(solution)/shard_map/ppermute | solution.py:94
  203.8 9.4 %collective-permute-start.14 = (f32[2,64]{1,0:T(2,128)S(1)}, f32[2,64]{1,0:T(2,128)S(1)}, u32[]{:S(2)}, u32[]{:S(2)}) collective-permute-start(f32[2,64]{1,0:T(2,128)S(1)} %add.267), channel_id=1, source_target_pairs={{0,32},{16,48},{32,0},{48,16},{1,33},{17,49},{33,1},{49,17},{2,34}... | collective-permute-start | bytes 1544 | tf_op jit(solution)/shard_map/ppermute | solution.py:63
  213.3 20.2 %collective-permute-start.16 = (f32[2,64]{1,0:T(2,128)S(1)}, f32[2,64]{1,0:T(2,128)S(1)}, u32[]{:S(2)}, u32[]{:S(2)}) collective-permute-start(f32[2,64]{1,0:T(2,128)S(1)} %add.270), channel_id=1, source_target_pairs={{0,256},{64,320},{128,384},{192,448},{256,512},{320,576},{384,640}... | collective-permute-start | bytes 1544 | tf_op jit(solution)/shard_map/ppermute | solution.py:75
  216.6 16.8 %collective-permute-start.17 = (f32[2,64]{1,0:T(2,128)S(1)}, f32[2,64]{1,0:T(2,128)S(1)}, u32[]{:S(2)}, u32[]{:S(2)}) collective-permute-start(f32[2,64]{1,0:T(2,128)S(1)} %add.270), channel_id=1, source_target_pairs={{0,512},{64,576},{128,640},{192,704},{256,0},{320,64},{384,128},{4... | collective-permute-start | bytes 1544 | tf_op jit(solution)/shard_map/ppermute | solution.py:76
  223.7 9.8 %collective-permute-start.18 = (f32[1161]{0:T(1024)S(1)}, f32[1161]{0:T(1024)S(1)}, u32[]{:S(2)}, u32[]{:S(2)}) collective-permute-start(f32[1161]{0:T(1024)S(1)} %select_add_fusion.6), channel_id=1, source_target_pairs={{0,256},{64,320},{128,384},{192,448},{256,512},{320,576},{384,640}... | collective-permute-start | bytes 13940 | tf_op jit(solution)/shard_map/ppermute | solution.py:75
  227.0 9.5 %collective-permute-start.19 = (f32[1161]{0:T(1024)S(1)}, f32[1161]{0:T(1024)S(1)}, u32[]{:S(2)}, u32[]{:S(2)}) collective-permute-start(f32[1161]{0:T(1024)S(1)} %select_add_fusion.6), channel_id=1, source_target_pairs={{0,512},{64,576},{128,640},{192,704},{256,0},{320,64},{384,128},{4... | collective-permute-start | bytes 13940 | tf_op jit(solution)/shard_map/ppermute | solution.py:76
  236.5 9.1 %collective-permute-start.21 = (f32[1161]{0:T(1024)S(1)}, f32[1161]{0:T(1024)S(1)}, u32[]{:S(2)}, u32[]{:S(2)}) collective-permute-start(f32[1161]{0:T(1024)S(1)} %select_add_fusion.5), channel_id=1, source_target_pairs={{0,64},{64,0},{128,192},{192,128},{256,320},{320,256},{384,448},{4... | collective-permute-start | bytes 13940 | tf_op jit(solution)/shard_map/ppermute | solution.py:63
  255.9 17.6 %collective-permute-start.29 = (f32[1161]{0:T(1024)S(1)}, f32[1161]{0:T(1024)S(1)}, u32[]{:S(2)}, u32[]{:S(2)}) collective-permute-start(f32[1161]{0:T(1024)S(1)} %add.282), channel_id=1, source_target_pairs={{0,32},{16,48},{32,0},{48,16},{1,33},{17,49},{33,1},{49,17},{2,34}... | collective-permute-start | bytes 13940 | tf_op jit(solution)/shard_map/ppermute | solution.py:105
  260.7 42.3 %collective-permute-start.23 = (bf16[1,1,8,64]{3,2,1,0:T(8,128)(2,1)S(1)}, bf16[1,1,8,64]{3,2,1,0:T(8,128)(2,1)S(1)}, u32[]{:S(2)}, u32[]{:S(2)}) collective-permute-start(bf16[1,1,8,64]{3,2,1,0:T(8,128)(2,1)S(1)} %get-tuple-element.327), channel_id=1, source_target_pairs={{0,16},{16,32},{32,48},{1,17},{17,33},{33,49},{2,18},{18,34},{34,5... | collective-permute-start | bytes 3080 | tf_op jit(solution)/shard_map/ppermute | solution.py:21
  262.0 41.2 %collective-permute-start.24 = (bf16[1,1,8,64]{3,2,1,0:T(8,128)(2,1)S(1)}, bf16[1,1,8,64]{3,2,1,0:T(8,128)(2,1)S(1)}, u32[]{:S(2)}, u32[]{:S(2)}) collective-permute-start(bf16[1,1,8,64]{3,2,1,0:T(8,128)(2,1)S(1)} %get-tuple-element.326), channel_id=1, source_target_pairs={{16,0},{32,16},{48,32},{17,1},{33,17},{49,33},{18,2},{34,18},{50,3... | collective-permute-start | bytes 3080 | tf_op jit(solution)/shard_map/ppermute | solution.py:23
  267.5 7.7 %collective-permute-start.28 = (bf16[1,1,40,64]{3,2,1,0:T(8,128)(2,1)S(1)}, bf16[1,1,40,64]{3,2,1,0:T(8,128)(2,1)S(1)}, u32[]{:S(2)}, u32[]{:S(2)}) collective-permute-start(bf16[1,1,40,64]{3,2,1,0:T(8,128)(2,1)S(1)} %maximum_bitcast_fusion.1), channel_id=1, source_target_pairs={{0,16},{16,0},{32,48},{48,32},{1,17},{17,1},{33,49},{49,33},{2,18}... | collective-permute-start | bytes 15368 | tf_op jit(solution)/shard_map/ppermute | solution.py:105
  280.2 9.6 %collective-permute-start.30 = (bf16[2,1,40,64]{3,2,1,0:T(8,128)(2,1)S(1)}, bf16[2,1,40,64]{3,2,1,0:T(8,128)(2,1)S(1)}, u32[]{:S(2)}, u32[]{:S(2)}) collective-permute-start(bf16[2,1,40,64]{3,2,1,0:T(8,128)(2,1)S(1)} %maximum_select_fusion.9), channel_id=1, source_target_pairs={{0,32},{16,48},{32,0},{48,16},{1,33},{17,49},{33,1},{49,17},{2,34}... | collective-permute-start | bytes 30728 | tf_op jit(solution)/shard_map/ppermute | solution.py:105
  309.3 9.7 %collective-permute-start.36 = (bf16[4,1,144,64]{2,3,1,0:T(8,128)(2,1)S(1)}, bf16[4,1,144,64]{2,3,1,0:T(8,128)(2,1)S(1)}, u32[]{:S(2)}, u32[]{:S(2)}) collective-permute-start(bf16[4,1,144,64]{2,3,1,0:T(8,128)(2,1)S(1)} %maximum_select_fusion.4), channel_id=1, source_target_pairs={{0,4},{1,5},{2,6},{3,7},{4,0},{5,1},{6,2},{7,3},{8,12},{9,13},{10,... | collective-permute-start | bytes 221192 | tf_op jit(solution)/shard_map/ppermute | solution.py:105
  311.6 16.5 %collective-permute-start.25 = (bf16[1,34,1,64]{1,3,2,0:T(8,128)(2,1)S(1)}, bf16[1,34,1,64]{1,3,2,0:T(8,128)(2,1)S(1)}, u32[]{:S(2)}, u32[]{:S(2)}) collective-permute-start(bf16[1,34,1,64]{1,3,2,0:T(8,128)(2,1)S(1)} %get-tuple-element.294), channel_id=1, source_target_pairs={{0,1},{1,2},{2,3},{3,4},{4,5},{5,6},{6,7},{7,8},{8,9},{9,10},{10,1... | collective-permute-start | bytes 13064 | tf_op jit(solution)/shard_map/ppermute | solution.py:21
  313.5 14.6 %collective-permute-start.26 = (bf16[1,34,1,64]{1,3,2,0:T(8,128)(2,1)S(1)}, bf16[1,34,1,64]{1,3,2,0:T(8,128)(2,1)S(1)}, u32[]{:S(2)}, u32[]{:S(2)}) collective-permute-start(bf16[1,34,1,64]{1,3,2,0:T(8,128)(2,1)S(1)} %get-tuple-element.295), channel_id=1, source_target_pairs={{1,0},{2,1},{3,2},{4,3},{5,4},{6,5},{7,6},{8,7},{9,8},{10,9},{11,1... | collective-permute-start | bytes 13064 | tf_op jit(solution)/shard_map/ppermute | solution.py:23
  324.4 11.7 %collective-permute-start.38 = (bf16[8,1,144,64]{2,3,1,0:T(8,128)(2,1)S(1)}, bf16[8,1,144,64]{2,3,1,0:T(8,128)(2,1)S(1)}, u32[]{:S(2)}, u32[]{:S(2)}) collective-permute-start(bf16[8,1,144,64]{2,3,1,0:T(8,128)(2,1)S(1)} %maximum_select_fusion.2), channel_id=1, source_target_pairs={{0,8},{1,9},{2,10},{3,11},{4,12},{5,13},{6,14},{7,15},{8,0},{9,1},... | collective-permute-start | bytes 442376 | tf_op jit(solution)/shard_map/ppermute | solution.py:105
  328.4 46.0 %collective-permute-start.39 = (f32[37152]{0:T(1024)S(1)}, f32[37152]{0:T(1024)S(1)}, u32[]{:S(2)}, u32[]{:S(2)}) collective-permute-start(f32[37152]{0:T(1024)S(1)} %maximum_select_fusion.3), channel_id=1, source_target_pairs={{0,1},{1,0},{2,3},{3,2},{4,5},{5,4},{6,7},{7,6},{8,9},{9,8},{10,11... | collective-permute-start | bytes 445832 | tf_op jit(solution)/shard_map/ppermute | solution.py:105
  (24 other events, 107.2 us)

commit v7 on v5

--- a/solution.py
+++ b/solution.py
@@ -10,21 +10,14 @@
 GAUSS_NORM = 0.3989422804014327
 
 
-def padded_2(cells, sides, width):
-    for axis, dim in sides:
-        count = lax.axis_size(axis)
-        ends = count - 1
-        head = lax.slice_in_dim(cells, 0, width, axis=dim)
-        tail = lax.slice_in_dim(cells, cells.shape[dim] - width, cells.shape[dim], axis=dim)
-        cells = jnp.concatenate(
-            [
-                lax.ppermute(tail, axis, [(i, (i + 1) % count) for i in range(ends)]),
-                cells,
-                lax.ppermute(head, axis, [((i + 1) % count, i) for i in range(ends)]),
-            ],
-            axis=dim,
-        )
-    return cells
+def halo_strips(cells, axis, dim):
+    count = lax.axis_size(axis)
+    ends = count - 1
+    head = lax.slice_in_dim(cells, 0, 1, axis=dim)
+    tail = lax.slice_in_dim(cells, cells.shape[dim] - 1, cells.shape[dim], axis=dim)
+    from_before = lax.ppermute(tail, axis, [(i, (i + 1) % count) for i in range(ends)])
+    from_after = lax.ppermute(head, axis, [((i + 1) % count, i) for i in range(ends)])
+    return from_before, from_after
 
 
 def gelu_slope(values):
@@ -171,14 +164,19 @@
                 return lax.all_gather(part, axis, axis=0, tiled=tiled)
             return carried.doubling(part, axis)
 
-        padded = padded_2(values, (("row", 1), ("col", 2)), 1)
         row_strip = jnp.where(row_index == 0, values[:, 0], values[:, tile_rows - 1])
         col_strip = jnp.where(col_index == 0, values[:, :, 0], values[:, :, tile_cols - 1])
+        above, below = halo_strips(values, "row", 1)
         by_row = gather(jnp.concatenate([row_strip, col_strip], axis=1), "row", False)
+        above, below, by_row = lax.optimization_barrier((above, below, by_row))
+        padded = jnp.concatenate([above, values, below], axis=1)
+        before_col, after_col = halo_strips(padded, "col", 2)
         top_seg = by_row[0, :, :tile_cols]
         bottom_seg = by_row[row_count - 1, :, :tile_cols]
         side_line = jnp.moveaxis(by_row[:, :, tile_cols:], 0, 1).reshape(local_faces, side, width)
         by_col = gather(jnp.concatenate([top_seg, bottom_seg, side_line], axis=1), "col", False)
+        before_col, after_col, by_col = lax.optimization_barrier((before_col, after_col, by_col))
+        padded = jnp.concatenate([before_col, padded, after_col], axis=2)
         top_row = jnp.moveaxis(by_col[:, :, :tile_cols], 0, 1).reshape(local_faces, side, width)
         bottom_row = jnp.moveaxis(by_col[:, :, tile_cols : 2 * tile_cols], 0, 1).reshape(
             local_faces, side, width

time: 375 us -> 371 us (0.989)
  waiting for transfers between devices: 29.3 us -> 24.7 us
    ppermute x10, waiting for transfers between devices: 23.5 us -> 17.2 us  [step_send(): return [lax.ppermute(values, axis, pairs) for pairs in pair_sets]]
  transfers between devices with their start and end apart: 24 -> 24, of which waited for: 10 -> 8; matrix products, arithmetic and copies ran while one was open for 9% -> 8% of each run, Pallas kernels for 0% -> 0%
where the time goes in v7:
time: 371 us; the launch traced here: 368 us
  blocking collectives  198 us (53%)
  starting transfers between devices  92.7 us (25%)
  local copies, waits for them, and re-layouts  26.7 us (7%)
  waiting for transfers between devices  24.7 us (7%)
  other arithmetic  13.5 us (4%)
  between operations  6.03 us (2%)
  matrix products  5.65 us (2%)
    all_gather x4, blocking collectives, gather(): return lax.all_gather(part, axis, axis=0, tiled=tiled)  96.7 us
    psum x3, blocking collectives, nested_sum(): lax.psum(part, axis)  52.7 us
    all_gather x3, blocking collectives, gathered_sum(): values = jnp.sum(lax.all_gather(values, axis, axis=0, tiled=False), axis=0)  49 us
    ppermute x10, starting transfers between devices, step_send(): return [lax.ppermute(values, axis, pairs) for pairs in pair_sets]  40.5 us
    ppermute x6, starting transfers between devices, doubling(): lax.ppermute(gathered, axis, [(i, i ^ step_size) for i in range(count)])  24.7 us
    ppermute x4, starting transfers between devices, halo_strips(): lax.ppermute(head, axis, [((i + 1) % count, i) for i in range(ends)])  21 us
    ppermute x10, waiting for transfers between devices, step_send(): return [lax.ppermute(values, axis, pairs) for pairs in pair_sets]  17.2 us
    ppermute x6, waiting for transfers between devices, doubling(): lax.ppermute(gathered, axis, [(i, i ^ step_size) for i in range(count)])  7.45 us
  transfers between devices with their start and end apart: 24, of which 8 were waited for; matrix products, arithmetic and copies ran while one was open for 8% of the time, Pallas kernels for 0%

profile of v7, /device:TPU:56, one launch (start us, length us, event | category | flops | bytes accessed | tf_op | source)
XLA Modules:
  0.0 367.7 jit_solution(3367591133024042933)
XLA Ops:
  2.9 5.4 %collective-permute-start.1 = (bf16[1,1,8,64]{3,2,1,0:T(8,128)(2,1)S(1)}, bf16[1,1,8,64]{3,2,1,0:T(8,128)(2,1)S(1)}, u32[]{:S(2)}, u32[]{:S(2)}) collective-permute-start(bf16[1,1,8,64]{3,2,1,0:T(8,128)(2,1)S(1)} %get-tuple-element.349), channel_id=1, source_target_pairs={{16,0},{32,16},{48,32},{17,1},{33,17},{49,33},{18,2},{34,18},{50,3... | collective-permute-start | bytes 3080 | tf_op jit(solution)/shard_map/ppermute | solution.py:19
  8.5 13.7 %all-gather = bf16[4,40,64]{2,1,0:T(8,128)(2,1)S(1)} all-gather(bf16[1,40,64]{2,1,0:T(8,128)(2,1)S(1)} %pad_maximum_fusion.18), channel_id=2, replica_groups=mesh['face'=12,'row'=4,'col'=16] {'row'}, dimensions={0}, use_global_device_ids=true | all-gather | bytes 25600 | tf_op jit(solution)/shard_map/all_gather | solution.py:164
  34.1 20.7 %all-gather.1 = bf16[16,144,64]{1,2,0:T(8,128)(2,1)S(1)} all-gather(bf16[1,144,64]{1,2,0:T(8,128)(2,1)S(1)} %pad_maximum_fusion.12), channel_id=3, replica_groups=mesh['face'=12,'row'=4,'col'=16] {'col'}, dimensions={0}, use_global_device_ids=true | all-gather | bytes 313344 | tf_op jit(solution)/shard_map/all_gather | solution.py:164
  55.7 36.8 %all_gather.40 = bf16[12,4,128,64]{2,3,1,0:T(8,128)(2,1)S(1)} all-gather(bf16[1,4,128,64]{2,3,1,0:T(8,128)(2,1)S(1)} %pad_maximum_fusion.10), channel_id=1, replica_groups=mesh['face'=12,'row'=4,'col'=16] {'face'}, dimensions={0}, use_global_device_ids=true | all-gather | bytes 851968 | tf_op jit(solution)/shard_map/all_gather | solution.py:164
  98.0 18.2 %all-gather.5 = f32[16,2,64]{2,1,0:T(2,128)S(1)} all-gather(f32[1,2,64]{2,1,0:T(2,128)S(1)} %maximum_bitcast_fusion.2), channel_id=4, replica_groups=mesh['face'=12,'row'=4,'col'=16] {'col'}, dimensions={0}, use_global_device_ids=true | all-gather | bytes 8704 | tf_op jit(solution)/shard_map/all_gather | solution.py:55
  116.2 11.2 %all-gather.6 = f32[4,2,64]{2,1,0:T(2,128)S(1)} all-gather(f32[1,2,64]{2,1,0:T(2,128)S(1)} %bitcast.409), channel_id=5, replica_groups=mesh['face'=12,'row'=4,'col'=16] {'row'}, dimensions={0}, use_global_device_ids=true | all-gather | bytes 2560 | tf_op jit(solution)/shard_map/all_gather | solution.py:55
  127.4 19.6 %all-gather.7 = f32[12,2,64]{2,1,0:T(2,128)S(1)} all-gather(f32[1,2,64]{2,1,0:T(2,128)S(1)} %bitcast.412), channel_id=6, replica_groups=mesh['face'=12,'row'=4,'col'=16] {'face'}, dimensions={0}, use_global_device_ids=true | all-gather | bytes 6656 | tf_op jit(solution)/shard_map/all_gather | solution.py:55
  154.1 6.4 %collective-permute-start.5 = (f32[74304]{0:T(1024)S(1)}, f32[74304]{0:T(1024)S(1)}, u32[]{:S(2)}, u32[]{:S(2)}) collective-permute-start(f32[74304]{0:T(1024)S(1)} %pad_maximum_fusion), channel_id=1, source_target_pairs={{0,512},{64,576},{128,640},{192,704},{256,0},{320,64},{384,128},{4... | collective-permute-start | bytes 891656 | tf_op jit(solution)/shard_map/ppermute | solution.py:83
  170.8 23.4 %all-reduce.3 = (f32[64]{0:T(128)S(1)}, f32[64]{0:T(128)S(1)}) all-reduce(f32[64]{0:T(128)S(1)} %get-tuple-element.236, f32[64]{0:T(128)S(1)} %get-tuple-element.237), channel_id=1, replica_groups=mesh['face'=12,'row'=4,'col'=16] {'col'}, use_global_device_ids=true, to_apply=%region_10.11 | all-reduce | flops 128 | bytes 1024 | tf_op jit(solution)/shard_map/psum | solution.py:45
  201.5 8.7 %all-reduce.5 = (f32[64]{0:T(128)S(1)}, f32[64]{0:T(128)S(1)}) all-reduce(f32[64]{0:T(128)S(1)} %get-tuple-element.239, f32[64]{0:T(128)S(1)} %get-tuple-element.240), channel_id=1, replica_groups=mesh['face'=12,'row'=4,'col'=16] {'row'}, use_global_device_ids=true, to_apply=%region_12.13 | all-reduce | flops 128 | bytes 1024 | tf_op jit(solution)/shard_map/psum | solution.py:45
  210.3 20.6 %all-reduce.4 = (f32[64]{0:T(128)S(1)}, f32[64]{0:T(128)S(1)}) all-reduce(f32[64]{0:T(128)S(1)} %get-tuple-element.242, f32[64]{0:T(128)S(1)} %get-tuple-element.241), channel_id=1, replica_groups=mesh['face'=12,'row'=4,'col'=16] {'face'}, use_global_device_ids=true, to_apply=%region_15.16 | all-reduce | flops 128 | bytes 1024 | tf_op jit(solution)/shard_map/psum | solution.py:45
  231.6 4.7 %collective-permute-start.9 = (f32[74304]{0:T(1024)S(1)}, f32[74304]{0:T(1024)S(1)}, u32[]{:S(2)}, u32[]{:S(2)}) collective-permute-start(f32[74304]{0:T(1024)S(1)} %add.217), channel_id=1, source_target_pairs={{0,128},{64,192},{128,0},{192,64},{256,384},{320,448},{384,256},{4... | collective-permute-start | bytes 891656 | tf_op jit(solution)/shard_map/ppermute | solution.py:83
  236.4 8.0 %collective-permute-done.9 = f32[74304]{0:T(1024)S(1)} collective-permute-done((f32[74304]{0:T(1024)S(1)}, f32[74304]{0:T(1024)S(1)}, u32[]{:S(2)}, u32[]{:S(2)}) %collective-permute-start.9) | collective-permute-done | bytes 297248 | tf_op jit(solution)/shard_map/ppermute | solution.py:83
  244.4 5.1 %collective-permute-start.10 = (f32[74304]{0:T(1024)S(1)}, f32[74304]{0:T(1024)S(1)}, u32[]{:S(2)}, u32[]{:S(2)}) collective-permute-start(f32[74304]{0:T(1024)S(1)} %add.221), channel_id=1, source_target_pairs={{0,32},{16,48},{32,0},{48,16},{1,33},{17,49},{33,1},{49,17},{2,34}... | collective-permute-start | bytes 891656 | tf_op jit(solution)/shard_map/ppermute | solution.py:83
  249.5 5.3 %collective-permute-start.11 = (bf16[1,1,40,64]{3,2,1,0:T(8,128)(2,1)S(1)}, bf16[1,1,40,64]{3,2,1,0:T(8,128)(2,1)S(1)}, u32[]{:S(2)}, u32[]{:S(2)}) collective-permute-start(bf16[1,1,40,64]{3,2,1,0:T(8,128)(2,1)S(1)} %maximum_bitcast_fusion.1), channel_id=1, source_target_pairs={{0,16},{16,0},{32,48},{48,32},{1,17},{17,1},{33,49},{49,33},{2,18}... | collective-permute-start | bytes 15368 | tf_op jit(solution)/shard_map/ppermute | solution.py:121
  257.4 5.1 %collective-permute-start.12 = (bf16[2,1,40,64]{3,2,1,0:T(8,128)(2,1)S(1)}, bf16[2,1,40,64]{3,2,1,0:T(8,128)(2,1)S(1)}, u32[]{:S(2)}, u32[]{:S(2)}) collective-permute-start(bf16[2,1,40,64]{3,2,1,0:T(8,128)(2,1)S(1)} %maximum_select_fusion.5), channel_id=1, source_target_pairs={{0,32},{16,48},{32,0},{48,16},{1,33},{17,49},{33,1},{49,17},{2,34}... | collective-permute-start | bytes 30728 | tf_op jit(solution)/shard_map/ppermute | solution.py:121
  265.1 8.3 %collective-permute-start.8 = (bf16[1,1,8,64]{3,2,1,0:T(8,128)(2,1)S(1)}, bf16[1,1,8,64]{3,2,1,0:T(8,128)(2,1)S(1)}, u32[]{:S(2)}, u32[]{:S(2)}) collective-permute-start(bf16[1,1,8,64]{3,2,1,0:T(8,128)(2,1)S(1)} %get-tuple-element.334), channel_id=1, source_target_pairs={{16,0},{32,16},{48,32},{17,1},{33,17},{49,33},{18,2},{34,18},{50,3... | collective-permute-start | bytes 3080 | tf_op jit(solution)/shard_map/ppermute | solution.py:19
  273.4 6.0 %collective-permute-start.15 = (f32[74304]{0:T(1024)S(1)}, f32[74304]{0:T(1024)S(1)}, u32[]{:S(2)}, u32[]{:S(2)}) collective-permute-start(f32[74304]{0:T(1024)S(1)} %add.222), channel_id=1, source_target_pairs={{0,16},{16,0},{32,48},{48,32},{1,17},{17,1},{33,49},{49,33},{2,18}... | collective-permute-start | bytes 891656 | tf_op jit(solution)/shard_map/ppermute | solution.py:83
  279.9 4.3 %collective-permute-done.15 = f32[74304]{0:T(1024)S(1)} collective-permute-done((f32[74304]{0:T(1024)S(1)}, f32[74304]{0:T(1024)S(1)}, u32[]{:S(2)}, u32[]{:S(2)}) %collective-permute-start.15) | collective-permute-done | bytes 297248 | tf_op jit(solution)/shard_map/ppermute | solution.py:83
  290.2 4.2 %collective-permute-done.16 = f32[74304]{0:T(1024)S(1)} collective-permute-done((f32[74304]{0:T(1024)S(1)}, f32[74304]{0:T(1024)S(1)}, u32[]{:S(2)}, u32[]{:S(2)}) %collective-permute-start.16) | collective-permute-done | bytes 297248 | tf_op jit(solution)/shard_map/ppermute | solution.py:83
  296.7 6.5 %collective-permute-start.19 = (bf16[2,1,144,64]{2,3,1,0:T(8,128)(2,1)S(1)}, bf16[2,1,144,64]{2,3,1,0:T(8,128)(2,1)S(1)}, u32[]{:S(2)}, u32[]{:S(2)}) collective-permute-start(bf16[2,1,144,64]{2,3,1,0:T(8,128)(2,1)S(1)} %maximum_select_fusion.3), channel_id=1, source_target_pairs={{0,2},{1,3},{2,0},{3,1},{4,6},{5,7},{6,4},{7,5},{8,10},{9,11},{10,... | collective-permute-start | bytes 110600 | tf_op jit(solution)/shard_map/ppermute | solution.py:121
  306.1 4.0 %collective-permute-start.20 = (f32[74304]{0:T(1024)S(1)}, f32[74304]{0:T(1024)S(1)}, u32[]{:S(2)}, u32[]{:S(2)}) collective-permute-start(f32[74304]{0:T(1024)S(1)} %add.228), channel_id=1, source_target_pairs={{0,2},{1,3},{2,0},{3,1},{4,6},{5,7},{6,4},{7,5},{8,10},{9,11},{10,... | collective-permute-start | bytes 891656 | tf_op jit(solution)/shard_map/ppermute | solution.py:83
  310.1 4.0 %collective-permute-start.21 = (bf16[4,1,144,64]{2,3,1,0:T(8,128)(2,1)S(1)}, bf16[4,1,144,64]{2,3,1,0:T(8,128)(2,1)S(1)}, u32[]{:S(2)}, u32[]{:S(2)}) collective-permute-start(bf16[4,1,144,64]{2,3,1,0:T(8,128)(2,1)S(1)} %maximum_select_fusion.2), channel_id=1, source_target_pairs={{0,4},{1,5},{2,6},{3,7},{4,0},{5,1},{6,2},{7,3},{8,12},{9,13},{10,... | collective-permute-start | bytes 221192 | tf_op jit(solution)/shard_map/ppermute | solution.py:121
  329.0 25.6 %all_gather.47 = bf16[12,4,128,64]{2,3,1,0:T(8,128)(2,1)S(1)} all-gather(bf16[1,4,128,64]{2,3,1,0:T(8,128)(2,1)S(1)} %pad_maximum_fusion.11), channel_id=1, replica_groups=mesh['face'=12,'row'=4,'col'=16] {'face'}, dimensions={0}, use_global_device_ids=true | all-gather | bytes 851968 | tf_op jit(solution)/shard_map/all_gather | solution.py:164
  (294 shorter events, 86.1 us)
Async XLA Ops:
  1.6 26.5 %collective-permute-start = (bf16[1,1,8,64]{3,2,1,0:T(8,128)(2,1)S(1)}, bf16[1,1,8,64]{3,2,1,0:T(8,128)(2,1)S(1)}, u32[]{:S(2)}, u32[]{:S(2)}) collective-permute-start(bf16[1,1,8,64]{3,2,1,0:T(8,128)(2,1)S(1)} %get-tuple-element.350), channel_id=1, source_target_pairs={{0,16},{16,32},{32,48},{1,17},{17,33},{33,49},{2,18},{18,34},{34,5... | collective-permute-start | bytes 3080 | tf_op jit(solution)/shard_map/ppermute | solution.py:18
  2.9 25.2 %collective-permute-start.1 = (bf16[1,1,8,64]{3,2,1,0:T(8,128)(2,1)S(1)}, bf16[1,1,8,64]{3,2,1,0:T(8,128)(2,1)S(1)}, u32[]{:S(2)}, u32[]{:S(2)}) collective-permute-start(bf16[1,1,8,64]{3,2,1,0:T(8,128)(2,1)S(1)} %get-tuple-element.349), channel_id=1, source_target_pairs={{16,0},{32,16},{48,32},{17,1},{33,17},{49,33},{18,2},{34,18},{50,3... | collective-permute-start | bytes 3080 | tf_op jit(solution)/shard_map/ppermute | solution.py:19
  28.1 26.6 %collective-permute-start.2 = (bf16[1,34,1,64]{3,2,1,0:T(2,128)(2,1)S(1)}, bf16[1,34,1,64]{3,2,1,0:T(2,128)(2,1)S(1)}, u32[]{:S(2)}, u32[]{:S(2)}) collective-permute-start(bf16[1,34,1,64]{3,2,1,0:T(2,128)(2,1)S(1)} %get-tuple-element.328), channel_id=1, source_target_pairs={{0,1},{1,2},{2,3},{3,4},{4,5},{5,6},{6,7},{7,8},{8,9},{9,10},{10,1... | collective-permute-start | bytes 13064 | tf_op jit(solution)/shard_map/ppermute | solution.py:18
  30.1 24.7 %collective-permute-start.3 = (bf16[1,34,1,64]{3,2,1,0:T(2,128)(2,1)S(1)}, bf16[1,34,1,64]{3,2,1,0:T(2,128)(2,1)S(1)}, u32[]{:S(2)}, u32[]{:S(2)}) collective-permute-start(bf16[1,34,1,64]{3,2,1,0:T(2,128)(2,1)S(1)} %get-tuple-element.327), channel_id=1, source_target_pairs={{1,0},{2,1},{3,2},{4,3},{5,4},{6,5},{7,6},{8,7},{9,8},{10,9},{11,1... | collective-permute-start | bytes 13064 | tf_op jit(solution)/shard_map/ppermute | solution.py:19
  150.8 43.4 %collective-permute-start.4 = (f32[74304]{0:T(1024)S(1)}, f32[74304]{0:T(1024)S(1)}, u32[]{:S(2)}, u32[]{:S(2)}) collective-permute-start(f32[74304]{0:T(1024)S(1)} %pad_maximum_fusion), channel_id=1, source_target_pairs={{0,256},{64,320},{128,384},{192,448},{256,512},{320,576},{384,640}... | collective-permute-start | bytes 891656 | tf_op jit(solution)/shard_map/ppermute | solution.py:83
  154.1 40.0 %collective-permute-start.5 = (f32[74304]{0:T(1024)S(1)}, f32[74304]{0:T(1024)S(1)}, u32[]{:S(2)}, u32[]{:S(2)}) collective-permute-start(f32[74304]{0:T(1024)S(1)} %pad_maximum_fusion), channel_id=1, source_target_pairs={{0,512},{64,576},{128,640},{192,704},{256,0},{320,64},{384,128},{4... | collective-permute-start | bytes 891656 | tf_op jit(solution)/shard_map/ppermute | solution.py:83
  194.3 15.9 %collective-permute-start.6 = (f32[74304]{0:T(1024)S(1)}, f32[74304]{0:T(1024)S(1)}, u32[]{:S(2)}, u32[]{:S(2)}) collective-permute-start(f32[74304]{0:T(1024)S(1)} %select_add_fusion), channel_id=1, source_target_pairs={{0,64},{64,0},{128,192},{192,128},{256,320},{320,256},{384,448},{4... | collective-permute-start | bytes 891656 | tf_op jit(solution)/shard_map/ppermute | solution.py:83
  231.6 12.8 %collective-permute-start.9 = (f32[74304]{0:T(1024)S(1)}, f32[74304]{0:T(1024)S(1)}, u32[]{:S(2)}, u32[]{:S(2)}) collective-permute-start(f32[74304]{0:T(1024)S(1)} %add.217), channel_id=1, source_target_pairs={{0,128},{64,192},{128,0},{192,64},{256,384},{320,448},{384,256},{4... | collective-permute-start | bytes 891656 | tf_op jit(solution)/shard_map/ppermute | solution.py:83
  244.4 12.9 %collective-permute-start.10 = (f32[74304]{0:T(1024)S(1)}, f32[74304]{0:T(1024)S(1)}, u32[]{:S(2)}, u32[]{:S(2)}) collective-permute-start(f32[74304]{0:T(1024)S(1)} %add.221), channel_id=1, source_target_pairs={{0,32},{16,48},{32,0},{48,16},{1,33},{17,49},{33,1},{49,17},{2,34}... | collective-permute-start | bytes 891656 | tf_op jit(solution)/shard_map/ppermute | solution.py:83
  249.5 7.0 %collective-permute-start.11 = (bf16[1,1,40,64]{3,2,1,0:T(8,128)(2,1)S(1)}, bf16[1,1,40,64]{3,2,1,0:T(8,128)(2,1)S(1)}, u32[]{:S(2)}, u32[]{:S(2)}) collective-permute-start(bf16[1,1,40,64]{3,2,1,0:T(8,128)(2,1)S(1)} %maximum_bitcast_fusion.1), channel_id=1, source_target_pairs={{0,16},{16,0},{32,48},{48,32},{1,17},{17,1},{33,49},{49,33},{2,18}... | collective-permute-start | bytes 15368 | tf_op jit(solution)/shard_map/ppermute | solution.py:121
  257.4 22.1 %collective-permute-start.12 = (bf16[2,1,40,64]{3,2,1,0:T(8,128)(2,1)S(1)}, bf16[2,1,40,64]{3,2,1,0:T(8,128)(2,1)S(1)}, u32[]{:S(2)}, u32[]{:S(2)}) collective-permute-start(bf16[2,1,40,64]{3,2,1,0:T(8,128)(2,1)S(1)} %maximum_select_fusion.5), channel_id=1, source_target_pairs={{0,32},{16,48},{32,0},{48,16},{1,33},{17,49},{33,1},{49,17},{2,34}... | collective-permute-start | bytes 30728 | tf_op jit(solution)/shard_map/ppermute | solution.py:121
  263.8 15.7 %collective-permute-start.7 = (bf16[1,1,8,64]{3,2,1,0:T(8,128)(2,1)S(1)}, bf16[1,1,8,64]{3,2,1,0:T(8,128)(2,1)S(1)}, u32[]{:S(2)}, u32[]{:S(2)}) collective-permute-start(bf16[1,1,8,64]{3,2,1,0:T(8,128)(2,1)S(1)} %get-tuple-element.335), channel_id=1, source_target_pairs={{0,16},{16,32},{32,48},{1,17},{17,33},{33,49},{2,18},{18,34},{34,5... | collective-permute-start | bytes 3080 | tf_op jit(solution)/shard_map/ppermute | solution.py:18
  265.1 14.4 %collective-permute-start.8 = (bf16[1,1,8,64]{3,2,1,0:T(8,128)(2,1)S(1)}, bf16[1,1,8,64]{3,2,1,0:T(8,128)(2,1)S(1)}, u32[]{:S(2)}, u32[]{:S(2)}) collective-permute-start(bf16[1,1,8,64]{3,2,1,0:T(8,128)(2,1)S(1)} %get-tuple-element.334), channel_id=1, source_target_pairs={{16,0},{32,16},{48,32},{17,1},{33,17},{49,33},{18,2},{34,18},{50,3... | collective-permute-start | bytes 3080 | tf_op jit(solution)/shard_map/ppermute | solution.py:19
  273.4 10.8 %collective-permute-start.15 = (f32[74304]{0:T(1024)S(1)}, f32[74304]{0:T(1024)S(1)}, u32[]{:S(2)}, u32[]{:S(2)}) collective-permute-start(f32[74304]{0:T(1024)S(1)} %add.222), channel_id=1, source_target_pairs={{0,16},{16,0},{32,48},{48,32},{1,17},{17,1},{33,49},{49,33},{2,18}... | collective-permute-start | bytes 891656 | tf_op jit(solution)/shard_map/ppermute | solution.py:83
  284.2 10.2 %collective-permute-start.16 = (f32[74304]{0:T(1024)S(1)}, f32[74304]{0:T(1024)S(1)}, u32[]{:S(2)}, u32[]{:S(2)}) collective-permute-start(f32[74304]{0:T(1024)S(1)} %add.225), channel_id=1, source_target_pairs={{0,8},{1,9},{2,10},{3,11},{4,12},{5,13},{6,14},{7,15},{8,0},{9,1},... | collective-permute-start | bytes 891656 | tf_op jit(solution)/shard_map/ppermute | solution.py:83
  287.1 3.1 collective-permute-start.17
  294.4 11.6 %collective-permute-start.18 = (f32[74304]{0:T(1024)S(1)}, f32[74304]{0:T(1024)S(1)}, u32[]{:S(2)}, u32[]{:S(2)}) collective-permute-start(f32[74304]{0:T(1024)S(1)} %add.226), channel_id=1, source_target_pairs={{0,4},{1,5},{2,6},{3,7},{4,0},{5,1},{6,2},{7,3},{8,12},{9,13},{10,... | collective-permute-start | bytes 891656 | tf_op jit(solution)/shard_map/ppermute | solution.py:83
  296.7 9.2 %collective-permute-start.19 = (bf16[2,1,144,64]{2,3,1,0:T(8,128)(2,1)S(1)}, bf16[2,1,144,64]{2,3,1,0:T(8,128)(2,1)S(1)}, u32[]{:S(2)}, u32[]{:S(2)}) collective-permute-start(bf16[2,1,144,64]{2,3,1,0:T(8,128)(2,1)S(1)} %maximum_select_fusion.3), channel_id=1, source_target_pairs={{0,2},{1,3},{2,0},{3,1},{4,6},{5,7},{6,4},{7,5},{8,10},{9,11},{10,... | collective-permute-start | bytes 110600 | tf_op jit(solution)/shard_map/ppermute | solution.py:121
  306.1 11.4 %collective-permute-start.20 = (f32[74304]{0:T(1024)S(1)}, f32[74304]{0:T(1024)S(1)}, u32[]{:S(2)}, u32[]{:S(2)}) collective-permute-start(f32[74304]{0:T(1024)S(1)} %add.228), channel_id=1, source_target_pairs={{0,2},{1,3},{2,0},{3,1},{4,6},{5,7},{6,4},{7,5},{8,10},{9,11},{10,... | collective-permute-start | bytes 891656 | tf_op jit(solution)/shard_map/ppermute | solution.py:83
  310.1 7.3 %collective-permute-start.21 = (bf16[4,1,144,64]{2,3,1,0:T(8,128)(2,1)S(1)}, bf16[4,1,144,64]{2,3,1,0:T(8,128)(2,1)S(1)}, u32[]{:S(2)}, u32[]{:S(2)}) collective-permute-start(bf16[4,1,144,64]{2,3,1,0:T(8,128)(2,1)S(1)} %maximum_select_fusion.2), channel_id=1, source_target_pairs={{0,4},{1,5},{2,6},{3,7},{4,0},{5,1},{6,2},{7,3},{8,12},{9,13},{10,... | collective-permute-start | bytes 221192 | tf_op jit(solution)/shard_map/ppermute | solution.py:121
  317.6 10.4 %collective-permute-start.22 = (bf16[8,1,144,64]{2,3,1,0:T(8,128)(2,1)S(1)}, bf16[8,1,144,64]{2,3,1,0:T(8,128)(2,1)S(1)}, u32[]{:S(2)}, u32[]{:S(2)}) collective-permute-start(bf16[8,1,144,64]{2,3,1,0:T(8,128)(2,1)S(1)} %maximum_select_fusion.1), channel_id=1, source_target_pairs={{0,8},{1,9},{2,10},{3,11},{4,12},{5,13},{6,14},{7,15},{8,0},{9,1},... | collective-permute-start | bytes 442376 | tf_op jit(solution)/shard_map/ppermute | solution.py:121
  320.3 7.9 %collective-permute-start.13 = (bf16[1,34,1,64]{1,3,2,0:T(8,128)(2,1)S(1)}, bf16[1,34,1,64]{1,3,2,0:T(8,128)(2,1)S(1)}, u32[]{:S(2)}, u32[]{:S(2)}) collective-permute-start(bf16[1,34,1,64]{1,3,2,0:T(8,128)(2,1)S(1)} %get-tuple-element.303), channel_id=1, source_target_pairs={{0,1},{1,2},{2,3},{3,4},{4,5},{5,6},{6,7},{7,8},{8,9},{9,10},{10,1... | collective-permute-start | bytes 13064 | tf_op jit(solution)/shard_map/ppermute | solution.py:18
  322.2 6.0 %collective-permute-start.14 = (bf16[1,34,1,64]{1,3,2,0:T(8,128)(2,1)S(1)}, bf16[1,34,1,64]{1,3,2,0:T(8,128)(2,1)S(1)}, u32[]{:S(2)}, u32[]{:S(2)}) collective-permute-start(bf16[1,34,1,64]{1,3,2,0:T(8,128)(2,1)S(1)} %get-tuple-element.302), channel_id=1, source_target_pairs={{1,0},{2,1},{3,2},{4,3},{5,4},{6,5},{7,6},{8,7},{9,8},{10,9},{11,1... | collective-permute-start | bytes 13064 | tf_op jit(solution)/shard_map/ppermute | solution.py:19
  325.8 39.4 %collective-permute-start.23 = (f32[74304]{0:T(1024)S(1)}, f32[74304]{0:T(1024)S(1)}, u32[]{:S(2)}, u32[]{:S(2)}) collective-permute-start(f32[74304]{0:T(1024)S(1)} %add.230), channel_id=1, source_target_pairs={{0,1},{1,0},{2,3},{3,2},{4,5},{5,4},{6,7},{7,6},{8,9},{9,8},{10,11... | collective-permute-start | bytes 891656 | tf_op jit(solution)/shard_map/ppermute | solution.py:83
  (9 other events, 114.0 us)

commit v8 on v7

--- a/solution.py
+++ b/solution.py
@@ -42,12 +42,18 @@
         if carried is None:
             values = lax.psum(values, axis)
         else:
-            values = carried.beside(lambda part, axis=axis: lax.psum(part, axis), values)
+            values = carried.beside(
+                lambda part, axis=axis: jnp.sum(
+                    lax.all_gather(part, axis, axis=0, tiled=False), axis=0
+                ),
+                values,
+            )
     return values
 
 
 def channel_pair(first_sum, second_sum, carried=None):
-    return nested_sum((first_sum, second_sum), carried)
+    both = nested_sum(jnp.stack([first_sum, second_sum]), carried)
+    return both[0], both[1]
 
 
 def gathered_sum(values):

time: 371 us -> 357 us (0.962)
  starting transfers between devices: 92.7 us -> 79.5 us
  blocking collectives: 198 us -> 192 us
    psum x3 -> x0, blocking collectives: 52.7 us -> none  [nested_sum(): lax.psum(part, axis)]
    all_gather x0 -> x3, blocking collectives: none -> 47.5 us  [nested_sum(): lax.all_gather(part, axis, axis=0, tiled=False)]
    ppermute x10, starting transfers between devices: 40.5 us -> 33.3 us  [step_send(): return [lax.ppermute(values, axis, pairs) for pairs in pair_sets]]
    ppermute x10, waiting for transfers between devices: 17.2 us -> 21.7 us  [step_send(): return [lax.ppermute(values, axis, pairs) for pairs in pair_sets]]
  transfers between devices with their start and end apart: 24 -> 24, of which waited for: 8 -> 6; matrix products, arithmetic and copies ran while one was open for 8% -> 9% of each run, Pallas kernels for 0% -> 0%
where the time goes in v8:
time: 357 us; the launch traced here: 353 us
  blocking collectives  192 us (54%)
  starting transfers between devices  79.5 us (22%)
  waiting for transfers between devices  28.4 us (8%)
  local copies, waits for them, and re-layouts  27.7 us (8%)
  other arithmetic  14 us (4%)
  between operations  5.92 us (2%)
  matrix products  5.65 us (2%)
    all_gather x4, blocking collectives, gather(): return lax.all_gather(part, axis, axis=0, tiled=tiled)  95.8 us
    all_gather x3, blocking collectives, gathered_sum(): values = jnp.sum(lax.all_gather(values, axis, axis=0, tiled=False), axis=0)  49 us
    all_gather x3, blocking collectives, nested_sum(): lax.all_gather(part, axis, axis=0, tiled=False)  47.5 us
    ppermute x10, starting transfers between devices, step_send(): return [lax.ppermute(values, axis, pairs) for pairs in pair_sets]  33.3 us
    ppermute x10, waiting for transfers between devices, step_send(): return [lax.ppermute(values, axis, pairs) for pairs in pair_sets]  21.7 us
    ppermute x6, starting transfers between devices, doubling(): lax.ppermute(gathered, axis, [(i, i ^ step_size) for i in range(count)])  21.6 us
    ppermute x4, starting transfers between devices, halo_strips(): lax.ppermute(head, axis, [((i + 1) % count, i) for i in range(ends)])  18.2 us
  transfers between devices with their start and end apart: 24, of which 6 were waited for; matrix products, arithmetic and copies ran while one was open for 9% of the time, Pallas kernels for 0%

profile of v8, /device:TPU:56, one launch (start us, length us, event | category | flops | bytes accessed | tf_op | source)
XLA Modules:
  0.0 353.4 jit_solution(7135849308360756758)
XLA Ops:
  2.8 5.4 %collective-permute-start.1 = (bf16[1,1,8,64]{3,2,1,0:T(8,128)(2,1)S(1)}, bf16[1,1,8,64]{3,2,1,0:T(8,128)(2,1)S(1)}, u32[]{:S(2)}, u32[]{:S(2)}) collective-permute-start(bf16[1,1,8,64]{3,2,1,0:T(8,128)(2,1)S(1)} %get-tuple-element.341), channel_id=1, source_target_pairs={{16,0},{32,16},{48,32},{17,1},{33,17},{49,33},{18,2},{34,18},{50,3... | collective-permute-start | bytes 3080 | tf_op jit(solution)/shard_map/ppermute | solution.py:19
  9.2 13.7 %all-gather = bf16[4,40,64]{2,1,0:T(8,128)(2,1)S(1)} all-gather(bf16[1,40,64]{2,1,0:T(8,128)(2,1)S(1)} %pad_maximum_fusion.18), channel_id=2, replica_groups=mesh['face'=12,'row'=4,'col'=16] {'row'}, dimensions={0}, use_global_device_ids=true | all-gather | bytes 25600 | tf_op jit(solution)/shard_map/all_gather | solution.py:170
  30.9 20.7 %all-gather.1 = bf16[16,144,64]{1,2,0:T(8,128)(2,1)S(1)} all-gather(bf16[1,144,64]{1,2,0:T(8,128)(2,1)S(1)} %pad_maximum_fusion.12), channel_id=3, replica_groups=mesh['face'=12,'row'=4,'col'=16] {'col'}, dimensions={0}, use_global_device_ids=true | all-gather | bytes 313344 | tf_op jit(solution)/shard_map/all_gather | solution.py:170
  52.4 36.8 %all_gather.58 = bf16[12,4,128,64]{2,3,1,0:T(8,128)(2,1)S(1)} all-gather(bf16[1,4,128,64]{2,3,1,0:T(8,128)(2,1)S(1)} %pad_maximum_fusion.10), channel_id=1, replica_groups=mesh['face'=12,'row'=4,'col'=16] {'face'}, dimensions={0}, use_global_device_ids=true | all-gather | bytes 851968 | tf_op jit(solution)/shard_map/all_gather | solution.py:170
  94.7 18.2 %all-gather.8 = f32[16,2,64]{2,1,0:T(2,128)S(1)} all-gather(f32[1,2,64]{2,1,0:T(2,128)S(1)} %maximum_bitcast_fusion.2), channel_id=4, replica_groups=mesh['face'=12,'row'=4,'col'=16] {'col'}, dimensions={0}, use_global_device_ids=true | all-gather | bytes 8704 | tf_op jit(solution)/shard_map/all_gather | solution.py:61
  112.9 11.2 %all-gather.9 = f32[4,2,64]{2,1,0:T(2,128)S(1)} all-gather(f32[1,2,64]{2,1,0:T(2,128)S(1)} %bitcast.423), channel_id=5, replica_groups=mesh['face'=12,'row'=4,'col'=16] {'row'}, dimensions={0}, use_global_device_ids=true | all-gather | bytes 2560 | tf_op jit(solution)/shard_map/all_gather | solution.py:61
  124.1 19.6 %all-gather.10 = f32[12,2,64]{2,1,0:T(2,128)S(1)} all-gather(f32[1,2,64]{2,1,0:T(2,128)S(1)} %bitcast.428), channel_id=6, replica_groups=mesh['face'=12,'row'=4,'col'=16] {'face'}, dimensions={0}, use_global_device_ids=true | all-gather | bytes 6656 | tf_op jit(solution)/shard_map/all_gather | solution.py:61
  150.9 6.4 %collective-permute-start.5 = (f32[74304]{0:T(1024)S(1)}, f32[74304]{0:T(1024)S(1)}, u32[]{:S(2)}, u32[]{:S(2)}) collective-permute-start(f32[74304]{0:T(1024)S(1)} %pad_maximum_fusion), channel_id=1, source_target_pairs={{0,512},{64,576},{128,640},{192,704},{256,0},{320,64},{384,128},{4... | collective-permute-start | bytes 891656 | tf_op jit(solution)/shard_map/ppermute | solution.py:89
  159.4 16.3 %all-gather.11 = f32[16,2,64]{2,1,0:T(2,128)S(1)} all-gather(f32[1,2,64]{2,1,0:T(2,128)S(1)} %bitcast.424), channel_id=7, replica_groups=mesh['face'=12,'row'=4,'col'=16] {'col'}, dimensions={0}, use_global_device_ids=true | all-gather | bytes 8704 | tf_op jit(solution)/shard_map/all_gather | solution.py:47
  175.8 3.9 %collective-permute-start.6 = (f32[74304]{0:T(1024)S(1)}, f32[74304]{0:T(1024)S(1)}, u32[]{:S(2)}, u32[]{:S(2)}) collective-permute-start(f32[74304]{0:T(1024)S(1)} %select_add_fusion), channel_id=1, source_target_pairs={{0,64},{64,0},{128,192},{192,128},{256,320},{320,256},{384,448},{4... | collective-permute-start | bytes 891656 | tf_op jit(solution)/shard_map/ppermute | solution.py:89
  180.4 7.9 %all-gather.12 = f32[4,2,64]{2,1,0:T(2,128)S(1)} all-gather(f32[1,2,64]{2,1,0:T(2,128)S(1)} %bitcast.422), channel_id=8, replica_groups=mesh['face'=12,'row'=4,'col'=16] {'row'}, dimensions={0}, use_global_device_ids=true | all-gather | bytes 2560 | tf_op jit(solution)/shard_map/all_gather | solution.py:47
  188.3 23.3 %all-gather.13 = f32[12,2,64]{2,1,0:T(2,128)S(1)} all-gather(f32[1,2,64]{2,1,0:T(2,128)S(1)} %bitcast.427), channel_id=9, replica_groups=mesh['face'=12,'row'=4,'col'=16] {'face'}, dimensions={0}, use_global_device_ids=true | all-gather | bytes 6656 | tf_op jit(solution)/shard_map/all_gather | solution.py:47
  216.4 8.6 %collective-permute-done.9 = f32[74304]{0:T(1024)S(1)} collective-permute-done((f32[74304]{0:T(1024)S(1)}, f32[74304]{0:T(1024)S(1)}, u32[]{:S(2)}, u32[]{:S(2)}) %collective-permute-start.9) | collective-permute-done | bytes 297248 | tf_op jit(solution)/shard_map/ppermute | solution.py:89
  225.1 4.3 %collective-permute-start.10 = (f32[74304]{0:T(1024)S(1)}, f32[74304]{0:T(1024)S(1)}, u32[]{:S(2)}, u32[]{:S(2)}) collective-permute-start(f32[74304]{0:T(1024)S(1)} %add.213), channel_id=1, source_target_pairs={{0,32},{16,48},{32,0},{48,16},{1,33},{17,49},{33,1},{49,17},{2,34}... | collective-permute-start | bytes 891656 | tf_op jit(solution)/shard_map/ppermute | solution.py:89
  233.4 5.1 %collective-permute-start.11 = (bf16[1,1,40,64]{3,2,1,0:T(8,128)(2,1)S(1)}, bf16[1,1,40,64]{3,2,1,0:T(8,128)(2,1)S(1)}, u32[]{:S(2)}, u32[]{:S(2)}) collective-permute-start(bf16[1,1,40,64]{3,2,1,0:T(8,128)(2,1)S(1)} %maximum_bitcast_fusion.1), channel_id=1, source_target_pairs={{0,16},{16,0},{32,48},{48,32},{1,17},{17,1},{33,49},{49,33},{2,18}... | collective-permute-start | bytes 15368 | tf_op jit(solution)/shard_map/ppermute | solution.py:127
  246.3 4.3 %collective-permute-start.12 = (bf16[2,1,40,64]{3,2,1,0:T(8,128)(2,1)S(1)}, bf16[2,1,40,64]{3,2,1,0:T(8,128)(2,1)S(1)}, u32[]{:S(2)}, u32[]{:S(2)}) collective-permute-start(bf16[2,1,40,64]{3,2,1,0:T(8,128)(2,1)S(1)} %maximum_select_fusion.5), channel_id=1, source_target_pairs={{0,32},{16,48},{32,0},{48,16},{1,33},{17,49},{33,1},{49,17},{2,34}... | collective-permute-start | bytes 30728 | tf_op jit(solution)/shard_map/ppermute | solution.py:127
  255.2 5.4 %collective-permute-start.8 = (bf16[1,1,8,64]{3,2,1,0:T(8,128)(2,1)S(1)}, bf16[1,1,8,64]{3,2,1,0:T(8,128)(2,1)S(1)}, u32[]{:S(2)}, u32[]{:S(2)}) collective-permute-start(bf16[1,1,8,64]{3,2,1,0:T(8,128)(2,1)S(1)} %get-tuple-element.326), channel_id=1, source_target_pairs={{16,0},{32,16},{48,32},{17,1},{33,17},{49,33},{18,2},{34,18},{50,3... | collective-permute-start | bytes 3080 | tf_op jit(solution)/shard_map/ppermute | solution.py:19
  260.6 4.0 %collective-permute-start.15 = (f32[74304]{0:T(1024)S(1)}, f32[74304]{0:T(1024)S(1)}, u32[]{:S(2)}, u32[]{:S(2)}) collective-permute-start(f32[74304]{0:T(1024)S(1)} %add.214), channel_id=1, source_target_pairs={{0,16},{16,0},{32,48},{48,32},{1,17},{17,1},{33,49},{49,33},{2,18}... | collective-permute-start | bytes 891656 | tf_op jit(solution)/shard_map/ppermute | solution.py:89
  265.1 8.3 %collective-permute-done.15 = f32[74304]{0:T(1024)S(1)} collective-permute-done((f32[74304]{0:T(1024)S(1)}, f32[74304]{0:T(1024)S(1)}, u32[]{:S(2)}, u32[]{:S(2)}) %collective-permute-start.15) | collective-permute-done | bytes 297248 | tf_op jit(solution)/shard_map/ppermute | solution.py:89
  279.3 4.3 %collective-permute-done.16 = f32[74304]{0:T(1024)S(1)} collective-permute-done((f32[74304]{0:T(1024)S(1)}, f32[74304]{0:T(1024)S(1)}, u32[]{:S(2)}, u32[]{:S(2)}) %collective-permute-start.16) | collective-permute-done | bytes 297248 | tf_op jit(solution)/shard_map/ppermute | solution.py:89
  287.8 4.0 %collective-permute-done.19 = bf16[2,1,144,64]{2,3,1,0:T(8,128)(2,1)S(1)} collective-permute-done((bf16[2,1,144,64]{2,3,1,0:T(8,128)(2,1)S(1)}, bf16[2,1,144,64]{2,3,1,0:T(8,128)(2,1)S(1)}, u32[]{:S(2)}, u32[]{:S(2)}) %collective-permute-start.19) | collective-permute-done | bytes 36896 | tf_op jit(solution)/shard_map/ppermute | solution.py:127
  294.5 4.1 %collective-permute-start.21 = (bf16[4,1,144,64]{2,3,1,0:T(8,128)(2,1)S(1)}, bf16[4,1,144,64]{2,3,1,0:T(8,128)(2,1)S(1)}, u32[]{:S(2)}, u32[]{:S(2)}) collective-permute-start(bf16[4,1,144,64]{2,3,1,0:T(8,128)(2,1)S(1)} %maximum_select_fusion.2), channel_id=1, source_target_pairs={{0,4},{1,5},{2,6},{3,7},{4,0},{5,1},{6,2},{7,3},{8,12},{9,13},{10,... | collective-permute-start | bytes 221192 | tf_op jit(solution)/shard_map/ppermute | solution.py:127
  301.7 4.3 %collective-permute-start.22 = (bf16[8,1,144,64]{2,3,1,0:T(8,128)(2,1)S(1)}, bf16[8,1,144,64]{2,3,1,0:T(8,128)(2,1)S(1)}, u32[]{:S(2)}, u32[]{:S(2)}) collective-permute-start(bf16[8,1,144,64]{2,3,1,0:T(8,128)(2,1)S(1)} %maximum_select_fusion.1), channel_id=1, source_target_pairs={{0,8},{1,9},{2,10},{3,11},{4,12},{5,13},{6,14},{7,15},{8,0},{9,1},... | collective-permute-start | bytes 442376 | tf_op jit(solution)/shard_map/ppermute | solution.py:127
  315.7 24.7 %all_gather.71 = bf16[12,4,128,64]{2,3,1,0:T(8,128)(2,1)S(1)} all-gather(bf16[1,4,128,64]{2,3,1,0:T(8,128)(2,1)S(1)} %pad_maximum_fusion.11), channel_id=1, replica_groups=mesh['face'=12,'row'=4,'col'=16] {'face'}, dimensions={0}, use_global_device_ids=true | all-gather | bytes 851968 | tf_op jit(solution)/shard_map/all_gather | solution.py:170
  (296 shorter events, 82.9 us)
Async XLA Ops:
  1.5 23.2 %collective-permute-start = (bf16[1,1,8,64]{3,2,1,0:T(8,128)(2,1)S(1)}, bf16[1,1,8,64]{3,2,1,0:T(8,128)(2,1)S(1)}, u32[]{:S(2)}, u32[]{:S(2)}) collective-permute-start(bf16[1,1,8,64]{3,2,1,0:T(8,128)(2,1)S(1)} %get-tuple-element.342), channel_id=1, source_target_pairs={{0,16},{16,32},{32,48},{1,17},{17,33},{33,49},{2,18},{18,34},{34,5... | collective-permute-start | bytes 3080 | tf_op jit(solution)/shard_map/ppermute | solution.py:18
  2.8 21.9 %collective-permute-start.1 = (bf16[1,1,8,64]{3,2,1,0:T(8,128)(2,1)S(1)}, bf16[1,1,8,64]{3,2,1,0:T(8,128)(2,1)S(1)}, u32[]{:S(2)}, u32[]{:S(2)}) collective-permute-start(bf16[1,1,8,64]{3,2,1,0:T(8,128)(2,1)S(1)} %get-tuple-element.341), channel_id=1, source_target_pairs={{16,0},{32,16},{48,32},{17,1},{33,17},{49,33},{18,2},{34,18},{50,3... | collective-permute-start | bytes 3080 | tf_op jit(solution)/shard_map/ppermute | solution.py:19
  24.9 26.6 %collective-permute-start.2 = (bf16[1,34,1,64]{3,2,1,0:T(2,128)(2,1)S(1)}, bf16[1,34,1,64]{3,2,1,0:T(2,128)(2,1)S(1)}, u32[]{:S(2)}, u32[]{:S(2)}) collective-permute-start(bf16[1,34,1,64]{3,2,1,0:T(2,128)(2,1)S(1)} %get-tuple-element.320), channel_id=1, source_target_pairs={{0,1},{1,2},{2,3},{3,4},{4,5},{5,6},{6,7},{7,8},{8,9},{9,10},{10,1... | collective-permute-start | bytes 13064 | tf_op jit(solution)/shard_map/ppermute | solution.py:18
  26.8 24.7 %collective-permute-start.3 = (bf16[1,34,1,64]{3,2,1,0:T(2,128)(2,1)S(1)}, bf16[1,34,1,64]{3,2,1,0:T(2,128)(2,1)S(1)}, u32[]{:S(2)}, u32[]{:S(2)}) collective-permute-start(bf16[1,34,1,64]{3,2,1,0:T(2,128)(2,1)S(1)} %get-tuple-element.319), channel_id=1, source_target_pairs={{1,0},{2,1},{3,2},{4,3},{5,4},{6,5},{7,6},{8,7},{9,8},{10,9},{11,1... | collective-permute-start | bytes 13064 | tf_op jit(solution)/shard_map/ppermute | solution.py:19
  147.5 28.2 %collective-permute-start.4 = (f32[74304]{0:T(1024)S(1)}, f32[74304]{0:T(1024)S(1)}, u32[]{:S(2)}, u32[]{:S(2)}) collective-permute-start(f32[74304]{0:T(1024)S(1)} %pad_maximum_fusion), channel_id=1, source_target_pairs={{0,256},{64,320},{128,384},{192,448},{256,512},{320,576},{384,640}... | collective-permute-start | bytes 891656 | tf_op jit(solution)/shard_map/ppermute | solution.py:89
  150.9 24.8 %collective-permute-start.5 = (f32[74304]{0:T(1024)S(1)}, f32[74304]{0:T(1024)S(1)}, u32[]{:S(2)}, u32[]{:S(2)}) collective-permute-start(f32[74304]{0:T(1024)S(1)} %pad_maximum_fusion), channel_id=1, source_target_pairs={{0,512},{64,576},{128,640},{192,704},{256,0},{320,64},{384,128},{4... | collective-permute-start | bytes 891656 | tf_op jit(solution)/shard_map/ppermute | solution.py:89
  175.8 12.5 %collective-permute-start.6 = (f32[74304]{0:T(1024)S(1)}, f32[74304]{0:T(1024)S(1)}, u32[]{:S(2)}, u32[]{:S(2)}) collective-permute-start(f32[74304]{0:T(1024)S(1)} %select_add_fusion), channel_id=1, source_target_pairs={{0,64},{64,0},{128,192},{192,128},{256,320},{320,256},{384,448},{4... | collective-permute-start | bytes 891656 | tf_op jit(solution)/shard_map/ppermute | solution.py:89
  212.9 12.1 %collective-permute-start.9 = (f32[74304]{0:T(1024)S(1)}, f32[74304]{0:T(1024)S(1)}, u32[]{:S(2)}, u32[]{:S(2)}) collective-permute-start(f32[74304]{0:T(1024)S(1)} %add.209), channel_id=1, source_target_pairs={{0,128},{64,192},{128,0},{192,64},{256,384},{320,448},{384,256},{4... | collective-permute-start | bytes 891656 | tf_op jit(solution)/shard_map/ppermute | solution.py:89
  225.1 21.1 %collective-permute-start.10 = (f32[74304]{0:T(1024)S(1)}, f32[74304]{0:T(1024)S(1)}, u32[]{:S(2)}, u32[]{:S(2)}) collective-permute-start(f32[74304]{0:T(1024)S(1)} %add.213), channel_id=1, source_target_pairs={{0,32},{16,48},{32,0},{48,16},{1,33},{17,49},{33,1},{49,17},{2,34}... | collective-permute-start | bytes 891656 | tf_op jit(solution)/shard_map/ppermute | solution.py:89
  233.4 12.8 %collective-permute-start.11 = (bf16[1,1,40,64]{3,2,1,0:T(8,128)(2,1)S(1)}, bf16[1,1,40,64]{3,2,1,0:T(8,128)(2,1)S(1)}, u32[]{:S(2)}, u32[]{:S(2)}) collective-permute-start(bf16[1,1,40,64]{3,2,1,0:T(8,128)(2,1)S(1)} %maximum_bitcast_fusion.1), channel_id=1, source_target_pairs={{0,16},{16,0},{32,48},{48,32},{1,17},{17,1},{33,49},{49,33},{2,18}... | collective-permute-start | bytes 15368 | tf_op jit(solution)/shard_map/ppermute | solution.py:127
  246.3 18.4 %collective-permute-start.12 = (bf16[2,1,40,64]{3,2,1,0:T(8,128)(2,1)S(1)}, bf16[2,1,40,64]{3,2,1,0:T(8,128)(2,1)S(1)}, u32[]{:S(2)}, u32[]{:S(2)}) collective-permute-start(bf16[2,1,40,64]{3,2,1,0:T(8,128)(2,1)S(1)} %maximum_select_fusion.5), channel_id=1, source_target_pairs={{0,32},{16,48},{32,0},{48,16},{1,33},{17,49},{33,1},{49,17},{2,34}... | collective-permute-start | bytes 30728 | tf_op jit(solution)/shard_map/ppermute | solution.py:127
  253.9 10.8 %collective-permute-start.7 = (bf16[1,1,8,64]{3,2,1,0:T(8,128)(2,1)S(1)}, bf16[1,1,8,64]{3,2,1,0:T(8,128)(2,1)S(1)}, u32[]{:S(2)}, u32[]{:S(2)}) collective-permute-start(bf16[1,1,8,64]{3,2,1,0:T(8,128)(2,1)S(1)} %get-tuple-element.327), channel_id=1, source_target_pairs={{0,16},{16,32},{32,48},{1,17},{17,33},{33,49},{2,18},{18,34},{34,5... | collective-permute-start | bytes 3080 | tf_op jit(solution)/shard_map/ppermute | solution.py:18
  255.2 9.5 %collective-permute-start.8 = (bf16[1,1,8,64]{3,2,1,0:T(8,128)(2,1)S(1)}, bf16[1,1,8,64]{3,2,1,0:T(8,128)(2,1)S(1)}, u32[]{:S(2)}, u32[]{:S(2)}) collective-permute-start(bf16[1,1,8,64]{3,2,1,0:T(8,128)(2,1)S(1)} %get-tuple-element.326), channel_id=1, source_target_pairs={{16,0},{32,16},{48,32},{17,1},{33,17},{49,33},{18,2},{34,18},{50,3... | collective-permute-start | bytes 3080 | tf_op jit(solution)/shard_map/ppermute | solution.py:19
  260.6 12.8 %collective-permute-start.15 = (f32[74304]{0:T(1024)S(1)}, f32[74304]{0:T(1024)S(1)}, u32[]{:S(2)}, u32[]{:S(2)}) collective-permute-start(f32[74304]{0:T(1024)S(1)} %add.214), channel_id=1, source_target_pairs={{0,16},{16,0},{32,48},{48,32},{1,17},{17,1},{33,49},{49,33},{2,18}... | collective-permute-start | bytes 891656 | tf_op jit(solution)/shard_map/ppermute | solution.py:89
  273.4 10.2 %collective-permute-start.16 = (f32[74304]{0:T(1024)S(1)}, f32[74304]{0:T(1024)S(1)}, u32[]{:S(2)}, u32[]{:S(2)}) collective-permute-start(f32[74304]{0:T(1024)S(1)} %add.217), channel_id=1, source_target_pairs={{0,8},{1,9},{2,10},{3,11},{4,12},{5,13},{6,14},{7,15},{8,0},{9,1},... | collective-permute-start | bytes 891656 | tf_op jit(solution)/shard_map/ppermute | solution.py:89
  276.0 3.3 collective-permute-start.17
  283.6 8.7 %collective-permute-start.18 = (f32[74304]{0:T(1024)S(1)}, f32[74304]{0:T(1024)S(1)}, u32[]{:S(2)}, u32[]{:S(2)}) collective-permute-start(f32[74304]{0:T(1024)S(1)} %add.218), channel_id=1, source_target_pairs={{0,4},{1,5},{2,6},{3,7},{4,0},{5,1},{6,2},{7,3},{8,12},{9,13},{10,... | collective-permute-start | bytes 891656 | tf_op jit(solution)/shard_map/ppermute | solution.py:89
  285.6 6.2 %collective-permute-start.19 = (bf16[2,1,144,64]{2,3,1,0:T(8,128)(2,1)S(1)}, bf16[2,1,144,64]{2,3,1,0:T(8,128)(2,1)S(1)}, u32[]{:S(2)}, u32[]{:S(2)}) collective-permute-start(bf16[2,1,144,64]{2,3,1,0:T(8,128)(2,1)S(1)} %maximum_select_fusion.3), channel_id=1, source_target_pairs={{0,2},{1,3},{2,0},{3,1},{4,6},{5,7},{6,4},{7,5},{8,10},{9,11},{10,... | collective-permute-start | bytes 110600 | tf_op jit(solution)/shard_map/ppermute | solution.py:127
  292.3 9.3 %collective-permute-start.20 = (f32[74304]{0:T(1024)S(1)}, f32[74304]{0:T(1024)S(1)}, u32[]{:S(2)}, u32[]{:S(2)}) collective-permute-start(f32[74304]{0:T(1024)S(1)} %add.220), channel_id=1, source_target_pairs={{0,2},{1,3},{2,0},{3,1},{4,6},{5,7},{6,4},{7,5},{8,10},{9,11},{10,... | collective-permute-start | bytes 891656 | tf_op jit(solution)/shard_map/ppermute | solution.py:89
  294.5 7.0 %collective-permute-start.21 = (bf16[4,1,144,64]{2,3,1,0:T(8,128)(2,1)S(1)}, bf16[4,1,144,64]{2,3,1,0:T(8,128)(2,1)S(1)}, u32[]{:S(2)}, u32[]{:S(2)}) collective-permute-start(bf16[4,1,144,64]{2,3,1,0:T(8,128)(2,1)S(1)} %maximum_select_fusion.2), channel_id=1, source_target_pairs={{0,4},{1,5},{2,6},{3,7},{4,0},{5,1},{6,2},{7,3},{8,12},{9,13},{10,... | collective-permute-start | bytes 221192 | tf_op jit(solution)/shard_map/ppermute | solution.py:127
  301.7 12.9 %collective-permute-start.22 = (bf16[8,1,144,64]{2,3,1,0:T(8,128)(2,1)S(1)}, bf16[8,1,144,64]{2,3,1,0:T(8,128)(2,1)S(1)}, u32[]{:S(2)}, u32[]{:S(2)}) collective-permute-start(bf16[8,1,144,64]{2,3,1,0:T(8,128)(2,1)S(1)} %maximum_select_fusion.1), channel_id=1, source_target_pairs={{0,8},{1,9},{2,10},{3,11},{4,12},{5,13},{6,14},{7,15},{8,0},{9,1},... | collective-permute-start | bytes 442376 | tf_op jit(solution)/shard_map/ppermute | solution.py:127
  306.9 7.9 %collective-permute-start.13 = (bf16[1,34,1,64]{1,3,2,0:T(8,128)(2,1)S(1)}, bf16[1,34,1,64]{1,3,2,0:T(8,128)(2,1)S(1)}, u32[]{:S(2)}, u32[]{:S(2)}) collective-permute-start(bf16[1,34,1,64]{1,3,2,0:T(8,128)(2,1)S(1)} %get-tuple-element.295), channel_id=1, source_target_pairs={{0,1},{1,2},{2,3},{3,4},{4,5},{5,6},{6,7},{7,8},{8,9},{9,10},{10,1... | collective-permute-start | bytes 13064 | tf_op jit(solution)/shard_map/ppermute | solution.py:18
  308.8 6.0 %collective-permute-start.14 = (bf16[1,34,1,64]{1,3,2,0:T(8,128)(2,1)S(1)}, bf16[1,34,1,64]{1,3,2,0:T(8,128)(2,1)S(1)}, u32[]{:S(2)}, u32[]{:S(2)}) collective-permute-start(bf16[1,34,1,64]{1,3,2,0:T(8,128)(2,1)S(1)} %get-tuple-element.294), channel_id=1, source_target_pairs={{1,0},{2,1},{3,2},{4,3},{5,4},{6,5},{7,6},{8,7},{9,8},{10,9},{11,1... | collective-permute-start | bytes 13064 | tf_op jit(solution)/shard_map/ppermute | solution.py:19
  312.5 38.5 %collective-permute-start.23 = (f32[74304]{0:T(1024)S(1)}, f32[74304]{0:T(1024)S(1)}, u32[]{:S(2)}, u32[]{:S(2)}) collective-permute-start(f32[74304]{0:T(1024)S(1)} %add.222), channel_id=1, source_target_pairs={{0,1},{1,0},{2,3},{3,2},{4,5},{5,4},{6,7},{7,6},{8,9},{9,8},{10,11... | collective-permute-start | bytes 891656 | tf_op jit(solution)/shard_map/ppermute | solution.py:89
  (8 other events, 10.0 us)

commit v9 on v8

--- a/solution.py
+++ b/solution.py
@@ -170,25 +170,45 @@
                 return lax.all_gather(part, axis, axis=0, tiled=tiled)
             return carried.doubling(part, axis)
 
-        row_strip = jnp.where(row_index == 0, values[:, 0], values[:, tile_rows - 1])
         col_strip = jnp.where(col_index == 0, values[:, :, 0], values[:, :, tile_cols - 1])
-        above, below = halo_strips(values, "row", 1)
-        by_row = gather(jnp.concatenate([row_strip, col_strip], axis=1), "row", False)
-        above, below, by_row = lax.optimization_barrier((above, below, by_row))
-        padded = jnp.concatenate([above, values, below], axis=1)
-        before_col, after_col = halo_strips(padded, "col", 2)
+        by_row = gather(
+            jnp.concatenate([values[:, 0], values[:, tile_rows - 1], col_strip], axis=1), "row", False
+        )
+        above = lax.dynamic_index_in_dim(by_row, (row_index + row_count - 1) % row_count, 0, False)
+        below = lax.dynamic_index_in_dim(by_row, (row_index + 1) % row_count, 0, False)
+        padded = jnp.concatenate(
+            [above[:, None, tile_cols : 2 * tile_cols], values, below[:, None, :tile_cols]], axis=1
+        )
         top_seg = by_row[0, :, :tile_cols]
-        bottom_seg = by_row[row_count - 1, :, :tile_cols]
-        side_line = jnp.moveaxis(by_row[:, :, tile_cols:], 0, 1).reshape(local_faces, side, width)
-        by_col = gather(jnp.concatenate([top_seg, bottom_seg, side_line], axis=1), "col", False)
-        before_col, after_col, by_col = lax.optimization_barrier((before_col, after_col, by_col))
-        padded = jnp.concatenate([before_col, padded, after_col], axis=2)
+        bottom_seg = by_row[row_count - 1, :, tile_cols : 2 * tile_cols]
+        side_line = jnp.moveaxis(by_row[:, :, 2 * tile_cols :], 0, 1).reshape(
+            local_faces, side, width
+        )
+        by_col = gather(
+            jnp.concatenate(
+                [top_seg, bottom_seg, side_line, padded[:, :, 0], padded[:, :, tile_cols - 1]],
+                axis=1,
+            ),
+            "col",
+            False,
+        )
+        lined_up = 2 * tile_cols + side
+        before_col = lax.dynamic_index_in_dim(by_col, (col_index + col_count - 1) % col_count, 0, False)
+        after_col = lax.dynamic_index_in_dim(by_col, (col_index + 1) % col_count, 0, False)
+        padded = jnp.concatenate(
+            [
+                before_col[:, lined_up + tile_rows + 2 :, None],
+                padded,
+                after_col[:, lined_up : lined_up + tile_rows + 2, None],
+            ],
+            axis=2,
+        )
         top_row = jnp.moveaxis(by_col[:, :, :tile_cols], 0, 1).reshape(local_faces, side, width)
         bottom_row = jnp.moveaxis(by_col[:, :, tile_cols : 2 * tile_cols], 0, 1).reshape(
             local_faces, side, width
         )
-        left_col = by_col[0, :, 2 * tile_cols :]
-        right_col = by_col[col_count - 1, :, 2 * tile_cols :]
+        left_col = by_col[0, :, 2 * tile_cols : lined_up]
+        right_col = by_col[col_count - 1, :, 2 * tile_cols : lined_up]
         cycle = jnp.stack([top_row[:, ::-1], left_col, bottom_row, right_col[:, ::-1]], axis=1)
         all_cycle = gather(cycle, "face", True)
         all_corner = all_cycle[:, :, side - 1]

time: 357 us -> 332 us (0.930)
  starting transfers between devices: 79.5 us -> 52.5 us
    ppermute x8 -> x0, starting transfers between devices: 24.6 us -> none  [the longest x4 18.2 us: halo_strips(): lax.ppermute(head, axis, [((i + 1) % count, i) for i in range(ends)])]
  transfers between devices with their start and end apart: 24 -> 16, of which waited for: 6 -> 7; matrix products, arithmetic and copies ran while one was open for 9% -> 8% of each run, Pallas kernels for 0% -> 0%
where the time goes in v9:
time: 332 us; the launch traced here: 329 us
  blocking collectives  194 us (58%)
  starting transfers between devices  52.5 us (16%)
  waiting for transfers between devices  30.9 us (9%)
  local copies, waits for them, and re-layouts  26 us (8%)
  other arithmetic  13.6 us (4%)
  between operations  5.9 us (2%)
  matrix products  5.66 us (2%)
    all_gather x4, blocking collectives, gather(): return lax.all_gather(part, axis, axis=0, tiled=tiled)  96.5 us
    all_gather x3, blocking collectives, nested_sum(): lax.all_gather(part, axis, axis=0, tiled=False)  49 us
    all_gather x3, blocking collectives, gathered_sum(): values = jnp.sum(lax.all_gather(values, axis, axis=0, tiled=False), axis=0)  48.7 us
    ppermute x10, starting transfers between devices, step_send(): return [lax.ppermute(values, axis, pairs) for pairs in pair_sets]  32 us
    ppermute x10, waiting for transfers between devices, step_send(): return [lax.ppermute(values, axis, pairs) for pairs in pair_sets]  21.2 us
    ppermute x6, starting transfers between devices, doubling(): lax.ppermute(gathered, axis, [(i, i ^ step_size) for i in range(count)])  20.5 us
    ppermute x6, waiting for transfers between devices, doubling(): lax.ppermute(gathered, axis, [(i, i ^ step_size) for i in range(count)])  9.72 us
  transfers between devices with their start and end apart: 16, of which 7 were waited for; matrix products, arithmetic and copies ran while one was open for 8% of the time, Pallas kernels for 0%

profile of v9, /device:TPU:56, one launch (start us, length us, event | category | flops | bytes accessed | tf_op | source)
XLA Modules:
  0.0 328.7 jit_solution(11826097705848468803)
XLA Ops:
  1.6 13.7 %all-gather = bf16[4,48,64]{2,1,0:T(8,128)(2,1)S(1)} all-gather(bf16[1,48,64]{2,1,0:T(8,128)(2,1)S(1)} %pad_maximum_fusion.20), channel_id=2, replica_groups=mesh['face'=12,'row'=4,'col'=16] {'row'}, dimensions={0}, use_global_device_ids=true | all-gather | bytes 30720 | tf_op jit(solution)/shard_map/all_gather | solution.py:170
  16.0 23.8 %all-gather.1 = bf16[16,212,64]{1,2,0:T(8,128)(2,1)S(1)} all-gather(bf16[1,212,64]{1,2,0:T(8,128)(2,1)S(1)} %concatenate.268), channel_id=3, replica_groups=mesh['face'=12,'row'=4,'col'=16] {'col'}, dimensions={0}, use_global_device_ids=true | all-gather | bytes 461312 | tf_op jit(solution)/shard_map/all_gather | solution.py:170
  41.8 32.7 %all_gather.58 = bf16[12,4,128,64]{2,3,1,0:T(8,128)(2,1)S(1)} all-gather(bf16[1,4,128,64]{2,3,1,0:T(8,128)(2,1)S(1)} %pad_maximum_fusion.10), channel_id=1, replica_groups=mesh['face'=12,'row'=4,'col'=16] {'face'}, dimensions={0}, use_global_device_ids=true | all-gather | bytes 851968 | tf_op jit(solution)/shard_map/all_gather | solution.py:170
  81.6 19.1 %all-gather.8 = f32[16,2,64]{2,1,0:T(2,128)S(1)} all-gather(f32[1,2,64]{2,1,0:T(2,128)S(1)} %maximum_bitcast_fusion.1), channel_id=4, replica_groups=mesh['face'=12,'row'=4,'col'=16] {'col'}, dimensions={0}, use_global_device_ids=true | all-gather | bytes 8704 | tf_op jit(solution)/shard_map/all_gather | solution.py:61
  100.7 10.0 %all-gather.9 = f32[4,2,64]{2,1,0:T(2,128)S(1)} all-gather(f32[1,2,64]{2,1,0:T(2,128)S(1)} %bitcast.463), channel_id=5, replica_groups=mesh['face'=12,'row'=4,'col'=16] {'row'}, dimensions={0}, use_global_device_ids=true | all-gather | bytes 2560 | tf_op jit(solution)/shard_map/all_gather | solution.py:61
  110.7 19.6 %all-gather.10 = f32[12,2,64]{2,1,0:T(2,128)S(1)} all-gather(f32[1,2,64]{2,1,0:T(2,128)S(1)} %bitcast.468), channel_id=6, replica_groups=mesh['face'=12,'row'=4,'col'=16] {'face'}, dimensions={0}, use_global_device_ids=true | all-gather | bytes 6656 | tf_op jit(solution)/shard_map/all_gather | solution.py:61
  134.4 3.4 %collective-permute-start = (f32[74304]{0:T(1024)S(1)}, f32[74304]{0:T(1024)S(1)}, u32[]{:S(2)}, u32[]{:S(2)}) collective-permute-start(f32[74304]{0:T(1024)S(1)} %pad_maximum_fusion), channel_id=1, source_target_pairs={{0,256},{64,320},{128,384},{192,448},{256,512},{320,576},{384,640}... | collective-permute-start | bytes 891656 | tf_op jit(solution)/shard_map/ppermute | solution.py:89
  137.7 6.4 %collective-permute-start.1 = (f32[74304]{0:T(1024)S(1)}, f32[74304]{0:T(1024)S(1)}, u32[]{:S(2)}, u32[]{:S(2)}) collective-permute-start(f32[74304]{0:T(1024)S(1)} %pad_maximum_fusion), channel_id=1, source_target_pairs={{0,512},{64,576},{128,640},{192,704},{256,0},{320,64},{384,128},{4... | collective-permute-start | bytes 891656 | tf_op jit(solution)/shard_map/ppermute | solution.py:89
  144.2 16.0 %all-gather.11 = f32[16,2,64]{2,1,0:T(2,128)S(1)} all-gather(f32[1,2,64]{2,1,0:T(2,128)S(1)} %bitcast.464), channel_id=7, replica_groups=mesh['face'=12,'row'=4,'col'=16] {'col'}, dimensions={0}, use_global_device_ids=true | all-gather | bytes 8704 | tf_op jit(solution)/shard_map/all_gather | solution.py:47
  162.3 3.9 %collective-permute-start.2 = (f32[74304]{0:T(1024)S(1)}, f32[74304]{0:T(1024)S(1)}, u32[]{:S(2)}, u32[]{:S(2)}) collective-permute-start(f32[74304]{0:T(1024)S(1)} %select_add_fusion), channel_id=1, source_target_pairs={{0,64},{64,0},{128,192},{192,128},{256,320},{320,256},{384,448},{4... | collective-permute-start | bytes 891656 | tf_op jit(solution)/shard_map/ppermute | solution.py:89
  166.9 9.1 %all-gather.12 = f32[4,2,64]{2,1,0:T(2,128)S(1)} all-gather(f32[1,2,64]{2,1,0:T(2,128)S(1)} %bitcast.462), channel_id=8, replica_groups=mesh['face'=12,'row'=4,'col'=16] {'row'}, dimensions={0}, use_global_device_ids=true | all-gather | bytes 2560 | tf_op jit(solution)/shard_map/all_gather | solution.py:47
  176.1 23.9 %all-gather.13 = f32[12,2,64]{2,1,0:T(2,128)S(1)} all-gather(f32[1,2,64]{2,1,0:T(2,128)S(1)} %bitcast.467), channel_id=9, replica_groups=mesh['face'=12,'row'=4,'col'=16] {'face'}, dimensions={0}, use_global_device_ids=true | all-gather | bytes 6656 | tf_op jit(solution)/shard_map/all_gather | solution.py:47
  203.6 8.6 %collective-permute-done.3 = f32[74304]{0:T(1024)S(1)} collective-permute-done((f32[74304]{0:T(1024)S(1)}, f32[74304]{0:T(1024)S(1)}, u32[]{:S(2)}, u32[]{:S(2)}) %collective-permute-start.3) | collective-permute-done | bytes 297248 | tf_op jit(solution)/shard_map/ppermute | solution.py:89
  212.3 5.0 %collective-permute-start.4 = (f32[74304]{0:T(1024)S(1)}, f32[74304]{0:T(1024)S(1)}, u32[]{:S(2)}, u32[]{:S(2)}) collective-permute-start(f32[74304]{0:T(1024)S(1)} %add.275), channel_id=1, source_target_pairs={{0,32},{16,48},{32,0},{48,16},{1,33},{17,49},{33,1},{49,17},{2,34}... | collective-permute-start | bytes 891656 | tf_op jit(solution)/shard_map/ppermute | solution.py:89
  221.3 4.1 %collective-permute-start.5 = (bf16[1,1,48,64]{3,2,1,0:T(8,128)(2,1)S(1)}, bf16[1,1,48,64]{3,2,1,0:T(8,128)(2,1)S(1)}, u32[]{:S(2)}, u32[]{:S(2)}) collective-permute-start(bf16[1,1,48,64]{3,2,1,0:T(8,128)(2,1)S(1)} %maximum_bitcast_fusion), channel_id=1, source_target_pairs={{0,16},{16,0},{32,48},{48,32},{1,17},{17,1},{33,49},{49,33},{2,18}... | collective-permute-start | bytes 18440 | tf_op jit(solution)/shard_map/ppermute | solution.py:127
  233.2 4.3 %collective-permute-start.7 = (bf16[2,1,48,64]{3,2,1,0:T(8,128)(2,1)S(1)}, bf16[2,1,48,64]{3,2,1,0:T(8,128)(2,1)S(1)}, u32[]{:S(2)}, u32[]{:S(2)}) collective-permute-start(bf16[2,1,48,64]{3,2,1,0:T(8,128)(2,1)S(1)} %maximum_select_fusion.5), channel_id=1, source_target_pairs={{0,32},{16,48},{32,0},{48,16},{1,33},{17,49},{33,1},{49,17},{2,34}... | collective-permute-start | bytes 36872 | tf_op jit(solution)/shard_map/ppermute | solution.py:127
  240.8 3.1 collective-permute-start.6
  245.8 7.7 %collective-permute-done.6 = f32[74304]{0:T(1024)S(1)} collective-permute-done((f32[74304]{0:T(1024)S(1)}, f32[74304]{0:T(1024)S(1)}, u32[]{:S(2)}, u32[]{:S(2)}) %collective-permute-start.6) | collective-permute-done | bytes 297248 | tf_op jit(solution)/shard_map/ppermute | solution.py:89
  259.4 4.3 %collective-permute-done.8 = f32[74304]{0:T(1024)S(1)} collective-permute-done((f32[74304]{0:T(1024)S(1)}, f32[74304]{0:T(1024)S(1)}, u32[]{:S(2)}, u32[]{:S(2)}) %collective-permute-start.8) | collective-permute-done | bytes 297248 | tf_op jit(solution)/shard_map/ppermute | solution.py:89
  268.0 4.0 %collective-permute-done.11 = bf16[2,1,212,64]{2,3,1,0:T(8,128)(2,1)S(1)} collective-permute-done((bf16[2,1,212,64]{2,3,1,0:T(8,128)(2,1)S(1)}, bf16[2,1,212,64]{2,3,1,0:T(8,128)(2,1)S(1)}, u32[]{:S(2)}, u32[]{:S(2)}) %collective-permute-start.11) | collective-permute-done | bytes 54304 | tf_op jit(solution)/shard_map/ppermute | solution.py:127
  274.7 4.1 %collective-permute-start.13 = (bf16[4,1,212,64]{2,3,1,0:T(8,128)(2,1)S(1)}, bf16[4,1,212,64]{2,3,1,0:T(8,128)(2,1)S(1)}, u32[]{:S(2)}, u32[]{:S(2)}) collective-permute-start(bf16[4,1,212,64]{2,3,1,0:T(8,128)(2,1)S(1)} %maximum_select_fusion.2), channel_id=1, source_target_pairs={{0,4},{1,5},{2,6},{3,7},{4,0},{5,1},{6,2},{7,3},{8,12},{9,13},{10,... | collective-permute-start | bytes 325640 | tf_op jit(solution)/shard_map/ppermute | solution.py:127
  281.9 4.3 %collective-permute-start.14 = (bf16[8,1,212,64]{2,3,1,0:T(8,128)(2,1)S(1)}, bf16[8,1,212,64]{2,3,1,0:T(8,128)(2,1)S(1)}, u32[]{:S(2)}, u32[]{:S(2)}) collective-permute-start(bf16[8,1,212,64]{2,3,1,0:T(8,128)(2,1)S(1)} %maximum_select_fusion.1), channel_id=1, source_target_pairs={{0,8},{1,9},{2,10},{3,11},{4,12},{5,13},{6,14},{7,15},{8,0},{9,1},... | collective-permute-start | bytes 651272 | tf_op jit(solution)/shard_map/ppermute | solution.py:127
  288.5 3.1 collective-permute-done.14
  292.7 26.3 %all_gather.71 = bf16[12,4,128,64]{2,3,1,0:T(8,128)(2,1)S(1)} all-gather(bf16[1,4,128,64]{2,3,1,0:T(8,128)(2,1)S(1)} %pad_maximum_fusion.11), channel_id=1, replica_groups=mesh['face'=12,'row'=4,'col'=16] {'face'}, dimensions={0}, use_global_device_ids=true | all-gather | bytes 851968 | tf_op jit(solution)/shard_map/all_gather | solution.py:170
  (292 shorter events, 62.4 us)
Async XLA Ops:
  39.9 0.9 copy-start.1
  75.3 0.7 copy-start.4
  130.9 0.7 copy-start.5
  131.0 0.8 copy-start.3
  131.9 0.7 copy-start.7
  134.4 27.9 %collective-permute-start = (f32[74304]{0:T(1024)S(1)}, f32[74304]{0:T(1024)S(1)}, u32[]{:S(2)}, u32[]{:S(2)}) collective-permute-start(f32[74304]{0:T(1024)S(1)} %pad_maximum_fusion), channel_id=1, source_target_pairs={{0,256},{64,320},{128,384},{192,448},{256,512},{320,576},{384,640}... | collective-permute-start | bytes 891656 | tf_op jit(solution)/shard_map/ppermute | solution.py:89
  137.7 24.5 %collective-permute-start.1 = (f32[74304]{0:T(1024)S(1)}, f32[74304]{0:T(1024)S(1)}, u32[]{:S(2)}, u32[]{:S(2)}) collective-permute-start(f32[74304]{0:T(1024)S(1)} %pad_maximum_fusion), channel_id=1, source_target_pairs={{0,512},{64,576},{128,640},{192,704},{256,0},{320,64},{384,128},{4... | collective-permute-start | bytes 891656 | tf_op jit(solution)/shard_map/ppermute | solution.py:89
  162.3 13.7 %collective-permute-start.2 = (f32[74304]{0:T(1024)S(1)}, f32[74304]{0:T(1024)S(1)}, u32[]{:S(2)}, u32[]{:S(2)}) collective-permute-start(f32[74304]{0:T(1024)S(1)} %select_add_fusion), channel_id=1, source_target_pairs={{0,64},{64,0},{128,192},{192,128},{256,320},{320,256},{384,448},{4... | collective-permute-start | bytes 891656 | tf_op jit(solution)/shard_map/ppermute | solution.py:89
  201.2 11.0 %collective-permute-start.3 = (f32[74304]{0:T(1024)S(1)}, f32[74304]{0:T(1024)S(1)}, u32[]{:S(2)}, u32[]{:S(2)}) collective-permute-start(f32[74304]{0:T(1024)S(1)} %add.271), channel_id=1, source_target_pairs={{0,128},{64,192},{128,0},{192,64},{256,384},{320,448},{384,256},{4... | collective-permute-start | bytes 891656 | tf_op jit(solution)/shard_map/ppermute | solution.py:89
  212.3 20.8 %collective-permute-start.4 = (f32[74304]{0:T(1024)S(1)}, f32[74304]{0:T(1024)S(1)}, u32[]{:S(2)}, u32[]{:S(2)}) collective-permute-start(f32[74304]{0:T(1024)S(1)} %add.275), channel_id=1, source_target_pairs={{0,32},{16,48},{32,0},{48,16},{1,33},{17,49},{33,1},{49,17},{2,34}... | collective-permute-start | bytes 891656 | tf_op jit(solution)/shard_map/ppermute | solution.py:89
  221.3 11.8 %collective-permute-start.5 = (bf16[1,1,48,64]{3,2,1,0:T(8,128)(2,1)S(1)}, bf16[1,1,48,64]{3,2,1,0:T(8,128)(2,1)S(1)}, u32[]{:S(2)}, u32[]{:S(2)}) collective-permute-start(bf16[1,1,48,64]{3,2,1,0:T(8,128)(2,1)S(1)} %maximum_bitcast_fusion), channel_id=1, source_target_pairs={{0,16},{16,0},{32,48},{48,32},{1,17},{17,1},{33,49},{49,33},{2,18}... | collective-permute-start | bytes 18440 | tf_op jit(solution)/shard_map/ppermute | solution.py:127
  233.2 10.7 %collective-permute-start.7 = (bf16[2,1,48,64]{3,2,1,0:T(8,128)(2,1)S(1)}, bf16[2,1,48,64]{3,2,1,0:T(8,128)(2,1)S(1)}, u32[]{:S(2)}, u32[]{:S(2)}) collective-permute-start(bf16[2,1,48,64]{3,2,1,0:T(8,128)(2,1)S(1)} %maximum_select_fusion.5), channel_id=1, source_target_pairs={{0,32},{16,48},{32,0},{48,16},{1,33},{17,49},{33,1},{49,17},{2,34}... | collective-permute-start | bytes 36872 | tf_op jit(solution)/shard_map/ppermute | solution.py:127
  240.8 12.8 %collective-permute-start.6 = (f32[74304]{0:T(1024)S(1)}, f32[74304]{0:T(1024)S(1)}, u32[]{:S(2)}, u32[]{:S(2)}) collective-permute-start(f32[74304]{0:T(1024)S(1)} %add.276), channel_id=1, source_target_pairs={{0,16},{16,0},{32,48},{48,32},{1,17},{17,1},{33,49},{49,33},{2,18}... | collective-permute-start | bytes 891656 | tf_op jit(solution)/shard_map/ppermute | solution.py:89
  244.6 0.8 slice-start.1
  253.6 10.2 %collective-permute-start.8 = (f32[74304]{0:T(1024)S(1)}, f32[74304]{0:T(1024)S(1)}, u32[]{:S(2)}, u32[]{:S(2)}) collective-permute-start(f32[74304]{0:T(1024)S(1)} %add.278), channel_id=1, source_target_pairs={{0,8},{1,9},{2,10},{3,11},{4,12},{5,13},{6,14},{7,15},{8,0},{9,1},... | collective-permute-start | bytes 891656 | tf_op jit(solution)/shard_map/ppermute | solution.py:89
  256.3 3.1 collective-permute-start.9
  263.8 8.7 %collective-permute-start.10 = (f32[74304]{0:T(1024)S(1)}, f32[74304]{0:T(1024)S(1)}, u32[]{:S(2)}, u32[]{:S(2)}) collective-permute-start(f32[74304]{0:T(1024)S(1)} %add.280), channel_id=1, source_target_pairs={{0,4},{1,5},{2,6},{3,7},{4,0},{5,1},{6,2},{7,3},{8,12},{9,13},{10,... | collective-permute-start | bytes 891656 | tf_op jit(solution)/shard_map/ppermute | solution.py:89
  265.7 6.2 %collective-permute-start.11 = (bf16[2,1,212,64]{2,3,1,0:T(8,128)(2,1)S(1)}, bf16[2,1,212,64]{2,3,1,0:T(8,128)(2,1)S(1)}, u32[]{:S(2)}, u32[]{:S(2)}) collective-permute-start(bf16[2,1,212,64]{2,3,1,0:T(8,128)(2,1)S(1)} %maximum_select_fusion.3), channel_id=1, source_target_pairs={{0,2},{1,3},{2,0},{3,1},{4,6},{5,7},{6,4},{7,5},{8,10},{9,11},{10,... | collective-permute-start | bytes 162824 | tf_op jit(solution)/shard_map/ppermute | solution.py:127
  272.5 9.3 %collective-permute-start.12 = (f32[74304]{0:T(1024)S(1)}, f32[74304]{0:T(1024)S(1)}, u32[]{:S(2)}, u32[]{:S(2)}) collective-permute-start(f32[74304]{0:T(1024)S(1)} %add.282), channel_id=1, source_target_pairs={{0,2},{1,3},{2,0},{3,1},{4,6},{5,7},{6,4},{7,5},{8,10},{9,11},{10,... | collective-permute-start | bytes 891656 | tf_op jit(solution)/shard_map/ppermute | solution.py:89
  274.7 7.0 %collective-permute-start.13 = (bf16[4,1,212,64]{2,3,1,0:T(8,128)(2,1)S(1)}, bf16[4,1,212,64]{2,3,1,0:T(8,128)(2,1)S(1)}, u32[]{:S(2)}, u32[]{:S(2)}) collective-permute-start(bf16[4,1,212,64]{2,3,1,0:T(8,128)(2,1)S(1)} %maximum_select_fusion.2), channel_id=1, source_target_pairs={{0,4},{1,5},{2,6},{3,7},{4,0},{5,1},{6,2},{7,3},{8,12},{9,13},{10,... | collective-permute-start | bytes 325640 | tf_op jit(solution)/shard_map/ppermute | solution.py:127
  281.9 9.8 %collective-permute-start.14 = (bf16[8,1,212,64]{2,3,1,0:T(8,128)(2,1)S(1)}, bf16[8,1,212,64]{2,3,1,0:T(8,128)(2,1)S(1)}, u32[]{:S(2)}, u32[]{:S(2)}) collective-permute-start(bf16[8,1,212,64]{2,3,1,0:T(8,128)(2,1)S(1)} %maximum_select_fusion.1), channel_id=1, source_target_pairs={{0,8},{1,9},{2,10},{3,11},{4,12},{5,13},{6,14},{7,15},{8,0},{9,1},... | collective-permute-start | bytes 651272 | tf_op jit(solution)/shard_map/ppermute | solution.py:127
  286.4 39.8 %collective-permute-start.15 = (f32[74304]{0:T(1024)S(1)}, f32[74304]{0:T(1024)S(1)}, u32[]{:S(2)}, u32[]{:S(2)}) collective-permute-start(f32[74304]{0:T(1024)S(1)} %add.284), channel_id=1, source_target_pairs={{0,1},{1,0},{2,3},{3,2},{4,5},{5,4},{6,7},{7,6},{8,9},{9,8},{10,11... | collective-permute-start | bytes 891656 | tf_op jit(solution)/shard_map/ppermute | solution.py:89
  326.2 0.7 copy-start
  327.1 0.7 slice-start
  (2 other events, 1.1 us)

commit v10 on v9

--- a/solution.py
+++ b/solution.py
@@ -73,14 +73,19 @@
             ],
         ),
         ("face", [[(i, i ^ 1) for i in range(faces)]]),
-        ("face", [[(i, i ^ 2) for i in range(faces)]]),
     ]
-    for axis in ("row", "col"):
-        count = lax.axis_size(axis)
-        step = count // 2
-        while step >= 1:
-            steps.append((axis, [[(i, i ^ step) for i in range(count)]]))
-            step //= 2
+    count = lax.axis_size("col")
+    steps.append(("col", [[(i, i ^ 1) for i in range(count)]]))
+    steps.append(("face", [[(i, i ^ 2) for i in range(faces)]]))
+    rows = lax.axis_size("row")
+    step = rows // 2
+    while step >= 1:
+        steps.append(("row", [[(i, i ^ step) for i in range(rows)]]))
+        step //= 2
+    step = count // 2
+    while step >= 2:
+        steps.append(("col", [[(i, i ^ step) for i in range(count)]]))
+        step //= 2
     return steps
 
 

time: 332 us -> 343 us (1.033)
  waiting for transfers between devices: 30.9 us -> 45.5 us
    ppermute x10, waiting for transfers between devices: 21.2 us -> 30.4 us  [step_send(): return [lax.ppermute(values, axis, pairs) for pairs in pair_sets]]
    ppermute x6, waiting for transfers between devices: 9.72 us -> 15.1 us  [doubling(): lax.ppermute(gathered, axis, [(i, i ^ step_size) for i in range(count)])]
where the time goes in v10:
time: 343 us; the launch traced here: 342 us
  blocking collectives  196 us (57%)
  starting transfers between devices  49.3 us (14%)
  waiting for transfers between devices  45.5 us (13%)
  local copies, waits for them, and re-layouts  26 us (8%)
  other arithmetic  13.6 us (4%)
  between operations  5.9 us (2%)
  matrix products  5.66 us (2%)
    all_gather x4, blocking collectives, gather(): return lax.all_gather(part, axis, axis=0, tiled=tiled)  98.2 us
    all_gather x3, blocking collectives, nested_sum(): lax.all_gather(part, axis, axis=0, tiled=False)  49 us
    all_gather x3, blocking collectives, gathered_sum(): values = jnp.sum(lax.all_gather(values, axis, axis=0, tiled=False), axis=0)  48.7 us
    ppermute x10, waiting for transfers between devices, step_send(): return [lax.ppermute(values, axis, pairs) for pairs in pair_sets]  30.4 us
    ppermute x10, starting transfers between devices, step_send(): return [lax.ppermute(values, axis, pairs) for pairs in pair_sets]  29.9 us
    ppermute x6, starting transfers between devices, doubling(): lax.ppermute(gathered, axis, [(i, i ^ step_size) for i in range(count)])  19.4 us
    ppermute x6, waiting for transfers between devices, doubling(): lax.ppermute(gathered, axis, [(i, i ^ step_size) for i in range(count)])  15.1 us
  transfers between devices with their start and end apart: 16, of which 7 were waited for; matrix products, arithmetic and copies ran while one was open for 8% of the time, Pallas kernels for 0%

profile of v10, /device:TPU:56, one launch (start us, length us, event | category | flops | bytes accessed | tf_op | source)
XLA Modules:
  0.0 341.8 jit_solution(6156403181804648681)
XLA Ops:
  1.6 13.7 %all-gather = bf16[4,48,64]{2,1,0:T(8,128)(2,1)S(1)} all-gather(bf16[1,48,64]{2,1,0:T(8,128)(2,1)S(1)} %pad_maximum_fusion.20), channel_id=2, replica_groups=mesh['face'=12,'row'=4,'col'=16] {'row'}, dimensions={0}, use_global_device_ids=true | all-gather | bytes 30720 | tf_op jit(solution)/shard_map/all_gather | solution.py:175
  16.0 23.8 %all-gather.1 = bf16[16,212,64]{1,2,0:T(8,128)(2,1)S(1)} all-gather(bf16[1,212,64]{1,2,0:T(8,128)(2,1)S(1)} %concatenate.268), channel_id=3, replica_groups=mesh['face'=12,'row'=4,'col'=16] {'col'}, dimensions={0}, use_global_device_ids=true | all-gather | bytes 461312 | tf_op jit(solution)/shard_map/all_gather | solution.py:175
  41.8 32.7 %all_gather.58 = bf16[12,4,128,64]{2,3,1,0:T(8,128)(2,1)S(1)} all-gather(bf16[1,4,128,64]{2,3,1,0:T(8,128)(2,1)S(1)} %pad_maximum_fusion.10), channel_id=1, replica_groups=mesh['face'=12,'row'=4,'col'=16] {'face'}, dimensions={0}, use_global_device_ids=true | all-gather | bytes 851968 | tf_op jit(solution)/shard_map/all_gather | solution.py:175
  81.6 19.1 %all-gather.8 = f32[16,2,64]{2,1,0:T(2,128)S(1)} all-gather(f32[1,2,64]{2,1,0:T(2,128)S(1)} %maximum_bitcast_fusion.1), channel_id=4, replica_groups=mesh['face'=12,'row'=4,'col'=16] {'col'}, dimensions={0}, use_global_device_ids=true | all-gather | bytes 8704 | tf_op jit(solution)/shard_map/all_gather | solution.py:61
  100.7 10.0 %all-gather.9 = f32[4,2,64]{2,1,0:T(2,128)S(1)} all-gather(f32[1,2,64]{2,1,0:T(2,128)S(1)} %bitcast.463), channel_id=5, replica_groups=mesh['face'=12,'row'=4,'col'=16] {'row'}, dimensions={0}, use_global_device_ids=true | all-gather | bytes 2560 | tf_op jit(solution)/shard_map/all_gather | solution.py:61
  110.7 19.6 %all-gather.10 = f32[12,2,64]{2,1,0:T(2,128)S(1)} all-gather(f32[1,2,64]{2,1,0:T(2,128)S(1)} %bitcast.468), channel_id=6, replica_groups=mesh['face'=12,'row'=4,'col'=16] {'face'}, dimensions={0}, use_global_device_ids=true | all-gather | bytes 6656 | tf_op jit(solution)/shard_map/all_gather | solution.py:61
  134.4 3.4 collective-permute-start
  137.7 6.4 %collective-permute-start.1 = (f32[74304]{0:T(1024)S(1)}, f32[74304]{0:T(1024)S(1)}, u32[]{:S(2)}, u32[]{:S(2)}) collective-permute-start(f32[74304]{0:T(1024)S(1)} %pad_maximum_fusion), channel_id=1, source_target_pairs={{0,512},{64,576},{128,640},{192,704},{256,0},{320,64},{384,128},{4... | collective-permute-start | bytes 891656 | tf_op jit(solution)/shard_map/ppermute | solution.py:94
  144.2 16.0 %all-gather.11 = f32[16,2,64]{2,1,0:T(2,128)S(1)} all-gather(f32[1,2,64]{2,1,0:T(2,128)S(1)} %bitcast.464), channel_id=7, replica_groups=mesh['face'=12,'row'=4,'col'=16] {'col'}, dimensions={0}, use_global_device_ids=true | all-gather | bytes 8704 | tf_op jit(solution)/shard_map/all_gather | solution.py:47
  162.3 3.9 %collective-permute-start.2 = (f32[74304]{0:T(1024)S(1)}, f32[74304]{0:T(1024)S(1)}, u32[]{:S(2)}, u32[]{:S(2)}) collective-permute-start(f32[74304]{0:T(1024)S(1)} %select_add_fusion), channel_id=1, source_target_pairs={{0,64},{64,0},{128,192},{192,128},{256,320},{320,256},{384,448},{4... | collective-permute-start | bytes 891656 | tf_op jit(solution)/shard_map/ppermute | solution.py:94
  166.9 9.1 %all-gather.12 = f32[4,2,64]{2,1,0:T(2,128)S(1)} all-gather(f32[1,2,64]{2,1,0:T(2,128)S(1)} %bitcast.462), channel_id=8, replica_groups=mesh['face'=12,'row'=4,'col'=16] {'row'}, dimensions={0}, use_global_device_ids=true | all-gather | bytes 2560 | tf_op jit(solution)/shard_map/all_gather | solution.py:47
  176.1 23.9 %all-gather.13 = f32[12,2,64]{2,1,0:T(2,128)S(1)} all-gather(f32[1,2,64]{2,1,0:T(2,128)S(1)} %bitcast.467), channel_id=9, replica_groups=mesh['face'=12,'row'=4,'col'=16] {'face'}, dimensions={0}, use_global_device_ids=true | all-gather | bytes 6656 | tf_op jit(solution)/shard_map/all_gather | solution.py:47
  210.9 3.6 %collective-permute-start.5 = (bf16[1,1,48,64]{3,2,1,0:T(8,128)(2,1)S(1)}, bf16[1,1,48,64]{3,2,1,0:T(8,128)(2,1)S(1)}, u32[]{:S(2)}, u32[]{:S(2)}) collective-permute-start(bf16[1,1,48,64]{3,2,1,0:T(8,128)(2,1)S(1)} %maximum_bitcast_fusion), channel_id=1, source_target_pairs={{0,16},{16,0},{32,48},{48,32},{1,17},{17,1},{33,49},{49,33},{2,18}... | collective-permute-start | bytes 18440 | tf_op jit(solution)/shard_map/ppermute | solution.py:132
  214.5 2.5 broadcast_select_fusion.2
  222.3 5.5 %collective-permute-start.7 = (bf16[2,1,48,64]{3,2,1,0:T(8,128)(2,1)S(1)}, bf16[2,1,48,64]{3,2,1,0:T(8,128)(2,1)S(1)}, u32[]{:S(2)}, u32[]{:S(2)}) collective-permute-start(bf16[2,1,48,64]{3,2,1,0:T(8,128)(2,1)S(1)} %maximum_select_fusion.5), channel_id=1, source_target_pairs={{0,32},{16,48},{32,0},{48,16},{1,33},{17,49},{33,1},{49,17},{2,34}... | collective-permute-start | bytes 36872 | tf_op jit(solution)/shard_map/ppermute | solution.py:132
  231.2 4.3 %collective-permute-start.6 = (f32[74304]{0:T(1024)S(1)}, f32[74304]{0:T(1024)S(1)}, u32[]{:S(2)}, u32[]{:S(2)}) collective-permute-start(f32[74304]{0:T(1024)S(1)} %add.276), channel_id=1, source_target_pairs={{0,32},{16,48},{32,0},{48,16},{1,33},{17,49},{33,1},{49,17},{2,34}... | collective-permute-start | bytes 891656 | tf_op jit(solution)/shard_map/ppermute | solution.py:94
  237.3 14.5 %collective-permute-done.6 = f32[74304]{0:T(1024)S(1)} collective-permute-done((f32[74304]{0:T(1024)S(1)}, f32[74304]{0:T(1024)S(1)}, u32[]{:S(2)}, u32[]{:S(2)}) %collective-permute-start.6) | collective-permute-done | bytes 297248 | tf_op jit(solution)/shard_map/ppermute | solution.py:94
  257.7 10.3 %collective-permute-done.8 = f32[74304]{0:T(1024)S(1)} collective-permute-done((f32[74304]{0:T(1024)S(1)}, f32[74304]{0:T(1024)S(1)}, u32[]{:S(2)}, u32[]{:S(2)}) %collective-permute-start.8) | collective-permute-done | bytes 297248 | tf_op jit(solution)/shard_map/ppermute | solution.py:94
  272.3 4.0 %collective-permute-done.11 = bf16[2,1,212,64]{2,3,1,0:T(8,128)(2,1)S(1)} collective-permute-done((bf16[2,1,212,64]{2,3,1,0:T(8,128)(2,1)S(1)}, bf16[2,1,212,64]{2,3,1,0:T(8,128)(2,1)S(1)}, u32[]{:S(2)}, u32[]{:S(2)}) %collective-permute-start.11) | collective-permute-done | bytes 54304 | tf_op jit(solution)/shard_map/ppermute | solution.py:132
  276.3 4.1 %collective-permute-done.10 = f32[74304]{0:T(1024)S(1)} collective-permute-done((f32[74304]{0:T(1024)S(1)}, f32[74304]{0:T(1024)S(1)}, u32[]{:S(2)}, u32[]{:S(2)}) %collective-permute-start.10) | collective-permute-done | bytes 297248 | tf_op jit(solution)/shard_map/ppermute | solution.py:94
  282.6 3.9 %collective-permute-start.13 = (bf16[4,1,212,64]{2,3,1,0:T(8,128)(2,1)S(1)}, bf16[4,1,212,64]{2,3,1,0:T(8,128)(2,1)S(1)}, u32[]{:S(2)}, u32[]{:S(2)}) collective-permute-start(bf16[4,1,212,64]{2,3,1,0:T(8,128)(2,1)S(1)} %maximum_select_fusion.2), channel_id=1, source_target_pairs={{0,4},{1,5},{2,6},{3,7},{4,0},{5,1},{6,2},{7,3},{8,12},{9,13},{10,... | collective-permute-start | bytes 325640 | tf_op jit(solution)/shard_map/ppermute | solution.py:132
  286.8 6.3 %collective-permute-done.13 = bf16[4,1,212,64]{2,3,1,0:T(8,128)(2,1)S(1)} collective-permute-done((bf16[4,1,212,64]{2,3,1,0:T(8,128)(2,1)S(1)}, bf16[4,1,212,64]{2,3,1,0:T(8,128)(2,1)S(1)}, u32[]{:S(2)}, u32[]{:S(2)}) %collective-permute-start.13) | collective-permute-done | bytes 108576 | tf_op jit(solution)/shard_map/ppermute | solution.py:132
  298.2 4.8 %collective-permute-done.14 = bf16[8,1,212,64]{2,3,1,0:T(8,128)(2,1)S(1)} collective-permute-done((bf16[8,1,212,64]{2,3,1,0:T(8,128)(2,1)S(1)}, bf16[8,1,212,64]{2,3,1,0:T(8,128)(2,1)S(1)}, u32[]{:S(2)}, u32[]{:S(2)}) %collective-permute-start.14) | collective-permute-done | bytes 217120 | tf_op jit(solution)/shard_map/ppermute | solution.py:132
  304.1 28.0 %all_gather.71 = bf16[12,4,128,64]{2,3,1,0:T(8,128)(2,1)S(1)} all-gather(bf16[1,4,128,64]{2,3,1,0:T(8,128)(2,1)S(1)} %pad_maximum_fusion.11), channel_id=1, replica_groups=mesh['face'=12,'row'=4,'col'=16] {'face'}, dimensions={0}, use_global_device_ids=true | all-gather | bytes 851968 | tf_op jit(solution)/shard_map/all_gather | solution.py:175
  (292 shorter events, 62.6 us)
Async XLA Ops:
  39.9 0.9 copy-start.1
  75.3 0.7 copy-start.4
  130.9 0.7 copy-start.5
  131.0 0.8 copy-start.3
  131.9 0.7 copy-start.7
  134.4 27.9 %collective-permute-start = (f32[74304]{0:T(1024)S(1)}, f32[74304]{0:T(1024)S(1)}, u32[]{:S(2)}, u32[]{:S(2)}) collective-permute-start(f32[74304]{0:T(1024)S(1)} %pad_maximum_fusion), channel_id=1, source_target_pairs={{0,256},{64,320},{128,384},{192,448},{256,512},{320,576},{384,640}... | collective-permute-start | bytes 891656 | tf_op jit(solution)/shard_map/ppermute | solution.py:94
  137.7 24.5 %collective-permute-start.1 = (f32[74304]{0:T(1024)S(1)}, f32[74304]{0:T(1024)S(1)}, u32[]{:S(2)}, u32[]{:S(2)}) collective-permute-start(f32[74304]{0:T(1024)S(1)} %pad_maximum_fusion), channel_id=1, source_target_pairs={{0,512},{64,576},{128,640},{192,704},{256,0},{320,64},{384,128},{4... | collective-permute-start | bytes 891656 | tf_op jit(solution)/shard_map/ppermute | solution.py:94
  162.3 13.7 %collective-permute-start.2 = (f32[74304]{0:T(1024)S(1)}, f32[74304]{0:T(1024)S(1)}, u32[]{:S(2)}, u32[]{:S(2)}) collective-permute-start(f32[74304]{0:T(1024)S(1)} %select_add_fusion), channel_id=1, source_target_pairs={{0,64},{64,0},{128,192},{192,128},{256,320},{320,256},{384,448},{4... | collective-permute-start | bytes 891656 | tf_op jit(solution)/shard_map/ppermute | solution.py:94
  201.2 3.5 %collective-permute-start.3 = (f32[74304]{0:T(1024)S(1)}, f32[74304]{0:T(1024)S(1)}, u32[]{:S(2)}, u32[]{:S(2)}) collective-permute-start(f32[74304]{0:T(1024)S(1)} %add.271), channel_id=1, source_target_pairs={{0,1},{1,0},{2,3},{3,2},{4,5},{5,4},{6,7},{7,6},{8,9},{9,8},{10,11... | collective-permute-start | bytes 891656 | tf_op jit(solution)/shard_map/ppermute | solution.py:94
  204.8 17.5 %collective-permute-start.4 = (f32[74304]{0:T(1024)S(1)}, f32[74304]{0:T(1024)S(1)}, u32[]{:S(2)}, u32[]{:S(2)}) collective-permute-start(f32[74304]{0:T(1024)S(1)} %add.275), channel_id=1, source_target_pairs={{0,128},{64,192},{128,0},{192,64},{256,384},{320,448},{384,256},{4... | collective-permute-start | bytes 891656 | tf_op jit(solution)/shard_map/ppermute | solution.py:94
  210.9 11.4 %collective-permute-start.5 = (bf16[1,1,48,64]{3,2,1,0:T(8,128)(2,1)S(1)}, bf16[1,1,48,64]{3,2,1,0:T(8,128)(2,1)S(1)}, u32[]{:S(2)}, u32[]{:S(2)}) collective-permute-start(bf16[1,1,48,64]{3,2,1,0:T(8,128)(2,1)S(1)} %maximum_bitcast_fusion), channel_id=1, source_target_pairs={{0,16},{16,0},{32,48},{48,32},{1,17},{17,1},{33,49},{49,33},{2,18}... | collective-permute-start | bytes 18440 | tf_op jit(solution)/shard_map/ppermute | solution.py:132
  222.3 13.1 %collective-permute-start.7 = (bf16[2,1,48,64]{3,2,1,0:T(8,128)(2,1)S(1)}, bf16[2,1,48,64]{3,2,1,0:T(8,128)(2,1)S(1)}, u32[]{:S(2)}, u32[]{:S(2)}) collective-permute-start(bf16[2,1,48,64]{3,2,1,0:T(8,128)(2,1)S(1)} %maximum_select_fusion.5), channel_id=1, source_target_pairs={{0,32},{16,48},{32,0},{48,16},{1,33},{17,49},{33,1},{49,17},{2,34}... | collective-permute-start | bytes 36872 | tf_op jit(solution)/shard_map/ppermute | solution.py:132
  231.2 20.6 %collective-permute-start.6 = (f32[74304]{0:T(1024)S(1)}, f32[74304]{0:T(1024)S(1)}, u32[]{:S(2)}, u32[]{:S(2)}) collective-permute-start(f32[74304]{0:T(1024)S(1)} %add.276), channel_id=1, source_target_pairs={{0,32},{16,48},{32,0},{48,16},{1,33},{17,49},{33,1},{49,17},{2,34}... | collective-permute-start | bytes 891656 | tf_op jit(solution)/shard_map/ppermute | solution.py:94
  236.1 0.8 slice-start.1
  251.8 16.2 %collective-permute-start.8 = (f32[74304]{0:T(1024)S(1)}, f32[74304]{0:T(1024)S(1)}, u32[]{:S(2)}, u32[]{:S(2)}) collective-permute-start(f32[74304]{0:T(1024)S(1)} %add.278), channel_id=1, source_target_pairs={{0,16},{16,0},{32,48},{48,32},{1,17},{17,1},{33,49},{49,33},{2,18}... | collective-permute-start | bytes 891656 | tf_op jit(solution)/shard_map/ppermute | solution.py:94
  254.6 3.1 collective-permute-start.9
  268.1 12.2 %collective-permute-start.10 = (f32[74304]{0:T(1024)S(1)}, f32[74304]{0:T(1024)S(1)}, u32[]{:S(2)}, u32[]{:S(2)}) collective-permute-start(f32[74304]{0:T(1024)S(1)} %add.280), channel_id=1, source_target_pairs={{0,8},{1,9},{2,10},{3,11},{4,12},{5,13},{6,14},{7,15},{8,0},{9,1},... | collective-permute-start | bytes 891656 | tf_op jit(solution)/shard_map/ppermute | solution.py:94
  270.1 6.2 %collective-permute-start.11 = (bf16[2,1,212,64]{2,3,1,0:T(8,128)(2,1)S(1)}, bf16[2,1,212,64]{2,3,1,0:T(8,128)(2,1)S(1)}, u32[]{:S(2)}, u32[]{:S(2)}) collective-permute-start(bf16[2,1,212,64]{2,3,1,0:T(8,128)(2,1)S(1)} %maximum_select_fusion.3), channel_id=1, source_target_pairs={{0,2},{1,3},{2,0},{3,1},{4,6},{5,7},{6,4},{7,5},{8,10},{9,11},{10,... | collective-permute-start | bytes 162824 | tf_op jit(solution)/shard_map/ppermute | solution.py:132
  280.4 12.8 %collective-permute-start.12 = (f32[74304]{0:T(1024)S(1)}, f32[74304]{0:T(1024)S(1)}, u32[]{:S(2)}, u32[]{:S(2)}) collective-permute-start(f32[74304]{0:T(1024)S(1)} %add.282), channel_id=1, source_target_pairs={{0,4},{1,5},{2,6},{3,7},{4,0},{5,1},{6,2},{7,3},{8,12},{9,13},{10,... | collective-permute-start | bytes 891656 | tf_op jit(solution)/shard_map/ppermute | solution.py:94
  282.6 10.5 %collective-permute-start.13 = (bf16[4,1,212,64]{2,3,1,0:T(8,128)(2,1)S(1)}, bf16[4,1,212,64]{2,3,1,0:T(8,128)(2,1)S(1)}, u32[]{:S(2)}, u32[]{:S(2)}) collective-permute-start(bf16[4,1,212,64]{2,3,1,0:T(8,128)(2,1)S(1)} %maximum_select_fusion.2), channel_id=1, source_target_pairs={{0,4},{1,5},{2,6},{3,7},{4,0},{5,1},{6,2},{7,3},{8,12},{9,13},{10,... | collective-permute-start | bytes 325640 | tf_op jit(solution)/shard_map/ppermute | solution.py:132
  293.2 9.8 %collective-permute-start.14 = (bf16[8,1,212,64]{2,3,1,0:T(8,128)(2,1)S(1)}, bf16[8,1,212,64]{2,3,1,0:T(8,128)(2,1)S(1)}, u32[]{:S(2)}, u32[]{:S(2)}) collective-permute-start(bf16[8,1,212,64]{2,3,1,0:T(8,128)(2,1)S(1)} %maximum_select_fusion.1), channel_id=1, source_target_pairs={{0,8},{1,9},{2,10},{3,11},{4,12},{5,13},{6,14},{7,15},{8,0},{9,1},... | collective-permute-start | bytes 651272 | tf_op jit(solution)/shard_map/ppermute | solution.py:132
  296.1 43.2 %collective-permute-start.15 = (f32[74304]{0:T(1024)S(1)}, f32[74304]{0:T(1024)S(1)}, u32[]{:S(2)}, u32[]{:S(2)}) collective-permute-start(f32[74304]{0:T(1024)S(1)} %add.284), channel_id=1, source_target_pairs={{0,2},{1,3},{2,0},{3,1},{4,6},{5,7},{6,4},{7,5},{8,10},{9,11},{10,... | collective-permute-start | bytes 891656 | tf_op jit(solution)/shard_map/ppermute | solution.py:94
  339.3 0.7 copy-start
  340.2 0.7 slice-start
  (2 other events, 1.1 us)

commit v11 on v9

--- a/solution.py
+++ b/solution.py
@@ -18,6 +18,22 @@
     from_before = lax.ppermute(tail, axis, [(i, (i + 1) % count) for i in range(ends)])
     from_after = lax.ppermute(head, axis, [((i + 1) % count, i) for i in range(ends)])
     return from_before, from_after
+
+
+def doubling_gather(part, axis):
+    count = lax.axis_size(axis)
+    index = lax.axis_index(axis)
+    gathered = part[None]
+    step_size = 1
+    while step_size < count:
+        arrived = lax.ppermute(gathered, axis, [(i, i ^ step_size) for i in range(count)])
+        gathered = jnp.where(
+            (index // step_size) % 2 == 1,
+            jnp.concatenate([arrived, gathered], axis=0),
+            jnp.concatenate([gathered, arrived], axis=0),
+        )
+        step_size *= 2
+    return gathered
 
 
 def gelu_slope(values):
@@ -166,8 +182,10 @@
 
     def extend(values, carried=None):
         def gather(part, axis, tiled):
-            if carried is None or axis == "face":
+            if axis == "face":
                 return lax.all_gather(part, axis, axis=0, tiled=tiled)
+            if carried is None:
+                return doubling_gather(part, axis)
             return carried.doubling(part, axis)
 
         col_strip = jnp.where(col_index == 0, values[:, :, 0], values[:, :, tile_cols - 1])

time: 332 us -> 340 us (1.024)
  blocking collectives: 194 us -> 156 us
  starting transfers between devices: 52.5 us -> 75.7 us
  waiting for transfers between devices: 30.9 us -> 51 us
    all_gather x4 -> x2, blocking collectives: 96.5 us -> 60.1 us  [gather(): return lax.all_gather(part, axis, axis=0, tiled=tiled)]
    ppermute x0 -> x6, starting transfers between devices: none -> 21.2 us  [doubling_gather(): lax.ppermute(gathered, axis, [(i, i ^ step_size) for i in range(count)])]
    ppermute x0 -> x6, waiting for transfers between devices: none -> 20.4 us  [doubling_gather(): lax.ppermute(gathered, axis, [(i, i ^ step_size) for i in range(count)])]
  transfers between devices with their start and end apart: 16 -> 22, of which waited for: 7 -> 13; matrix products, arithmetic and copies ran while one was open for 8% -> 8% of each run, Pallas kernels for 0% -> 0%
where the time goes in v11:
time: 340 us; the launch traced here: 336 us
  blocking collectives  156 us (46%)
  starting transfers between devices  75.7 us (22%)
  waiting for transfers between devices  51 us (15%)
  local copies, waits for them, and re-layouts  27.2 us (8%)
  other arithmetic  14.3 us (4%)
  between operations  6.11 us (2%)
  matrix products  5.66 us (2%)
    all_gather x2, blocking collectives, gather(): return lax.all_gather(part, axis, axis=0, tiled=tiled)  60.1 us
    all_gather x3, blocking collectives, nested_sum(): lax.all_gather(part, axis, axis=0, tiled=False)  48.9 us
    all_gather x3, blocking collectives, gathered_sum(): values = jnp.sum(lax.all_gather(values, axis, axis=0, tiled=False), axis=0)  47 us
    ppermute x10, starting transfers between devices, step_send(): return [lax.ppermute(values, axis, pairs) for pairs in pair_sets]  33.8 us
    ppermute x6, starting transfers between devices, doubling_gather(): lax.ppermute(gathered, axis, [(i, i ^ step_size) for i in range(count)])  21.2 us
    ppermute x10, waiting for transfers between devices, step_send(): return [lax.ppermute(values, axis, pairs) for pairs in pair_sets]  20.9 us
    ppermute x6, starting transfers between devices, doubling(): lax.ppermute(gathered, axis, [(i, i ^ step_size) for i in range(count)])  20.7 us
    ppermute x6, waiting for transfers between devices, doubling_gather(): lax.ppermute(gathered, axis, [(i, i ^ step_size) for i in range(count)])  20.4 us
  transfers between devices with their start and end apart: 22, of which 13 were waited for; matrix products, arithmetic and copies ran while one was open for 8% of the time, Pallas kernels for 0%

profile of v11, /device:TPU:56, one launch (start us, length us, event | category | flops | bytes accessed | tf_op | source)
XLA Modules:
  0.0 335.9 jit_solution(11104605698091306612)
XLA Ops:
  1.6 4.0 %collective-permute-start = (bf16[1,1,48,64]{3,2,0,1:T(8,128)(2,1)S(1)}, bf16[1,1,48,64]{3,2,0,1:T(8,128)(2,1)S(1)}, u32[]{:S(2)}, u32[]{:S(2)}) collective-permute-start(bf16[1,1,48,64]{3,2,0,1:T(8,128)(2,1)S(1)} %maximum_bitcast_fusion), channel_id=1, source_target_pairs={{0,16},{16,0},{32,48},{48,32},{1,17},{17,1},{33,49},{49,33},{2,18}... | collective-permute-start | bytes 18440 | tf_op jit(solution)/shard_map/ppermute | solution.py:29
  8.1 4.7 %collective-permute-start.1 = (bf16[2,1,48,64]{3,2,0,1:T(8,128)(2,1)S(1)}, bf16[2,1,48,64]{3,2,0,1:T(8,128)(2,1)S(1)}, u32[]{:S(2)}, u32[]{:S(2)}) collective-permute-start(bf16[2,1,48,64]{3,2,0,1:T(8,128)(2,1)S(1)} %maximum_select_fusion.12), channel_id=1, source_target_pairs={{0,32},{16,48},{32,0},{48,16},{1,33},{17,49},{33,1},{49,17},{2,34}... | collective-permute-start | bytes 36872 | tf_op jit(solution)/shard_map/ppermute | solution.py:29
  12.9 4.9 %collective-permute-done.1 = bf16[2,1,48,64]{3,2,0,1:T(8,128)(2,1)S(1)} collective-permute-done((bf16[2,1,48,64]{3,2,0,1:T(8,128)(2,1)S(1)}, bf16[2,1,48,64]{3,2,0,1:T(8,128)(2,1)S(1)}, u32[]{:S(2)}, u32[]{:S(2)}) %collective-permute-start.1) | collective-permute-done | bytes 12320 | tf_op jit(solution)/shard_map/ppermute | solution.py:29
  22.9 5.6 %collective-permute-start.3 = (bf16[2,1,212,64]{2,3,1,0:T(8,128)(2,1)S(1)}, bf16[2,1,212,64]{2,3,1,0:T(8,128)(2,1)S(1)}, u32[]{:S(2)}, u32[]{:S(2)}) collective-permute-start(bf16[2,1,212,64]{2,3,1,0:T(8,128)(2,1)S(1)} %bitcast_select_fusion), channel_id=1, source_target_pairs={{0,2},{1,3},{2,0},{3,1},{4,6},{5,7},{6,4},{7,5},{8,10},{9,11},{10,... | collective-permute-start | bytes 162824 | tf_op jit(solution)/shard_map/ppermute | solution.py:29
  33.0 5.0 %collective-permute-done.4 = bf16[4,1,212,64]{2,3,0,1:T(8,128)(2,1)S(1)} collective-permute-done((bf16[4,1,212,64]{2,3,0,1:T(8,128)(2,1)S(1)}, bf16[4,1,212,64]{2,3,0,1:T(8,128)(2,1)S(1)}, u32[]{:S(2)}, u32[]{:S(2)}) %collective-permute-start.4) | collective-permute-done | bytes 108576 | tf_op jit(solution)/shard_map/ppermute | solution.py:29
  42.4 6.0 %collective-permute-done.5 = bf16[8,1,212,64]{2,3,0,1:T(8,128)(2,1)S(1)} collective-permute-done((bf16[8,1,212,64]{2,3,0,1:T(8,128)(2,1)S(1)}, bf16[8,1,212,64]{2,3,0,1:T(8,128)(2,1)S(1)}, u32[]{:S(2)}, u32[]{:S(2)}) %collective-permute-start.5) | collective-permute-done | bytes 217120 | tf_op jit(solution)/shard_map/ppermute | solution.py:29
  49.8 34.5 %all_gather.42 = bf16[12,4,128,64]{2,3,1,0:T(8,128)(2,1)S(1)} all-gather(bf16[1,4,128,64]{2,3,1,0:T(8,128)(2,1)S(1)} %pad_maximum_fusion.10), channel_id=1, replica_groups=mesh['face'=12,'row'=4,'col'=16] {'face'}, dimensions={0}, use_global_device_ids=true | all-gather | bytes 851968 | tf_op jit(solution)/shard_map/all_gather | solution.py:186
  89.8 17.3 %all-gather.6 = f32[16,2,64]{2,1,0:T(2,128)S(1)} all-gather(f32[1,2,64]{2,1,0:T(2,128)S(1)} %maximum_bitcast_fusion.2), channel_id=2, replica_groups=mesh['face'=12,'row'=4,'col'=16] {'col'}, dimensions={0}, use_global_device_ids=true | all-gather | bytes 8704 | tf_op jit(solution)/shard_map/all_gather | solution.py:77
  107.1 10.1 %all-gather.7 = f32[4,2,64]{2,1,0:T(2,128)S(1)} all-gather(f32[1,2,64]{2,1,0:T(2,128)S(1)} %bitcast.500), channel_id=3, replica_groups=mesh['face'=12,'row'=4,'col'=16] {'row'}, dimensions={0}, use_global_device_ids=true | all-gather | bytes 2560 | tf_op jit(solution)/shard_map/all_gather | solution.py:77
  117.2 19.6 %all-gather.8 = f32[12,2,64]{2,1,0:T(2,128)S(1)} all-gather(f32[1,2,64]{2,1,0:T(2,128)S(1)} %bitcast.505), channel_id=4, replica_groups=mesh['face'=12,'row'=4,'col'=16] {'face'}, dimensions={0}, use_global_device_ids=true | all-gather | bytes 6656 | tf_op jit(solution)/shard_map/all_gather | solution.py:77
  140.6 4.1 %collective-permute-start.6 = (f32[74304]{0:T(1024)S(1)}, f32[74304]{0:T(1024)S(1)}, u32[]{:S(2)}, u32[]{:S(2)}) collective-permute-start(f32[74304]{0:T(1024)S(1)} %pad_maximum_fusion), channel_id=1, source_target_pairs={{0,256},{64,320},{128,384},{192,448},{256,512},{320,576},{384,640}... | collective-permute-start | bytes 891656 | tf_op jit(solution)/shard_map/ppermute | solution.py:105
  144.6 5.7 %collective-permute-start.7 = (f32[74304]{0:T(1024)S(1)}, f32[74304]{0:T(1024)S(1)}, u32[]{:S(2)}, u32[]{:S(2)}) collective-permute-start(f32[74304]{0:T(1024)S(1)} %pad_maximum_fusion), channel_id=1, source_target_pairs={{0,512},{64,576},{128,640},{192,704},{256,0},{320,64},{384,128},{4... | collective-permute-start | bytes 891656 | tf_op jit(solution)/shard_map/ppermute | solution.py:105
  152.6 18.7 %all-gather.9 = f32[16,2,64]{2,1,0:T(2,128)S(1)} all-gather(f32[1,2,64]{2,1,0:T(2,128)S(1)} %bitcast.501), channel_id=5, replica_groups=mesh['face'=12,'row'=4,'col'=16] {'col'}, dimensions={0}, use_global_device_ids=true | all-gather | bytes 8704 | tf_op jit(solution)/shard_map/all_gather | solution.py:63
  176.0 9.4 %all-gather.10 = f32[4,2,64]{2,1,0:T(2,128)S(1)} all-gather(f32[1,2,64]{2,1,0:T(2,128)S(1)} %bitcast.499), channel_id=6, replica_groups=mesh['face'=12,'row'=4,'col'=16] {'row'}, dimensions={0}, use_global_device_ids=true | all-gather | bytes 2560 | tf_op jit(solution)/shard_map/all_gather | solution.py:63
  185.4 20.9 %all-gather.11 = f32[12,2,64]{2,1,0:T(2,128)S(1)} all-gather(f32[1,2,64]{2,1,0:T(2,128)S(1)} %bitcast.504), channel_id=7, replica_groups=mesh['face'=12,'row'=4,'col'=16] {'face'}, dimensions={0}, use_global_device_ids=true | all-gather | bytes 6656 | tf_op jit(solution)/shard_map/all_gather | solution.py:63
  207.6 4.2 %collective-permute-start.9 = (f32[74304]{0:T(1024)S(1)}, f32[74304]{0:T(1024)S(1)}, u32[]{:S(2)}, u32[]{:S(2)}) collective-permute-start(f32[74304]{0:T(1024)S(1)} %add.283), channel_id=1, source_target_pairs={{0,128},{64,192},{128,0},{192,64},{256,384},{320,448},{384,256},{4... | collective-permute-start | bytes 891656 | tf_op jit(solution)/shard_map/ppermute | solution.py:105
  211.9 8.4 %collective-permute-done.9 = f32[74304]{0:T(1024)S(1)} collective-permute-done((f32[74304]{0:T(1024)S(1)}, f32[74304]{0:T(1024)S(1)}, u32[]{:S(2)}, u32[]{:S(2)}) %collective-permute-start.9) | collective-permute-done | bytes 297248 | tf_op jit(solution)/shard_map/ppermute | solution.py:105
  220.4 5.0 %collective-permute-start.10 = (f32[74304]{0:T(1024)S(1)}, f32[74304]{0:T(1024)S(1)}, u32[]{:S(2)}, u32[]{:S(2)}) collective-permute-start(f32[74304]{0:T(1024)S(1)} %add.286), channel_id=1, source_target_pairs={{0,32},{16,48},{32,0},{48,16},{1,33},{17,49},{33,1},{49,17},{2,34}... | collective-permute-start | bytes 891656 | tf_op jit(solution)/shard_map/ppermute | solution.py:105
  241.2 4.3 %collective-permute-start.13 = (bf16[2,1,48,64]{3,2,0,1:T(8,128)(2,1)S(1)}, bf16[2,1,48,64]{3,2,0,1:T(8,128)(2,1)S(1)}, u32[]{:S(2)}, u32[]{:S(2)}) collective-permute-start(bf16[2,1,48,64]{3,2,0,1:T(8,128)(2,1)S(1)} %maximum_select_fusion.14), channel_id=1, source_target_pairs={{0,32},{16,48},{32,0},{48,16},{1,33},{17,49},{33,1},{49,17},{2,34}... | collective-permute-start | bytes 36872 | tf_op jit(solution)/shard_map/ppermute | solution.py:143
  253.8 7.7 %collective-permute-done.12 = f32[74304]{0:T(1024)S(1)} collective-permute-done((f32[74304]{0:T(1024)S(1)}, f32[74304]{0:T(1024)S(1)}, u32[]{:S(2)}, u32[]{:S(2)}) %collective-permute-start.12) | collective-permute-done | bytes 297248 | tf_op jit(solution)/shard_map/ppermute | solution.py:105
  267.4 4.3 %collective-permute-done.14 = f32[74304]{0:T(1024)S(1)} collective-permute-done((f32[74304]{0:T(1024)S(1)}, f32[74304]{0:T(1024)S(1)}, u32[]{:S(2)}, u32[]{:S(2)}) %collective-permute-start.14) | collective-permute-done | bytes 297248 | tf_op jit(solution)/shard_map/ppermute | solution.py:105
  282.6 4.2 %collective-permute-start.19 = (bf16[4,1,212,64]{2,3,0,1:T(8,128)(2,1)S(1)}, bf16[4,1,212,64]{2,3,0,1:T(8,128)(2,1)S(1)}, u32[]{:S(2)}, u32[]{:S(2)}) collective-permute-start(bf16[4,1,212,64]{2,3,0,1:T(8,128)(2,1)S(1)} %maximum_select_fusion.7), channel_id=1, source_target_pairs={{0,4},{1,5},{2,6},{3,7},{4,0},{5,1},{6,2},{7,3},{8,12},{9,13},{10,... | collective-permute-start | bytes 325640 | tf_op jit(solution)/shard_map/ppermute | solution.py:143
  289.8 4.4 %collective-permute-start.20 = (bf16[8,1,212,64]{2,3,0,1:T(8,128)(2,1)S(1)}, bf16[8,1,212,64]{2,3,0,1:T(8,128)(2,1)S(1)}, u32[]{:S(2)}, u32[]{:S(2)}) collective-permute-start(bf16[8,1,212,64]{2,3,0,1:T(8,128)(2,1)S(1)} %maximum_select_fusion.4), channel_id=1, source_target_pairs={{0,8},{1,9},{2,10},{3,11},{4,12},{5,13},{6,14},{7,15},{8,0},{9,1},... | collective-permute-start | bytes 651272 | tf_op jit(solution)/shard_map/ppermute | solution.py:143
  300.6 25.5 %all_gather.55 = bf16[12,4,128,64]{2,3,1,0:T(8,128)(2,1)S(1)} all-gather(bf16[1,4,128,64]{2,3,1,0:T(8,128)(2,1)S(1)} %pad_maximum_fusion.11), channel_id=1, replica_groups=mesh['face'=12,'row'=4,'col'=16] {'face'}, dimensions={0}, use_global_device_ids=true | all-gather | bytes 851968 | tf_op jit(solution)/shard_map/all_gather | solution.py:186
  (319 shorter events, 91.2 us)
Async XLA Ops:
  0.6 5.1 %copy-start.1 = (bf16[9,64,64]{2,1,0:T(8,128)(2,1)S(1)}, bf16[9,64,64]{2,1,0:T(8,128)(2,1)}, u32[]{:S(2)}) copy-start(bf16[9,64,64]{2,1,0:T(8,128)(2,1)} %param.39) | copy-start | bytes 221188
  1.6 6.5 %collective-permute-start = (bf16[1,1,48,64]{3,2,0,1:T(8,128)(2,1)S(1)}, bf16[1,1,48,64]{3,2,0,1:T(8,128)(2,1)S(1)}, u32[]{:S(2)}, u32[]{:S(2)}) collective-permute-start(bf16[1,1,48,64]{3,2,0,1:T(8,128)(2,1)S(1)} %maximum_bitcast_fusion), channel_id=1, source_target_pairs={{0,16},{16,0},{32,48},{48,32},{1,17},{17,1},{33,49},{49,33},{2,18}... | collective-permute-start | bytes 18440 | tf_op jit(solution)/shard_map/ppermute | solution.py:29
  8.1 9.7 %collective-permute-start.1 = (bf16[2,1,48,64]{3,2,0,1:T(8,128)(2,1)S(1)}, bf16[2,1,48,64]{3,2,0,1:T(8,128)(2,1)S(1)}, u32[]{:S(2)}, u32[]{:S(2)}) collective-permute-start(bf16[2,1,48,64]{3,2,0,1:T(8,128)(2,1)S(1)} %maximum_select_fusion.12), channel_id=1, source_target_pairs={{0,32},{16,48},{32,0},{48,16},{1,33},{17,49},{33,1},{49,17},{2,34}... | collective-permute-start | bytes 36872 | tf_op jit(solution)/shard_map/ppermute | solution.py:29
  18.5 0.9 copy-start.3
  19.7 3.1 collective-permute-start.2
  22.9 8.0 %collective-permute-start.3 = (bf16[2,1,212,64]{2,3,1,0:T(8,128)(2,1)S(1)}, bf16[2,1,212,64]{2,3,1,0:T(8,128)(2,1)S(1)}, u32[]{:S(2)}, u32[]{:S(2)}) collective-permute-start(bf16[2,1,212,64]{2,3,1,0:T(8,128)(2,1)S(1)} %bitcast_select_fusion), channel_id=1, source_target_pairs={{0,2},{1,3},{2,0},{3,1},{4,6},{5,7},{6,4},{7,5},{8,10},{9,11},{10,... | collective-permute-start | bytes 162824 | tf_op jit(solution)/shard_map/ppermute | solution.py:29
  31.0 6.9 %collective-permute-start.4 = (bf16[4,1,212,64]{2,3,0,1:T(8,128)(2,1)S(1)}, bf16[4,1,212,64]{2,3,0,1:T(8,128)(2,1)S(1)}, u32[]{:S(2)}, u32[]{:S(2)}) collective-permute-start(bf16[4,1,212,64]{2,3,0,1:T(8,128)(2,1)S(1)} %maximum_select_fusion.5), channel_id=1, source_target_pairs={{0,4},{1,5},{2,6},{3,7},{4,0},{5,1},{6,2},{7,3},{8,12},{9,13},{10,... | collective-permute-start | bytes 325640 | tf_op jit(solution)/shard_map/ppermute | solution.py:29
  38.0 10.4 %collective-permute-start.5 = (bf16[8,1,212,64]{2,3,0,1:T(8,128)(2,1)S(1)}, bf16[8,1,212,64]{2,3,0,1:T(8,128)(2,1)S(1)}, u32[]{:S(2)}, u32[]{:S(2)}) collective-permute-start(bf16[8,1,212,64]{2,3,0,1:T(8,128)(2,1)S(1)} %maximum_select_fusion.2), channel_id=1, source_target_pairs={{0,8},{1,9},{2,10},{3,11},{4,12},{5,13},{6,14},{7,15},{8,0},{9,1},... | collective-permute-start | bytes 651272 | tf_op jit(solution)/shard_map/ppermute | solution.py:29
  140.6 30.7 %collective-permute-start.6 = (f32[74304]{0:T(1024)S(1)}, f32[74304]{0:T(1024)S(1)}, u32[]{:S(2)}, u32[]{:S(2)}) collective-permute-start(f32[74304]{0:T(1024)S(1)} %pad_maximum_fusion), channel_id=1, source_target_pairs={{0,256},{64,320},{128,384},{192,448},{256,512},{320,576},{384,640}... | collective-permute-start | bytes 891656 | tf_op jit(solution)/shard_map/ppermute | solution.py:105
  144.6 26.6 %collective-permute-start.7 = (f32[74304]{0:T(1024)S(1)}, f32[74304]{0:T(1024)S(1)}, u32[]{:S(2)}, u32[]{:S(2)}) collective-permute-start(f32[74304]{0:T(1024)S(1)} %pad_maximum_fusion), channel_id=1, source_target_pairs={{0,512},{64,576},{128,640},{192,704},{256,0},{320,64},{384,128},{4... | collective-permute-start | bytes 891656 | tf_op jit(solution)/shard_map/ppermute | solution.py:105
  171.4 14.0 %collective-permute-start.8 = (f32[74304]{0:T(1024)S(1)}, f32[74304]{0:T(1024)S(1)}, u32[]{:S(2)}, u32[]{:S(2)}) collective-permute-start(f32[74304]{0:T(1024)S(1)} %select_add_fusion), channel_id=1, source_target_pairs={{0,64},{64,0},{128,192},{192,128},{256,320},{320,256},{384,448},{4... | collective-permute-start | bytes 891656 | tf_op jit(solution)/shard_map/ppermute | solution.py:105
  207.6 12.8 %collective-permute-start.9 = (f32[74304]{0:T(1024)S(1)}, f32[74304]{0:T(1024)S(1)}, u32[]{:S(2)}, u32[]{:S(2)}) collective-permute-start(f32[74304]{0:T(1024)S(1)} %add.283), channel_id=1, source_target_pairs={{0,128},{64,192},{128,0},{192,64},{256,384},{320,448},{384,256},{4... | collective-permute-start | bytes 891656 | tf_op jit(solution)/shard_map/ppermute | solution.py:105
  220.4 20.8 %collective-permute-start.10 = (f32[74304]{0:T(1024)S(1)}, f32[74304]{0:T(1024)S(1)}, u32[]{:S(2)}, u32[]{:S(2)}) collective-permute-start(f32[74304]{0:T(1024)S(1)} %add.286), channel_id=1, source_target_pairs={{0,32},{16,48},{32,0},{48,16},{1,33},{17,49},{33,1},{49,17},{2,34}... | collective-permute-start | bytes 891656 | tf_op jit(solution)/shard_map/ppermute | solution.py:105
  229.4 11.8 %collective-permute-start.11 = (bf16[1,1,48,64]{3,2,0,1:T(8,128)(2,1)S(1)}, bf16[1,1,48,64]{3,2,0,1:T(8,128)(2,1)S(1)}, u32[]{:S(2)}, u32[]{:S(2)}) collective-permute-start(bf16[1,1,48,64]{3,2,0,1:T(8,128)(2,1)S(1)} %maximum_bitcast_fusion.1), channel_id=1, source_target_pairs={{0,16},{16,0},{32,48},{48,32},{1,17},{17,1},{33,49},{49,33},{2,18}... | collective-permute-start | bytes 18440 | tf_op jit(solution)/shard_map/ppermute | solution.py:143
  241.2 10.7 %collective-permute-start.13 = (bf16[2,1,48,64]{3,2,0,1:T(8,128)(2,1)S(1)}, bf16[2,1,48,64]{3,2,0,1:T(8,128)(2,1)S(1)}, u32[]{:S(2)}, u32[]{:S(2)}) collective-permute-start(bf16[2,1,48,64]{3,2,0,1:T(8,128)(2,1)S(1)} %maximum_select_fusion.14), channel_id=1, source_target_pairs={{0,32},{16,48},{32,0},{48,16},{1,33},{17,49},{33,1},{49,17},{2,34}... | collective-permute-start | bytes 36872 | tf_op jit(solution)/shard_map/ppermute | solution.py:143
  248.8 12.8 %collective-permute-start.12 = (f32[74304]{0:T(1024)S(1)}, f32[74304]{0:T(1024)S(1)}, u32[]{:S(2)}, u32[]{:S(2)}) collective-permute-start(f32[74304]{0:T(1024)S(1)} %add.287), channel_id=1, source_target_pairs={{0,16},{16,0},{32,48},{48,32},{1,17},{17,1},{33,49},{49,33},{2,18}... | collective-permute-start | bytes 891656 | tf_op jit(solution)/shard_map/ppermute | solution.py:105
  261.5 10.2 %collective-permute-start.14 = (f32[74304]{0:T(1024)S(1)}, f32[74304]{0:T(1024)S(1)}, u32[]{:S(2)}, u32[]{:S(2)}) collective-permute-start(f32[74304]{0:T(1024)S(1)} %add.288), channel_id=1, source_target_pairs={{0,8},{1,9},{2,10},{3,11},{4,12},{5,13},{6,14},{7,15},{8,0},{9,1},... | collective-permute-start | bytes 891656 | tf_op jit(solution)/shard_map/ppermute | solution.py:105
  264.2 3.1 collective-permute-start.15
  271.8 8.7 %collective-permute-start.16 = (f32[74304]{0:T(1024)S(1)}, f32[74304]{0:T(1024)S(1)}, u32[]{:S(2)}, u32[]{:S(2)}) collective-permute-start(f32[74304]{0:T(1024)S(1)} %add.289), channel_id=1, source_target_pairs={{0,4},{1,5},{2,6},{3,7},{4,0},{5,1},{6,2},{7,3},{8,12},{9,13},{10,... | collective-permute-start | bytes 891656 | tf_op jit(solution)/shard_map/ppermute | solution.py:105
  273.7 6.2 %collective-permute-start.17 = (bf16[2,1,212,64]{2,3,0,1:T(8,128)(2,1)S(1)}, bf16[2,1,212,64]{2,3,0,1:T(8,128)(2,1)S(1)}, u32[]{:S(2)}, u32[]{:S(2)}) collective-permute-start(bf16[2,1,212,64]{2,3,0,1:T(8,128)(2,1)S(1)} %maximum_select_fusion.9), channel_id=1, source_target_pairs={{0,2},{1,3},{2,0},{3,1},{4,6},{5,7},{6,4},{7,5},{8,10},{9,11},{10,... | collective-permute-start | bytes 162824 | tf_op jit(solution)/shard_map/ppermute | solution.py:143
  280.5 9.3 %collective-permute-start.18 = (f32[74304]{0:T(1024)S(1)}, f32[74304]{0:T(1024)S(1)}, u32[]{:S(2)}, u32[]{:S(2)}) collective-permute-start(f32[74304]{0:T(1024)S(1)} %add.290), channel_id=1, source_target_pairs={{0,2},{1,3},{2,0},{3,1},{4,6},{5,7},{6,4},{7,5},{8,10},{9,11},{10,... | collective-permute-start | bytes 891656 | tf_op jit(solution)/shard_map/ppermute | solution.py:105
  282.6 7.0 %collective-permute-start.19 = (bf16[4,1,212,64]{2,3,0,1:T(8,128)(2,1)S(1)}, bf16[4,1,212,64]{2,3,0,1:T(8,128)(2,1)S(1)}, u32[]{:S(2)}, u32[]{:S(2)}) collective-permute-start(bf16[4,1,212,64]{2,3,0,1:T(8,128)(2,1)S(1)} %maximum_select_fusion.7), channel_id=1, source_target_pairs={{0,4},{1,5},{2,6},{3,7},{4,0},{5,1},{6,2},{7,3},{8,12},{9,13},{10,... | collective-permute-start | bytes 325640 | tf_op jit(solution)/shard_map/ppermute | solution.py:143
  289.8 9.8 %collective-permute-start.20 = (bf16[8,1,212,64]{2,3,0,1:T(8,128)(2,1)S(1)}, bf16[8,1,212,64]{2,3,0,1:T(8,128)(2,1)S(1)}, u32[]{:S(2)}, u32[]{:S(2)}) collective-permute-start(bf16[8,1,212,64]{2,3,0,1:T(8,128)(2,1)S(1)} %maximum_select_fusion.4), channel_id=1, source_target_pairs={{0,8},{1,9},{2,10},{3,11},{4,12},{5,13},{6,14},{7,15},{8,0},{9,1},... | collective-permute-start | bytes 651272 | tf_op jit(solution)/shard_map/ppermute | solution.py:143
  294.4 38.9 %collective-permute-start.21 = (f32[74304]{0:T(1024)S(1)}, f32[74304]{0:T(1024)S(1)}, u32[]{:S(2)}, u32[]{:S(2)}) collective-permute-start(f32[74304]{0:T(1024)S(1)} %add.291), channel_id=1, source_target_pairs={{0,1},{1,0},{2,3},{3,2},{4,5},{5,4},{6,7},{7,6},{8,9},{9,8},{10,11... | collective-permute-start | bytes 891656 | tf_op jit(solution)/shard_map/ppermute | solution.py:105
  (11 other events, 7.5 us)

commit v12 on v10

--- a/solution.py
+++ b/solution.py
@@ -64,6 +64,7 @@
 
 def sum_steps():
     faces = lax.axis_size("face")
+    rows = lax.axis_size("row")
     steps = [
         (
             "face",
@@ -72,18 +73,17 @@
                 [(i, (i + 8) % faces) for i in range(faces)],
             ],
         ),
+        ("row", [[(i, i ^ (rows // 2)) for i in range(rows)]]),
+        ("face", [[(i, i ^ 2) for i in range(faces)]]),
         ("face", [[(i, i ^ 1) for i in range(faces)]]),
     ]
-    count = lax.axis_size("col")
-    steps.append(("col", [[(i, i ^ 1) for i in range(count)]]))
-    steps.append(("face", [[(i, i ^ 2) for i in range(faces)]]))
-    rows = lax.axis_size("row")
-    step = rows // 2
+    step = rows // 4
     while step >= 1:
         steps.append(("row", [[(i, i ^ step) for i in range(rows)]]))
         step //= 2
+    count = lax.axis_size("col")
     step = count // 2
-    while step >= 2:
+    while step >= 1:
         steps.append(("col", [[(i, i ^ step) for i in range(count)]]))
         step //= 2
     return steps

time: 343 us -> 340 us (level)
  waiting for transfers between devices: 45.5 us -> 30 us
  blocking collectives: 196 us -> 201 us
  starting transfers between devices: 49.3 us -> 53.8 us
    ppermute x10, waiting for transfers between devices: 30.4 us -> 20.3 us  [step_send(): return [lax.ppermute(values, axis, pairs) for pairs in pair_sets]]
    all_gather x3, blocking collectives: 49 us -> 54.4 us  [nested_sum(): lax.all_gather(part, axis, axis=0, tiled=False)]
    ppermute x6, waiting for transfers between devices: 15.1 us -> 9.72 us  [doubling(): lax.ppermute(gathered, axis, [(i, i ^ step_size) for i in range(count)])]
where the time goes in v12:
time: 340 us; the launch traced here: 336 us
  blocking collectives  201 us (59%)
  starting transfers between devices  53.8 us (16%)
  waiting for transfers between devices  30 us (9%)
  local copies, waits for them, and re-layouts  26 us (8%)
  other arithmetic  13.6 us (4%)
  between operations  5.9 us (2%)
  matrix products  5.66 us (2%)
    all_gather x4, blocking collectives, gather(): return lax.all_gather(part, axis, axis=0, tiled=tiled)  97.9 us
    all_gather x3, blocking collectives, nested_sum(): lax.all_gather(part, axis, axis=0, tiled=False)  54.4 us
    all_gather x3, blocking collectives, gathered_sum(): values = jnp.sum(lax.all_gather(values, axis, axis=0, tiled=False), axis=0)  48.7 us
    ppermute x10, starting transfers between devices, step_send(): return [lax.ppermute(values, axis, pairs) for pairs in pair_sets]  31.1 us
    ppermute x6, starting transfers between devices, doubling(): lax.ppermute(gathered, axis, [(i, i ^ step_size) for i in range(count)])  22.7 us
    ppermute x10, waiting for transfers between devices, step_send(): return [lax.ppermute(values, axis, pairs) for pairs in pair_sets]  20.3 us
    ppermute x6, waiting for transfers between devices, doubling(): lax.ppermute(gathered, axis, [(i, i ^ step_size) for i in range(count)])  9.72 us
  transfers between devices with their start and end apart: 16, of which 7 were waited for; matrix products, arithmetic and copies ran while one was open for 8% of the time, Pallas kernels for 0%

profile of v12, /device:TPU:56, one launch (start us, length us, event | category | flops | bytes accessed | tf_op | source)
XLA Modules:
  0.0 335.9 jit_solution(11884833832093902196)
XLA Ops:
  1.6 13.7 %all-gather = bf16[4,48,64]{2,1,0:T(8,128)(2,1)S(1)} all-gather(bf16[1,48,64]{2,1,0:T(8,128)(2,1)S(1)} %pad_maximum_fusion.20), channel_id=2, replica_groups=mesh['face'=12,'row'=4,'col'=16] {'row'}, dimensions={0}, use_global_device_ids=true | all-gather | bytes 30720 | tf_op jit(solution)/shard_map/all_gather | solution.py:175
  16.0 23.8 %all-gather.1 = bf16[16,212,64]{1,2,0:T(8,128)(2,1)S(1)} all-gather(bf16[1,212,64]{1,2,0:T(8,128)(2,1)S(1)} %concatenate.268), channel_id=3, replica_groups=mesh['face'=12,'row'=4,'col'=16] {'col'}, dimensions={0}, use_global_device_ids=true | all-gather | bytes 461312 | tf_op jit(solution)/shard_map/all_gather | solution.py:175
  41.8 32.7 %all_gather.58 = bf16[12,4,128,64]{2,3,1,0:T(8,128)(2,1)S(1)} all-gather(bf16[1,4,128,64]{2,3,1,0:T(8,128)(2,1)S(1)} %pad_maximum_fusion.10), channel_id=1, replica_groups=mesh['face'=12,'row'=4,'col'=16] {'face'}, dimensions={0}, use_global_device_ids=true | all-gather | bytes 851968 | tf_op jit(solution)/shard_map/all_gather | solution.py:175
  81.6 19.1 %all-gather.8 = f32[16,2,64]{2,1,0:T(2,128)S(1)} all-gather(f32[1,2,64]{2,1,0:T(2,128)S(1)} %maximum_bitcast_fusion.1), channel_id=4, replica_groups=mesh['face'=12,'row'=4,'col'=16] {'col'}, dimensions={0}, use_global_device_ids=true | all-gather | bytes 8704 | tf_op jit(solution)/shard_map/all_gather | solution.py:61
  100.7 10.0 %all-gather.9 = f32[4,2,64]{2,1,0:T(2,128)S(1)} all-gather(f32[1,2,64]{2,1,0:T(2,128)S(1)} %bitcast.463), channel_id=5, replica_groups=mesh['face'=12,'row'=4,'col'=16] {'row'}, dimensions={0}, use_global_device_ids=true | all-gather | bytes 2560 | tf_op jit(solution)/shard_map/all_gather | solution.py:61
  110.7 19.6 %all-gather.10 = f32[12,2,64]{2,1,0:T(2,128)S(1)} all-gather(f32[1,2,64]{2,1,0:T(2,128)S(1)} %bitcast.468), channel_id=6, replica_groups=mesh['face'=12,'row'=4,'col'=16] {'face'}, dimensions={0}, use_global_device_ids=true | all-gather | bytes 6656 | tf_op jit(solution)/shard_map/all_gather | solution.py:61
  134.4 3.4 collective-permute-start
  137.7 6.4 %collective-permute-start.1 = (f32[74304]{0:T(1024)S(1)}, f32[74304]{0:T(1024)S(1)}, u32[]{:S(2)}, u32[]{:S(2)}) collective-permute-start(f32[74304]{0:T(1024)S(1)} %pad_maximum_fusion), channel_id=1, source_target_pairs={{0,512},{64,576},{128,640},{192,704},{256,0},{320,64},{384,128},{4... | collective-permute-start | bytes 891656 | tf_op jit(solution)/shard_map/ppermute | solution.py:94
  144.2 16.0 %all-gather.11 = f32[16,2,64]{2,1,0:T(2,128)S(1)} all-gather(f32[1,2,64]{2,1,0:T(2,128)S(1)} %bitcast.464), channel_id=7, replica_groups=mesh['face'=12,'row'=4,'col'=16] {'col'}, dimensions={0}, use_global_device_ids=true | all-gather | bytes 8704 | tf_op jit(solution)/shard_map/all_gather | solution.py:47
  162.3 4.3 %collective-permute-start.2 = (f32[74304]{0:T(1024)S(1)}, f32[74304]{0:T(1024)S(1)}, u32[]{:S(2)}, u32[]{:S(2)}) collective-permute-start(f32[74304]{0:T(1024)S(1)} %select_add_fusion), channel_id=1, source_target_pairs={{0,32},{16,48},{32,0},{48,16},{1,33},{17,49},{33,1},{49,17},{2,34}... | collective-permute-start | bytes 891656 | tf_op jit(solution)/shard_map/ppermute | solution.py:94
  167.3 16.8 %all-gather.12 = f32[4,2,64]{2,1,0:T(2,128)S(1)} all-gather(f32[1,2,64]{2,1,0:T(2,128)S(1)} %bitcast.462), channel_id=8, replica_groups=mesh['face'=12,'row'=4,'col'=16] {'row'}, dimensions={0}, use_global_device_ids=true | all-gather | bytes 2560 | tf_op jit(solution)/shard_map/all_gather | solution.py:47
  184.1 21.6 %all-gather.13 = f32[12,2,64]{2,1,0:T(2,128)S(1)} all-gather(f32[1,2,64]{2,1,0:T(2,128)S(1)} %bitcast.467), channel_id=9, replica_groups=mesh['face'=12,'row'=4,'col'=16] {'face'}, dimensions={0}, use_global_device_ids=true | all-gather | bytes 6656 | tf_op jit(solution)/shard_map/all_gather | solution.py:47
  207.0 5.4 %collective-permute-start.3 = (f32[74304]{0:T(1024)S(1)}, f32[74304]{0:T(1024)S(1)}, u32[]{:S(2)}, u32[]{:S(2)}) collective-permute-start(f32[74304]{0:T(1024)S(1)} %add.271), channel_id=1, source_target_pairs={{0,128},{64,192},{128,0},{192,64},{256,384},{320,448},{384,256},{4... | collective-permute-start | bytes 891656 | tf_op jit(solution)/shard_map/ppermute | solution.py:94
  212.5 7.3 %collective-permute-done.3 = f32[74304]{0:T(1024)S(1)} collective-permute-done((f32[74304]{0:T(1024)S(1)}, f32[74304]{0:T(1024)S(1)}, u32[]{:S(2)}, u32[]{:S(2)}) %collective-permute-start.3) | collective-permute-done | bytes 297248 | tf_op jit(solution)/shard_map/ppermute | solution.py:94
  225.7 5.8 %collective-permute-start.5 = (bf16[1,1,48,64]{3,2,1,0:T(8,128)(2,1)S(1)}, bf16[1,1,48,64]{3,2,1,0:T(8,128)(2,1)S(1)}, u32[]{:S(2)}, u32[]{:S(2)}) collective-permute-start(bf16[1,1,48,64]{3,2,1,0:T(8,128)(2,1)S(1)} %maximum_bitcast_fusion), channel_id=1, source_target_pairs={{0,16},{16,0},{32,48},{48,32},{1,17},{17,1},{33,49},{49,33},{2,18}... | collective-permute-start | bytes 18440 | tf_op jit(solution)/shard_map/ppermute | solution.py:132
  239.4 4.6 %collective-permute-start.7 = (bf16[2,1,48,64]{3,2,1,0:T(8,128)(2,1)S(1)}, bf16[2,1,48,64]{3,2,1,0:T(8,128)(2,1)S(1)}, u32[]{:S(2)}, u32[]{:S(2)}) collective-permute-start(bf16[2,1,48,64]{3,2,1,0:T(8,128)(2,1)S(1)} %maximum_select_fusion.5), channel_id=1, source_target_pairs={{0,32},{16,48},{32,0},{48,16},{1,33},{17,49},{33,1},{49,17},{2,34}... | collective-permute-start | bytes 36872 | tf_op jit(solution)/shard_map/ppermute | solution.py:132
  251.2 8.2 %collective-permute-done.6 = f32[74304]{0:T(1024)S(1)} collective-permute-done((f32[74304]{0:T(1024)S(1)}, f32[74304]{0:T(1024)S(1)}, u32[]{:S(2)}, u32[]{:S(2)}) %collective-permute-start.6) | collective-permute-done | bytes 297248 | tf_op jit(solution)/shard_map/ppermute | solution.py:94
  265.3 4.3 %collective-permute-done.8 = f32[74304]{0:T(1024)S(1)} collective-permute-done((f32[74304]{0:T(1024)S(1)}, f32[74304]{0:T(1024)S(1)}, u32[]{:S(2)}, u32[]{:S(2)}) %collective-permute-start.8) | collective-permute-done | bytes 297248 | tf_op jit(solution)/shard_map/ppermute | solution.py:94
  273.8 4.0 %collective-permute-done.11 = bf16[2,1,212,64]{2,3,1,0:T(8,128)(2,1)S(1)} collective-permute-done((bf16[2,1,212,64]{2,3,1,0:T(8,128)(2,1)S(1)}, bf16[2,1,212,64]{2,3,1,0:T(8,128)(2,1)S(1)}, u32[]{:S(2)}, u32[]{:S(2)}) %collective-permute-start.11) | collective-permute-done | bytes 54304 | tf_op jit(solution)/shard_map/ppermute | solution.py:132
  280.5 4.1 %collective-permute-start.13 = (bf16[4,1,212,64]{2,3,1,0:T(8,128)(2,1)S(1)}, bf16[4,1,212,64]{2,3,1,0:T(8,128)(2,1)S(1)}, u32[]{:S(2)}, u32[]{:S(2)}) collective-permute-start(bf16[4,1,212,64]{2,3,1,0:T(8,128)(2,1)S(1)} %maximum_select_fusion.2), channel_id=1, source_target_pairs={{0,4},{1,5},{2,6},{3,7},{4,0},{5,1},{6,2},{7,3},{8,12},{9,13},{10,... | collective-permute-start | bytes 325640 | tf_op jit(solution)/shard_map/ppermute | solution.py:132
  284.8 2.7 collective-permute-done.13
  287.7 4.3 %collective-permute-start.14 = (bf16[8,1,212,64]{2,3,1,0:T(8,128)(2,1)S(1)}, bf16[8,1,212,64]{2,3,1,0:T(8,128)(2,1)S(1)}, u32[]{:S(2)}, u32[]{:S(2)}) collective-permute-start(bf16[8,1,212,64]{2,3,1,0:T(8,128)(2,1)S(1)} %maximum_select_fusion.1), channel_id=1, source_target_pairs={{0,8},{1,9},{2,10},{3,11},{4,12},{5,13},{6,14},{7,15},{8,0},{9,1},... | collective-permute-start | bytes 651272 | tf_op jit(solution)/shard_map/ppermute | solution.py:132
  294.4 3.1 collective-permute-done.14
  298.5 27.7 %all_gather.71 = bf16[12,4,128,64]{2,3,1,0:T(8,128)(2,1)S(1)} all-gather(bf16[1,4,128,64]{2,3,1,0:T(8,128)(2,1)S(1)} %pad_maximum_fusion.11), channel_id=1, replica_groups=mesh['face'=12,'row'=4,'col'=16] {'face'}, dimensions={0}, use_global_device_ids=true | all-gather | bytes 851968 | tf_op jit(solution)/shard_map/all_gather | solution.py:175
  (292 shorter events, 61.3 us)
Async XLA Ops:
  39.9 0.9 copy-start.1
  75.3 0.7 copy-start.4
  130.9 0.7 copy-start.5
  131.0 0.8 copy-start.3
  131.9 0.7 copy-start.7
  134.4 27.9 %collective-permute-start = (f32[74304]{0:T(1024)S(1)}, f32[74304]{0:T(1024)S(1)}, u32[]{:S(2)}, u32[]{:S(2)}) collective-permute-start(f32[74304]{0:T(1024)S(1)} %pad_maximum_fusion), channel_id=1, source_target_pairs={{0,256},{64,320},{128,384},{192,448},{256,512},{320,576},{384,640}... | collective-permute-start | bytes 891656 | tf_op jit(solution)/shard_map/ppermute | solution.py:94
  137.7 24.5 %collective-permute-start.1 = (f32[74304]{0:T(1024)S(1)}, f32[74304]{0:T(1024)S(1)}, u32[]{:S(2)}, u32[]{:S(2)}) collective-permute-start(f32[74304]{0:T(1024)S(1)} %pad_maximum_fusion), channel_id=1, source_target_pairs={{0,512},{64,576},{128,640},{192,704},{256,0},{320,64},{384,128},{4... | collective-permute-start | bytes 891656 | tf_op jit(solution)/shard_map/ppermute | solution.py:94
  162.3 21.7 %collective-permute-start.2 = (f32[74304]{0:T(1024)S(1)}, f32[74304]{0:T(1024)S(1)}, u32[]{:S(2)}, u32[]{:S(2)}) collective-permute-start(f32[74304]{0:T(1024)S(1)} %select_add_fusion), channel_id=1, source_target_pairs={{0,32},{16,48},{32,0},{48,16},{1,33},{17,49},{33,1},{49,17},{2,34}... | collective-permute-start | bytes 891656 | tf_op jit(solution)/shard_map/ppermute | solution.py:94
  207.0 12.8 %collective-permute-start.3 = (f32[74304]{0:T(1024)S(1)}, f32[74304]{0:T(1024)S(1)}, u32[]{:S(2)}, u32[]{:S(2)}) collective-permute-start(f32[74304]{0:T(1024)S(1)} %add.271), channel_id=1, source_target_pairs={{0,128},{64,192},{128,0},{192,64},{256,384},{320,448},{384,256},{4... | collective-permute-start | bytes 891656 | tf_op jit(solution)/shard_map/ppermute | solution.py:94
  219.9 19.5 %collective-permute-start.4 = (f32[74304]{0:T(1024)S(1)}, f32[74304]{0:T(1024)S(1)}, u32[]{:S(2)}, u32[]{:S(2)}) collective-permute-start(f32[74304]{0:T(1024)S(1)} %add.275), channel_id=1, source_target_pairs={{0,64},{64,0},{128,192},{192,128},{256,320},{320,256},{384,448},{4... | collective-permute-start | bytes 891656 | tf_op jit(solution)/shard_map/ppermute | solution.py:94
  225.7 13.6 %collective-permute-start.5 = (bf16[1,1,48,64]{3,2,1,0:T(8,128)(2,1)S(1)}, bf16[1,1,48,64]{3,2,1,0:T(8,128)(2,1)S(1)}, u32[]{:S(2)}, u32[]{:S(2)}) collective-permute-start(bf16[1,1,48,64]{3,2,1,0:T(8,128)(2,1)S(1)} %maximum_bitcast_fusion), channel_id=1, source_target_pairs={{0,16},{16,0},{32,48},{48,32},{1,17},{17,1},{33,49},{49,33},{2,18}... | collective-permute-start | bytes 18440 | tf_op jit(solution)/shard_map/ppermute | solution.py:132
  239.4 9.9 %collective-permute-start.7 = (bf16[2,1,48,64]{3,2,1,0:T(8,128)(2,1)S(1)}, bf16[2,1,48,64]{3,2,1,0:T(8,128)(2,1)S(1)}, u32[]{:S(2)}, u32[]{:S(2)}) collective-permute-start(bf16[2,1,48,64]{3,2,1,0:T(8,128)(2,1)S(1)} %maximum_select_fusion.5), channel_id=1, source_target_pairs={{0,32},{16,48},{32,0},{48,16},{1,33},{17,49},{33,1},{49,17},{2,34}... | collective-permute-start | bytes 36872 | tf_op jit(solution)/shard_map/ppermute | solution.py:132
  247.4 12.0 %collective-permute-start.6 = (f32[74304]{0:T(1024)S(1)}, f32[74304]{0:T(1024)S(1)}, u32[]{:S(2)}, u32[]{:S(2)}) collective-permute-start(f32[74304]{0:T(1024)S(1)} %add.276), channel_id=1, source_target_pairs={{0,16},{16,0},{32,48},{48,32},{1,17},{17,1},{33,49},{49,33},{2,18}... | collective-permute-start | bytes 891656 | tf_op jit(solution)/shard_map/ppermute | solution.py:94
  250.0 0.8 slice-start.1
  259.4 10.2 %collective-permute-start.8 = (f32[74304]{0:T(1024)S(1)}, f32[74304]{0:T(1024)S(1)}, u32[]{:S(2)}, u32[]{:S(2)}) collective-permute-start(f32[74304]{0:T(1024)S(1)} %add.278), channel_id=1, source_target_pairs={{0,8},{1,9},{2,10},{3,11},{4,12},{5,13},{6,14},{7,15},{8,0},{9,1},... | collective-permute-start | bytes 891656 | tf_op jit(solution)/shard_map/ppermute | solution.py:94
  262.1 3.1 collective-permute-start.9
  269.6 8.7 %collective-permute-start.10 = (f32[74304]{0:T(1024)S(1)}, f32[74304]{0:T(1024)S(1)}, u32[]{:S(2)}, u32[]{:S(2)}) collective-permute-start(f32[74304]{0:T(1024)S(1)} %add.280), channel_id=1, source_target_pairs={{0,4},{1,5},{2,6},{3,7},{4,0},{5,1},{6,2},{7,3},{8,12},{9,13},{10,... | collective-permute-start | bytes 891656 | tf_op jit(solution)/shard_map/ppermute | solution.py:94
  271.6 6.2 %collective-permute-start.11 = (bf16[2,1,212,64]{2,3,1,0:T(8,128)(2,1)S(1)}, bf16[2,1,212,64]{2,3,1,0:T(8,128)(2,1)S(1)}, u32[]{:S(2)}, u32[]{:S(2)}) collective-permute-start(bf16[2,1,212,64]{2,3,1,0:T(8,128)(2,1)S(1)} %maximum_select_fusion.3), channel_id=1, source_target_pairs={{0,2},{1,3},{2,0},{3,1},{4,6},{5,7},{6,4},{7,5},{8,10},{9,11},{10,... | collective-permute-start | bytes 162824 | tf_op jit(solution)/shard_map/ppermute | solution.py:132
  278.3 9.3 %collective-permute-start.12 = (f32[74304]{0:T(1024)S(1)}, f32[74304]{0:T(1024)S(1)}, u32[]{:S(2)}, u32[]{:S(2)}) collective-permute-start(f32[74304]{0:T(1024)S(1)} %add.282), channel_id=1, source_target_pairs={{0,2},{1,3},{2,0},{3,1},{4,6},{5,7},{6,4},{7,5},{8,10},{9,11},{10,... | collective-permute-start | bytes 891656 | tf_op jit(solution)/shard_map/ppermute | solution.py:94
  280.5 7.0 %collective-permute-start.13 = (bf16[4,1,212,64]{2,3,1,0:T(8,128)(2,1)S(1)}, bf16[4,1,212,64]{2,3,1,0:T(8,128)(2,1)S(1)}, u32[]{:S(2)}, u32[]{:S(2)}) collective-permute-start(bf16[4,1,212,64]{2,3,1,0:T(8,128)(2,1)S(1)} %maximum_select_fusion.2), channel_id=1, source_target_pairs={{0,4},{1,5},{2,6},{3,7},{4,0},{5,1},{6,2},{7,3},{8,12},{9,13},{10,... | collective-permute-start | bytes 325640 | tf_op jit(solution)/shard_map/ppermute | solution.py:132
  287.7 9.8 %collective-permute-start.14 = (bf16[8,1,212,64]{2,3,1,0:T(8,128)(2,1)S(1)}, bf16[8,1,212,64]{2,3,1,0:T(8,128)(2,1)S(1)}, u32[]{:S(2)}, u32[]{:S(2)}) collective-permute-start(bf16[8,1,212,64]{2,3,1,0:T(8,128)(2,1)S(1)} %maximum_select_fusion.1), channel_id=1, source_target_pairs={{0,8},{1,9},{2,10},{3,11},{4,12},{5,13},{6,14},{7,15},{8,0},{9,1},... | collective-permute-start | bytes 651272 | tf_op jit(solution)/shard_map/ppermute | solution.py:132
  292.3 41.2 %collective-permute-start.15 = (f32[74304]{0:T(1024)S(1)}, f32[74304]{0:T(1024)S(1)}, u32[]{:S(2)}, u32[]{:S(2)}) collective-permute-start(f32[74304]{0:T(1024)S(1)} %add.284), channel_id=1, source_target_pairs={{0,1},{1,0},{2,3},{3,2},{4,5},{5,4},{6,7},{7,6},{8,9},{9,8},{10,11... | collective-permute-start | bytes 891656 | tf_op jit(solution)/shard_map/ppermute | solution.py:94
  333.5 0.7 copy-start
  334.3 0.7 slice-start
  (2 other events, 1.1 us)

commit v13 on v9

--- a/solution.py
+++ b/solution.py
@@ -38,7 +38,7 @@
 
 
 def nested_sum(values, carried=None):
-    for axis in ("col", "row", "face"):
+    for axis in ("col", "face", "row"):
         if carried is None:
             values = lax.psum(values, axis)
         else:

time: 332 us -> 333 us (level)
  no operation moved by 1% of the time
where the time goes in v13:
time: 333 us; the launch traced here: 329 us
  blocking collectives  194 us (58%)
  starting transfers between devices  52.3 us (16%)
  waiting for transfers between devices  31.6 us (9%)
  local copies, waits for them, and re-layouts  26 us (8%)
  other arithmetic  13.6 us (4%)
  between operations  5.9 us (2%)
  matrix products  5.66 us (2%)
    all_gather x4, blocking collectives, gather(): return lax.all_gather(part, axis, axis=0, tiled=tiled)  96.3 us
    all_gather x3, blocking collectives, nested_sum(): lax.all_gather(part, axis, axis=0, tiled=False)  49 us
    all_gather x3, blocking collectives, gathered_sum(): values = jnp.sum(lax.all_gather(values, axis, axis=0, tiled=False), axis=0)  48.7 us
    ppermute x10, starting transfers between devices, step_send(): return [lax.ppermute(values, axis, pairs) for pairs in pair_sets]  31.8 us
    ppermute x10, waiting for transfers between devices, step_send(): return [lax.ppermute(values, axis, pairs) for pairs in pair_sets]  22 us
    ppermute x6, starting transfers between devices, doubling(): lax.ppermute(gathered, axis, [(i, i ^ step_size) for i in range(count)])  20.5 us
    ppermute x6, waiting for transfers between devices, doubling(): lax.ppermute(gathered, axis, [(i, i ^ step_size) for i in range(count)])  9.62 us
  transfers between devices with their start and end apart: 16, of which 7 were waited for; matrix products, arithmetic and copies ran while one was open for 8% of the time, Pallas kernels for 0%

profile of v13, /device:TPU:56, one launch (start us, length us, event | category | flops | bytes accessed | tf_op | source)
XLA Modules:
  0.0 329.0 jit_solution(17876954629225383705)
XLA Ops:
  1.6 13.7 %all-gather = bf16[4,48,64]{2,1,0:T(8,128)(2,1)S(1)} all-gather(bf16[1,48,64]{2,1,0:T(8,128)(2,1)S(1)} %pad_maximum_fusion.20), channel_id=2, replica_groups=mesh['face'=12,'row'=4,'col'=16] {'row'}, dimensions={0}, use_global_device_ids=true | all-gather | bytes 30720 | tf_op jit(solution)/shard_map/all_gather | solution.py:170
  16.0 23.8 %all-gather.1 = bf16[16,212,64]{1,2,0:T(8,128)(2,1)S(1)} all-gather(bf16[1,212,64]{1,2,0:T(8,128)(2,1)S(1)} %concatenate.268), channel_id=3, replica_groups=mesh['face'=12,'row'=4,'col'=16] {'col'}, dimensions={0}, use_global_device_ids=true | all-gather | bytes 461312 | tf_op jit(solution)/shard_map/all_gather | solution.py:170
  41.8 32.7 %all_gather.58 = bf16[12,4,128,64]{2,3,1,0:T(8,128)(2,1)S(1)} all-gather(bf16[1,4,128,64]{2,3,1,0:T(8,128)(2,1)S(1)} %pad_maximum_fusion.10), channel_id=1, replica_groups=mesh['face'=12,'row'=4,'col'=16] {'face'}, dimensions={0}, use_global_device_ids=true | all-gather | bytes 851968 | tf_op jit(solution)/shard_map/all_gather | solution.py:170
  81.6 19.1 %all-gather.8 = f32[16,2,64]{2,1,0:T(2,128)S(1)} all-gather(f32[1,2,64]{2,1,0:T(2,128)S(1)} %maximum_bitcast_fusion.1), channel_id=4, replica_groups=mesh['face'=12,'row'=4,'col'=16] {'col'}, dimensions={0}, use_global_device_ids=true | all-gather | bytes 8704 | tf_op jit(solution)/shard_map/all_gather | solution.py:61
  100.7 10.0 %all-gather.9 = f32[4,2,64]{2,1,0:T(2,128)S(1)} all-gather(f32[1,2,64]{2,1,0:T(2,128)S(1)} %bitcast.463), channel_id=5, replica_groups=mesh['face'=12,'row'=4,'col'=16] {'row'}, dimensions={0}, use_global_device_ids=true | all-gather | bytes 2560 | tf_op jit(solution)/shard_map/all_gather | solution.py:61
  110.7 19.6 %all-gather.10 = f32[12,2,64]{2,1,0:T(2,128)S(1)} all-gather(f32[1,2,64]{2,1,0:T(2,128)S(1)} %bitcast.468), channel_id=6, replica_groups=mesh['face'=12,'row'=4,'col'=16] {'face'}, dimensions={0}, use_global_device_ids=true | all-gather | bytes 6656 | tf_op jit(solution)/shard_map/all_gather | solution.py:61
  134.4 3.4 %collective-permute-start = (f32[74304]{0:T(1024)S(1)}, f32[74304]{0:T(1024)S(1)}, u32[]{:S(2)}, u32[]{:S(2)}) collective-permute-start(f32[74304]{0:T(1024)S(1)} %pad_maximum_fusion), channel_id=1, source_target_pairs={{0,256},{64,320},{128,384},{192,448},{256,512},{320,576},{384,640}... | collective-permute-start | bytes 891656 | tf_op jit(solution)/shard_map/ppermute | solution.py:89
  137.7 6.4 %collective-permute-start.1 = (f32[74304]{0:T(1024)S(1)}, f32[74304]{0:T(1024)S(1)}, u32[]{:S(2)}, u32[]{:S(2)}) collective-permute-start(f32[74304]{0:T(1024)S(1)} %pad_maximum_fusion), channel_id=1, source_target_pairs={{0,512},{64,576},{128,640},{192,704},{256,0},{320,64},{384,128},{4... | collective-permute-start | bytes 891656 | tf_op jit(solution)/shard_map/ppermute | solution.py:89
  144.2 16.0 %all-gather.11 = f32[16,2,64]{2,1,0:T(2,128)S(1)} all-gather(f32[1,2,64]{2,1,0:T(2,128)S(1)} %bitcast.464), channel_id=7, replica_groups=mesh['face'=12,'row'=4,'col'=16] {'col'}, dimensions={0}, use_global_device_ids=true | all-gather | bytes 8704 | tf_op jit(solution)/shard_map/all_gather | solution.py:47
  162.3 3.9 %collective-permute-start.2 = (f32[74304]{0:T(1024)S(1)}, f32[74304]{0:T(1024)S(1)}, u32[]{:S(2)}, u32[]{:S(2)}) collective-permute-start(f32[74304]{0:T(1024)S(1)} %select_add_fusion), channel_id=1, source_target_pairs={{0,64},{64,0},{128,192},{192,128},{256,320},{320,256},{384,448},{4... | collective-permute-start | bytes 891656 | tf_op jit(solution)/shard_map/ppermute | solution.py:89
  166.9 23.9 %all-gather.12 = f32[12,2,64]{2,1,0:T(2,128)S(1)} all-gather(f32[1,2,64]{2,1,0:T(2,128)S(1)} %bitcast.467), channel_id=8, replica_groups=mesh['face'=12,'row'=4,'col'=16] {'face'}, dimensions={0}, use_global_device_ids=true | all-gather | bytes 6656 | tf_op jit(solution)/shard_map/all_gather | solution.py:47
  190.9 9.1 %all-gather.13 = f32[4,2,64]{2,1,0:T(2,128)S(1)} all-gather(f32[1,2,64]{2,1,0:T(2,128)S(1)} %bitcast.462), channel_id=9, replica_groups=mesh['face'=12,'row'=4,'col'=16] {'row'}, dimensions={0}, use_global_device_ids=true | all-gather | bytes 2560 | tf_op jit(solution)/shard_map/all_gather | solution.py:47
  203.5 9.5 %collective-permute-done.3 = f32[74304]{0:T(1024)S(1)} collective-permute-done((f32[74304]{0:T(1024)S(1)}, f32[74304]{0:T(1024)S(1)}, u32[]{:S(2)}, u32[]{:S(2)}) %collective-permute-start.3) | collective-permute-done | bytes 297248 | tf_op jit(solution)/shard_map/ppermute | solution.py:89
  213.0 5.0 %collective-permute-start.4 = (f32[74304]{0:T(1024)S(1)}, f32[74304]{0:T(1024)S(1)}, u32[]{:S(2)}, u32[]{:S(2)}) collective-permute-start(f32[74304]{0:T(1024)S(1)} %add.275), channel_id=1, source_target_pairs={{0,32},{16,48},{32,0},{48,16},{1,33},{17,49},{33,1},{49,17},{2,34}... | collective-permute-start | bytes 891656 | tf_op jit(solution)/shard_map/ppermute | solution.py:89
  222.0 4.1 %collective-permute-start.5 = (bf16[1,1,48,64]{3,2,1,0:T(8,128)(2,1)S(1)}, bf16[1,1,48,64]{3,2,1,0:T(8,128)(2,1)S(1)}, u32[]{:S(2)}, u32[]{:S(2)}) collective-permute-start(bf16[1,1,48,64]{3,2,1,0:T(8,128)(2,1)S(1)} %maximum_bitcast_fusion), channel_id=1, source_target_pairs={{0,16},{16,0},{32,48},{48,32},{1,17},{17,1},{33,49},{49,33},{2,18}... | collective-permute-start | bytes 18440 | tf_op jit(solution)/shard_map/ppermute | solution.py:127
  233.9 4.3 %collective-permute-start.7 = (bf16[2,1,48,64]{3,2,1,0:T(8,128)(2,1)S(1)}, bf16[2,1,48,64]{3,2,1,0:T(8,128)(2,1)S(1)}, u32[]{:S(2)}, u32[]{:S(2)}) collective-permute-start(bf16[2,1,48,64]{3,2,1,0:T(8,128)(2,1)S(1)} %maximum_select_fusion.5), channel_id=1, source_target_pairs={{0,32},{16,48},{32,0},{48,16},{1,33},{17,49},{33,1},{49,17},{2,34}... | collective-permute-start | bytes 36872 | tf_op jit(solution)/shard_map/ppermute | solution.py:127
  241.5 3.1 collective-permute-start.6
  246.5 7.7 %collective-permute-done.6 = f32[74304]{0:T(1024)S(1)} collective-permute-done((f32[74304]{0:T(1024)S(1)}, f32[74304]{0:T(1024)S(1)}, u32[]{:S(2)}, u32[]{:S(2)}) %collective-permute-start.6) | collective-permute-done | bytes 297248 | tf_op jit(solution)/shard_map/ppermute | solution.py:89
  260.1 4.3 %collective-permute-done.8 = f32[74304]{0:T(1024)S(1)} collective-permute-done((f32[74304]{0:T(1024)S(1)}, f32[74304]{0:T(1024)S(1)}, u32[]{:S(2)}, u32[]{:S(2)}) %collective-permute-start.8) | collective-permute-done | bytes 297248 | tf_op jit(solution)/shard_map/ppermute | solution.py:89
  268.6 4.0 %collective-permute-done.11 = bf16[2,1,212,64]{2,3,1,0:T(8,128)(2,1)S(1)} collective-permute-done((bf16[2,1,212,64]{2,3,1,0:T(8,128)(2,1)S(1)}, bf16[2,1,212,64]{2,3,1,0:T(8,128)(2,1)S(1)}, u32[]{:S(2)}, u32[]{:S(2)}) %collective-permute-start.11) | collective-permute-done | bytes 54304 | tf_op jit(solution)/shard_map/ppermute | solution.py:127
  275.4 3.9 %collective-permute-start.13 = (bf16[4,1,212,64]{2,3,1,0:T(8,128)(2,1)S(1)}, bf16[4,1,212,64]{2,3,1,0:T(8,128)(2,1)S(1)}, u32[]{:S(2)}, u32[]{:S(2)}) collective-permute-start(bf16[4,1,212,64]{2,3,1,0:T(8,128)(2,1)S(1)} %maximum_select_fusion.2), channel_id=1, source_target_pairs={{0,4},{1,5},{2,6},{3,7},{4,0},{5,1},{6,2},{7,3},{8,12},{9,13},{10,... | collective-permute-start | bytes 325640 | tf_op jit(solution)/shard_map/ppermute | solution.py:127
  282.4 4.4 %collective-permute-start.14 = (bf16[8,1,212,64]{2,3,1,0:T(8,128)(2,1)S(1)}, bf16[8,1,212,64]{2,3,1,0:T(8,128)(2,1)S(1)}, u32[]{:S(2)}, u32[]{:S(2)}) collective-permute-start(bf16[8,1,212,64]{2,3,1,0:T(8,128)(2,1)S(1)} %maximum_select_fusion.1), channel_id=1, source_target_pairs={{0,8},{1,9},{2,10},{3,11},{4,12},{5,13},{6,14},{7,15},{8,0},{9,1},... | collective-permute-start | bytes 651272 | tf_op jit(solution)/shard_map/ppermute | solution.py:127
  289.2 3.0 collective-permute-done.14
  293.3 26.1 %all_gather.71 = bf16[12,4,128,64]{2,3,1,0:T(8,128)(2,1)S(1)} all-gather(bf16[1,4,128,64]{2,3,1,0:T(8,128)(2,1)S(1)} %pad_maximum_fusion.11), channel_id=1, replica_groups=mesh['face'=12,'row'=4,'col'=16] {'face'}, dimensions={0}, use_global_device_ids=true | all-gather | bytes 851968 | tf_op jit(solution)/shard_map/all_gather | solution.py:170
  (292 shorter events, 62.3 us)
Async XLA Ops:
  39.9 0.9 copy-start.1
  75.3 0.7 copy-start.4
  130.9 0.7 copy-start.5
  131.0 0.8 copy-start.3
  131.9 0.7 copy-start.7
  134.4 27.9 %collective-permute-start = (f32[74304]{0:T(1024)S(1)}, f32[74304]{0:T(1024)S(1)}, u32[]{:S(2)}, u32[]{:S(2)}) collective-permute-start(f32[74304]{0:T(1024)S(1)} %pad_maximum_fusion), channel_id=1, source_target_pairs={{0,256},{64,320},{128,384},{192,448},{256,512},{320,576},{384,640}... | collective-permute-start | bytes 891656 | tf_op jit(solution)/shard_map/ppermute | solution.py:89
  137.7 24.5 %collective-permute-start.1 = (f32[74304]{0:T(1024)S(1)}, f32[74304]{0:T(1024)S(1)}, u32[]{:S(2)}, u32[]{:S(2)}) collective-permute-start(f32[74304]{0:T(1024)S(1)} %pad_maximum_fusion), channel_id=1, source_target_pairs={{0,512},{64,576},{128,640},{192,704},{256,0},{320,64},{384,128},{4... | collective-permute-start | bytes 891656 | tf_op jit(solution)/shard_map/ppermute | solution.py:89
  162.3 28.5 %collective-permute-start.2 = (f32[74304]{0:T(1024)S(1)}, f32[74304]{0:T(1024)S(1)}, u32[]{:S(2)}, u32[]{:S(2)}) collective-permute-start(f32[74304]{0:T(1024)S(1)} %select_add_fusion), channel_id=1, source_target_pairs={{0,64},{64,0},{128,192},{192,128},{256,320},{320,256},{384,448},{4... | collective-permute-start | bytes 891656 | tf_op jit(solution)/shard_map/ppermute | solution.py:89
  201.2 11.7 %collective-permute-start.3 = (f32[74304]{0:T(1024)S(1)}, f32[74304]{0:T(1024)S(1)}, u32[]{:S(2)}, u32[]{:S(2)}) collective-permute-start(f32[74304]{0:T(1024)S(1)} %add.271), channel_id=1, source_target_pairs={{0,128},{64,192},{128,0},{192,64},{256,384},{320,448},{384,256},{4... | collective-permute-start | bytes 891656 | tf_op jit(solution)/shard_map/ppermute | solution.py:89
  213.0 20.8 %collective-permute-start.4 = (f32[74304]{0:T(1024)S(1)}, f32[74304]{0:T(1024)S(1)}, u32[]{:S(2)}, u32[]{:S(2)}) collective-permute-start(f32[74304]{0:T(1024)S(1)} %add.275), channel_id=1, source_target_pairs={{0,32},{16,48},{32,0},{48,16},{1,33},{17,49},{33,1},{49,17},{2,34}... | collective-permute-start | bytes 891656 | tf_op jit(solution)/shard_map/ppermute | solution.py:89
  222.0 11.8 %collective-permute-start.5 = (bf16[1,1,48,64]{3,2,1,0:T(8,128)(2,1)S(1)}, bf16[1,1,48,64]{3,2,1,0:T(8,128)(2,1)S(1)}, u32[]{:S(2)}, u32[]{:S(2)}) collective-permute-start(bf16[1,1,48,64]{3,2,1,0:T(8,128)(2,1)S(1)} %maximum_bitcast_fusion), channel_id=1, source_target_pairs={{0,16},{16,0},{32,48},{48,32},{1,17},{17,1},{33,49},{49,33},{2,18}... | collective-permute-start | bytes 18440 | tf_op jit(solution)/shard_map/ppermute | solution.py:127
  233.9 10.7 %collective-permute-start.7 = (bf16[2,1,48,64]{3,2,1,0:T(8,128)(2,1)S(1)}, bf16[2,1,48,64]{3,2,1,0:T(8,128)(2,1)S(1)}, u32[]{:S(2)}, u32[]{:S(2)}) collective-permute-start(bf16[2,1,48,64]{3,2,1,0:T(8,128)(2,1)S(1)} %maximum_select_fusion.5), channel_id=1, source_target_pairs={{0,32},{16,48},{32,0},{48,16},{1,33},{17,49},{33,1},{49,17},{2,34}... | collective-permute-start | bytes 36872 | tf_op jit(solution)/shard_map/ppermute | solution.py:127
  241.5 12.8 %collective-permute-start.6 = (f32[74304]{0:T(1024)S(1)}, f32[74304]{0:T(1024)S(1)}, u32[]{:S(2)}, u32[]{:S(2)}) collective-permute-start(f32[74304]{0:T(1024)S(1)} %add.276), channel_id=1, source_target_pairs={{0,16},{16,0},{32,48},{48,32},{1,17},{17,1},{33,49},{49,33},{2,18}... | collective-permute-start | bytes 891656 | tf_op jit(solution)/shard_map/ppermute | solution.py:89
  245.3 0.8 slice-start.1
  254.3 10.2 %collective-permute-start.8 = (f32[74304]{0:T(1024)S(1)}, f32[74304]{0:T(1024)S(1)}, u32[]{:S(2)}, u32[]{:S(2)}) collective-permute-start(f32[74304]{0:T(1024)S(1)} %add.278), channel_id=1, source_target_pairs={{0,8},{1,9},{2,10},{3,11},{4,12},{5,13},{6,14},{7,15},{8,0},{9,1},... | collective-permute-start | bytes 891656 | tf_op jit(solution)/shard_map/ppermute | solution.py:89
  257.0 3.1 collective-permute-start.9
  264.5 8.7 %collective-permute-start.10 = (f32[74304]{0:T(1024)S(1)}, f32[74304]{0:T(1024)S(1)}, u32[]{:S(2)}, u32[]{:S(2)}) collective-permute-start(f32[74304]{0:T(1024)S(1)} %add.280), channel_id=1, source_target_pairs={{0,4},{1,5},{2,6},{3,7},{4,0},{5,1},{6,2},{7,3},{8,12},{9,13},{10,... | collective-permute-start | bytes 891656 | tf_op jit(solution)/shard_map/ppermute | solution.py:89
  266.4 6.2 %collective-permute-start.11 = (bf16[2,1,212,64]{2,3,1,0:T(8,128)(2,1)S(1)}, bf16[2,1,212,64]{2,3,1,0:T(8,128)(2,1)S(1)}, u32[]{:S(2)}, u32[]{:S(2)}) collective-permute-start(bf16[2,1,212,64]{2,3,1,0:T(8,128)(2,1)S(1)} %maximum_select_fusion.3), channel_id=1, source_target_pairs={{0,2},{1,3},{2,0},{3,1},{4,6},{5,7},{6,4},{7,5},{8,10},{9,11},{10,... | collective-permute-start | bytes 162824 | tf_op jit(solution)/shard_map/ppermute | solution.py:127
  273.2 9.2 %collective-permute-start.12 = (f32[74304]{0:T(1024)S(1)}, f32[74304]{0:T(1024)S(1)}, u32[]{:S(2)}, u32[]{:S(2)}) collective-permute-start(f32[74304]{0:T(1024)S(1)} %add.282), channel_id=1, source_target_pairs={{0,2},{1,3},{2,0},{3,1},{4,6},{5,7},{6,4},{7,5},{8,10},{9,11},{10,... | collective-permute-start | bytes 891656 | tf_op jit(solution)/shard_map/ppermute | solution.py:89
  275.4 6.9 %collective-permute-start.13 = (bf16[4,1,212,64]{2,3,1,0:T(8,128)(2,1)S(1)}, bf16[4,1,212,64]{2,3,1,0:T(8,128)(2,1)S(1)}, u32[]{:S(2)}, u32[]{:S(2)}) collective-permute-start(bf16[4,1,212,64]{2,3,1,0:T(8,128)(2,1)S(1)} %maximum_select_fusion.2), channel_id=1, source_target_pairs={{0,4},{1,5},{2,6},{3,7},{4,0},{5,1},{6,2},{7,3},{8,12},{9,13},{10,... | collective-permute-start | bytes 325640 | tf_op jit(solution)/shard_map/ppermute | solution.py:127
  282.4 9.8 %collective-permute-start.14 = (bf16[8,1,212,64]{2,3,1,0:T(8,128)(2,1)S(1)}, bf16[8,1,212,64]{2,3,1,0:T(8,128)(2,1)S(1)}, u32[]{:S(2)}, u32[]{:S(2)}) collective-permute-start(bf16[8,1,212,64]{2,3,1,0:T(8,128)(2,1)S(1)} %maximum_select_fusion.1), channel_id=1, source_target_pairs={{0,8},{1,9},{2,10},{3,11},{4,12},{5,13},{6,14},{7,15},{8,0},{9,1},... | collective-permute-start | bytes 651272 | tf_op jit(solution)/shard_map/ppermute | solution.py:127
  287.1 39.4 %collective-permute-start.15 = (f32[74304]{0:T(1024)S(1)}, f32[74304]{0:T(1024)S(1)}, u32[]{:S(2)}, u32[]{:S(2)}) collective-permute-start(f32[74304]{0:T(1024)S(1)} %add.284), channel_id=1, source_target_pairs={{0,1},{1,0},{2,3},{3,2},{4,5},{5,4},{6,7},{7,6},{8,9},{9,8},{10,11... | collective-permute-start | bytes 891656 | tf_op jit(solution)/shard_map/ppermute | solution.py:89
  326.6 0.7 copy-start
  327.4 0.7 slice-start
  (2 other events, 1.1 us)
